TPU v7x, 128 devices: a whole 4x4x4 slice. The times are simulated.
128 devices in a mesh: sec: 4 (over z_hi, core), pts: 32 (over x, z_lo, y).
Axes of the slice: x: 4, y: 4, z: 4 (z_hi: 2, z_lo: 2; z = z_hi * 2 + z_lo), core: 2. Of those that a mesh axis runs over, the one named last changes fastest.
Arguments:
- points: bfloat16 [4, 32768, 1024], P('sec', 'pts'), may hold values from -10 to 10
- counts: int32 [4, 32], P('sec', 'pts'), may hold values from 256 to 1024, as said below
- input_gain: float32 [4, 1024], P('sec'), may hold values from 0.1 to 1.9
- key_weight: bfloat16 [4, 1024, 1024], P('sec', 'pts'), may hold values from -0.375 to 0.375
- value_weight: bfloat16 [4, 1024, 1024], P('sec', 'pts'), may hold values from -0.375 to 0.375
- query_weight: bfloat16 [1024, 1024], replicated, may hold values from -0.1875 to 0.1875
- output_weight: bfloat16 [1024, 1024], replicated, may hold values from -0.75 to 0.75
- middle_gain: float32 [1024], replicated, may hold values from 0.1 to 1.9
- up_weight: bfloat16 [1024, 4096], P(None, 'sec'), may hold values from -0.1875 to 0.1875
- down_weight: bfloat16 [4096, 1024], P('sec'), may hold values from -0.09375 to 0.09375
Outputs:
- updated: bfloat16 [32768, 1024], P('pts', 'sec')
Inputs may be any that keep to these rules, and one draw needn't show every extreme that they name: `counts`: each block has 1024 slots; in every section some block is full.
All inputs are finite; a program needn't handle non-finite values.
Results may differ from a plain program's by a relative error of at most 0.0049.
Values may be sent and summed in bfloat16 or wider, within the bound.
No kernel may reach another device: no remote copies, remote signals or barrier semaphores. Data moves between devices by JAX's collectives and lax.ppermute only.
A program may use at most 128 MiB of HBM per device.

v0:
```python
import jax
import jax.numpy as jnp
from jax import lax
from jax.sharding import PartitionSpec as P

HEAD_DIM = 128


def broadcast(value, axis, root):
    mine = lax.axis_index(axis) == root
    return lax.psum(jnp.where(mine, value, jnp.zeros_like(value)), axis)


def layer_normalizer(values, gain):
    mean = jnp.mean(values, axis=-1, keepdims=True)
    centred = values - mean
    spread = jnp.mean(centred * centred, axis=-1, keepdims=True)
    return centred * lax.rsqrt(spread + 1e-05) * gain


def feature_map(values):
    return jax.nn.elu(values) + 1.0


def on_device(
    points,
    counts,
    input_gain,
    key_weight,
    value_weight,
    query_weight,
    output_weight,
    middle_gain,
    up_weight,
    down_weight,
):
    block = points[0]
    rows = block.shape[0]
    width = block.shape[1]
    heads = width // HEAD_DIM
    sections = lax.axis_size("sec")
    normed = layer_normalizer(block.astype(jnp.float32), input_gain[0]).astype(jnp.bfloat16)

    def add_rows(piece):
        return jnp.dot(normed, piece[0], preferred_element_type=jnp.float32)

    summed_keys = add_rows(lax.all_gather(key_weight, "pts", axis=1, tiled=True))
    value_sums = add_rows(lax.all_gather(value_weight, "pts", axis=1, tiled=True))
    valid = jnp.arange(rows) < counts[0, 0]
    key_feats = feature_map(summed_keys).astype(jnp.bfloat16)
    key_feats = jnp.where(valid[:, None], key_feats, jnp.zeros_like(key_feats))
    value_rows = value_sums.astype(jnp.bfloat16)
    local_state = jnp.einsum(
        "yzl,yzn->zln",
        key_feats.reshape(rows, heads, HEAD_DIM),
        value_rows.reshape(rows, heads, HEAD_DIM),
        preferred_element_type=jnp.float32,
    ).reshape(width, HEAD_DIM)
    local_total = jnp.sum(key_feats.astype(jnp.float32), axis=0)
    part_state, part_total = (
        lax.all_gather(local_state[None], "sec", axis=0, tiled=True),
        lax.all_gather(local_total[None], "sec", axis=0, tiled=True),
    )
    state_matrices, totals = lax.psum((part_state, part_total), "pts")
    query_feats = feature_map(
        jnp.dot(normed, query_weight, preferred_element_type=jnp.float32)
    ).astype(jnp.bfloat16)
    query_feats = lax.optimization_barrier(query_feats)
    per_head_queries = query_feats.astype(jnp.float32).reshape(rows, heads, HEAD_DIM)
    state_heads = state_matrices.reshape(sections, heads, HEAD_DIM, HEAD_DIM)
    total_heads = totals.reshape(sections, heads, HEAD_DIM)
    numerator = jnp.einsum(
        "rhk,shkv->srhv", per_head_queries, state_heads, precision=lax.Precision.HIGHEST
    )
    denom = jnp.einsum(
        "rhk,shk->srh", per_head_queries, total_heads, precision=lax.Precision.HIGHEST
    )
    attended = (
        jnp.sum(numerator / denom[:, :, :, None], axis=0).reshape(rows, width).astype(jnp.bfloat16)
    )
    mixed = block.astype(jnp.float32) + jnp.dot(
        attended, output_weight, preferred_element_type=jnp.float32
    )
    centred = layer_normalizer(mixed, middle_gain).astype(jnp.bfloat16)
    shared = broadcast(centred, "sec", sections - 1)
    hidden = jax.nn.gelu(
        jnp.dot(shared, up_weight, preferred_element_type=jnp.float32), approximate=True
    ).astype(jnp.bfloat16)
    is_query = (lax.axis_index("sec") == sections - 1).astype(jnp.float32)
    term = jnp.dot(hidden, down_weight, preferred_element_type=jnp.float32) + is_query * mixed
    return lax.psum_scatter(term, "sec", scatter_dimension=1, tiled=True).astype(jnp.bfloat16)


def solution(mesh):
    placed = (
        P("sec", "pts", None),
        P("sec", "pts"),
        P("sec", None),
        P("sec", "pts", None),
        P("sec", "pts", None),
        P(),
        P(),
        P(),
        P(None, "sec"),
        P("sec", None),
    )
    return jax.shard_map(
        on_device, mesh=mesh, in_specs=placed, out_specs=P("pts", "sec"), check_vma=False
    )
```

profile of v0, /device:TPU:16, one launch (start us, length us, event | category | flops | bytes accessed | tf_op | source)
XLA Modules:
  0.0 816.8 jit_solution(15731884587893129483)
XLA Ops:
  6.5 0.7 all-gather.7.cloned.1.call-update
  7.3 0.7 all-gather.5.cloned.1.call-update
  8.0 0.0 all-gather.9.cloned.1.call-start
  8.7 4.0 copy.41
  12.7 2.1 convert_reduce_fusion
  14.8 0.1 copy-done.1
  14.9 0.6 fusion.5
  15.5 143.7 %all-gather.7.cloned.1.call-done = bf16[1,1024,1024]{2,1,0:T(8,128)(2,1)} async-done(((bf16[1,32,1024]{2,1,0:T(8,128)(2,1)}), bf16[1,1024,1024]{2,1,0:T(8,128)(2,1)}) %all-gather.7.cloned.1.call-update) | async-done | bytes 2097168 | tf_op jit(solution)/shard_map/all_gather | solution.py:48
  159.2 6.2 fusion.45
  165.4 148.2 %all-gather.5.cloned.1.call-done = bf16[1,1024,1024]{2,1,0:T(8,128)(2,1)} async-done(((bf16[1,32,1024]{2,1,0:T(8,128)(2,1)}), bf16[1,1024,1024]{2,1,0:T(8,128)(2,1)}) %all-gather.5.cloned.1.call-update) | async-done | bytes 2097168 | tf_op jit(solution)/shard_map/all_gather | solution.py:47
  313.6 6.8 convert_reduce_fusion.1
  320.3 1.5 fusion.61
  321.9 0.0 all-reduce.3.cloned.1.call-start
  321.9 31.6 %all-gather.9.cloned.1.call-done = f32[4,1024,128]{2,1,0:T(8,128)} async-done(((f32[1,1024,128]{2,1,0:T(8,128)}), f32[4,1024,128]{2,1,0:T(8,128)}) %all-gather.9.cloned.1.call-update) | async-done | bytes 2097168 | tf_op jit(solution)/shard_map/all_gather | solution.py:61
  353.5 2.9 copy.43
  356.4 0.2 all-reduce.5.cloned.1.call-start
  356.7 7.6 fusion.24
  364.2 6.7 all-gather
  370.9 151.9 %psum.22 = f32[4,8,128]{2,0,1:T(4,128)S(1)} all-reduce(f32[4,8,128]{2,0,1:T(4,128)S(1)} %copy.48), channel_id=1, replica_groups=mesh['sec'=4,'pts'=32] {'pts'}, use_global_device_ids=true, to_apply=%region_4.5 | all-reduce | flops 4096 | bytes 32768 | tf_op jit(solution)/shard_map/psum | solution.py:64
  522.8 2.5 convolution_bitcast_fusion
  525.3 140.1 %all-reduce.3.cloned.1.call-done = f32[4,8,128,128]{2,3,0,1:T(8,128)} async-done(((f32[4,8,128,128]{2,3,0,1:T(8,128)}), f32[4,8,128,128]{2,3,0,1:T(8,128)}) %all-reduce.3.cloned.1.call-update) | async-done | bytes 2097168 | tf_op jit(solution)/shard_map/psum | solution.py:64
  665.5 9.9 %fusion = bf16[1024,8,128]{0,2,1:T(8,128)(2,1)S(1)} fusion(f32[4,8,128,128]{2,3,0,1:T(8,128)} %all-reduce.3.cloned.1.call-done, bf16[1024,8,128,1]{0,2,3,1:T(8,128)(2,1)} %bitcast.71, f32[4,1024,8]{1,0,2:T(4,128)S(1)} %convolution_bitcast_fusion), kind=kOutput, calls=%fused_computation.1 | convolution fusion | flops 6449790976 | bytes 6422528 | tf_op jit(solution)/shard_map/rhk,shkv->srhv/dot_general | solution.py:72
  675.4 2.6 fusion.58
  678.1 0.5 multiply_reduce_fusion
  678.6 1.4 copy-done.3
  680.0 2.0 fusion.25
  682.0 0.3 reduce-scatter.2.cloned.1.call-start
  682.3 63.1 %all-reduce.5.cloned.1.call-done = bf16[1024,1024]{0,1:T(8,128)(2,1)} async-done(((bf16[1024,1024]{0,1:T(8,128)(2,1)}), bf16[1024,1024]{0,1:T(8,128)(2,1)}) %all-reduce.5.cloned.1.call-update) | async-done | bytes 2097168 | tf_op jit(solution)/shard_map/psum | solution.py:11
  745.4 11.3 %multiply_add_fusion = f32[1024,1024]{0,1:T(8,128)} fusion(f32[1024,1024]{0,1:T(8,128)} %copy-done.3, f32[]{:T(128)S(6)} %convert_element_type.62, bf16[1024,1024]{1,0:T(8,128)(2,1)} %param.19, bf16[1024,1024]{0,1:T(8,128)(2,1)} %all-reduce.5.cloned.1.call-done, bf16[1024,1024]{1,0:T(8,128)(2,1)} %param.18), kind=kOutput, calls=%fused_computation.34 | convolution fusion | flops 4306501632 | bytes 14680068 | tf_op jit(solution)/shard_map/dot_general | solution.py:90
  756.7 51.0 %reduce-scatter.2.cloned.1.call-done = f32[1024,256]{0,1:T(8,128)} async-done(((f32[1024,1024]{0,1:T(8,128)}), f32[1024,256]{0,1:T(8,128)}) %reduce-scatter.2.cloned.1.call-update) | async-done | bytes 1048592 | tf_op jit(solution)/shard_map/reduce_scatter | solution.py:91
  807.7 1.3 convert_element_type.63
  809.0 1.0 copy.56
  (24 shorter events, 0.2 us)
Async XLA Ops:
  6.5 668.9 %copy-start = (bf16[1024,1024]{1,0:T(8,128)(2,1)S(1)}, bf16[1024,1024]{1,0:T(8,128)(2,1)}, u32[]{:S(2)}) copy-start(bf16[1024,1024]{1,0:T(8,128)(2,1)} %param.16) | copy-start | bytes 6291460
  6.5 152.6 %all-gather.7.cloned.1.call-start = ((), (), s32[]{:S(2)}) async-start(), calls=%async_computation.2 | async-start | bytes 2162688 | tf_op jit(solution)/shard_map/all_gather | solution.py:48
  7.3 306.3 %all-gather.5.cloned.1.call-start = ((), (), s32[]{:S(2)}) async-start(), calls=%async_computation.1 | async-start | bytes 2162688 | tf_op jit(solution)/shard_map/all_gather | solution.py:47
  8.0 345.5 %all-gather.9.cloned.1.call-start = ((), (), s32[]{:S(2)}) async-start(), calls=%async_computation.3 | async-start | bytes 2621440 | tf_op jit(solution)/shard_map/all_gather | solution.py:61
  12.7 2.2 copy-start.1
  12.7 146.5 %copy-start.6 = (f32[1,1024]{1,0:T(1,128)S(1)}, f32[1,1024]{1,0:T(1,128)}, u32[]{:S(2)}) copy-start(f32[1,1024]{1,0:T(1,128)} %param.12) | copy-start | bytes 12292
  313.6 6.8 copy-start.4
  321.9 343.6 %all-reduce.3.cloned.1.call-start = ((), (), s32[]{:S(2)}) async-start(), calls=%async_computation.4 | async-start | bytes 4194304 | tf_op jit(solution)/shard_map/psum | solution.py:64
  356.4 389.0 %all-reduce.5.cloned.1.call-start = ((), (), s32[]{:S(2)}) async-start(), calls=%async_computation.5 | async-start | bytes 4194304 | tf_op jit(solution)/shard_map/psum | solution.py:11
  665.5 10.0 %copy-start.2 = (bf16[1,1024,1024]{1,2,0:T(8,128)(2,1)S(1)}, bf16[1,1024,1024]{1,2,0:T(8,128)(2,1)}, u32[]{:S(2)}) copy-start(bf16[1,1024,1024]{1,2,0:T(8,128)(2,1)} %copy.41) | copy-start | bytes 6291460
  678.1 1.9 copy-start.3
  678.1 1.9 copy-start.5
  682.0 125.7 %reduce-scatter.2.cloned.1.call-start = ((), (), s32[]{:S(2)}) async-start(), calls=%async_computation.6 | async-start | bytes 5242880 | tf_op jit(solution)/shard_map/reduce_scatter | solution.py:91
Sparse Core Ops, SparseCore 0:
  9.0 150.1 all-gather.6
  160.8 152.6 all-gather.4
  322.0 31.4 all-gather.8
  356.5 308.8 all-reduce.2
  682.1 63.2 all-reduce.4
  756.8 50.8 reduce-scatter.1
where the time goes:
time: 818 us; the launch traced here: 817 us
  waiting for transfers between devices  579 us (71%)
  blocking collectives  159 us (19%)
  matrix products  48.4 us (6%)
  between operations  14.2 us (2%)
  local copies, waits for them, and re-layouts  9.38 us (1%)
    psum x1, blocking collectives, on_device(): state_matrices, totals = lax.psum((part_state, part_total), 'pts')  152 us
    all_gather x1, waiting for transfers between devices, on_device(): lax.all_gather(key_weight, 'pts', axis=1, tiled=True)  148 us
    all_gather x1, waiting for transfers between devices, on_device(): lax.all_gather(value_weight, 'pts', axis=1, tiled=True)  144 us
    psum x1, waiting for transfers between devices, on_device(): state_matrices, totals = lax.psum((part_state, part_total), 'pts')  140 us
    psum x1, waiting for transfers between devices, broadcast(): return lax.psum(jnp.where(mine, value, jnp.zeros_like(value)), axis)  63.1 us
    reduce_scatter x1, waiting for transfers between devices, on_device(): lax.psum_scatter(term, 'sec', scatter_dimension=1, tiled=True)  51 us
    all_gather x1, waiting for transfers between devices, on_device(): lax.all_gather(local_state[None], 'sec', axis=0, tiled=True)  31.6 us
  transfers between devices with their start and end apart: 6, of which 6 were waited for; matrix products, arithmetic and copies ran while one was open for 3% of the time, Pallas kernels for 0%

commit v1 on v0

v1 whole, which is shorter than its diff:
```python
import jax
import jax.numpy as jnp
from jax import lax
from jax.sharding import PartitionSpec as P

HEAD_DIM = 128


def layer_normalizer(values, gain):
    mean = jnp.mean(values, axis=-1, keepdims=True)
    centred = values - mean
    spread = jnp.mean(centred * centred, axis=-1, keepdims=True)
    return centred * lax.rsqrt(spread + 1e-05) * gain


def feature_map(values):
    return jax.nn.elu(values) + 1.0


def from_last(value, axis, sections):
    me = lax.axis_index(axis)
    last = sections - 1
    if sections != 4:
        out = value
        for target in range(last):
            got = lax.ppermute(value, axis, [(last, target)])
            out = jnp.where(me == target, got, out)
        return out
    far = lax.ppermute(value, axis, [(3, 1)])
    near = lax.ppermute(value, axis, [(3, 2)])
    farther = lax.ppermute(far, axis, [(1, 0)])
    return jnp.where(
        me == 3, value, jnp.where(me == 2, near, jnp.where(me == 1, far, farther))
    )


def gather_a2a(value, axis, count):
    spread = jnp.broadcast_to(value[None], (count,) + value.shape)
    return lax.all_to_all(spread, axis, 0, 0, tiled=False)


def on_device(
    points,
    counts,
    input_gain,
    key_weight,
    value_weight,
    query_weight,
    output_weight,
    middle_gain,
    up_weight,
    down_weight,
):
    block = points[0]
    rows = block.shape[0]
    width = block.shape[1]
    heads = width // HEAD_DIM
    sections = lax.axis_size("sec")
    blocks = lax.axis_size("pts")
    me = lax.axis_index("sec")

    query_block = from_last(block, "sec", sections)
    query_gain = from_last(input_gain[0], "sec", sections)

    stacked = jnp.concatenate([key_weight[0], value_weight[0]], axis=1)
    weights = gather_a2a(stacked, "pts", blocks).reshape(width, 2 * width)

    normed = layer_normalizer(block.astype(jnp.float32), input_gain[0]).astype(jnp.bfloat16)
    projected = jnp.dot(normed, weights, preferred_element_type=jnp.float32)
    valid = jnp.arange(rows) < counts[0, 0]
    key_feats = feature_map(projected[:, :width]).astype(jnp.bfloat16)
    key_feats = jnp.where(valid[:, None], key_feats, jnp.zeros_like(key_feats))
    value_rows = projected[:, width:].astype(jnp.bfloat16)
    local_state = jnp.einsum(
        "yzl,yzn->zln",
        key_feats.reshape(rows, heads, HEAD_DIM),
        value_rows.reshape(rows, heads, HEAD_DIM),
        preferred_element_type=jnp.float32,
    ).reshape(width, HEAD_DIM)
    local_total = jnp.sum(key_feats.astype(jnp.float32), axis=0).reshape(heads, HEAD_DIM)

    packed_rows = width + heads
    piece = -(-packed_rows // blocks)
    packed = jnp.concatenate(
        [
            local_state,
            local_total,
            jnp.zeros((piece * blocks - packed_rows, HEAD_DIM), jnp.float32),
        ],
        axis=0,
    ).reshape(blocks, piece, HEAD_DIM)
    reduced = jnp.sum(lax.all_to_all(packed, "pts", 0, 0, tiled=False), axis=0)
    by_section = gather_a2a(reduced, "sec", sections)
    whole = gather_a2a(by_section, "pts", blocks)
    whole = whole.transpose(1, 0, 2, 3).reshape(sections, blocks * piece, HEAD_DIM)
    state_heads = whole[:, :width].reshape(sections, heads, HEAD_DIM, HEAD_DIM)
    total_heads = whole[:, width:packed_rows].reshape(sections, heads, HEAD_DIM)

    query_normed = layer_normalizer(query_block.astype(jnp.float32), query_gain).astype(
        jnp.bfloat16
    )
    query_feats = feature_map(
        jnp.dot(query_normed, query_weight, preferred_element_type=jnp.float32)
    ).astype(jnp.bfloat16)
    per_head_queries = query_feats.astype(jnp.float32).reshape(rows, heads, HEAD_DIM)
    numerator = jnp.einsum(
        "rhk,shkv->srhv", per_head_queries, state_heads, precision=lax.Precision.HIGHEST
    )
    denom = jnp.einsum(
        "rhk,shk->srh", per_head_queries, total_heads, precision=lax.Precision.HIGHEST
    )
    attended = (
        jnp.sum(numerator / denom[:, :, :, None], axis=0).reshape(rows, width).astype(jnp.bfloat16)
    )
    mixed = query_block.astype(jnp.float32) + jnp.dot(
        attended, output_weight, preferred_element_type=jnp.float32
    )
    centred = layer_normalizer(mixed, middle_gain).astype(jnp.bfloat16)
    hidden = jax.nn.gelu(
        jnp.dot(centred, up_weight, preferred_element_type=jnp.float32), approximate=True
    ).astype(jnp.bfloat16)
    term = jnp.dot(hidden, down_weight, preferred_element_type=jnp.float32)
    share = width // sections
    parts = term.astype(jnp.bfloat16).reshape(rows, sections, share).transpose(1, 0, 2)
    summed = jnp.sum(lax.all_to_all(parts, "sec", 0, 0, tiled=False).astype(jnp.float32), axis=0)
    own_mixed = lax.dynamic_slice_in_dim(mixed, me * share, share, axis=1)
    return (own_mixed + summed).astype(jnp.bfloat16)


def solution(mesh):
    placed = (
        P("sec", "pts", None),
        P("sec", "pts"),
        P("sec", None),
        P("sec", "pts", None),
        P("sec", "pts", None),
        P(),
        P(),
        P(),
        P(None, "sec"),
        P("sec", None),
    )
    return jax.shard_map(
        on_device, mesh=mesh, in_specs=placed, out_specs=P("pts", "sec"), check_vma=False
    )
```

time: 818 us -> 245 us (0.30)
  waiting for transfers between devices: 579 us -> 105 us
  blocking collectives: 159 us -> 28.1 us
  starting transfers between devices: 0.61 us -> 27.3 us
  local copies, waits for them, and re-layouts: 9.38 us -> 23.9 us
  between operations: 14.2 us -> 1.08 us
  other arithmetic: 6.49 us -> 17.1 us
    all_gather x3 -> x0, waiting for transfers between devices: 323 us -> none  [the longest x1 148 us: on_device(): lax.all_gather(key_weight, 'pts', axis=1, tiled=True)]
    psum x2 -> x0, waiting for transfers between devices: 203 us -> none  [the longest x1 140 us: on_device(): state_matrices, totals = lax.psum((part_state, part_total), 'pts')]
    psum x1 -> x0, blocking collectives: 152 us -> none  [on_device(): state_matrices, totals = lax.psum((part_state, part_total), 'pts')]
    ppermute x0 -> x6, waiting for transfers between devices: none -> 77.9 us  [the longest x2 77.9 us: from_last(): farther = lax.ppermute(far, axis, [(1, 0)])]
    reduce_scatter x1 -> x0, waiting for transfers between devices: 51 us -> none  [on_device(): lax.psum_scatter(term, 'sec', scatter_dimension=1, tiled=True)]
    all_to_all x0 -> x2, blocking collectives: none -> 28.1 us  [the longest x1 20 us: on_device(): reduced = jnp.sum(lax.all_to_all(packed, 'pts', 0, 0, tiled=False), axis=0)]
    all_to_all x0 -> x3, waiting for transfers between devices: none -> 27.2 us  [the longest x1 27.2 us: on_device(): lax.all_to_all(parts, 'sec', 0, 0, tiled=False).astype(jnp.float32)]
    all_to_all x0 -> x3, starting transfers between devices: none -> 19.2 us  [the longest x2 14.8 us: gather_a2a(): return lax.all_to_all(spread, axis, 0, 0, tiled=False)]
  transfers between devices with their start and end apart: 6 -> 9, of which waited for: 6 -> 3; matrix products, arithmetic and copies ran while one was open for 3% -> 8% of each run, Pallas kernels for 0% -> 0%
where the time goes in v1:
time: 245 us; the launch traced here: 244 us
  waiting for transfers between devices  105 us (43%)
  matrix products  41.4 us (17%)
  blocking collectives  28.1 us (11%)
  starting transfers between devices  27.3 us (11%)
  local copies, waits for them, and re-layouts  23.9 us (10%)
  other arithmetic  17.1 us (7%)
    ppermute x2, waiting for transfers between devices, from_last(): farther = lax.ppermute(far, axis, [(1, 0)])  77.9 us
    all_to_all x1, waiting for transfers between devices, on_device(): lax.all_to_all(parts, 'sec', 0, 0, tiled=False).astype(jnp.float32)  27.2 us
    all_to_all x1, blocking collectives, on_device(): reduced = jnp.sum(lax.all_to_all(packed, 'pts', 0, 0, tiled=False), axis=0)  20 us
    all_to_all x2, starting transfers between devices, gather_a2a(): return lax.all_to_all(spread, axis, 0, 0, tiled=False)  14.8 us
    unnamed x24, local copies, waits for them, and re-layouts  12.8 us
    dot_general x1, matrix products, on_device(): term = jnp.dot(hidden, down_weight, preferred_element_type=jnp.float32)  10.2 us
    dot_general x1, matrix products, on_device(): jnp.einsum('rhk,shkv->srhv', per_head_queries, state_heads, precision=lax...  8.47 us
    all_to_all x1, blocking collectives, gather_a2a(): return lax.all_to_all(spread, axis, 0, 0, tiled=False)  8.08 us
  transfers between devices with their start and end apart: 9, of which 3 were waited for; matrix products, arithmetic and copies ran while one was open for 8% of the time, Pallas kernels for 0%

profile of v1, /device:TPU:16, one launch (start us, length us, event | category | flops | bytes accessed | tf_op | source)
XLA Modules:
  0.0 244.0 jit_solution(18196368116831032152)
XLA Ops:
  0.0 4.1 %copy.31 = bf16[1,1024,1024]{1,2,0:T(8,128)(2,1)} copy(bf16[1,1024,1024]{2,1,0:T(8,128)(2,1)} %param.10) | data formatting | bytes 4194304 | tf_op args[0]
  4.1 2.0 collective-permute-start.1
  6.1 2.5 %broadcast_in_dim.23 = bf16[32,32,2048]{2,1,0:T(8,128)(2,1)} broadcast(bf16[32,2048]{1,0:T(8,128)(2,1)S(1)} %pad_maximum_fusion), dimensions={1,2} | broadcast | bytes 4325376 | tf_op jit(solution)/shard_map/broadcast_in_dim | solution.py:38
  8.6 8.8 %all-to-all-start = ((bf16[32,32,2048]{2,1,0:T(8,128)(2,1)}), bf16[32,32,2048]{2,1,0:T(8,128)(2,1)}, u32[]{:S(2)}, u32[]{:S(2)}) async-start(bf16[32,32,2048]{2,1,0:T(8,128)(2,1)} %broadcast_in_dim.23), calls=%async_computation | async-start | bytes 8388608 | tf_op jit(solution)/shard_map/all_to_all | solution.py:39
  17.4 2.0 collective-permute-start
  21.6 2.0 convert_reduce_fusion.1
  23.6 57.7 %collective-permute-done.2 = bf16[1024,1024]{0,1:T(8,128)(2,1)} collective-permute-done((bf16[1024,1024]{0,1:T(8,128)(2,1)}, bf16[1024,1024]{0,1:T(8,128)(2,1)}, u32[]{:S(2)}, u32[]{:S(2)}) %collective-permute-start.2) | collective-permute-done | bytes 2097184 | tf_op jit(solution)/shard_map/ppermute | solution.py:31
  81.3 5.1 %convert_reduce_fusion = (f32[1024]{0:T(1024)S(1)}, bf16[1024,1024]{0,1:T(8,128)(2,1)}, f32[1024]{0:T(1024)S(1)}) fusion(bf16[1024,1024]{0,1:T(8,128)(2,1)} %collective-permute-done, bf16[1024,1024]{0,1:T(8,128)(2,1)} %collective-permute-done.1, bf16[1024,1024]{0,1:T(8,128)(2,1)} %collective-permute-done.2, pred[]{:T(512)S(6)} %eq.14, pred[]{:T(512)S(6)} %eq.13, ...), kind=kLoop, calls=%fused_computation.9 | loop fusion | flops 9435136 | bytes 10498051 | tf_op jit(solution)/shard_map/reduce_sum | solution.py:10
  86.4 7.1 %fusion.23 = f32[1024,2048]{1,0:T(8,128)S(1)} fusion(bf16[1024,2048]{1,0:T(8,128)(2,1)} %bitcast.6, bf16[1,1024,1024]{2,1,0:T(8,128)(2,1)} %param.10, f32[1024]{0:T(1024)S(1)} %bitcast.70, f32[1024]{0:T(1024)S(1)} %add_rsqrt_fusion.2, f32[1024]{0:T(1024)S(1)} %broadcast_multiply_fusion.2), kind=kOutput, calls=%fused_computation.40 | convolution fusion | flops 4300210176 | bytes 14692352 | tf_op jit(solution)/shard_map/dot_general | solution.py:69
  93.5 3.2 %copy-done.2 = f32[1024,2048]{1,0:T(8,128)} copy-done((f32[1024,2048]{1,0:T(8,128)}, f32[1024,2048]{1,0:T(8,128)S(1)}, u32[]{:S(2)}) %copy-start.2) | copy-done | bytes 8388632
  96.7 3.6 %convert_reduce_fusion.3 = (f32[1024]{0:T(1024)S(1)}, bf16[1024,1024]{1,0:T(8,128)(2,1)}) fusion(f32[1024,2048]{1,0:T(8,128)S(1)} %fusion.23, pred[1024]{0:T(1024)(128)(4,1)S(1)} %iota_compare_fusion), kind=kLoop, calls=%fused_computation.37 | loop fusion | flops 8387584 | bytes 6296576 | tf_op jit(solution)/shard_map/reduce_sum | solution.py:80
  100.3 3.9 %copy.46 = bf16[1024,1024]{0,1:T(8,128)(2,1)} copy(bf16[1024,1024]{1,0:T(8,128)(2,1)} %get-tuple-element.8) | data formatting | bytes 4194304 | tf_op jit(solution)/shard_map/reshape | solution.py:76
  104.3 3.6 %fusion.35 = f32[8,128,128]{2,1,0:T(8,128)S(1)} fusion(bf16[1024,8,128]{0,2,1:T(8,128)(2,1)} %bitcast.61, f32[1024,2048]{1,0:T(8,128)} %copy-done.2), kind=kOutput, calls=%fused_computation.49 | convolution fusion | flops 268435456 | bytes 4718592 | tf_op jit(solution)/shard_map/yzl,yzn->zln/dot_general | solution.py:74
  108.1 20.0 %all_to_all.25 = f32[32,33,128]{2,1,0:T(8,128)S(1)} all-to-all(f32[32,33,128]{2,1,0:T(8,128)S(1)} %reshape.104), channel_id=1, replica_groups=mesh['sec'=4,'pts'=32] {'pts'}, dimensions={0} | all-to-all | bytes 1081344 | tf_op jit(solution)/shard_map/all_to_all | solution.py:92
  128.2 8.1 %all_to_all.26 = f32[4,33,128]{2,1,0:T(8,128)S(1)} all-to-all(f32[4,33,128]{2,1,0:T(8,128)S(1)} %broadcast_in_dim.26), channel_id=1, replica_groups=mesh['sec'=4,'pts'=32] {'sec'}, dimensions={0} | all-to-all | bytes 135168 | tf_op jit(solution)/shard_map/all_to_all | solution.py:39
  136.3 1.6 broadcast_in_dim.27
  137.9 6.0 %all-to-all-start.3 = ((f32[32,4,33,128]{3,1,2,0:T(4,128)}), f32[32,4,33,128]{3,1,2,0:T(4,128)}, u32[]{:S(2)}, u32[]{:S(2)}) async-start(f32[32,4,33,128]{3,1,2,0:T(4,128)} %broadcast_in_dim.27), calls=%async_computation.3 | async-start | bytes 4325376 | tf_op jit(solution)/shard_map/all_to_all | solution.py:39
  145.3 1.5 collective-permute-start.5
  146.8 20.1 %collective-permute-done.5 = f32[1024]{0:T(1024)S(1)} collective-permute-done((f32[1024]{0:T(1024)S(1)}, f32[1024]{0:T(1024)S(1)}, u32[]{:S(2)}, u32[]{:S(2)}) %collective-permute-start.5) | collective-permute-done | bytes 4128 | tf_op jit(solution)/shard_map/ppermute | solution.py:31
  166.9 2.2 fusion.3
  169.1 6.2 %fusion.21 = bf16[1024,1024]{1,0:T(8,128)(2,1)S(1)} fusion(bf16[1024,1024]{1,0:T(8,128)(2,1)} %param.15, bf16[1024,1024]{0,1:T(8,128)(2,1)} %get-tuple-element.6, f32[1024]{0:T(1024)S(1)} %select_select_fusion.1, f32[1024]{0:T(1024)S(1)} %add_rsqrt_fusion.1, f32[1024]{0:T(1024)S(1)} %broadcast_multiply_fusion.1), kind=kOutput, calls=%fused_computation.32 | convolution fusion | flops 2157969408 | bytes 6303744 | tf_op jit(solution)/shard_map/dot_general | solution.py:103
  176.6 2.0 copy.54
  178.6 3.3 %fusion.58 = f32[4,1024,8]{1,0,2:T(4,128)S(1)} fusion(f32[4,1056,128]{2,0,1:T(4,128)} %bitcast.11, bf16[1024,1024]{1,0:T(8,128)(2,1)} %copy-done.5), kind=kOutput, calls=%fused_computation.69 | convolution fusion | flops 50331648 | bytes 4390912 | tf_op jit(solution)/shard_map/rhk,shk->srh/dot_general | solution.py:109
  181.9 1.9 slice.19
  184.2 8.5 %fusion = bf16[1024,8,128]{0,2,1:T(8,128)(2,1)S(1)} fusion(f32[4,1024,8]{1,0,2:T(4,128)S(1)} %fusion.58, bf16[1024,8,128,1]{2,1,0,3:T(8,128)(2,1)S(1)} %bitcast.64, f32[4,8,128,128]{3,0,2,1:T(4,128)S(1)} %bitcast.65), kind=kOutput, calls=%fused_computation.1 | convolution fusion | flops 6449790976 | bytes 6422528 | tf_op jit(solution)/shard_map/rhk,shkv->srhv/dot_general | solution.py:106
  192.7 2.6 %fusion.66 = (f32[1024]{0:T(1024)S(1)}, f32[1024,1024]{0,1:T(8,128)S(1)}) fusion(bf16[1024,1024]{0,1:T(8,128)(2,1)S(1)} %bitcast.74, bf16[1024,1024]{1,0:T(8,128)(2,1)S(1)} %copy-done, bf16[1024,1024]{0,1:T(8,128)(2,1)S(1)} %copy-done.3), kind=kOutput, calls=%fused_computation.85 | convolution fusion | flops 2150628352 | bytes 10489856 | tf_op jit(solution)/shard_map/dot_general | solution.py:115
  195.3 1.9 copy-done.4
  197.7 10.2 %fusion.53 = bf16[1024,1024]{0,1:T(8,128)(2,1)} fusion(bf16[1024,1024]{1,0:T(8,128)(2,1)} %param.19, bf16[1024,1024]{1,0:T(8,128)(2,1)} %param.18, f32[1024,1024]{0,1:T(8,128)} %copy-done.4, f32[1024]{0:T(1024)S(1)} %copy-done.10, f32[1024]{0:T(1024)S(1)} %add_rsqrt_fusion, f32[1024]{0:T(1024)S(1)} %broadcast_multiply_fusion), kind=kOutput, calls=%fused_computation.68 | convolution fusion | flops 4309647360 | bytes 10498048 | tf_op jit(solution)/shard_map/dot_general | solution.py:122
  207.8 4.4 %all-to-all-start.4 = ((bf16[4,1024,256]{1,2,0:T(8,128)(2,1)}), bf16[4,1024,256]{1,2,0:T(8,128)(2,1)}, u32[]{:S(2)}, u32[]{:S(2)}) async-start(bf16[4,1024,256]{1,2,0:T(8,128)(2,1)} %bitcast.62), calls=%async_computation.4 | async-start | bytes 4194304 | tf_op jit(solution)/shard_map/all_to_all | solution.py:125
  212.3 27.2 %all-to-all-done.4 = bf16[4,1024,256]{1,2,0:T(8,128)(2,1)} async-done(((bf16[4,1024,256]{1,2,0:T(8,128)(2,1)}), bf16[4,1024,256]{1,2,0:T(8,128)(2,1)}, u32[]{:S(2)}, u32[]{:S(2)}) %all-to-all-start.4) | async-done | bytes 2097184 | tf_op jit(solution)/shard_map/all_to_all | solution.py:125
  239.5 2.1 convert_reduce_fusion.2
  241.6 1.4 add_convert_fusion
  (47 shorter events, 6.2 us)
Async XLA Ops:
  0.0 192.6 %copy-start = (bf16[1024,1024]{1,0:T(8,128)(2,1)S(1)}, bf16[1024,1024]{1,0:T(8,128)(2,1)}, u32[]{:S(2)}) copy-start(bf16[1024,1024]{1,0:T(8,128)(2,1)} %param.16) | copy-start | bytes 6291460
  0.0 6.1 %copy-start.7 = (bf16[1,32,1024]{2,1,0:T(8,128)(2,1)S(1)}, bf16[1,32,1024]{2,1,0:T(8,128)(2,1)}, u32[]{:S(2)}) copy-start(bf16[1,32,1024]{2,1,0:T(8,128)(2,1)} %param.14) | copy-start | bytes 196612
  0.0 6.1 %copy-start.8 = (bf16[1,32,1024]{2,1,0:T(8,128)(2,1)S(1)}, bf16[1,32,1024]{2,1,0:T(8,128)(2,1)}, u32[]{:S(2)}) copy-start(bf16[1,32,1024]{2,1,0:T(8,128)(2,1)} %param.13) | copy-start | bytes 196612
  4.1 15.3 %collective-permute-start.1 = (bf16[1024,1024]{0,1:T(8,128)(2,1)}, bf16[1024,1024]{0,1:T(8,128)(2,1)}, u32[]{:S(2)}, u32[]{:S(2)}) collective-permute-start(bf16[1024,1024]{0,1:T(8,128)(2,1)} %bitcast.59), channel_id=1, source_target_pairs={{96,32},{97,33},{98,34},{99,35},{100,36},{101,37},{102,38},{103,39... | collective-permute-start | bytes 6291464 | tf_op jit(solution)/shard_map/ppermute | solution.py:29
  8.6 77.9 %all-to-all-start = ((bf16[32,32,2048]{2,1,0:T(8,128)(2,1)}), bf16[32,32,2048]{2,1,0:T(8,128)(2,1)}, u32[]{:S(2)}, u32[]{:S(2)}) async-start(bf16[32,32,2048]{2,1,0:T(8,128)(2,1)} %broadcast_in_dim.23), calls=%async_computation | async-start | bytes 8388608 | tf_op jit(solution)/shard_map/all_to_all | solution.py:39
  17.4 6.2 %collective-permute-start = (bf16[1024,1024]{0,1:T(8,128)(2,1)}, bf16[1024,1024]{0,1:T(8,128)(2,1)}, u32[]{:S(2)}, u32[]{:S(2)}) collective-permute-start(bf16[1024,1024]{0,1:T(8,128)(2,1)} %bitcast.60), channel_id=1, source_target_pairs={{96,64},{97,65},{98,66},{99,67},{100,68},{101,69},{102,70},{103,71... | collective-permute-start | bytes 6291464 | tf_op jit(solution)/shard_map/ppermute | solution.py:30
  19.4 61.9 %collective-permute-start.2 = (bf16[1024,1024]{0,1:T(8,128)(2,1)}, bf16[1024,1024]{0,1:T(8,128)(2,1)}, u32[]{:S(2)}, u32[]{:S(2)}) collective-permute-start(bf16[1024,1024]{0,1:T(8,128)(2,1)} %collective-permute-done.1), channel_id=1, source_target_pairs={{32,0},{33,1},{34,2},{35,3},{36,4},{37,5},{38,6},{39,7},{40,8},{41... | collective-permute-start | bytes 6291464 | tf_op jit(solution)/shard_map/ppermute | solution.py:31
  20.7 60.6 %copy-start.1 = (bf16[1,1024,1024]{1,2,0:T(8,128)(2,1)S(1)}, bf16[1,1024,1024]{1,2,0:T(8,128)(2,1)}, u32[]{:S(2)}) copy-start(bf16[1,1024,1024]{1,2,0:T(8,128)(2,1)} %copy.31) | copy-start | bytes 6291460
  23.6 62.8 %copy-start.9 = (f32[1,1024]{1,0:T(1,128)S(1)}, f32[1,1024]{1,0:T(1,128)}, u32[]{:S(2)}) copy-start(f32[1,1024]{1,0:T(1,128)} %param.12) | copy-start | bytes 12292
  93.5 3.2 %copy-start.2 = (f32[1024,2048]{1,0:T(8,128)}, f32[1024,2048]{1,0:T(8,128)S(1)}, u32[]{:S(2)}) copy-start(f32[1024,2048]{1,0:T(8,128)S(1)} %fusion.23) | copy-start | bytes 25165828
  137.9 40.7 %all-to-all-start.3 = ((f32[32,4,33,128]{3,1,2,0:T(4,128)}), f32[32,4,33,128]{3,1,2,0:T(4,128)}, u32[]{:S(2)}, u32[]{:S(2)}) async-start(f32[32,4,33,128]{3,1,2,0:T(4,128)} %broadcast_in_dim.27), calls=%async_computation.3 | async-start | bytes 4325376 | tf_op jit(solution)/shard_map/all_to_all | solution.py:39
  143.9 1.3 collective-permute-start.4
  144.6 2.2 collective-permute-start.3
  145.3 21.6 %collective-permute-start.5 = (f32[1024]{0:T(1024)S(1)}, f32[1024]{0:T(1024)S(1)}, u32[]{:S(2)}, u32[]{:S(2)}) collective-permute-start(f32[1024]{0:T(1024)S(1)} %collective-permute-done.4), channel_id=1, source_target_pairs={{32,0},{33,1},{34,2},{35,3},{36,4},{37,5},{38,6},{39,7},{40,8},{41... | collective-permute-start | bytes 12296 | tf_op jit(solution)/shard_map/ppermute | solution.py:31
  175.3 1.3 copy-start.5
  181.9 2.2 copy-start.6
  184.2 8.5 %copy-start.3 = (bf16[1024,1024]{0,1:T(8,128)(2,1)S(1)}, bf16[1024,1024]{0,1:T(8,128)(2,1)}, u32[]{:S(2)}) copy-start(bf16[1024,1024]{0,1:T(8,128)(2,1)} %get-tuple-element.6) | copy-start | bytes 6291460
  195.2 1.9 copy-start.4
  195.2 2.4 copy-start.10
  207.8 31.7 %all-to-all-start.4 = ((bf16[4,1024,256]{1,2,0:T(8,128)(2,1)}), bf16[4,1024,256]{1,2,0:T(8,128)(2,1)}, u32[]{:S(2)}, u32[]{:S(2)}) async-start(bf16[4,1024,256]{1,2,0:T(8,128)(2,1)} %bitcast.62), calls=%async_computation.4 | async-start | bytes 4194304 | tf_op jit(solution)/shard_map/all_to_all | solution.py:125

commit v2 on v1

--- a/solution.py
+++ b/solution.py
@@ -102,29 +102,53 @@
     query_feats = feature_map(
         jnp.dot(query_normed, query_weight, preferred_element_type=jnp.float32)
     ).astype(jnp.bfloat16)
-    per_head_queries = query_feats.astype(jnp.float32).reshape(rows, heads, HEAD_DIM)
-    numerator = jnp.einsum(
-        "rhk,shkv->srhv", per_head_queries, state_heads, precision=lax.Precision.HIGHEST
+    per_head_queries = query_feats.reshape(rows, heads, HEAD_DIM)
+
+    joined = jnp.concatenate(
+        [
+            state_heads.transpose(1, 2, 0, 3).reshape(heads, HEAD_DIM, sections * HEAD_DIM),
+            total_heads.transpose(1, 2, 0),
+            jnp.zeros((heads, HEAD_DIM, HEAD_DIM - sections), jnp.float32),
+        ],
+        axis=2,
     )
-    denom = jnp.einsum(
-        "rhk,shk->srh", per_head_queries, total_heads, precision=lax.Precision.HIGHEST
-    )
-    attended = (
-        jnp.sum(numerator / denom[:, :, :, None], axis=0).reshape(rows, width).astype(jnp.bfloat16)
-    )
-    mixed = query_block.astype(jnp.float32) + jnp.dot(
-        attended, output_weight, preferred_element_type=jnp.float32
-    )
-    centred = layer_normalizer(mixed, middle_gain).astype(jnp.bfloat16)
-    hidden = jax.nn.gelu(
-        jnp.dot(centred, up_weight, preferred_element_type=jnp.float32), approximate=True
-    ).astype(jnp.bfloat16)
-    term = jnp.dot(hidden, down_weight, preferred_element_type=jnp.float32)
+    high = joined.astype(jnp.bfloat16)
+    rest = joined - high.astype(jnp.float32)
+    middle = rest.astype(jnp.bfloat16)
+    low = (rest - middle.astype(jnp.float32)).astype(jnp.bfloat16)
+
     share = width // sections
-    parts = term.astype(jnp.bfloat16).reshape(rows, sections, share).transpose(1, 0, 2)
-    summed = jnp.sum(lax.all_to_all(parts, "sec", 0, 0, tiled=False).astype(jnp.float32), axis=0)
-    own_mixed = lax.dynamic_slice_in_dim(mixed, me * share, share, axis=1)
-    return (own_mixed + summed).astype(jnp.bfloat16)
+    chunks = 2 if rows % 16 == 0 else 1
+    step = rows // chunks
+    outs = []
+    for c in range(chunks):
+        queries = per_head_queries[c * step : (c + 1) * step]
+        products = sum(
+            jnp.einsum("rhk,hkc->rhc", queries, term, preferred_element_type=jnp.float32)
+            for term in (high, middle, low)
+        )
+        numerator = products[:, :, : sections * HEAD_DIM].reshape(step, heads, sections, HEAD_DIM)
+        denom = products[:, :, sections * HEAD_DIM : sections * HEAD_DIM + sections]
+        attended = (
+            jnp.sum(numerator / denom[:, :, :, None], axis=2)
+            .reshape(step, width)
+            .astype(jnp.bfloat16)
+        )
+        mixed = query_block[c * step : (c + 1) * step].astype(jnp.float32) + jnp.dot(
+            attended, output_weight, preferred_element_type=jnp.float32
+        )
+        centred = layer_normalizer(mixed, middle_gain).astype(jnp.bfloat16)
+        hidden = jax.nn.gelu(
+            jnp.dot(centred, up_weight, preferred_element_type=jnp.float32), approximate=True
+        ).astype(jnp.bfloat16)
+        term = jnp.dot(hidden, down_weight, preferred_element_type=jnp.float32)
+        parts = term.astype(jnp.bfloat16).reshape(step, sections, share).transpose(1, 0, 2)
+        summed = jnp.sum(
+            lax.all_to_all(parts, "sec", 0, 0, tiled=False).astype(jnp.float32), axis=0
+        )
+        own_mixed = lax.dynamic_slice_in_dim(mixed, me * share, share, axis=1)
+        outs.append((own_mixed + summed).astype(jnp.bfloat16))
+    return jnp.concatenate(outs, axis=0)
 
 
 def solution(mesh):

time: 245 us -> 286 us (1.17)
  matrix products: 41.4 us -> 62.5 us
  local copies, waits for them, and re-layouts: 23.9 us -> 37.9 us
  other arithmetic: 17.1 us -> 24.6 us
  waiting for transfers between devices: 105 us -> 99 us
  starting transfers between devices: 27.3 us -> 31.1 us
    dot_general x2 -> x6, matrix products: 11.8 us -> 32.3 us  [on_device(): jnp.einsum('rhk,hkc->rhc', queries, term, preferred_element_type=jnp.floa...]
    slice x0 -> x5, local copies, waits for them, and re-layouts: none -> 9.57 us  [the longest x3 8.65 us: on_device(): products[:, :, :sections * HEAD_DIM]]
    reduce_sum x0 -> x2, other arithmetic: none -> 6 us  [on_device(): jnp.sum(numerator / denom[:, :, :, None], axis=2).reshape(step, width)]
    all_to_all x1 -> x2, waiting for transfers between devices: 27.2 us -> 22.1 us  [on_device(): lax.all_to_all(parts, 'sec', 0, 0, tiled=False).astype(jnp.float32)]
    transpose x0 -> x2, local copies, waits for them, and re-layouts: none -> 3.66 us  [the longest x1 2.94 us: on_device(): state_heads.transpose(1, 2, 0, 3)]
    reshape x0 -> x2, local copies, waits for them, and re-layouts: none -> 3.35 us  [on_device(): term.astype(jnp.bfloat16).reshape(step, sections, share).transpose(1, 0, 2)]
    all_to_all x1 -> x2, starting transfers between devices: 4.44 us -> 7.77 us  [on_device(): lax.all_to_all(parts, 'sec', 0, 0, tiled=False).astype(jnp.float32)]
    unnamed x24 -> x25, local copies, waits for them, and re-layouts: 12.8 us -> 10 us
  transfers between devices with their start and end apart: 9 -> 10, of which waited for: 3 -> 4; matrix products, arithmetic and copies ran while one was open for 8% -> 10% of each run, Pallas kernels for 0% -> 0%
where the time goes in v2:
time: 286 us; the launch traced here: 285 us
  waiting for transfers between devices  99 us (35%)
  matrix products  62.5 us (22%)
  local copies, waits for them, and re-layouts  37.9 us (13%)
  starting transfers between devices  31.1 us (11%)
  blocking collectives  29 us (10%)
  other arithmetic  24.6 us (9%)
    ppermute x2, waiting for transfers between devices, from_last(): farther = lax.ppermute(far, axis, [(1, 0)])  76.9 us
    dot_general x6, matrix products, on_device(): jnp.einsum('rhk,hkc->rhc', queries, term, preferred_element_type=jnp.floa...  32.3 us
    all_to_all x2, waiting for transfers between devices, on_device(): lax.all_to_all(parts, 'sec', 0, 0, tiled=False).astype(jnp.float32)  22.1 us
    all_to_all x1, blocking collectives, on_device(): reduced = jnp.sum(lax.all_to_all(packed, 'pts', 0, 0, tiled=False), axis=0)  20 us
    all_to_all x2, starting transfers between devices, gather_a2a(): return lax.all_to_all(spread, axis, 0, 0, tiled=False)  15 us
    dot_general x2, matrix products, on_device(): term = jnp.dot(hidden, down_weight, preferred_element_type=jnp.float32)  11.6 us
    unnamed x25, local copies, waits for them, and re-layouts  10 us
    all_to_all x1, blocking collectives, gather_a2a(): return lax.all_to_all(spread, axis, 0, 0, tiled=False)  8.97 us
  transfers between devices with their start and end apart: 10, of which 4 were waited for; matrix products, arithmetic and copies ran while one was open for 10% of the time, Pallas kernels for 0%

profile of v2, /device:TPU:16, one launch (start us, length us, event | category | flops | bytes accessed | tf_op | source)
XLA Modules:
  0.0 285.3 jit_solution(14814931001816341968)
XLA Ops:
  3.1 2.5 broadcast_in_dim.25
  5.6 8.8 %all-to-all-start = ((bf16[32,32,2048]{2,1,0:T(8,128)(2,1)}), bf16[32,32,2048]{2,1,0:T(8,128)(2,1)}, u32[]{:S(2)}, u32[]{:S(2)}) async-start(bf16[32,32,2048]{2,1,0:T(8,128)(2,1)} %broadcast_in_dim.25), calls=%async_computation | async-start | bytes 8388608 | tf_op jit(solution)/shard_map/all_to_all | solution.py:39
  20.5 56.8 %collective-permute-done.2 = bf16[1024,1024]{1,0:T(8,128)(2,1)} collective-permute-done((bf16[1024,1024]{1,0:T(8,128)(2,1)}, bf16[1024,1024]{1,0:T(8,128)(2,1)}, u32[]{:S(2)}, u32[]{:S(2)}) %collective-permute-start.2) | collective-permute-done | bytes 2097184 | tf_op jit(solution)/shard_map/ppermute | solution.py:31
  77.4 4.5 %convert_reduce_fusion = (f32[1024]{0:T(1024)S(1)}, bf16[1024,1024]{1,0:T(8,128)(2,1)}, f32[1024]{0:T(1024)S(1)}) fusion(bf16[1024,1024]{1,0:T(8,128)(2,1)} %collective-permute-done, bf16[1024,1024]{1,0:T(8,128)(2,1)} %collective-permute-done.1, bf16[1024,1024]{1,0:T(8,128)(2,1)} %collective-permute-done.2, pred[]{:T(512)S(6)} %eq.14, pred[]{:T(512)S(6)} %eq.13, ...), kind=kLoop, calls=%fused_computation.9 | loop fusion | flops 9435136 | bytes 10498051 | tf_op jit(solution)/shard_map/reduce_sum | solution.py:10
  81.9 7.0 %fusion.31 = f32[1024,2048]{1,0:T(8,128)S(1)} fusion(bf16[1024,2048]{1,0:T(8,128)(2,1)} %bitcast.6, bf16[1,1024,1024]{2,1,0:T(8,128)(2,1)} %param.10, f32[1024]{0:T(1024)S(1)} %bitcast.106, f32[1024]{0:T(1024)S(1)} %add_rsqrt_fusion.1, f32[1024]{0:T(1024)S(1)} %broadcast_multiply_fusion.1), kind=kOutput, calls=%fused_computation.51 | convolution fusion | flops 4300210176 | bytes 14692352 | tf_op jit(solution)/shard_map/dot_general | solution.py:69
  89.0 3.2 %copy-done.8 = f32[1024,2048]{1,0:T(8,128)} copy-done((f32[1024,2048]{1,0:T(8,128)}, f32[1024,2048]{1,0:T(8,128)S(1)}, u32[]{:S(2)}) %copy-start.8) | copy-done | bytes 8388632
  92.2 3.6 %convert_reduce_fusion.2 = (f32[1024]{0:T(1024)S(1)}, bf16[1024,1024]{1,0:T(8,128)(2,1)}) fusion(f32[1024,2048]{1,0:T(8,128)S(1)} %fusion.31, pred[1024]{0:T(1024)(128)(4,1)S(1)} %iota_compare_fusion), kind=kLoop, calls=%fused_computation.26 | loop fusion | flops 8387584 | bytes 6296576 | tf_op jit(solution)/shard_map/reduce_sum | solution.py:80
  95.8 3.9 %copy.51 = bf16[1024,1024]{0,1:T(8,128)(2,1)} copy(bf16[1024,1024]{1,0:T(8,128)(2,1)} %get-tuple-element.10) | data formatting | bytes 4194304 | tf_op jit(solution)/shard_map/reshape | solution.py:76
  99.7 3.6 %fusion.37 = f32[8,128,128]{2,1,0:T(8,128)S(1)} fusion(bf16[1024,8,128]{0,2,1:T(8,128)(2,1)} %bitcast.92, f32[1024,2048]{1,0:T(8,128)} %copy-done.8), kind=kOutput, calls=%fused_computation.55 | convolution fusion | flops 268435456 | bytes 4718592 | tf_op jit(solution)/shard_map/yzl,yzn->zln/dot_general | solution.py:74
  103.6 20.0 %all_to_all.30 = f32[32,33,128]{2,1,0:T(8,128)S(1)} all-to-all(f32[32,33,128]{2,1,0:T(8,128)S(1)} %reshape.131), channel_id=1, replica_groups=mesh['sec'=4,'pts'=32] {'pts'}, dimensions={0} | all-to-all | bytes 1081344 | tf_op jit(solution)/shard_map/all_to_all | solution.py:92
  123.7 9.0 %all_to_all.31 = f32[4,33,128]{2,1,0:T(8,128)S(1)} all-to-all(f32[4,33,128]{2,1,0:T(8,128)S(1)} %broadcast_in_dim.28), channel_id=1, replica_groups=mesh['sec'=4,'pts'=32] {'sec'}, dimensions={0} | all-to-all | bytes 135168 | tf_op jit(solution)/shard_map/all_to_all | solution.py:39
  134.3 6.1 %all-to-all-start.3 = ((f32[32,4,33,128]{3,1,2,0:T(4,128)}), f32[32,4,33,128]{3,1,2,0:T(4,128)}, u32[]{:S(2)}, u32[]{:S(2)}) async-start(f32[32,4,33,128]{3,1,2,0:T(4,128)} %broadcast_in_dim.29), calls=%async_computation.3 | async-start | bytes 4325376 | tf_op jit(solution)/shard_map/all_to_all | solution.py:39
  143.5 20.1 %collective-permute-done.5 = f32[1024]{0:T(1024)S(1)} collective-permute-done((f32[1024]{0:T(1024)S(1)}, f32[1024]{0:T(1024)S(1)}, u32[]{:S(2)}, u32[]{:S(2)}) %collective-permute-start.5) | collective-permute-done | bytes 4128 | tf_op jit(solution)/shard_map/ppermute | solution.py:31
  163.6 2.3 fusion.2
  165.9 5.1 %fusion.12 = bf16[1024,1024]{1,0:T(8,128)(2,1)S(1)} fusion(bf16[1024,1024]{1,0:T(8,128)(2,1)} %param.15, bf16[1024,1024]{1,0:T(8,128)(2,1)S(1)} %copy-done.4, f32[1024]{0:T(1024)S(1)} %select_select_fusion.1, f32[1024]{0:T(1024)S(1)} %add_rsqrt_fusion, f32[1024]{0:T(1024)S(1)} %broadcast_multiply_fusion), kind=kOutput, calls=%fused_computation.24 | convolution fusion | flops 2157969408 | bytes 6303744 | tf_op jit(solution)/shard_map/dot_general | solution.py:103
  172.1 3.0 %slice.60 = f32[4,1024,128]{2,0,1:T(4,128)} slice(f32[4,1056,128]{2,0,1:T(4,128)} %bitcast.11), slice={[0:4], [0:1024], [0:128]} | slice | bytes 4194304 | tf_op jit(solution)/shard_map/slice | solution.py:96
  175.9 2.9 %copy.38 = f32[8,128,4,128]{1,3,2,0:T(8,128)} copy(f32[8,128,4,128]{3,2,1,0:T(4,128)} %bitcast.93) | data formatting | bytes 4194304 | tf_op jit(solution)/shard_map/transpose | solution.py:109
  178.8 3.6 %fusion.57 = f32[8,640,512]{2,1,0:T(8,128)S(1)} fusion(bf16[64,8,8,128]{3,2,1,0:T(8,128)(2,1)} %get-tuple-element.15, f32[8,128,4]{1,2,0:T(4,128)S(1)} %slice_bitcast_fusion.2, f32[8,128,512]{1,2,0:T(8,128)} %bitcast.84, f32[640]{0:T(1024)S(1)} %pad.4.clone), kind=kOutput, calls=%fused_computation.86 | convolution fusion | flops 675020800 | bytes 13650432 | tf_op jit(solution)/shard_map/rhk,hkc->rhc/dot_general | solution.py:127
  182.4 5.6 %fusion.59 = f32[8,640,512]{2,1,0:T(8,128)} fusion(bf16[64,8,8,128]{3,2,1,0:T(8,128)(2,1)S(1)} %copy-done.3, f32[8,128,4]{1,2,0:T(4,128)S(1)} %slice_bitcast_fusion.2, f32[8,128,512]{1,2,0:T(8,128)S(1)} %bitcast.85, f32[640]{0:T(1024)S(1)} %pad.4.clone), kind=kOutput, calls=%fused_computation.88 | convolution fusion | flops 675020800 | bytes 13650432 | tf_op jit(solution)/shard_map/rhk,hkc->rhc/dot_general | solution.py:127
  188.0 8.2 %add_bitcast_fusion.1 = f32[512,8,640]{0,2,1:T(8,128)} fusion(f32[8,640,512]{2,1,0:T(8,128)} %fusion.59, f32[8,640,512]{2,1,0:T(8,128)S(1)} %fusion.57, bf16[64,8,8,128]{3,2,1,0:T(8,128)(2,1)} %get-tuple-element.15, f32[8,128,4]{1,2,0:T(4,128)S(1)} %slice_bitcast_fusion.2, f32[8,128,512]{1,2,0:T(8,128)S(1)} %bitcast.86, f32[640]{0:T(1024)S(1)} %pad.4.clone), kind=kOutput, calls=%fused_computation.5 | convolution fusion | flops 682229760 | bytes 34621952 | tf_op jit(solution)/shard_map/rhk,hkc->rhc/dot_general | solution.py:127
  196.2 7.7 %slice.63 = f32[512,8,512]{0,2,1:T(8,128)} slice(f32[512,8,640]{0,2,1:T(8,128)} %add_bitcast_fusion.1), slice={[0:512], [0:8], [0:512]} | slice | bytes 16777216 | tf_op jit(solution)/shard_map/slice | solution.py:130
  206.3 5.6 %fusion.54 = f32[8,640,512]{2,1,0:T(8,128)} fusion(bf16[64,8,8,128]{3,2,1,0:T(8,128)(2,1)S(1)} %get-tuple-element.16, f32[8,128,4]{1,2,0:T(4,128)S(1)} %slice_bitcast_fusion.2, f32[8,128,512]{1,2,0:T(8,128)S(1)} %bitcast.88, f32[640]{0:T(1024)S(1)} %pad.4.clone), kind=kOutput, calls=%fused_computation.82 | convolution fusion | flops 675020800 | bytes 13650432 | tf_op jit(solution)/shard_map/rhk,hkc->rhc/dot_general | solution.py:127
  211.9 7.9 %add_bitcast_fusion = f32[512,8,640]{0,2,1:T(8,128)} fusion(f32[8,640,512]{2,1,0:T(8,128)} %fusion.54, f32[8,640,512]{2,1,0:T(8,128)S(1)} %fusion.52, bf16[64,8,8,128]{3,2,1,0:T(8,128)(2,1)S(1)} %get-tuple-element.16, f32[8,128,4]{1,2,0:T(4,128)S(1)} %slice_bitcast_fusion.2, f32[8,128,512]{1,2,0:T(8,128)S(1)} %bitcast.89, f32[640]{0:T(1024)S(1)} %pad.4.clone), kind=kOutput, calls=%fused_computation.4 | convolution fusion | flops 682229760 | bytes 34621952 | tf_op jit(solution)/shard_map/rhk,hkc->rhc/dot_general | solution.py:127
  219.8 4.0 %copy-done.2 = f32[512,8,640]{0,2,1:T(8,128)S(1)} copy-done((f32[512,8,640]{0,2,1:T(8,128)S(1)}, f32[512,8,640]{0,2,1:T(8,128)}, u32[]{:S(2)}) %copy-start.2) | copy-done | bytes 10485784
  223.8 4.8 %divide_reduce_fusion.1 = bf16[512,8,128]{0,2,1:T(8,128)(2,1)S(1)} fusion(f32[512,8,4,128]{0,3,2,1:T(8,128)} %bitcast.91, f32[512,8,4]{0,2,1:T(4,128)S(1)} %slice.64), kind=kLoop, calls=%fused_computation.7 | loop fusion | flops 3670016 | bytes 9502720 | tf_op jit(solution)/shard_map/reduce_sum | solution.py:133
  235.8 5.3 %convolution_convert_fusion.1 = bf16[512,1024]{1,0:T(8,128)(2,1)S(1)} fusion(bf16[1024,1024]{1,0:T(8,128)(2,1)} %param.19, bf16[1024,1024]{1,0:T(8,128)(2,1)} %param.18, f32[512,1024]{1,0:T(8,128)} %copy-done.7, f32[1024]{0:T(1024)S(1)} %copy-done.11, f32[512]{0:T(512)S(1)} %add_rsqrt_fusion.3, f32[512]{0:T(512)S(1)} %broadcast_multiply_fusion.3), kind=kOutput, calls=%fused_computation.74 | convolution fusion | flops 2154823680 | bytes 7348224 | tf_op jit(solution)/shard_map/dot_general | solution.py:144
  242.2 3.5 %all-to-all-start.4 = ((bf16[4,512,256]{2,1,0:T(8,128)(2,1)}), bf16[4,512,256]{2,1,0:T(8,128)(2,1)S(1)}, u32[]{:S(2)}, u32[]{:S(2)}) async-start(bf16[4,512,256]{2,1,0:T(8,128)(2,1)} %bitcast.99), calls=%async_computation.4 | async-start | bytes 2097152 | tf_op jit(solution)/shard_map/all_to_all | solution.py:147
  245.8 6.3 %convolution_convert_fusion = bf16[512,1024]{1,0:T(8,128)(2,1)} fusion(bf16[1024,1024]{1,0:T(8,128)(2,1)} %param.19, bf16[1024,1024]{1,0:T(8,128)(2,1)} %param.18, f32[512,1024]{1,0:T(8,128)} %copy-done.6, f32[512]{0:T(512)S(1)} %add_rsqrt_fusion.2, f32[512]{0:T(512)S(1)} %broadcast_multiply_fusion.2, f32[1024]{0:T(1024)S(1)} %copy-done.11), kind=kOutput, calls=%fused_computation.73 | convolution fusion | flops 2154823680 | bytes 7348224 | tf_op jit(solution)/shard_map/dot_general | solution.py:144
  252.1 2.3 copy.87
  254.4 7.3 %all-to-all-done.4 = bf16[4,512,256]{2,1,0:T(8,128)(2,1)S(1)} async-done(((bf16[4,512,256]{2,1,0:T(8,128)(2,1)}), bf16[4,512,256]{2,1,0:T(8,128)(2,1)S(1)}, u32[]{:S(2)}, u32[]{:S(2)}) %all-to-all-start.4) | async-done | bytes 1048608 | tf_op jit(solution)/shard_map/all_to_all | solution.py:147
  261.7 4.3 %all-to-all-start.5 = ((bf16[4,512,256]{2,1,0:T(8,128)(2,1)}), bf16[4,512,256]{2,1,0:T(8,128)(2,1)}, u32[]{:S(2)}, u32[]{:S(2)}) async-start(bf16[4,512,256]{2,1,0:T(8,128)(2,1)} %bitcast.98), calls=%async_computation.5 | async-start | bytes 2097152 | tf_op jit(solution)/shard_map/all_to_all | solution.py:147
  267.2 14.7 %all-to-all-done.5 = bf16[4,512,256]{2,1,0:T(8,128)(2,1)} async-done(((bf16[4,512,256]{2,1,0:T(8,128)(2,1)}), bf16[4,512,256]{2,1,0:T(8,128)(2,1)}, u32[]{:S(2)}, u32[]{:S(2)}) %all-to-all-start.5) | async-done | bytes 1048608 | tf_op jit(solution)/shard_map/all_to_all | solution.py:147
  (73 shorter events, 30.6 us)
Async XLA Ops:
  0.0 230.8 %copy-start = (bf16[1024,1024]{1,0:T(8,128)(2,1)S(1)}, bf16[1024,1024]{1,0:T(8,128)(2,1)}, u32[]{:S(2)}) copy-start(bf16[1024,1024]{1,0:T(8,128)(2,1)} %param.16) | copy-start | bytes 6291460
  0.0 16.4 %collective-permute-start.1 = (bf16[1024,1024]{1,0:T(8,128)(2,1)}, bf16[1024,1024]{1,0:T(8,128)(2,1)}, u32[]{:S(2)}, u32[]{:S(2)}) collective-permute-start(bf16[1024,1024]{1,0:T(8,128)(2,1)} %bitcast.94), channel_id=1, source_target_pairs={{96,32},{97,33},{98,34},{99,35},{100,36},{101,37},{102,38},{103,39... | collective-permute-start | bytes 6291464 | tf_op jit(solution)/shard_map/ppermute | solution.py:29
  5.6 76.3 %all-to-all-start = ((bf16[32,32,2048]{2,1,0:T(8,128)(2,1)}), bf16[32,32,2048]{2,1,0:T(8,128)(2,1)}, u32[]{:S(2)}, u32[]{:S(2)}) async-start(bf16[32,32,2048]{2,1,0:T(8,128)(2,1)} %broadcast_in_dim.25), calls=%async_computation | async-start | bytes 8388608 | tf_op jit(solution)/shard_map/all_to_all | solution.py:39
  14.4 6.1 %collective-permute-start = (bf16[1024,1024]{1,0:T(8,128)(2,1)}, bf16[1024,1024]{1,0:T(8,128)(2,1)}, u32[]{:S(2)}, u32[]{:S(2)}) collective-permute-start(bf16[1024,1024]{1,0:T(8,128)(2,1)} %bitcast.95), channel_id=1, source_target_pairs={{96,64},{97,65},{98,66},{99,67},{100,68},{101,69},{102,70},{103,71... | collective-permute-start | bytes 6291464 | tf_op jit(solution)/shard_map/ppermute | solution.py:30
  16.4 61.0 %collective-permute-start.2 = (bf16[1024,1024]{1,0:T(8,128)(2,1)}, bf16[1024,1024]{1,0:T(8,128)(2,1)}, u32[]{:S(2)}, u32[]{:S(2)}) collective-permute-start(bf16[1024,1024]{1,0:T(8,128)(2,1)} %collective-permute-done.1), channel_id=1, source_target_pairs={{32,0},{33,1},{34,2},{35,3},{36,4},{37,5},{38,6},{39,7},{40,8},{41... | collective-permute-start | bytes 6291464 | tf_op jit(solution)/shard_map/ppermute | solution.py:31
  17.7 59.7 %copy-start.9 = (bf16[1,1024,1024]{2,1,0:T(8,128)(2,1)S(1)}, bf16[1,1024,1024]{2,1,0:T(8,128)(2,1)}, u32[]{:S(2)}) copy-start(bf16[1,1024,1024]{2,1,0:T(8,128)(2,1)} %param.10) | copy-start | bytes 6291460
  20.5 61.4 %copy-start.10 = (f32[1,1024]{1,0:T(1,128)S(1)}, f32[1,1024]{1,0:T(1,128)}, u32[]{:S(2)}) copy-start(f32[1,1024]{1,0:T(1,128)} %param.12) | copy-start | bytes 12292
  89.0 3.2 %copy-start.8 = (f32[1024,2048]{1,0:T(8,128)}, f32[1024,2048]{1,0:T(8,128)S(1)}, u32[]{:S(2)}) copy-start(f32[1024,2048]{1,0:T(8,128)S(1)} %fusion.31) | copy-start | bytes 25165828
  134.3 37.9 %all-to-all-start.3 = ((f32[32,4,33,128]{3,1,2,0:T(4,128)}), f32[32,4,33,128]{3,1,2,0:T(4,128)}, u32[]{:S(2)}, u32[]{:S(2)}) async-start(f32[32,4,33,128]{3,1,2,0:T(4,128)} %broadcast_in_dim.29), calls=%async_computation.3 | async-start | bytes 4325376 | tf_op jit(solution)/shard_map/all_to_all | solution.py:39
  140.4 25.4 %copy-start.4 = (bf16[1024,1024]{1,0:T(8,128)(2,1)S(1)}, bf16[1024,1024]{1,0:T(8,128)(2,1)}, u32[]{:S(2)}) copy-start(bf16[1024,1024]{1,0:T(8,128)(2,1)} %get-tuple-element.12) | copy-start | bytes 6291460
  140.4 1.5 collective-permute-start.4
  141.2 2.2 collective-permute-start.3
  141.9 21.6 %collective-permute-start.5 = (f32[1024]{0:T(1024)S(1)}, f32[1024]{0:T(1024)S(1)}, u32[]{:S(2)}, u32[]{:S(2)}) collective-permute-start(f32[1024]{0:T(1024)S(1)} %collective-permute-done.4), channel_id=1, source_target_pairs={{32,0},{33,1},{34,2},{35,3},{36,4},{37,5},{38,6},{39,7},{40,8},{41... | collective-permute-start | bytes 12296 | tf_op jit(solution)/shard_map/ppermute | solution.py:31
  178.8 3.6 %copy-start.1 = (f32[8,128,4,128]{1,3,2,0:T(8,128)S(1)}, f32[8,128,4,128]{1,3,2,0:T(8,128)}, u32[]{:S(2)}) copy-start(f32[8,128,4,128]{1,3,2,0:T(8,128)} %copy.38) | copy-start | bytes 6291460
  178.8 3.6 %copy-start.3 = (bf16[64,8,8,128]{3,2,1,0:T(8,128)(2,1)S(1)}, bf16[64,8,8,128]{3,2,1,0:T(8,128)(2,1)}, u32[]{:S(2)}) copy-start(bf16[64,8,8,128]{3,2,1,0:T(8,128)(2,1)} %get-tuple-element.15) | copy-start | bytes 3145732
  219.8 4.0 %copy-start.2 = (f32[512,8,640]{0,2,1:T(8,128)S(1)}, f32[512,8,640]{0,2,1:T(8,128)}, u32[]{:S(2)}) copy-start(f32[512,8,640]{0,2,1:T(8,128)} %add_bitcast_fusion) | copy-start | bytes 31457284
  223.8 5.8 %slice-start = ((f32[512,8,640]{0,2,1:T(8,128)}), f32[512,8,512]{0,2,1:T(8,128)S(1)}, s32[]{:S(2)}) async-start(f32[512,8,640]{0,2,1:T(8,128)} %add_bitcast_fusion), calls=%async_computation.6 | async-start | bytes 16777216 | tf_op jit(solution)/shard_map/slice | solution.py:130
  230.8 1.6 copy-start.5
  233.9 1.4 copy-start.6
  233.9 1.9 copy-start.7
  233.9 1.9 copy-start.11
  242.2 19.4 %all-to-all-start.4 = ((bf16[4,512,256]{2,1,0:T(8,128)(2,1)}), bf16[4,512,256]{2,1,0:T(8,128)(2,1)S(1)}, u32[]{:S(2)}, u32[]{:S(2)}) async-start(bf16[4,512,256]{2,1,0:T(8,128)(2,1)} %bitcast.99), calls=%async_computation.4 | async-start | bytes 2097152 | tf_op jit(solution)/shard_map/all_to_all | solution.py:147
  261.7 20.3 %all-to-all-start.5 = ((bf16[4,512,256]{2,1,0:T(8,128)(2,1)}), bf16[4,512,256]{2,1,0:T(8,128)(2,1)}, u32[]{:S(2)}, u32[]{:S(2)}) async-start(bf16[4,512,256]{2,1,0:T(8,128)(2,1)} %bitcast.98), calls=%async_computation.5 | async-start | bytes 2097152 | tf_op jit(solution)/shard_map/all_to_all | solution.py:147

commit v3 on v2

--- a/solution.py
+++ b/solution.py
@@ -116,37 +116,37 @@
     rest = joined - high.astype(jnp.float32)
     middle = rest.astype(jnp.bfloat16)
     low = (rest - middle.astype(jnp.float32)).astype(jnp.bfloat16)
+    terms = jnp.concatenate([high, middle, low], axis=1)
+
+    head_queries = per_head_queries.transpose(1, 0, 2)
+    tripled = jnp.concatenate([head_queries] * 3, axis=2)
+    products = jnp.einsum("hrk,hkc->hrc", tripled, terms, preferred_element_type=jnp.float32)
+    numerator = products[:, :, : sections * HEAD_DIM].reshape(heads, rows, sections, HEAD_DIM)
+    denom = products[:, :, sections * HEAD_DIM : sections * HEAD_DIM + sections]
+    attended = jnp.sum(numerator / denom[:, :, :, None], axis=2).astype(jnp.bfloat16)
+    mixed = query_block.astype(jnp.float32) + jnp.einsum(
+        "hrv,hvd->rd",
+        attended,
+        output_weight.reshape(heads, HEAD_DIM, width),
+        preferred_element_type=jnp.float32,
+    )
+    centred = layer_normalizer(mixed, middle_gain).astype(jnp.bfloat16)
 
     share = width // sections
     chunks = 2 if rows % 16 == 0 else 1
     step = rows // chunks
     outs = []
     for c in range(chunks):
-        queries = per_head_queries[c * step : (c + 1) * step]
-        products = sum(
-            jnp.einsum("rhk,hkc->rhc", queries, term, preferred_element_type=jnp.float32)
-            for term in (high, middle, low)
-        )
-        numerator = products[:, :, : sections * HEAD_DIM].reshape(step, heads, sections, HEAD_DIM)
-        denom = products[:, :, sections * HEAD_DIM : sections * HEAD_DIM + sections]
-        attended = (
-            jnp.sum(numerator / denom[:, :, :, None], axis=2)
-            .reshape(step, width)
-            .astype(jnp.bfloat16)
-        )
-        mixed = query_block[c * step : (c + 1) * step].astype(jnp.float32) + jnp.dot(
-            attended, output_weight, preferred_element_type=jnp.float32
-        )
-        centred = layer_normalizer(mixed, middle_gain).astype(jnp.bfloat16)
         hidden = jax.nn.gelu(
-            jnp.dot(centred, up_weight, preferred_element_type=jnp.float32), approximate=True
+            jnp.dot(centred[c * step : (c + 1) * step], up_weight, preferred_element_type=jnp.float32),
+            approximate=True,
         ).astype(jnp.bfloat16)
         term = jnp.dot(hidden, down_weight, preferred_element_type=jnp.float32)
         parts = term.astype(jnp.bfloat16).reshape(step, sections, share).transpose(1, 0, 2)
         summed = jnp.sum(
             lax.all_to_all(parts, "sec", 0, 0, tiled=False).astype(jnp.float32), axis=0
         )
-        own_mixed = lax.dynamic_slice_in_dim(mixed, me * share, share, axis=1)
+        own_mixed = lax.dynamic_slice_in_dim(mixed[c * step : (c + 1) * step], me * share, share, axis=1)
         outs.append((own_mixed + summed).astype(jnp.bfloat16))
     return jnp.concatenate(outs, axis=0)
 

time: 286 us -> 295 us (1.031)
  local copies, waits for them, and re-layouts: 37.9 us -> 56.1 us
  matrix products: 62.5 us -> 49 us
  other arithmetic: 24.6 us -> 34.7 us
  waiting for transfers between devices: 99 us -> 94.2 us
    dot_general x8 -> x2, matrix products: 35.2 us -> 21 us  [the longest x1 16.3 us: on_device(): jnp.einsum('hrk,hkc->hrc', tripled, terms, preferred_element_type=jnp.flo...]
    slice x0 -> x2, local copies, waits for them, and re-layouts: none -> 7.2 us  [the longest x1 4.63 us: on_device(): mixed[c * step:(c + 1) * step]]
    convert_element_type x0 -> x3, other arithmetic: none -> 6.08 us  [the longest x1 2.22 us: on_device(): middle = rest.astype(jnp.bfloat16)]
    all_to_all x2, waiting for transfers between devices: 22.1 us -> 16.7 us  [on_device(): lax.all_to_all(parts, 'sec', 0, 0, tiled=False).astype(jnp.float32)]
    unnamed x25 -> x22, local copies, waits for them, and re-layouts: 10 us -> 14.3 us
    reduce_sum x2 -> x1, other arithmetic: 6 us -> 10.3 us  [on_device(): jnp.sum(numerator / denom[:, :, :, None], axis=2).astype(jnp.bfloat16)]
    slice x3 -> x1, local copies, waits for them, and re-layouts: 8.65 us -> 11.9 us  [on_device(): products[:, :, :sections * HEAD_DIM]]
  transfers between devices with their start and end apart: 10 -> 10, of which waited for: 4 -> 4; matrix products, arithmetic and copies ran while one was open for 10% -> 13% of each run, Pallas kernels for 0% -> 0%
where the time goes in v3:
time: 295 us; the launch traced here: 294 us
  waiting for transfers between devices  94.2 us (32%)
  local copies, waits for them, and re-layouts  56.1 us (19%)
  matrix products  49 us (17%)
  other arithmetic  34.7 us (12%)
  starting transfers between devices  30.9 us (10%)
  blocking collectives  28.1 us (10%)
    ppermute x2, waiting for transfers between devices, from_last(): farther = lax.ppermute(far, axis, [(1, 0)])  77.5 us
    all_to_all x1, blocking collectives, on_device(): reduced = jnp.sum(lax.all_to_all(packed, 'pts', 0, 0, tiled=False), axis=0)  20 us
    all_to_all x2, waiting for transfers between devices, on_device(): lax.all_to_all(parts, 'sec', 0, 0, tiled=False).astype(jnp.float32)  16.7 us
    dot_general x1, matrix products, on_device(): jnp.einsum('hrk,hkc->hrc', tripled, terms, preferred_element_type=jnp.flo...  16.3 us
    all_to_all x2, starting transfers between devices, gather_a2a(): return lax.all_to_all(spread, axis, 0, 0, tiled=False)  14.8 us
    unnamed x22, local copies, waits for them, and re-layouts  14.3 us
    slice x1, local copies, waits for them, and re-layouts, on_device(): products[:, :, :sections * HEAD_DIM]  11.9 us
    dot_general x2, matrix products, on_device(): term = jnp.dot(hidden, down_weight, preferred_element_type=jnp.float32)  11.1 us
  transfers between devices with their start and end apart: 10, of which 4 were waited for; matrix products, arithmetic and copies ran while one was open for 13% of the time, Pallas kernels for 0%

profile of v3, /device:TPU:16, one launch (start us, length us, event | category | flops | bytes accessed | tf_op | source)
XLA Modules:
  0.0 294.1 jit_solution(17099214346212396925)
XLA Ops:
  0.0 4.1 %copy.25 = bf16[1,1024,1024]{1,2,0:T(8,128)(2,1)} copy(bf16[1,1024,1024]{2,1,0:T(8,128)(2,1)} %param.10) | data formatting | bytes 4194304 | tf_op args[0]
  6.2 2.5 broadcast_in_dim.25
  8.7 8.8 %all-to-all-start = ((bf16[32,32,2048]{2,1,0:T(8,128)(2,1)}), bf16[32,32,2048]{2,1,0:T(8,128)(2,1)}, u32[]{:S(2)}, u32[]{:S(2)}) async-start(bf16[32,32,2048]{2,1,0:T(8,128)(2,1)} %broadcast_in_dim.25), calls=%async_computation | async-start | bytes 8388608 | tf_op jit(solution)/shard_map/all_to_all | solution.py:39
  23.7 57.6 %collective-permute-done.2 = bf16[1024,1024]{0,1:T(8,128)(2,1)} collective-permute-done((bf16[1024,1024]{0,1:T(8,128)(2,1)}, bf16[1024,1024]{0,1:T(8,128)(2,1)}, u32[]{:S(2)}, u32[]{:S(2)}) %collective-permute-start.2) | collective-permute-done | bytes 2097184 | tf_op jit(solution)/shard_map/ppermute | solution.py:31
  81.4 5.0 %convert_reduce_fusion = (f32[1024]{0:T(1024)S(1)}, bf16[1024,1024]{0,1:T(8,128)(2,1)}, f32[1024]{0:T(1024)S(1)}) fusion(bf16[1024,1024]{0,1:T(8,128)(2,1)} %collective-permute-done, bf16[1024,1024]{0,1:T(8,128)(2,1)} %collective-permute-done.1, bf16[1024,1024]{0,1:T(8,128)(2,1)} %collective-permute-done.2, pred[]{:T(512)S(6)} %eq.14, pred[]{:T(512)S(6)} %eq.13, ...), kind=kLoop, calls=%fused_computation.13 | loop fusion | flops 9435136 | bytes 10498051 | tf_op jit(solution)/shard_map/reduce_sum | solution.py:10
  86.4 7.1 %fusion.42 = f32[1024,2048]{1,0:T(8,128)S(1)} fusion(bf16[1024,2048]{1,0:T(8,128)(2,1)} %bitcast.8, bf16[1,1024,1024]{2,1,0:T(8,128)(2,1)} %param.10, f32[1024]{0:T(1024)S(1)} %bitcast.80, f32[1024]{0:T(1024)S(1)} %add_rsqrt_fusion.1, f32[1024]{0:T(1024)S(1)} %broadcast_multiply_fusion.1), kind=kOutput, calls=%fused_computation.62 | convolution fusion | flops 4300210176 | bytes 14692352 | tf_op jit(solution)/shard_map/dot_general | solution.py:69
  93.4 3.2 %copy-done.4 = f32[1024,2048]{1,0:T(8,128)} copy-done((f32[1024,2048]{1,0:T(8,128)}, f32[1024,2048]{1,0:T(8,128)S(1)}, u32[]{:S(2)}) %copy-start.4) | copy-done | bytes 8388632
  96.7 2.6 slice.41
  99.2 5.4 %copy.44 = f32[1024,1024]{0,1:T(8,128)} copy(f32[1024,1024]{1,0:T(8,128)} %slice.41) | data formatting | bytes 8388608
  104.6 4.5 %convert_reduce_fusion.2 = (f32[1024]{0:T(1024)S(1)}, bf16[1024,1024]{0,1:T(8,128)(2,1)S(1)}) fusion(f32[1024,1024]{0,1:T(8,128)} %copy.44, pred[1024]{0:T(1024)(128)(4,1)S(1)} %iota_compare_fusion), kind=kLoop, calls=%fused_computation.32 | loop fusion | flops 8387584 | bytes 6296576 | tf_op jit(solution)/shard_map/reduce_sum | solution.py:80
  109.1 3.0 %fusion.48 = f32[8,128,128]{2,1,0:T(8,128)S(1)} fusion(bf16[1024,8,128]{0,2,1:T(8,128)(2,1)S(1)} %bitcast.68, f32[1024,2048]{1,0:T(8,128)} %copy-done.4), kind=kOutput, calls=%fused_computation.66 | convolution fusion | flops 268435456 | bytes 4718592 | tf_op jit(solution)/shard_map/yzl,yzn->zln/dot_general | solution.py:74
  112.3 20.0 %all_to_all.30 = f32[32,33,128]{2,1,0:T(8,128)S(1)} all-to-all(f32[32,33,128]{2,1,0:T(8,128)S(1)} %reshape.115), channel_id=1, replica_groups=mesh['sec'=4,'pts'=32] {'pts'}, dimensions={0} | all-to-all | bytes 1081344 | tf_op jit(solution)/shard_map/all_to_all | solution.py:92
  132.4 8.1 %all_to_all.31 = f32[4,33,128]{2,1,0:T(8,128)S(1)} all-to-all(f32[4,33,128]{2,1,0:T(8,128)S(1)} %broadcast_in_dim.28), channel_id=1, replica_groups=mesh['sec'=4,'pts'=32] {'sec'}, dimensions={0} | all-to-all | bytes 135168 | tf_op jit(solution)/shard_map/all_to_all | solution.py:39
  142.1 6.0 %all-to-all-start.3 = ((f32[32,4,33,128]{3,1,2,0:T(4,128)}), f32[32,4,33,128]{3,1,2,0:T(4,128)}, u32[]{:S(2)}, u32[]{:S(2)}) async-start(f32[32,4,33,128]{3,1,2,0:T(4,128)} %broadcast_in_dim.29), calls=%async_computation.3 | async-start | bytes 4325376 | tf_op jit(solution)/shard_map/all_to_all | solution.py:39
  151.2 19.9 %collective-permute-done.5 = f32[1024]{0:T(1024)S(1)} collective-permute-done((f32[1024]{0:T(1024)S(1)}, f32[1024]{0:T(1024)S(1)}, u32[]{:S(2)}, u32[]{:S(2)}) %collective-permute-start.5) | collective-permute-done | bytes 4128 | tf_op jit(solution)/shard_map/ppermute | solution.py:31
  173.3 6.9 %fusion.15 = bf16[1024,1024]{0,1:T(8,128)(2,1)} fusion(bf16[1024,1024]{1,0:T(8,128)(2,1)} %param.15, bf16[1024,1024]{0,1:T(8,128)(2,1)S(1)} %copy-done.5, f32[1024]{0:T(1024)S(1)} %select_select_fusion.1, f32[1024]{0:T(1024)S(1)} %add_rsqrt_fusion.2, f32[1024]{0:T(1024)S(1)} %broadcast_multiply_fusion.2), kind=kOutput, calls=%fused_computation.25 | convolution fusion | flops 2157969408 | bytes 6303744 | tf_op jit(solution)/shard_map/dot_general | solution.py:103
  180.3 3.9 %copy.26 = bf16[1024,8,128]{2,0,1:T(8,128)(2,1)} copy(bf16[1024,8,128]{0,2,1:T(8,128)(2,1)} %bitcast.73) | data formatting | bytes 4194304 | tf_op jit(solution)/shard_map/reshape | solution.py:105
  184.9 3.1 %slice.43 = f32[4,1024,128]{2,0,1:T(4,128)} slice(f32[4,1056,128]{2,0,1:T(4,128)} %bitcast.13), slice={[0:4], [0:1024], [0:128]} | slice | bytes 4194304 | tf_op jit(solution)/shard_map/slice | solution.py:96
  188.0 3.0 %copy.30 = f32[8,128,4,128]{1,3,2,0:T(8,128)} copy(f32[8,128,4,128]{3,2,1,0:T(4,128)} %bitcast.69) | data formatting | bytes 4194304 | tf_op jit(solution)/shard_map/transpose | solution.py:109
  193.1 2.2 fusion.60
  195.4 16.3 %fusion = f32[8,1024,640]{1,2,0:T(8,128)} fusion(bf16[8,1024,128]{2,1,0:T(8,128)(2,1)} %bitcast.72, bf16[8,128,640]{1,2,0:T(8,128)(2,1)} %get-tuple-element.12, bf16[8,128,640]{1,2,0:T(8,128)(2,1)} %get-tuple-element.11, bf16[8,128,640]{1,2,0:T(8,128)(2,1)S(1)} %fusion.24), kind=kOutput, calls=%fused_computation.5 | convolution fusion | flops 4057202688 | bytes 27000832 | tf_op jit(solution)/shard_map/hrk,hkc->hrc/dot_general | solution.py:123
  212.6 11.9 %slice.45 = f32[8,1024,512]{1,2,0:T(8,128)} slice(f32[8,1024,640]{1,2,0:T(8,128)} %fusion), slice={[0:8], [0:1024], [0:512]} | slice | bytes 33554432 | tf_op jit(solution)/shard_map/slice | solution.py:124
  224.6 10.3 %divide_reduce_fusion = bf16[8,1024,128]{1,2,0:T(8,128)(2,1)} fusion(f32[8,1024,4,128]{1,3,2,0:T(8,128)} %bitcast.63, f32[8,1024,4]{1,2,0:T(4,128)S(1)} %slice.46), kind=kLoop, calls=%fused_computation | loop fusion | flops 7340032 | bytes 19005440 | tf_op jit(solution)/shard_map/reduce_sum | solution.py:126
  234.8 4.7 %fusion.94 = (f32[1024]{0:T(1024)S(1)}, f32[1024,1024]{0,1:T(8,128)S(1)}) fusion(bf16[8,1024,128]{1,2,0:T(8,128)(2,1)} %divide_reduce_fusion, bf16[8,128,1024]{2,1,0:T(8,128)(2,1)S(1)} %bitcast.62, bf16[1024,1024]{0,1:T(8,128)(2,1)} %get-tuple-element.8), kind=kOutput, calls=%fused_computation.120 | convolution fusion | flops 2150628352 | bytes 10489856 | tf_op jit(solution)/shard_map/hrv,hvd->rd/dot_general | solution.py:127
  243.3 5.1 %convolution_convert_fusion = bf16[512,1024]{1,0:T(8,128)(2,1)S(1)} fusion(bf16[1024,1024]{1,0:T(8,128)(2,1)} %param.19, bf16[1024,1024]{1,0:T(8,128)(2,1)} %param.18, bf16[1024,1024]{0,1:T(8,128)(2,1)} %multiply_convert_fusion), kind=kOutput, calls=%fused_computation.79 | convolution fusion | flops 2152726528 | bytes 6291456 | tf_op jit(solution)/shard_map/dot_general | solution.py:144
  249.4 3.5 %all-to-all-start.5 = ((bf16[4,512,256]{2,1,0:T(8,128)(2,1)}), bf16[4,512,256]{2,1,0:T(8,128)(2,1)S(1)}, u32[]{:S(2)}, u32[]{:S(2)}) async-start(bf16[4,512,256]{2,1,0:T(8,128)(2,1)} %bitcast.71), calls=%async_computation.5 | async-start | bytes 2097152 | tf_op jit(solution)/shard_map/all_to_all | solution.py:147
  252.9 6.0 %convolution_convert_fusion.1 = bf16[512,1024]{1,0:T(8,128)(2,1)} fusion(bf16[1024,1024]{1,0:T(8,128)(2,1)} %param.19, bf16[1024,1024]{1,0:T(8,128)(2,1)} %param.18, bf16[1024,1024]{0,1:T(8,128)(2,1)} %multiply_convert_fusion), kind=kOutput, calls=%fused_computation.80 | convolution fusion | flops 2152726528 | bytes 6291456 | tf_op jit(solution)/shard_map/dot_general | solution.py:144
  259.0 2.4 copy.55
  261.4 7.5 %all-to-all-done.5 = bf16[4,512,256]{2,1,0:T(8,128)(2,1)S(1)} async-done(((bf16[4,512,256]{2,1,0:T(8,128)(2,1)}), bf16[4,512,256]{2,1,0:T(8,128)(2,1)S(1)}, u32[]{:S(2)}, u32[]{:S(2)}) %all-to-all-start.5) | async-done | bytes 1048608 | tf_op jit(solution)/shard_map/all_to_all | solution.py:147
  268.9 4.2 %all-to-all-start.4 = ((bf16[4,512,256]{2,1,0:T(8,128)(2,1)}), bf16[4,512,256]{2,1,0:T(8,128)(2,1)}, u32[]{:S(2)}, u32[]{:S(2)}) async-start(bf16[4,512,256]{2,1,0:T(8,128)(2,1)} %bitcast.70), calls=%async_computation.4 | async-start | bytes 2097152 | tf_op jit(solution)/shard_map/all_to_all | solution.py:147
  273.1 4.6 %fusion.93 = (f32[512,1024]{0,1:T(8,128)}, f32[512,1024]{0,1:T(8,128)}) fusion(f32[1024,1024]{0,1:T(8,128)} %copy-done.1), kind=kLoop, calls=%fused_computation.119 | loop fusion | bytes 8388608 | tf_op jit(solution)/shard_map/slice | solution.py:149
  279.9 9.2 %all-to-all-done.4 = bf16[4,512,256]{2,1,0:T(8,128)(2,1)} async-done(((bf16[4,512,256]{2,1,0:T(8,128)(2,1)}), bf16[4,512,256]{2,1,0:T(8,128)(2,1)}, u32[]{:S(2)}, u32[]{:S(2)}) %all-to-all-start.4) | async-done | bytes 1048608 | tf_op jit(solution)/shard_map/all_to_all | solution.py:147
  (65 shorter events, 30.5 us)
Async XLA Ops:
  0.0 234.8 %copy-start = (bf16[1024,1024]{1,0:T(8,128)(2,1)S(1)}, bf16[1024,1024]{1,0:T(8,128)(2,1)}, u32[]{:S(2)}) copy-start(bf16[1024,1024]{1,0:T(8,128)(2,1)} %param.16) | copy-start | bytes 6291460
  0.0 6.2 %copy-start.6 = (bf16[1,32,1024]{2,1,0:T(8,128)(2,1)S(1)}, bf16[1,32,1024]{2,1,0:T(8,128)(2,1)}, u32[]{:S(2)}) copy-start(bf16[1,32,1024]{2,1,0:T(8,128)(2,1)} %param.14) | copy-start | bytes 196612
  0.0 6.2 %copy-start.7 = (bf16[1,32,1024]{2,1,0:T(8,128)(2,1)S(1)}, bf16[1,32,1024]{2,1,0:T(8,128)(2,1)}, u32[]{:S(2)}) copy-start(bf16[1,32,1024]{2,1,0:T(8,128)(2,1)} %param.13) | copy-start | bytes 196612
  4.1 15.4 %collective-permute-start.1 = (bf16[1024,1024]{0,1:T(8,128)(2,1)}, bf16[1024,1024]{0,1:T(8,128)(2,1)}, u32[]{:S(2)}, u32[]{:S(2)}) collective-permute-start(bf16[1024,1024]{0,1:T(8,128)(2,1)} %bitcast.64), channel_id=1, source_target_pairs={{96,32},{97,33},{98,34},{99,35},{100,36},{101,37},{102,38},{103,39... | collective-permute-start | bytes 6291464 | tf_op jit(solution)/shard_map/ppermute | solution.py:29
  8.7 77.7 %all-to-all-start = ((bf16[32,32,2048]{2,1,0:T(8,128)(2,1)}), bf16[32,32,2048]{2,1,0:T(8,128)(2,1)}, u32[]{:S(2)}, u32[]{:S(2)}) async-start(bf16[32,32,2048]{2,1,0:T(8,128)(2,1)} %broadcast_in_dim.25), calls=%async_computation | async-start | bytes 8388608 | tf_op jit(solution)/shard_map/all_to_all | solution.py:39
  17.5 6.2 %collective-permute-start = (bf16[1024,1024]{0,1:T(8,128)(2,1)}, bf16[1024,1024]{0,1:T(8,128)(2,1)}, u32[]{:S(2)}, u32[]{:S(2)}) collective-permute-start(bf16[1024,1024]{0,1:T(8,128)(2,1)} %bitcast.65), channel_id=1, source_target_pairs={{96,64},{97,65},{98,66},{99,67},{100,68},{101,69},{102,70},{103,71... | collective-permute-start | bytes 6291464 | tf_op jit(solution)/shard_map/ppermute | solution.py:30
  19.6 61.8 %collective-permute-start.2 = (bf16[1024,1024]{0,1:T(8,128)(2,1)}, bf16[1024,1024]{0,1:T(8,128)(2,1)}, u32[]{:S(2)}, u32[]{:S(2)}) collective-permute-start(bf16[1024,1024]{0,1:T(8,128)(2,1)} %collective-permute-done.1), channel_id=1, source_target_pairs={{32,0},{33,1},{34,2},{35,3},{36,4},{37,5},{38,6},{39,7},{40,8},{41... | collective-permute-start | bytes 6291464 | tf_op jit(solution)/shard_map/ppermute | solution.py:31
  20.9 60.5 %copy-start.2 = (bf16[1,1024,1024]{1,2,0:T(8,128)(2,1)S(1)}, bf16[1,1024,1024]{1,2,0:T(8,128)(2,1)}, u32[]{:S(2)}) copy-start(bf16[1,1024,1024]{1,2,0:T(8,128)(2,1)} %copy.25) | copy-start | bytes 6291460
  23.7 62.6 %copy-start.8 = (f32[1,1024]{1,0:T(1,128)S(1)}, f32[1,1024]{1,0:T(1,128)}, u32[]{:S(2)}) copy-start(f32[1,1024]{1,0:T(1,128)} %param.12) | copy-start | bytes 12292
  93.4 3.2 %copy-start.4 = (f32[1024,2048]{1,0:T(8,128)}, f32[1024,2048]{1,0:T(8,128)S(1)}, u32[]{:S(2)}) copy-start(f32[1024,2048]{1,0:T(8,128)S(1)} %fusion.42) | copy-start | bytes 25165828
  142.1 42.1 %all-to-all-start.3 = ((f32[32,4,33,128]{3,1,2,0:T(4,128)}), f32[32,4,33,128]{3,1,2,0:T(4,128)}, u32[]{:S(2)}, u32[]{:S(2)}) async-start(f32[32,4,33,128]{3,1,2,0:T(4,128)} %broadcast_in_dim.29), calls=%async_computation.3 | async-start | bytes 4325376 | tf_op jit(solution)/shard_map/all_to_all | solution.py:39
  148.1 25.2 %copy-start.5 = (bf16[1024,1024]{0,1:T(8,128)(2,1)S(1)}, bf16[1024,1024]{0,1:T(8,128)(2,1)}, u32[]{:S(2)}) copy-start(bf16[1024,1024]{0,1:T(8,128)(2,1)} %get-tuple-element.8) | copy-start | bytes 6291460
  148.1 1.5 collective-permute-start.4
  148.9 2.2 collective-permute-start.3
  149.6 21.5 %collective-permute-start.5 = (f32[1024]{0:T(1024)S(1)}, f32[1024]{0:T(1024)S(1)}, u32[]{:S(2)}, u32[]{:S(2)}) collective-permute-start(f32[1024]{0:T(1024)S(1)} %collective-permute-done.4), channel_id=1, source_target_pairs={{32,0},{33,1},{34,2},{35,3},{36,4},{37,5},{38,6},{39,7},{40,8},{41... | collective-permute-start | bytes 12296 | tf_op jit(solution)/shard_map/ppermute | solution.py:31
  190.9 2.2 copy-start.3
  239.5 1.9 copy-start.1
  239.5 1.9 copy-start.9
  249.4 19.4 %all-to-all-start.5 = ((bf16[4,512,256]{2,1,0:T(8,128)(2,1)}), bf16[4,512,256]{2,1,0:T(8,128)(2,1)S(1)}, u32[]{:S(2)}, u32[]{:S(2)}) async-start(bf16[4,512,256]{2,1,0:T(8,128)(2,1)} %bitcast.71), calls=%async_computation.5 | async-start | bytes 2097152 | tf_op jit(solution)/shard_map/all_to_all | solution.py:147
  268.9 20.3 %all-to-all-start.4 = ((bf16[4,512,256]{2,1,0:T(8,128)(2,1)}), bf16[4,512,256]{2,1,0:T(8,128)(2,1)}, u32[]{:S(2)}, u32[]{:S(2)}) async-start(bf16[4,512,256]{2,1,0:T(8,128)(2,1)} %bitcast.70), calls=%async_computation.4 | async-start | bytes 2097152 | tf_op jit(solution)/shard_map/all_to_all | solution.py:147

commit v4 on v1

--- a/solution.py
+++ b/solution.py
@@ -39,6 +39,24 @@
     return lax.all_to_all(spread, axis, 0, 0, tiled=False)
 
 
+def scatter_sum(term, me, sections):
+    rows, width = term.shape
+    share = width // sections
+    if sections != 4:
+        parts = term.astype(jnp.bfloat16).reshape(rows, sections, share).transpose(1, 0, 2)
+        got = lax.all_to_all(parts, "sec", 0, 0, tiled=False)
+        return jnp.sum(got.astype(jnp.float32), axis=0)
+    half = width // 2
+    mine = me // 2
+    sent = lax.dynamic_slice_in_dim(term, (1 - mine) * half, half, axis=1)
+    got = lax.ppermute(sent.astype(jnp.bfloat16), "sec", [(0, 2), (2, 0), (1, 3), (3, 1)])
+    halved = lax.dynamic_slice_in_dim(term, mine * half, half, axis=1) + got.astype(jnp.float32)
+    inner = me % 2
+    sent = lax.dynamic_slice_in_dim(halved, (1 - inner) * share, share, axis=1)
+    got = lax.ppermute(sent.astype(jnp.bfloat16), "sec", [(0, 1), (1, 0), (2, 3), (3, 2)])
+    return lax.dynamic_slice_in_dim(halved, inner * share, share, axis=1) + got.astype(jnp.float32)
+
+
 def on_device(
     points,
     counts,
@@ -59,11 +77,12 @@
     blocks = lax.axis_size("pts")
     me = lax.axis_index("sec")
 
-    query_block = from_last(block, "sec", sections)
-    query_gain = from_last(input_gain[0], "sec", sections)
-
     stacked = jnp.concatenate([key_weight[0], value_weight[0]], axis=1)
     weights = gather_a2a(stacked, "pts", blocks).reshape(width, 2 * width)
+
+    late_block, late_gain, weights = lax.optimization_barrier((block, input_gain[0], weights))
+    query_block = from_last(late_block, "sec", sections)
+    query_gain = from_last(late_gain, "sec", sections)
 
     normed = layer_normalizer(block.astype(jnp.float32), input_gain[0]).astype(jnp.bfloat16)
     projected = jnp.dot(normed, weights, preferred_element_type=jnp.float32)
@@ -121,10 +140,8 @@
     ).astype(jnp.bfloat16)
     term = jnp.dot(hidden, down_weight, preferred_element_type=jnp.float32)
     share = width // sections
-    parts = term.astype(jnp.bfloat16).reshape(rows, sections, share).transpose(1, 0, 2)
-    summed = jnp.sum(lax.all_to_all(parts, "sec", 0, 0, tiled=False).astype(jnp.float32), axis=0)
     own_mixed = lax.dynamic_slice_in_dim(mixed, me * share, share, axis=1)
-    return (own_mixed + summed).astype(jnp.bfloat16)
+    return (own_mixed + scatter_sum(term, me, sections)).astype(jnp.bfloat16)
 
 
 def solution(mesh):

time: 245 us -> 240 us (0.980); the launches traced: 244 us -> 237 us
  blocking collectives: 28.1 us -> 19.4 us
  starting transfers between devices: 27.3 us -> 32.6 us
    ppermute x2, waiting for transfers between devices: 77.9 us -> 22 us  [from_last(): farther = lax.ppermute(far, axis, [(1, 0)])]
    all_to_all x2 -> x3, waiting for transfers between devices: 0.01 us -> 55.6 us  [gather_a2a(): return lax.all_to_all(spread, axis, 0, 0, tiled=False)]
    all_to_all x1 -> x0, waiting for transfers between devices: 27.2 us -> none  [on_device(): lax.all_to_all(parts, 'sec', 0, 0, tiled=False).astype(jnp.float32)]
    ppermute x0 -> x2, waiting for transfers between devices: none -> 25.3 us  [the longest x1 23.4 us: scatter_sum(): lax.ppermute(sent.astype(jnp.bfloat16), 'sec', [(0, 2), (2, 0), (1, 3), (...]
    all_to_all x1 -> x0, blocking collectives: 8.08 us -> none  [gather_a2a(): return lax.all_to_all(spread, axis, 0, 0, tiled=False)]
    all_to_all x2 -> x3, starting transfers between devices: 14.8 us -> 21.6 us  [gather_a2a(): return lax.all_to_all(spread, axis, 0, 0, tiled=False)]
    all_to_all x1 -> x0, starting transfers between devices: 4.44 us -> none  [on_device(): lax.all_to_all(parts, 'sec', 0, 0, tiled=False).astype(jnp.float32)]
    ppermute x0 -> x2, starting transfers between devices: none -> 2.96 us  [the longest x1 2.87 us: scatter_sum(): lax.ppermute(sent.astype(jnp.bfloat16), 'sec', [(0, 2), (2, 0), (1, 3), (...]
  transfers between devices with their start and end apart: 9 -> 11, of which waited for: 3 -> 6; matrix products, arithmetic and copies ran while one was open for 8% -> 12% of each run, Pallas kernels for 0% -> 0%
where the time goes in v4:
time: 240 us; the launch traced here: 237 us
  waiting for transfers between devices  103 us (43%)
  matrix products  39.1 us (16%)
  starting transfers between devices  32.6 us (14%)
  local copies, waits for them, and re-layouts  24.9 us (10%)
  blocking collectives  19.4 us (8%)
  other arithmetic  16.4 us (7%)
    all_to_all x3, waiting for transfers between devices, gather_a2a(): return lax.all_to_all(spread, axis, 0, 0, tiled=False)  55.6 us
    ppermute x1, waiting for transfers between devices, scatter_sum(): lax.ppermute(sent.astype(jnp.bfloat16), 'sec', [(0, 2), (2, 0), (1, 3), (...  23.4 us
    ppermute x2, waiting for transfers between devices, from_last(): farther = lax.ppermute(far, axis, [(1, 0)])  22 us
    all_to_all x3, starting transfers between devices, gather_a2a(): return lax.all_to_all(spread, axis, 0, 0, tiled=False)  21.6 us
    all_to_all x1, blocking collectives, on_device(): reduced = jnp.sum(lax.all_to_all(packed, 'pts', 0, 0, tiled=False), axis=0)  19.4 us
    unnamed x20, local copies, waits for them, and re-layouts  11.4 us
    dot_general x1, matrix products, on_device(): term = jnp.dot(hidden, down_weight, preferred_element_type=jnp.float32)  10.7 us
    dot_general x1, matrix products, on_device(): jnp.einsum('rhk,shkv->srhv', per_head_queries, state_heads, precision=lax...  8.47 us
  transfers between devices with their start and end apart: 11, of which 6 were waited for; matrix products, arithmetic and copies ran while one was open for 12% of the time, Pallas kernels for 0%

profile of v4, /device:TPU:16, one launch (start us, length us, event | category | flops | bytes accessed | tf_op | source)
XLA Modules:
  0.0 236.5 jit_solution(7956941792710584428)
XLA Ops:
  1.0 2.5 %broadcast_in_dim.22 = bf16[32,32,2048]{2,1,0:T(8,128)(2,1)} broadcast(bf16[32,2048]{1,0:T(8,128)(2,1)S(1)} %pad_maximum_fusion), dimensions={1,2} | broadcast | bytes 4325376 | tf_op jit(solution)/shard_map/broadcast_in_dim | solution.py:38
  3.5 8.8 %all-to-all-start = ((bf16[32,32,2048]{2,1,0:T(8,128)(2,1)}), bf16[32,32,2048]{2,1,0:T(8,128)(2,1)}, u32[]{:S(2)}, u32[]{:S(2)}) async-start(bf16[32,32,2048]{2,1,0:T(8,128)(2,1)} %broadcast_in_dim.22), calls=%async_computation | async-start | bytes 8388608 | tf_op jit(solution)/shard_map/all_to_all | solution.py:39
  12.4 3.9 %copy.35 = bf16[1,1024,1024]{1,2,0:T(8,128)(2,1)} copy(bf16[1,1024,1024]{2,1,0:T(8,128)(2,1)} %param.10) | data formatting | bytes 4194304 | tf_op args[0]
  17.2 2.0 convert_reduce_fusion.1
  19.8 50.2 %all-to-all-done = bf16[32,32,2048]{2,1,0:T(8,128)(2,1)} async-done(((bf16[32,32,2048]{2,1,0:T(8,128)(2,1)}), bf16[32,32,2048]{2,1,0:T(8,128)(2,1)}, u32[]{:S(2)}, u32[]{:S(2)}) %all-to-all-start) | async-done | bytes 4194336 | tf_op jit(solution)/shard_map/all_to_all | solution.py:39
  70.0 2.0 collective-permute-start.1
  72.0 7.3 %fusion.30 = f32[1024,2048]{1,0:T(8,128)S(1)} fusion(bf16[1024,2048]{1,0:T(8,128)(2,1)} %bitcast.4, f32[1024]{0:T(1024)S(1)} %bitcast.66, f32[1024]{0:T(1024)S(1)} %add_rsqrt_fusion.2, f32[1024]{0:T(1024)S(1)} %broadcast_multiply_fusion.2, bf16[1,1024,1024]{1,2,0:T(8,128)(2,1)} %copy.35), kind=kOutput, calls=%fused_computation.44 | convolution fusion | flops 4300210176 | bytes 14692352 | tf_op jit(solution)/shard_map/dot_general | solution.py:88
  79.3 3.2 %copy-done.3 = f32[1024,2048]{1,0:T(8,128)} copy-done((f32[1024,2048]{1,0:T(8,128)}, f32[1024,2048]{1,0:T(8,128)S(1)}, u32[]{:S(2)}) %copy-start.3) | copy-done | bytes 8388632
  82.5 3.6 %convert_reduce_fusion.2 = (f32[1024]{0:T(1024)S(1)}, bf16[1024,1024]{1,0:T(8,128)(2,1)}) fusion(f32[1024,2048]{1,0:T(8,128)S(1)} %fusion.30, pred[1024]{0:T(1024)(128)(4,1)S(1)} %iota_compare_fusion), kind=kLoop, calls=%fused_computation.39 | loop fusion | flops 8387584 | bytes 6296576 | tf_op jit(solution)/shard_map/reduce_sum | solution.py:99
  86.1 3.9 %copy.53 = bf16[1024,1024]{0,1:T(8,128)(2,1)} copy(bf16[1024,1024]{1,0:T(8,128)(2,1)} %get-tuple-element.14) | data formatting | bytes 4194304 | tf_op jit(solution)/shard_map/reshape | solution.py:95
  90.0 3.6 %fusion.37 = f32[8,128,128]{2,1,0:T(8,128)S(1)} fusion(bf16[1024,8,128]{0,2,1:T(8,128)(2,1)} %bitcast.58, f32[1024,2048]{1,0:T(8,128)} %copy-done.3), kind=kOutput, calls=%fused_computation.49 | convolution fusion | flops 268435456 | bytes 4718592 | tf_op jit(solution)/shard_map/yzl,yzn->zln/dot_general | solution.py:93
  93.9 19.4 %all_to_all.20 = f32[32,33,128]{2,1,0:T(8,128)S(1)} all-to-all(f32[32,33,128]{2,1,0:T(8,128)S(1)} %reshape.80), channel_id=1, replica_groups=mesh['sec'=4,'pts'=32] {'pts'}, dimensions={0} | all-to-all | bytes 1081344 | tf_op jit(solution)/shard_map/all_to_all | solution.py:111
  114.0 7.0 %all-to-all-start.2 = ((f32[4,33,128]{2,1,0:T(8,128)}), f32[4,33,128]{2,1,0:T(8,128)S(1)}, u32[]{:S(2)}, u32[]{:S(2)}) async-start(f32[4,33,128]{2,1,0:T(8,128)} %broadcast_in_dim.26), calls=%async_computation.2 | async-start | bytes 163840 | tf_op jit(solution)/shard_map/all_to_all | solution.py:39
  121.0 2.0 collective-permute-start
  124.3 2.4 %all-to-all-done.2 = f32[4,33,128]{2,1,0:T(8,128)S(1)} async-done(((f32[4,33,128]{2,1,0:T(8,128)}), f32[4,33,128]{2,1,0:T(8,128)S(1)}, u32[]{:S(2)}, u32[]{:S(2)}) %all-to-all-start.2) | async-done | bytes 67616 | tf_op jit(solution)/shard_map/all_to_all | solution.py:39
  128.3 5.8 %all-to-all-start.3 = ((f32[32,4,33,128]{3,1,2,0:T(4,128)}), f32[32,4,33,128]{3,1,2,0:T(4,128)}, u32[]{:S(2)}, u32[]{:S(2)}) async-start(f32[32,4,33,128]{3,1,2,0:T(4,128)} %broadcast_in_dim.27), calls=%async_computation.3 | async-start | bytes 4325376 | tf_op jit(solution)/shard_map/all_to_all | solution.py:39
  137.0 22.0 %collective-permute-done.5 = f32[1024]{0:T(1024)S(1)} collective-permute-done((f32[1024]{0:T(1024)S(1)}, f32[1024]{0:T(1024)S(1)}, u32[]{:S(2)}, u32[]{:S(2)}) %collective-permute-start.5) | collective-permute-done | bytes 4128 | tf_op jit(solution)/shard_map/ppermute | solution.py:31
  159.0 2.9 %all-to-all-done.3 = f32[32,4,33,128]{3,1,2,0:T(4,128)} async-done(((f32[32,4,33,128]{3,1,2,0:T(4,128)}), f32[32,4,33,128]{3,1,2,0:T(4,128)}, u32[]{:S(2)}, u32[]{:S(2)}) %all-to-all-start.3) | async-done | bytes 2162720 | tf_op jit(solution)/shard_map/all_to_all | solution.py:39
  162.0 1.9 slice.19
  164.2 3.8 %convert_reduce_fusion = (f32[1024]{0:T(1024)S(1)}, bf16[1024,1024]{0,1:T(8,128)(2,1)S(1)}) fusion(bf16[1024,1024]{0,1:T(8,128)(2,1)S(1)} %bitcast.57, bf16[1024,1024]{0,1:T(8,128)(2,1)} %collective-permute-done, bf16[1024,1024]{0,1:T(8,128)(2,1)} %collective-permute-done.1, bf16[1024,1024]{0,1:T(8,128)(2,1)} %collective-permute-done.2, pred[]{:T(512)S(6)} %eq.16, ...), kind=kLoop, calls=%fused_computation.9 | loop fusion | flops 5241856 | bytes 10489859 | tf_op jit(solution)/shard_map/reduce_sum | solution.py:10
  168.7 4.1 %fusion.24 = bf16[1024,1024]{1,0:T(8,128)(2,1)S(1)} fusion(bf16[1024,1024]{1,0:T(8,128)(2,1)S(1)} %copy-done.7, bf16[1024,1024]{0,1:T(8,128)(2,1)S(1)} %get-tuple-element.12, f32[1024]{0:T(1024)S(1)} %select_select_fusion.1, f32[1024]{0:T(1024)S(1)} %add_rsqrt_fusion.1, f32[1024]{0:T(1024)S(1)} %broadcast_multiply_fusion.1), kind=kOutput, calls=%fused_computation.35 | convolution fusion | flops 2157969408 | bytes 6303744 | tf_op jit(solution)/shard_map/dot_general | solution.py:122
  172.7 2.4 %fusion.57 = f32[4,1024,8]{1,0,2:T(4,128)S(1)} fusion(f32[4,1056,128]{2,0,1:T(4,128)} %bitcast.10, bf16[1024,1024]{1,0:T(8,128)(2,1)S(1)} %fusion.24), kind=kOutput, calls=%fused_computation.70 | convolution fusion | flops 50331648 | bytes 4390912 | tf_op jit(solution)/shard_map/rhk,shk->srh/dot_general | solution.py:128
  175.8 8.5 %fusion = bf16[1024,8,128]{0,2,1:T(8,128)(2,1)S(1)} fusion(f32[4,1024,8]{1,0,2:T(4,128)S(1)} %fusion.57, bf16[1024,8,128,1]{2,1,0,3:T(8,128)(2,1)S(1)} %bitcast.61, f32[4,8,128,128]{3,0,2,1:T(4,128)S(1)} %bitcast.59), kind=kOutput, calls=%fused_computation.1 | convolution fusion | flops 6449790976 | bytes 6422528 | tf_op jit(solution)/shard_map/rhk,shkv->srhv/dot_general | solution.py:125
  184.3 2.6 %fusion.66 = (f32[1024]{0:T(1024)S(1)}, f32[1024,1024]{0,1:T(8,128)S(1)}) fusion(bf16[1024,1024]{0,1:T(8,128)(2,1)S(1)} %bitcast.70, bf16[1024,1024]{1,0:T(8,128)(2,1)S(1)} %copy-done, bf16[1024,1024]{0,1:T(8,128)(2,1)S(1)} %get-tuple-element.12), kind=kOutput, calls=%fused_computation.88 | convolution fusion | flops 2150628352 | bytes 10489856 | tf_op jit(solution)/shard_map/dot_general | solution.py:134
  186.9 1.9 copy-done.4
  189.3 10.7 %fusion.28 = f32[1024,1024]{0,1:T(8,128)} fusion(bf16[1024,1024]{1,0:T(8,128)(2,1)} %param.19, bf16[1024,1024]{1,0:T(8,128)(2,1)} %param.18, f32[1024,1024]{0,1:T(8,128)} %copy-done.4, f32[1024]{0:T(1024)S(1)} %copy-done.8, f32[1024]{0:T(1024)S(1)} %add_rsqrt_fusion, f32[1024]{0:T(1024)S(1)} %broadcast_multiply_fusion), kind=kOutput, calls=%fused_computation.43 | convolution fusion | flops 4308598784 | bytes 12595200 | tf_op jit(solution)/shard_map/dot_general | solution.py:141
  200.0 1.7 dynamic-slice_convert_fusion
  201.8 2.9 %collective-permute-start.6 = (bf16[1024,512]{0,1:T(8,128)(2,1)S(1)}, bf16[1024,512]{0,1:T(8,128)(2,1)}, u32[]{:S(2)}, u32[]{:S(2)}) collective-permute-start(bf16[1024,512]{0,1:T(8,128)(2,1)S(1)} %dynamic-slice_convert_fusion), channel_id=1, source_target_pairs={{0,64},{64,0},{32,96},{96,32},{1,65},{65,1},{33,97},{97,33},{2,66}... | collective-permute-start | bytes 3145736 | tf_op jit(solution)/shard_map/ppermute | solution.py:52
  204.7 23.4 %collective-permute-done.6 = bf16[1024,512]{0,1:T(8,128)(2,1)} collective-permute-done((bf16[1024,512]{0,1:T(8,128)(2,1)S(1)}, bf16[1024,512]{0,1:T(8,128)(2,1)}, u32[]{:S(2)}, u32[]{:S(2)}) %collective-permute-start.6) | collective-permute-done | bytes 1048608 | tf_op jit(solution)/shard_map/ppermute | solution.py:52
  228.1 2.2 convert_add_fusion.1
  231.8 1.9 collective-permute-done.7
  233.7 1.8 add_convert_fusion
  (49 shorter events, 13.0 us)
Async XLA Ops:
  0.0 184.3 %copy-start = (bf16[1024,1024]{1,0:T(8,128)(2,1)S(1)}, bf16[1024,1024]{1,0:T(8,128)(2,1)}, u32[]{:S(2)}) copy-start(bf16[1024,1024]{1,0:T(8,128)(2,1)} %param.16) | copy-start | bytes 6291460
  3.5 66.5 %all-to-all-start = ((bf16[32,32,2048]{2,1,0:T(8,128)(2,1)}), bf16[32,32,2048]{2,1,0:T(8,128)(2,1)}, u32[]{:S(2)}, u32[]{:S(2)}) async-start(bf16[32,32,2048]{2,1,0:T(8,128)(2,1)} %broadcast_in_dim.22), calls=%async_computation | async-start | bytes 8388608 | tf_op jit(solution)/shard_map/all_to_all | solution.py:39
  16.3 2.9 %copy-start.1 = (bf16[1,1024,1024]{1,2,0:T(8,128)(2,1)S(1)}, bf16[1,1024,1024]{1,2,0:T(8,128)(2,1)}, u32[]{:S(2)}) copy-start(bf16[1,1024,1024]{1,2,0:T(8,128)(2,1)} %copy.35) | copy-start | bytes 6291460
  16.3 55.7 %copy-start.6 = (f32[1,1024]{1,0:T(1,128)S(1)}, f32[1,1024]{1,0:T(1,128)}, u32[]{:S(2)}) copy-start(f32[1,1024]{1,0:T(1,128)} %param.12) | copy-start | bytes 12292
  70.0 52.9 %collective-permute-start.1 = (bf16[1024,1024]{0,1:T(8,128)(2,1)}, bf16[1024,1024]{0,1:T(8,128)(2,1)}, u32[]{:S(2)}, u32[]{:S(2)}) collective-permute-start(bf16[1024,1024]{0,1:T(8,128)(2,1)} %bitcast.55), channel_id=1, source_target_pairs={{96,32},{97,33},{98,34},{99,35},{100,36},{101,37},{102,38},{103,39... | collective-permute-start | bytes 6291464 | tf_op jit(solution)/shard_map/ppermute | solution.py:29
  79.2 3.2 %copy-start.3 = (f32[1024,2048]{1,0:T(8,128)}, f32[1024,2048]{1,0:T(8,128)S(1)}, u32[]{:S(2)}) copy-start(f32[1024,2048]{1,0:T(8,128)S(1)} %fusion.30) | copy-start | bytes 25165828
  114.0 12.7 %all-to-all-start.2 = ((f32[4,33,128]{2,1,0:T(8,128)}), f32[4,33,128]{2,1,0:T(8,128)S(1)}, u32[]{:S(2)}, u32[]{:S(2)}) async-start(f32[4,33,128]{2,1,0:T(8,128)} %broadcast_in_dim.26), calls=%async_computation.2 | async-start | bytes 163840 | tf_op jit(solution)/shard_map/all_to_all | solution.py:39
  121.0 42.9 %collective-permute-start = (bf16[1024,1024]{0,1:T(8,128)(2,1)}, bf16[1024,1024]{0,1:T(8,128)(2,1)}, u32[]{:S(2)}, u32[]{:S(2)}) collective-permute-start(bf16[1024,1024]{0,1:T(8,128)(2,1)} %bitcast.56), channel_id=1, source_target_pairs={{96,64},{97,65},{98,66},{99,67},{100,68},{101,69},{102,70},{103,71... | collective-permute-start | bytes 6291464 | tf_op jit(solution)/shard_map/ppermute | solution.py:30
  123.0 40.9 %collective-permute-start.2 = (bf16[1024,1024]{0,1:T(8,128)(2,1)}, bf16[1024,1024]{0,1:T(8,128)(2,1)}, u32[]{:S(2)}, u32[]{:S(2)}) collective-permute-start(bf16[1024,1024]{0,1:T(8,128)(2,1)} %collective-permute-done.1), channel_id=1, source_target_pairs={{32,0},{33,1},{34,2},{35,3},{36,4},{37,5},{38,6},{39,7},{40,8},{41... | collective-permute-start | bytes 6291464 | tf_op jit(solution)/shard_map/ppermute | solution.py:31
  128.3 33.7 %all-to-all-start.3 = ((f32[32,4,33,128]{3,1,2,0:T(4,128)}), f32[32,4,33,128]{3,1,2,0:T(4,128)}, u32[]{:S(2)}, u32[]{:S(2)}) async-start(f32[32,4,33,128]{3,1,2,0:T(4,128)} %broadcast_in_dim.27), calls=%async_computation.3 | async-start | bytes 4325376 | tf_op jit(solution)/shard_map/all_to_all | solution.py:39
  134.1 1.3 collective-permute-start.4
  134.8 2.2 collective-permute-start.3
  135.5 23.6 %collective-permute-start.5 = (f32[1024]{0:T(1024)S(1)}, f32[1024]{0:T(1024)S(1)}, u32[]{:S(2)}, u32[]{:S(2)}) collective-permute-start(f32[1024]{0:T(1024)S(1)} %collective-permute-done.4), channel_id=1, source_target_pairs={{32,0},{33,1},{34,2},{35,3},{36,4},{37,5},{38,6},{39,7},{40,8},{41... | collective-permute-start | bytes 12296 | tf_op jit(solution)/shard_map/ppermute | solution.py:31
  162.0 2.2 copy-start.2
  163.9 4.8 %copy-start.7 = (bf16[1024,1024]{1,0:T(8,128)(2,1)S(1)}, bf16[1024,1024]{1,0:T(8,128)(2,1)}, u32[]{:S(2)}) copy-start(bf16[1024,1024]{1,0:T(8,128)(2,1)} %param.15) | copy-start | bytes 6291460
  186.9 1.9 copy-start.4
  186.9 2.4 %copy-start.8 = (f32[1024]{0:T(1024)S(1)}, f32[1024]{0:T(1024)}, u32[]{:S(2)}) copy-start(f32[1024]{0:T(1024)} %param.17) | copy-start | bytes 12292
  201.8 26.3 %collective-permute-start.6 = (bf16[1024,512]{0,1:T(8,128)(2,1)S(1)}, bf16[1024,512]{0,1:T(8,128)(2,1)}, u32[]{:S(2)}, u32[]{:S(2)}) collective-permute-start(bf16[1024,512]{0,1:T(8,128)(2,1)S(1)} %dynamic-slice_convert_fusion), channel_id=1, source_target_pairs={{0,64},{64,0},{32,96},{96,32},{1,65},{65,1},{33,97},{97,33},{2,66}... | collective-permute-start | bytes 3145736 | tf_op jit(solution)/shard_map/ppermute | solution.py:52
  230.3 1.3 copy-start.5
  231.7 2.0 collective-permute-start.7

commit v5 on v4

--- a/solution.py
+++ b/solution.py
@@ -46,15 +46,17 @@
         parts = term.astype(jnp.bfloat16).reshape(rows, sections, share).transpose(1, 0, 2)
         got = lax.all_to_all(parts, "sec", 0, 0, tiled=False)
         return jnp.sum(got.astype(jnp.float32), axis=0)
-    half = width // 2
-    mine = me // 2
-    sent = lax.dynamic_slice_in_dim(term, (1 - mine) * half, half, axis=1)
-    got = lax.ppermute(sent.astype(jnp.bfloat16), "sec", [(0, 2), (2, 0), (1, 3), (3, 1)])
-    halved = lax.dynamic_slice_in_dim(term, mine * half, half, axis=1) + got.astype(jnp.float32)
-    inner = me % 2
-    sent = lax.dynamic_slice_in_dim(halved, (1 - inner) * share, share, axis=1)
+    parity = me % 2
+    quarters = term.reshape(rows, 2, 2, share)
+    kept = lax.dynamic_index_in_dim(quarters, parity, axis=2, keepdims=False)
+    sent = lax.dynamic_index_in_dim(quarters, 1 - parity, axis=2, keepdims=False)
     got = lax.ppermute(sent.astype(jnp.bfloat16), "sec", [(0, 1), (1, 0), (2, 3), (3, 2)])
-    return lax.dynamic_slice_in_dim(halved, inner * share, share, axis=1) + got.astype(jnp.float32)
+    chip = kept + got.astype(jnp.float32)
+    side = me // 2
+    mine = lax.dynamic_index_in_dim(chip, side, axis=1, keepdims=False)
+    other = lax.dynamic_index_in_dim(chip, 1 - side, axis=1, keepdims=False)
+    got = lax.ppermute(other.astype(jnp.bfloat16), "sec", [(0, 2), (2, 0), (1, 3), (3, 1)])
+    return mine + got.astype(jnp.float32)
 
 
 def on_device(

time: 240 us -> 230 us (0.958)
  waiting for transfers between devices: 103 us -> 93.1 us
    ppermute x1, waiting for transfers between devices: 23.4 us -> 12.7 us  [scatter_sum(): lax.ppermute(other.astype(jnp.bfloat16), 'sec', [(0, 2), (2, 0), (1, 3),...]
  transfers between devices with their start and end apart: 11 -> 11, of which waited for: 6 -> 6; matrix products, arithmetic and copies ran while one was open for 12% -> 13% of each run, Pallas kernels for 0% -> 0%
where the time goes in v5:
time: 230 us; the launch traced here: 227 us
  waiting for transfers between devices  93.1 us (40%)
  matrix products  39.1 us (17%)
  starting transfers between devices  32.6 us (14%)
  local copies, waits for them, and re-layouts  24.9 us (11%)
  blocking collectives  19.4 us (8%)
  other arithmetic  16.4 us (7%)
    all_to_all x3, waiting for transfers between devices, gather_a2a(): return lax.all_to_all(spread, axis, 0, 0, tiled=False)  55.6 us
    ppermute x2, waiting for transfers between devices, from_last(): farther = lax.ppermute(far, axis, [(1, 0)])  22 us
    all_to_all x3, starting transfers between devices, gather_a2a(): return lax.all_to_all(spread, axis, 0, 0, tiled=False)  21.6 us
    all_to_all x1, blocking collectives, on_device(): reduced = jnp.sum(lax.all_to_all(packed, 'pts', 0, 0, tiled=False), axis=0)  19.4 us
    ppermute x1, waiting for transfers between devices, scatter_sum(): lax.ppermute(other.astype(jnp.bfloat16), 'sec', [(0, 2), (2, 0), (1, 3),...  12.7 us
    unnamed x20, local copies, waits for them, and re-layouts  11.4 us
    dot_general x1, matrix products, on_device(): term = jnp.dot(hidden, down_weight, preferred_element_type=jnp.float32)  10.7 us
    dot_general x1, matrix products, on_device(): jnp.einsum('rhk,shkv->srhv', per_head_queries, state_heads, precision=lax...  8.47 us
  transfers between devices with their start and end apart: 11, of which 6 were waited for; matrix products, arithmetic and copies ran while one was open for 13% of the time, Pallas kernels for 0%

profile of v5, /device:TPU:16, one launch (start us, length us, event | category | flops | bytes accessed | tf_op | source)
XLA Modules:
  0.0 226.6 jit_solution(9186696766516070594)
XLA Ops:
  1.0 2.5 %broadcast_in_dim.22 = bf16[32,32,2048]{2,1,0:T(8,128)(2,1)} broadcast(bf16[32,2048]{1,0:T(8,128)(2,1)S(1)} %pad_maximum_fusion), dimensions={1,2} | broadcast | bytes 4325376 | tf_op jit(solution)/shard_map/broadcast_in_dim | solution.py:38
  3.5 8.8 %all-to-all-start = ((bf16[32,32,2048]{2,1,0:T(8,128)(2,1)}), bf16[32,32,2048]{2,1,0:T(8,128)(2,1)}, u32[]{:S(2)}, u32[]{:S(2)}) async-start(bf16[32,32,2048]{2,1,0:T(8,128)(2,1)} %broadcast_in_dim.22), calls=%async_computation | async-start | bytes 8388608 | tf_op jit(solution)/shard_map/all_to_all | solution.py:39
  12.4 3.9 %copy.32 = bf16[1,1024,1024]{1,2,0:T(8,128)(2,1)} copy(bf16[1,1024,1024]{2,1,0:T(8,128)(2,1)} %param.10) | data formatting | bytes 4194304 | tf_op args[0]
  17.2 2.0 convert_reduce_fusion.1
  19.8 50.2 %all-to-all-done = bf16[32,32,2048]{2,1,0:T(8,128)(2,1)} async-done(((bf16[32,32,2048]{2,1,0:T(8,128)(2,1)}), bf16[32,32,2048]{2,1,0:T(8,128)(2,1)}, u32[]{:S(2)}, u32[]{:S(2)}) %all-to-all-start) | async-done | bytes 4194336 | tf_op jit(solution)/shard_map/all_to_all | solution.py:39
  70.0 2.0 collective-permute-start.1
  72.0 7.3 %fusion.30 = f32[1024,2048]{1,0:T(8,128)S(1)} fusion(bf16[1024,2048]{1,0:T(8,128)(2,1)} %bitcast.4, f32[1024]{0:T(1024)S(1)} %bitcast.85, f32[1024]{0:T(1024)S(1)} %add_rsqrt_fusion.2, f32[1024]{0:T(1024)S(1)} %broadcast_multiply_fusion.2, bf16[1,1024,1024]{1,2,0:T(8,128)(2,1)} %copy.32), kind=kOutput, calls=%fused_computation.44 | convolution fusion | flops 4300210176 | bytes 14692352 | tf_op jit(solution)/shard_map/dot_general | solution.py:90
  79.3 3.2 %copy-done.3 = f32[1024,2048]{1,0:T(8,128)} copy-done((f32[1024,2048]{1,0:T(8,128)}, f32[1024,2048]{1,0:T(8,128)S(1)}, u32[]{:S(2)}) %copy-start.3) | copy-done | bytes 8388632
  82.5 3.6 %convert_reduce_fusion.2 = (f32[1024]{0:T(1024)S(1)}, bf16[1024,1024]{1,0:T(8,128)(2,1)}) fusion(f32[1024,2048]{1,0:T(8,128)S(1)} %fusion.30, pred[1024]{0:T(1024)(128)(4,1)S(1)} %iota_compare_fusion), kind=kLoop, calls=%fused_computation.39 | loop fusion | flops 8387584 | bytes 6296576 | tf_op jit(solution)/shard_map/reduce_sum | solution.py:101
  86.1 3.9 %copy.48 = bf16[1024,1024]{0,1:T(8,128)(2,1)} copy(bf16[1024,1024]{1,0:T(8,128)(2,1)} %get-tuple-element.14) | data formatting | bytes 4194304 | tf_op jit(solution)/shard_map/reshape | solution.py:97
  90.0 3.6 %fusion.37 = f32[8,128,128]{2,1,0:T(8,128)S(1)} fusion(bf16[1024,8,128]{0,2,1:T(8,128)(2,1)} %bitcast.75, f32[1024,2048]{1,0:T(8,128)} %copy-done.3), kind=kOutput, calls=%fused_computation.49 | convolution fusion | flops 268435456 | bytes 4718592 | tf_op jit(solution)/shard_map/yzl,yzn->zln/dot_general | solution.py:95
  93.9 19.4 %all_to_all.20 = f32[32,33,128]{2,1,0:T(8,128)S(1)} all-to-all(f32[32,33,128]{2,1,0:T(8,128)S(1)} %reshape.85), channel_id=1, replica_groups=mesh['sec'=4,'pts'=32] {'pts'}, dimensions={0} | all-to-all | bytes 1081344 | tf_op jit(solution)/shard_map/all_to_all | solution.py:113
  114.0 7.0 %all-to-all-start.2 = ((f32[4,33,128]{2,1,0:T(8,128)}), f32[4,33,128]{2,1,0:T(8,128)S(1)}, u32[]{:S(2)}, u32[]{:S(2)}) async-start(f32[4,33,128]{2,1,0:T(8,128)} %broadcast_in_dim.26), calls=%async_computation.2 | async-start | bytes 163840 | tf_op jit(solution)/shard_map/all_to_all | solution.py:39
  121.0 2.0 collective-permute-start
  124.3 2.4 %all-to-all-done.2 = f32[4,33,128]{2,1,0:T(8,128)S(1)} async-done(((f32[4,33,128]{2,1,0:T(8,128)}), f32[4,33,128]{2,1,0:T(8,128)S(1)}, u32[]{:S(2)}, u32[]{:S(2)}) %all-to-all-start.2) | async-done | bytes 67616 | tf_op jit(solution)/shard_map/all_to_all | solution.py:39
  128.3 5.8 %all-to-all-start.3 = ((f32[32,4,33,128]{3,1,2,0:T(4,128)}), f32[32,4,33,128]{3,1,2,0:T(4,128)}, u32[]{:S(2)}, u32[]{:S(2)}) async-start(f32[32,4,33,128]{3,1,2,0:T(4,128)} %broadcast_in_dim.27), calls=%async_computation.3 | async-start | bytes 4325376 | tf_op jit(solution)/shard_map/all_to_all | solution.py:39
  137.0 22.0 %collective-permute-done.5 = f32[1024]{0:T(1024)S(1)} collective-permute-done((f32[1024]{0:T(1024)S(1)}, f32[1024]{0:T(1024)S(1)}, u32[]{:S(2)}, u32[]{:S(2)}) %collective-permute-start.5) | collective-permute-done | bytes 4128 | tf_op jit(solution)/shard_map/ppermute | solution.py:31
  159.0 2.9 %all-to-all-done.3 = f32[32,4,33,128]{3,1,2,0:T(4,128)} async-done(((f32[32,4,33,128]{3,1,2,0:T(4,128)}), f32[32,4,33,128]{3,1,2,0:T(4,128)}, u32[]{:S(2)}, u32[]{:S(2)}) %all-to-all-start.3) | async-done | bytes 2162720 | tf_op jit(solution)/shard_map/all_to_all | solution.py:39
  162.0 1.9 slice.19
  164.2 3.8 %convert_reduce_fusion = (f32[1024]{0:T(1024)S(1)}, bf16[1024,1024]{0,1:T(8,128)(2,1)S(1)}) fusion(bf16[1024,1024]{0,1:T(8,128)(2,1)S(1)} %bitcast.74, bf16[1024,1024]{0,1:T(8,128)(2,1)} %collective-permute-done, bf16[1024,1024]{0,1:T(8,128)(2,1)} %collective-permute-done.1, bf16[1024,1024]{0,1:T(8,128)(2,1)} %collective-permute-done.2, pred[]{:T(512)S(6)} %eq.16, ...), kind=kLoop, calls=%fused_computation.9 | loop fusion | flops 5241856 | bytes 10489859 | tf_op jit(solution)/shard_map/reduce_sum | solution.py:10
  168.7 4.1 %fusion.24 = bf16[1024,1024]{1,0:T(8,128)(2,1)S(1)} fusion(bf16[1024,1024]{1,0:T(8,128)(2,1)S(1)} %copy-done.7, bf16[1024,1024]{0,1:T(8,128)(2,1)S(1)} %get-tuple-element.12, f32[1024]{0:T(1024)S(1)} %select_select_fusion.1, f32[1024]{0:T(1024)S(1)} %add_rsqrt_fusion.1, f32[1024]{0:T(1024)S(1)} %broadcast_multiply_fusion.1), kind=kOutput, calls=%fused_computation.35 | convolution fusion | flops 2157969408 | bytes 6303744 | tf_op jit(solution)/shard_map/dot_general | solution.py:124
  172.7 2.4 %fusion.57 = f32[4,1024,8]{1,0,2:T(4,128)S(1)} fusion(f32[4,1056,128]{2,0,1:T(4,128)} %bitcast.10, bf16[1024,1024]{1,0:T(8,128)(2,1)S(1)} %fusion.24), kind=kOutput, calls=%fused_computation.70 | convolution fusion | flops 50331648 | bytes 4390912 | tf_op jit(solution)/shard_map/rhk,shk->srh/dot_general | solution.py:130
  175.8 8.5 %fusion = bf16[1024,8,128]{0,2,1:T(8,128)(2,1)S(1)} fusion(f32[4,1024,8]{1,0,2:T(4,128)S(1)} %fusion.57, bf16[1024,8,128,1]{2,1,0,3:T(8,128)(2,1)S(1)} %bitcast.80, f32[4,8,128,128]{3,0,2,1:T(4,128)S(1)} %bitcast.78), kind=kOutput, calls=%fused_computation.1 | convolution fusion | flops 6449790976 | bytes 6422528 | tf_op jit(solution)/shard_map/rhk,shkv->srhv/dot_general | solution.py:127
  184.3 2.6 %fusion.70 = (f32[1024]{0:T(1024)S(1)}, f32[1024,1024]{0,1:T(8,128)S(1)}) fusion(bf16[1024,1024]{0,1:T(8,128)(2,1)S(1)} %bitcast.89, bf16[1024,1024]{1,0:T(8,128)(2,1)S(1)} %copy-done, bf16[1024,1024]{0,1:T(8,128)(2,1)S(1)} %get-tuple-element.12), kind=kOutput, calls=%fused_computation.92 | convolution fusion | flops 2150628352 | bytes 10489856 | tf_op jit(solution)/shard_map/dot_general | solution.py:136
  186.9 1.9 copy-done.4
  189.3 10.7 %fusion.28 = f32[1024,1024]{0,1:T(8,128)} fusion(bf16[1024,1024]{1,0:T(8,128)(2,1)} %param.19, bf16[1024,1024]{1,0:T(8,128)(2,1)} %param.18, f32[1024,1024]{0,1:T(8,128)} %copy-done.4, f32[1024]{0:T(1024)S(1)} %copy-done.8, f32[1024]{0:T(1024)S(1)} %add_rsqrt_fusion, f32[1024]{0:T(1024)S(1)} %broadcast_multiply_fusion), kind=kOutput, calls=%fused_computation.43 | convolution fusion | flops 4308598784 | bytes 12595200 | tf_op jit(solution)/shard_map/dot_general | solution.py:143
  200.0 1.7 fusion.60
  201.9 2.7 %collective-permute-done.6 = bf16[1024,2,256]{0,2,1:T(8,128)(2,1)} collective-permute-done((bf16[1024,2,256]{0,2,1:T(8,128)(2,1)S(1)}, bf16[1024,2,256]{0,2,1:T(8,128)(2,1)}, u32[]{:S(2)}, u32[]{:S(2)}) %collective-permute-start.6) | collective-permute-done | bytes 1048608 | tf_op jit(solution)/shard_map/ppermute | solution.py:53
  204.6 2.2 bitcast_add_fusion
  208.3 2.9 %collective-permute-start.7 = (bf16[1024,256]{0,1:T(8,128)(2,1)S(1)}, bf16[1024,256]{0,1:T(8,128)(2,1)S(1)}, u32[]{:S(2)}, u32[]{:S(2)}) collective-permute-start(bf16[1024,256]{0,1:T(8,128)(2,1)S(1)} %fusion.63), channel_id=1, source_target_pairs={{0,64},{64,0},{32,96},{96,32},{1,65},{65,1},{33,97},{97,33},{2,66}... | collective-permute-start | bytes 1572872 | tf_op jit(solution)/shard_map/ppermute | solution.py:58
  211.2 12.7 %collective-permute-done.7 = bf16[1024,256]{0,1:T(8,128)(2,1)S(1)} collective-permute-done((bf16[1024,256]{0,1:T(8,128)(2,1)S(1)}, bf16[1024,256]{0,1:T(8,128)(2,1)S(1)}, u32[]{:S(2)}, u32[]{:S(2)}) %collective-permute-start.7) | collective-permute-done | bytes 524320 | tf_op jit(solution)/shard_map/ppermute | solution.py:58
  223.8 1.8 fusion.62
  (49 shorter events, 13.0 us)
Async XLA Ops:
  0.0 184.3 %copy-start = (bf16[1024,1024]{1,0:T(8,128)(2,1)S(1)}, bf16[1024,1024]{1,0:T(8,128)(2,1)}, u32[]{:S(2)}) copy-start(bf16[1024,1024]{1,0:T(8,128)(2,1)} %param.16) | copy-start | bytes 6291460
  3.5 66.5 %all-to-all-start = ((bf16[32,32,2048]{2,1,0:T(8,128)(2,1)}), bf16[32,32,2048]{2,1,0:T(8,128)(2,1)}, u32[]{:S(2)}, u32[]{:S(2)}) async-start(bf16[32,32,2048]{2,1,0:T(8,128)(2,1)} %broadcast_in_dim.22), calls=%async_computation | async-start | bytes 8388608 | tf_op jit(solution)/shard_map/all_to_all | solution.py:39
  16.3 2.9 %copy-start.1 = (bf16[1,1024,1024]{1,2,0:T(8,128)(2,1)S(1)}, bf16[1,1024,1024]{1,2,0:T(8,128)(2,1)}, u32[]{:S(2)}) copy-start(bf16[1,1024,1024]{1,2,0:T(8,128)(2,1)} %copy.32) | copy-start | bytes 6291460
  16.3 55.7 %copy-start.6 = (f32[1,1024]{1,0:T(1,128)S(1)}, f32[1,1024]{1,0:T(1,128)}, u32[]{:S(2)}) copy-start(f32[1,1024]{1,0:T(1,128)} %param.12) | copy-start | bytes 12292
  70.0 52.9 %collective-permute-start.1 = (bf16[1024,1024]{0,1:T(8,128)(2,1)}, bf16[1024,1024]{0,1:T(8,128)(2,1)}, u32[]{:S(2)}, u32[]{:S(2)}) collective-permute-start(bf16[1024,1024]{0,1:T(8,128)(2,1)} %bitcast.72), channel_id=1, source_target_pairs={{96,32},{97,33},{98,34},{99,35},{100,36},{101,37},{102,38},{103,39... | collective-permute-start | bytes 6291464 | tf_op jit(solution)/shard_map/ppermute | solution.py:29
  79.2 3.2 %copy-start.3 = (f32[1024,2048]{1,0:T(8,128)}, f32[1024,2048]{1,0:T(8,128)S(1)}, u32[]{:S(2)}) copy-start(f32[1024,2048]{1,0:T(8,128)S(1)} %fusion.30) | copy-start | bytes 25165828
  114.0 12.7 %all-to-all-start.2 = ((f32[4,33,128]{2,1,0:T(8,128)}), f32[4,33,128]{2,1,0:T(8,128)S(1)}, u32[]{:S(2)}, u32[]{:S(2)}) async-start(f32[4,33,128]{2,1,0:T(8,128)} %broadcast_in_dim.26), calls=%async_computation.2 | async-start | bytes 163840 | tf_op jit(solution)/shard_map/all_to_all | solution.py:39
  121.0 42.9 %collective-permute-start = (bf16[1024,1024]{0,1:T(8,128)(2,1)}, bf16[1024,1024]{0,1:T(8,128)(2,1)}, u32[]{:S(2)}, u32[]{:S(2)}) collective-permute-start(bf16[1024,1024]{0,1:T(8,128)(2,1)} %bitcast.73), channel_id=1, source_target_pairs={{96,64},{97,65},{98,66},{99,67},{100,68},{101,69},{102,70},{103,71... | collective-permute-start | bytes 6291464 | tf_op jit(solution)/shard_map/ppermute | solution.py:30
  123.0 40.9 %collective-permute-start.2 = (bf16[1024,1024]{0,1:T(8,128)(2,1)}, bf16[1024,1024]{0,1:T(8,128)(2,1)}, u32[]{:S(2)}, u32[]{:S(2)}) collective-permute-start(bf16[1024,1024]{0,1:T(8,128)(2,1)} %collective-permute-done.1), channel_id=1, source_target_pairs={{32,0},{33,1},{34,2},{35,3},{36,4},{37,5},{38,6},{39,7},{40,8},{41... | collective-permute-start | bytes 6291464 | tf_op jit(solution)/shard_map/ppermute | solution.py:31
  128.3 33.7 %all-to-all-start.3 = ((f32[32,4,33,128]{3,1,2,0:T(4,128)}), f32[32,4,33,128]{3,1,2,0:T(4,128)}, u32[]{:S(2)}, u32[]{:S(2)}) async-start(f32[32,4,33,128]{3,1,2,0:T(4,128)} %broadcast_in_dim.27), calls=%async_computation.3 | async-start | bytes 4325376 | tf_op jit(solution)/shard_map/all_to_all | solution.py:39
  134.1 1.3 collective-permute-start.4
  134.8 2.2 collective-permute-start.3
  135.5 23.6 %collective-permute-start.5 = (f32[1024]{0:T(1024)S(1)}, f32[1024]{0:T(1024)S(1)}, u32[]{:S(2)}, u32[]{:S(2)}) collective-permute-start(f32[1024]{0:T(1024)S(1)} %collective-permute-done.4), channel_id=1, source_target_pairs={{32,0},{33,1},{34,2},{35,3},{36,4},{37,5},{38,6},{39,7},{40,8},{41... | collective-permute-start | bytes 12296 | tf_op jit(solution)/shard_map/ppermute | solution.py:31
  162.0 2.2 copy-start.2
  163.9 4.8 %copy-start.7 = (bf16[1024,1024]{1,0:T(8,128)(2,1)S(1)}, bf16[1024,1024]{1,0:T(8,128)(2,1)}, u32[]{:S(2)}) copy-start(bf16[1024,1024]{1,0:T(8,128)(2,1)} %param.15) | copy-start | bytes 6291460
  186.9 1.9 copy-start.4
  186.9 2.4 %copy-start.8 = (f32[1024]{0:T(1024)S(1)}, f32[1024]{0:T(1024)}, u32[]{:S(2)}) copy-start(f32[1024]{0:T(1024)} %param.17) | copy-start | bytes 12292
  201.8 2.9 %collective-permute-start.6 = (bf16[1024,2,256]{0,2,1:T(8,128)(2,1)S(1)}, bf16[1024,2,256]{0,2,1:T(8,128)(2,1)}, u32[]{:S(2)}, u32[]{:S(2)}) collective-permute-start(bf16[1024,2,256]{0,2,1:T(8,128)(2,1)S(1)} %fusion.60), channel_id=1, source_target_pairs={{0,32},{32,0},{64,96},{96,64},{1,33},{33,1},{65,97},{97,65},{2,34}... | collective-permute-start | bytes 3145736 | tf_op jit(solution)/shard_map/ppermute | solution.py:53
  206.9 1.3 copy-start.5
  208.3 15.5 %collective-permute-start.7 = (bf16[1024,256]{0,1:T(8,128)(2,1)S(1)}, bf16[1024,256]{0,1:T(8,128)(2,1)S(1)}, u32[]{:S(2)}, u32[]{:S(2)}) collective-permute-start(bf16[1024,256]{0,1:T(8,128)(2,1)S(1)} %fusion.63), channel_id=1, source_target_pairs={{0,64},{64,0},{32,96},{96,32},{1,65},{65,1},{33,97},{97,33},{2,66}... | collective-permute-start | bytes 1572872 | tf_op jit(solution)/shard_map/ppermute | solution.py:58

commit v6 on v5

--- a/solution.py
+++ b/solution.py
@@ -125,10 +125,10 @@
     ).astype(jnp.bfloat16)
     per_head_queries = query_feats.astype(jnp.float32).reshape(rows, heads, HEAD_DIM)
     numerator = jnp.einsum(
-        "rhk,shkv->srhv", per_head_queries, state_heads, precision=lax.Precision.HIGHEST
+        "rhk,shkv->srhv", per_head_queries, state_heads, precision=lax.Precision.HIGH
     )
     denom = jnp.einsum(
-        "rhk,shk->srh", per_head_queries, total_heads, precision=lax.Precision.HIGHEST
+        "rhk,shk->srh", per_head_queries, total_heads, precision=lax.Precision.HIGH
     )
     attended = (
         jnp.sum(numerator / denom[:, :, :, None], axis=0).reshape(rows, width).astype(jnp.bfloat16)

time: 230 us -> 227 us (0.987)
  matrix products: 39.1 us -> 36.2 us
    dot_general x1, matrix products: 8.47 us -> 6.09 us  [on_device(): jnp.einsum('rhk,shkv->srhv', per_head_queries, state_heads, precision=lax...]
where the time goes in v6:
time: 227 us; the launch traced here: 224 us
  waiting for transfers between devices  93.1 us (41%)
  matrix products  36.2 us (16%)
  starting transfers between devices  32.6 us (14%)
  local copies, waits for them, and re-layouts  24.9 us (11%)
  blocking collectives  19.4 us (9%)
  other arithmetic  16.4 us (7%)
    all_to_all x3, waiting for transfers between devices, gather_a2a(): return lax.all_to_all(spread, axis, 0, 0, tiled=False)  55.6 us
    ppermute x2, waiting for transfers between devices, from_last(): farther = lax.ppermute(far, axis, [(1, 0)])  22 us
    all_to_all x3, starting transfers between devices, gather_a2a(): return lax.all_to_all(spread, axis, 0, 0, tiled=False)  21.6 us
    all_to_all x1, blocking collectives, on_device(): reduced = jnp.sum(lax.all_to_all(packed, 'pts', 0, 0, tiled=False), axis=0)  19.4 us
    ppermute x1, waiting for transfers between devices, scatter_sum(): lax.ppermute(other.astype(jnp.bfloat16), 'sec', [(0, 2), (2, 0), (1, 3),...  12.7 us
    unnamed x20, local copies, waits for them, and re-layouts  11.4 us
    dot_general x1, matrix products, on_device(): term = jnp.dot(hidden, down_weight, preferred_element_type=jnp.float32)  10.7 us
    dot_general x1, matrix products, on_device(): projected = jnp.dot(normed, weights, preferred_element_type=jnp.float32)  7.25 us
  transfers between devices with their start and end apart: 11, of which 6 were waited for; matrix products, arithmetic and copies ran while one was open for 13% of the time, Pallas kernels for 0%

profile of v6, /device:TPU:16, one launch (start us, length us, event | category | flops | bytes accessed | tf_op | source)
XLA Modules:
  0.0 223.7 jit_solution(9907085906386411709)
XLA Ops:
  1.0 2.5 %broadcast_in_dim.22 = bf16[32,32,2048]{2,1,0:T(8,128)(2,1)} broadcast(bf16[32,2048]{1,0:T(8,128)(2,1)S(1)} %pad_maximum_fusion), dimensions={1,2} | broadcast | bytes 4325376 | tf_op jit(solution)/shard_map/broadcast_in_dim | solution.py:38
  3.5 8.8 %all-to-all-start = ((bf16[32,32,2048]{2,1,0:T(8,128)(2,1)}), bf16[32,32,2048]{2,1,0:T(8,128)(2,1)}, u32[]{:S(2)}, u32[]{:S(2)}) async-start(bf16[32,32,2048]{2,1,0:T(8,128)(2,1)} %broadcast_in_dim.22), calls=%async_computation | async-start | bytes 8388608 | tf_op jit(solution)/shard_map/all_to_all | solution.py:39
  12.4 3.9 %copy.32 = bf16[1,1024,1024]{1,2,0:T(8,128)(2,1)} copy(bf16[1,1024,1024]{2,1,0:T(8,128)(2,1)} %param.10) | data formatting | bytes 4194304 | tf_op args[0]
  17.2 2.0 convert_reduce_fusion.1
  19.8 50.2 %all-to-all-done = bf16[32,32,2048]{2,1,0:T(8,128)(2,1)} async-done(((bf16[32,32,2048]{2,1,0:T(8,128)(2,1)}), bf16[32,32,2048]{2,1,0:T(8,128)(2,1)}, u32[]{:S(2)}, u32[]{:S(2)}) %all-to-all-start) | async-done | bytes 4194336 | tf_op jit(solution)/shard_map/all_to_all | solution.py:39
  70.0 2.0 collective-permute-start.1
  72.0 7.3 %fusion.30 = f32[1024,2048]{1,0:T(8,128)S(1)} fusion(bf16[1024,2048]{1,0:T(8,128)(2,1)} %bitcast.4, f32[1024]{0:T(1024)S(1)} %bitcast.85, f32[1024]{0:T(1024)S(1)} %add_rsqrt_fusion.2, f32[1024]{0:T(1024)S(1)} %broadcast_multiply_fusion.2, bf16[1,1024,1024]{1,2,0:T(8,128)(2,1)} %copy.32), kind=kOutput, calls=%fused_computation.44 | convolution fusion | flops 4300210176 | bytes 14692352 | tf_op jit(solution)/shard_map/dot_general | solution.py:90
  79.3 3.2 %copy-done.3 = f32[1024,2048]{1,0:T(8,128)} copy-done((f32[1024,2048]{1,0:T(8,128)}, f32[1024,2048]{1,0:T(8,128)S(1)}, u32[]{:S(2)}) %copy-start.3) | copy-done | bytes 8388632
  82.5 3.6 %convert_reduce_fusion.2 = (f32[1024]{0:T(1024)S(1)}, bf16[1024,1024]{1,0:T(8,128)(2,1)}) fusion(f32[1024,2048]{1,0:T(8,128)S(1)} %fusion.30, pred[1024]{0:T(1024)(128)(4,1)S(1)} %iota_compare_fusion), kind=kLoop, calls=%fused_computation.39 | loop fusion | flops 8387584 | bytes 6296576 | tf_op jit(solution)/shard_map/reduce_sum | solution.py:101
  86.1 3.9 %copy.48 = bf16[1024,1024]{0,1:T(8,128)(2,1)} copy(bf16[1024,1024]{1,0:T(8,128)(2,1)} %get-tuple-element.14) | data formatting | bytes 4194304 | tf_op jit(solution)/shard_map/reshape | solution.py:97
  90.0 3.6 %fusion.37 = f32[8,128,128]{2,1,0:T(8,128)S(1)} fusion(bf16[1024,8,128]{0,2,1:T(8,128)(2,1)} %bitcast.75, f32[1024,2048]{1,0:T(8,128)} %copy-done.3), kind=kOutput, calls=%fused_computation.49 | convolution fusion | flops 268435456 | bytes 4718592 | tf_op jit(solution)/shard_map/yzl,yzn->zln/dot_general | solution.py:95
  93.9 19.4 %all_to_all.20 = f32[32,33,128]{2,1,0:T(8,128)S(1)} all-to-all(f32[32,33,128]{2,1,0:T(8,128)S(1)} %reshape.85), channel_id=1, replica_groups=mesh['sec'=4,'pts'=32] {'pts'}, dimensions={0} | all-to-all | bytes 1081344 | tf_op jit(solution)/shard_map/all_to_all | solution.py:113
  114.0 7.0 %all-to-all-start.2 = ((f32[4,33,128]{2,1,0:T(8,128)}), f32[4,33,128]{2,1,0:T(8,128)S(1)}, u32[]{:S(2)}, u32[]{:S(2)}) async-start(f32[4,33,128]{2,1,0:T(8,128)} %broadcast_in_dim.26), calls=%async_computation.2 | async-start | bytes 163840 | tf_op jit(solution)/shard_map/all_to_all | solution.py:39
  121.0 2.0 collective-permute-start
  124.3 2.4 %all-to-all-done.2 = f32[4,33,128]{2,1,0:T(8,128)S(1)} async-done(((f32[4,33,128]{2,1,0:T(8,128)}), f32[4,33,128]{2,1,0:T(8,128)S(1)}, u32[]{:S(2)}, u32[]{:S(2)}) %all-to-all-start.2) | async-done | bytes 67616 | tf_op jit(solution)/shard_map/all_to_all | solution.py:39
  128.3 5.8 %all-to-all-start.3 = ((f32[32,4,33,128]{3,1,2,0:T(4,128)}), f32[32,4,33,128]{3,1,2,0:T(4,128)}, u32[]{:S(2)}, u32[]{:S(2)}) async-start(f32[32,4,33,128]{3,1,2,0:T(4,128)} %broadcast_in_dim.27), calls=%async_computation.3 | async-start | bytes 4325376 | tf_op jit(solution)/shard_map/all_to_all | solution.py:39
  137.0 22.0 %collective-permute-done.5 = f32[1024]{0:T(1024)S(1)} collective-permute-done((f32[1024]{0:T(1024)S(1)}, f32[1024]{0:T(1024)S(1)}, u32[]{:S(2)}, u32[]{:S(2)}) %collective-permute-start.5) | collective-permute-done | bytes 4128 | tf_op jit(solution)/shard_map/ppermute | solution.py:31
  159.0 2.9 %all-to-all-done.3 = f32[32,4,33,128]{3,1,2,0:T(4,128)} async-done(((f32[32,4,33,128]{3,1,2,0:T(4,128)}), f32[32,4,33,128]{3,1,2,0:T(4,128)}, u32[]{:S(2)}, u32[]{:S(2)}) %all-to-all-start.3) | async-done | bytes 2162720 | tf_op jit(solution)/shard_map/all_to_all | solution.py:39
  162.0 1.9 slice.19
  164.2 3.8 %convert_reduce_fusion = (f32[1024]{0:T(1024)S(1)}, bf16[1024,1024]{0,1:T(8,128)(2,1)S(1)}) fusion(bf16[1024,1024]{0,1:T(8,128)(2,1)S(1)} %bitcast.74, bf16[1024,1024]{0,1:T(8,128)(2,1)} %collective-permute-done, bf16[1024,1024]{0,1:T(8,128)(2,1)} %collective-permute-done.1, bf16[1024,1024]{0,1:T(8,128)(2,1)} %collective-permute-done.2, pred[]{:T(512)S(6)} %eq.16, ...), kind=kLoop, calls=%fused_computation.9 | loop fusion | flops 5241856 | bytes 10489859 | tf_op jit(solution)/shard_map/reduce_sum | solution.py:10
  168.7 4.1 %fusion.24 = bf16[1024,1024]{1,0:T(8,128)(2,1)S(1)} fusion(bf16[1024,1024]{1,0:T(8,128)(2,1)S(1)} %copy-done.7, bf16[1024,1024]{0,1:T(8,128)(2,1)S(1)} %get-tuple-element.12, f32[1024]{0:T(1024)S(1)} %select_select_fusion.1, f32[1024]{0:T(1024)S(1)} %add_rsqrt_fusion.1, f32[1024]{0:T(1024)S(1)} %broadcast_multiply_fusion.1), kind=kOutput, calls=%fused_computation.35 | convolution fusion | flops 2157969408 | bytes 6303744 | tf_op jit(solution)/shard_map/dot_general | solution.py:124
  172.7 1.9 fusion.57
  175.3 6.1 %fusion = bf16[1024,8,128]{0,2,1:T(8,128)(2,1)S(1)} fusion(f32[4,1024,8]{1,0,2:T(4,128)S(1)} %fusion.57, bf16[1024,8,128,1]{2,1,0,3:T(8,128)(2,1)S(1)} %bitcast.80, f32[4,8,128,128]{3,0,2,1:T(4,128)S(1)} %bitcast.78), kind=kOutput, calls=%fused_computation.1 | convolution fusion | flops 3228565504 | bytes 6422528 | tf_op jit(solution)/shard_map/rhk,shkv->srhv/dot_general | solution.py:127
  181.4 2.6 %fusion.70 = (f32[1024]{0:T(1024)S(1)}, f32[1024,1024]{0,1:T(8,128)S(1)}) fusion(bf16[1024,1024]{0,1:T(8,128)(2,1)S(1)} %bitcast.89, bf16[1024,1024]{1,0:T(8,128)(2,1)S(1)} %copy-done, bf16[1024,1024]{0,1:T(8,128)(2,1)S(1)} %get-tuple-element.12), kind=kOutput, calls=%fused_computation.92 | convolution fusion | flops 2150628352 | bytes 10489856 | tf_op jit(solution)/shard_map/dot_general | solution.py:136
  184.0 1.9 copy-done.4
  186.4 10.7 %fusion.28 = f32[1024,1024]{0,1:T(8,128)} fusion(bf16[1024,1024]{1,0:T(8,128)(2,1)} %param.19, bf16[1024,1024]{1,0:T(8,128)(2,1)} %param.18, f32[1024,1024]{0,1:T(8,128)} %copy-done.4, f32[1024]{0:T(1024)S(1)} %copy-done.8, f32[1024]{0:T(1024)S(1)} %add_rsqrt_fusion, f32[1024]{0:T(1024)S(1)} %broadcast_multiply_fusion), kind=kOutput, calls=%fused_computation.43 | convolution fusion | flops 4308598784 | bytes 12595200 | tf_op jit(solution)/shard_map/dot_general | solution.py:143
  197.1 1.7 fusion.60
  199.0 2.7 %collective-permute-done.6 = bf16[1024,2,256]{0,2,1:T(8,128)(2,1)} collective-permute-done((bf16[1024,2,256]{0,2,1:T(8,128)(2,1)S(1)}, bf16[1024,2,256]{0,2,1:T(8,128)(2,1)}, u32[]{:S(2)}, u32[]{:S(2)}) %collective-permute-start.6) | collective-permute-done | bytes 1048608 | tf_op jit(solution)/shard_map/ppermute | solution.py:53
  201.7 2.2 bitcast_add_fusion
  205.4 2.9 %collective-permute-start.7 = (bf16[1024,256]{0,1:T(8,128)(2,1)S(1)}, bf16[1024,256]{0,1:T(8,128)(2,1)S(1)}, u32[]{:S(2)}, u32[]{:S(2)}) collective-permute-start(bf16[1024,256]{0,1:T(8,128)(2,1)S(1)} %fusion.63), channel_id=1, source_target_pairs={{0,64},{64,0},{32,96},{96,32},{1,65},{65,1},{33,97},{97,33},{2,66}... | collective-permute-start | bytes 1572872 | tf_op jit(solution)/shard_map/ppermute | solution.py:58
  208.2 12.7 %collective-permute-done.7 = bf16[1024,256]{0,1:T(8,128)(2,1)S(1)} collective-permute-done((bf16[1024,256]{0,1:T(8,128)(2,1)S(1)}, bf16[1024,256]{0,1:T(8,128)(2,1)S(1)}, u32[]{:S(2)}, u32[]{:S(2)}) %collective-permute-start.7) | collective-permute-done | bytes 524320 | tf_op jit(solution)/shard_map/ppermute | solution.py:58
  220.9 1.8 fusion.62
  (49 shorter events, 13.0 us)
Async XLA Ops:
  0.0 181.4 %copy-start = (bf16[1024,1024]{1,0:T(8,128)(2,1)S(1)}, bf16[1024,1024]{1,0:T(8,128)(2,1)}, u32[]{:S(2)}) copy-start(bf16[1024,1024]{1,0:T(8,128)(2,1)} %param.16) | copy-start | bytes 6291460
  3.5 66.5 %all-to-all-start = ((bf16[32,32,2048]{2,1,0:T(8,128)(2,1)}), bf16[32,32,2048]{2,1,0:T(8,128)(2,1)}, u32[]{:S(2)}, u32[]{:S(2)}) async-start(bf16[32,32,2048]{2,1,0:T(8,128)(2,1)} %broadcast_in_dim.22), calls=%async_computation | async-start | bytes 8388608 | tf_op jit(solution)/shard_map/all_to_all | solution.py:39
  16.3 2.9 %copy-start.1 = (bf16[1,1024,1024]{1,2,0:T(8,128)(2,1)S(1)}, bf16[1,1024,1024]{1,2,0:T(8,128)(2,1)}, u32[]{:S(2)}) copy-start(bf16[1,1024,1024]{1,2,0:T(8,128)(2,1)} %copy.32) | copy-start | bytes 6291460
  16.3 55.7 %copy-start.6 = (f32[1,1024]{1,0:T(1,128)S(1)}, f32[1,1024]{1,0:T(1,128)}, u32[]{:S(2)}) copy-start(f32[1,1024]{1,0:T(1,128)} %param.12) | copy-start | bytes 12292
  70.0 52.9 %collective-permute-start.1 = (bf16[1024,1024]{0,1:T(8,128)(2,1)}, bf16[1024,1024]{0,1:T(8,128)(2,1)}, u32[]{:S(2)}, u32[]{:S(2)}) collective-permute-start(bf16[1024,1024]{0,1:T(8,128)(2,1)} %bitcast.72), channel_id=1, source_target_pairs={{96,32},{97,33},{98,34},{99,35},{100,36},{101,37},{102,38},{103,39... | collective-permute-start | bytes 6291464 | tf_op jit(solution)/shard_map/ppermute | solution.py:29
  79.2 3.2 %copy-start.3 = (f32[1024,2048]{1,0:T(8,128)}, f32[1024,2048]{1,0:T(8,128)S(1)}, u32[]{:S(2)}) copy-start(f32[1024,2048]{1,0:T(8,128)S(1)} %fusion.30) | copy-start | bytes 25165828
  114.0 12.7 %all-to-all-start.2 = ((f32[4,33,128]{2,1,0:T(8,128)}), f32[4,33,128]{2,1,0:T(8,128)S(1)}, u32[]{:S(2)}, u32[]{:S(2)}) async-start(f32[4,33,128]{2,1,0:T(8,128)} %broadcast_in_dim.26), calls=%async_computation.2 | async-start | bytes 163840 | tf_op jit(solution)/shard_map/all_to_all | solution.py:39
  121.0 42.9 %collective-permute-start = (bf16[1024,1024]{0,1:T(8,128)(2,1)}, bf16[1024,1024]{0,1:T(8,128)(2,1)}, u32[]{:S(2)}, u32[]{:S(2)}) collective-permute-start(bf16[1024,1024]{0,1:T(8,128)(2,1)} %bitcast.73), channel_id=1, source_target_pairs={{96,64},{97,65},{98,66},{99,67},{100,68},{101,69},{102,70},{103,71... | collective-permute-start | bytes 6291464 | tf_op jit(solution)/shard_map/ppermute | solution.py:30
  123.0 40.9 %collective-permute-start.2 = (bf16[1024,1024]{0,1:T(8,128)(2,1)}, bf16[1024,1024]{0,1:T(8,128)(2,1)}, u32[]{:S(2)}, u32[]{:S(2)}) collective-permute-start(bf16[1024,1024]{0,1:T(8,128)(2,1)} %collective-permute-done.1), channel_id=1, source_target_pairs={{32,0},{33,1},{34,2},{35,3},{36,4},{37,5},{38,6},{39,7},{40,8},{41... | collective-permute-start | bytes 6291464 | tf_op jit(solution)/shard_map/ppermute | solution.py:31
  128.3 33.7 %all-to-all-start.3 = ((f32[32,4,33,128]{3,1,2,0:T(4,128)}), f32[32,4,33,128]{3,1,2,0:T(4,128)}, u32[]{:S(2)}, u32[]{:S(2)}) async-start(f32[32,4,33,128]{3,1,2,0:T(4,128)} %broadcast_in_dim.27), calls=%async_computation.3 | async-start | bytes 4325376 | tf_op jit(solution)/shard_map/all_to_all | solution.py:39
  134.1 1.3 collective-permute-start.4
  134.8 2.2 collective-permute-start.3
  135.5 23.6 %collective-permute-start.5 = (f32[1024]{0:T(1024)S(1)}, f32[1024]{0:T(1024)S(1)}, u32[]{:S(2)}, u32[]{:S(2)}) collective-permute-start(f32[1024]{0:T(1024)S(1)} %collective-permute-done.4), channel_id=1, source_target_pairs={{32,0},{33,1},{34,2},{35,3},{36,4},{37,5},{38,6},{39,7},{40,8},{41... | collective-permute-start | bytes 12296 | tf_op jit(solution)/shard_map/ppermute | solution.py:31
  162.0 2.2 copy-start.2
  163.9 4.8 %copy-start.7 = (bf16[1024,1024]{1,0:T(8,128)(2,1)S(1)}, bf16[1024,1024]{1,0:T(8,128)(2,1)}, u32[]{:S(2)}) copy-start(bf16[1024,1024]{1,0:T(8,128)(2,1)} %param.15) | copy-start | bytes 6291460
  184.0 1.9 copy-start.4
  184.0 2.4 %copy-start.8 = (f32[1024]{0:T(1024)S(1)}, f32[1024]{0:T(1024)}, u32[]{:S(2)}) copy-start(f32[1024]{0:T(1024)} %param.17) | copy-start | bytes 12292
  198.8 2.9 %collective-permute-start.6 = (bf16[1024,2,256]{0,2,1:T(8,128)(2,1)S(1)}, bf16[1024,2,256]{0,2,1:T(8,128)(2,1)}, u32[]{:S(2)}, u32[]{:S(2)}) collective-permute-start(bf16[1024,2,256]{0,2,1:T(8,128)(2,1)S(1)} %fusion.60), channel_id=1, source_target_pairs={{0,32},{32,0},{64,96},{96,64},{1,33},{33,1},{65,97},{97,65},{2,34}... | collective-permute-start | bytes 3145736 | tf_op jit(solution)/shard_map/ppermute | solution.py:53
  203.9 1.3 copy-start.5
  205.4 15.5 %collective-permute-start.7 = (bf16[1024,256]{0,1:T(8,128)(2,1)S(1)}, bf16[1024,256]{0,1:T(8,128)(2,1)S(1)}, u32[]{:S(2)}, u32[]{:S(2)}) collective-permute-start(bf16[1024,256]{0,1:T(8,128)(2,1)S(1)} %fusion.63), channel_id=1, source_target_pairs={{0,64},{64,0},{32,96},{96,32},{1,65},{65,1},{33,97},{97,33},{2,66}... | collective-permute-start | bytes 1572872 | tf_op jit(solution)/shard_map/ppermute | solution.py:58

commit v7 on v6

--- a/solution.py
+++ b/solution.py
@@ -111,8 +111,8 @@
         axis=0,
     ).reshape(blocks, piece, HEAD_DIM)
     reduced = jnp.sum(lax.all_to_all(packed, "pts", 0, 0, tiled=False), axis=0)
-    by_section = gather_a2a(reduced, "sec", sections)
-    whole = gather_a2a(by_section, "pts", blocks)
+    by_section = gather_a2a(reduced.astype(jnp.bfloat16), "sec", sections)
+    whole = gather_a2a(by_section, "pts", blocks).astype(jnp.float32)
     whole = whole.transpose(1, 0, 2, 3).reshape(sections, blocks * piece, HEAD_DIM)
     state_heads = whole[:, :width].reshape(sections, heads, HEAD_DIM, HEAD_DIM)
     total_heads = whole[:, width:packed_rows].reshape(sections, heads, HEAD_DIM)

time: 227 us -> 212 us (0.934)
  blocking collectives: 19.4 us -> 31.9 us
  waiting for transfers between devices: 93.1 us -> 81.6 us
  starting transfers between devices: 32.6 us -> 23.2 us
  matrix products: 36.2 us -> 32.4 us
  local copies, waits for them, and re-layouts: 24.9 us -> 22.1 us
    all_to_all x0 -> x1, blocking collectives: none -> 13 us  [gather_a2a(): return lax.all_to_all(spread, axis, 0, 0, tiled=False)]
    ppermute x2, waiting for transfers between devices: 22 us -> 10.3 us  [from_last(): farther = lax.ppermute(far, axis, [(1, 0)])]
    all_to_all x3 -> x2, starting transfers between devices: 21.6 us -> 14.2 us  [gather_a2a(): return lax.all_to_all(spread, axis, 0, 0, tiled=False)]
    dot_general x1, matrix products: 6.09 us -> 3.52 us  [on_device(): jnp.einsum('rhk,shkv->srhv', per_head_queries, state_heads, precision=lax...]
    all_to_all x3 -> x2, waiting for transfers between devices: 55.6 us -> 53.8 us  [gather_a2a(): return lax.all_to_all(spread, axis, 0, 0, tiled=False)]
    unnamed x20 -> x16, local copies, waits for them, and re-layouts: 11.4 us -> 11 us
  transfers between devices with their start and end apart: 11 -> 10, of which waited for: 6 -> 5; matrix products, arithmetic and copies ran while one was open for 13% -> 14% of each run, Pallas kernels for 0% -> 0%
where the time goes in v7:
time: 212 us; the launch traced here: 210 us
  waiting for transfers between devices  81.6 us (38%)
  matrix products  32.4 us (15%)
  blocking collectives  31.9 us (15%)
  starting transfers between devices  23.2 us (11%)
  local copies, waits for them, and re-layouts  22.1 us (10%)
  other arithmetic  18 us (8%)
    all_to_all x2, waiting for transfers between devices, gather_a2a(): return lax.all_to_all(spread, axis, 0, 0, tiled=False)  53.8 us
    all_to_all x1, blocking collectives, on_device(): reduced = jnp.sum(lax.all_to_all(packed, 'pts', 0, 0, tiled=False), axis=0)  19 us
    ppermute x1, waiting for transfers between devices, scatter_sum(): lax.ppermute(other.astype(jnp.bfloat16), 'sec', [(0, 2), (2, 0), (1, 3),...  14.7 us
    all_to_all x2, starting transfers between devices, gather_a2a(): return lax.all_to_all(spread, axis, 0, 0, tiled=False)  14.2 us
    all_to_all x1, blocking collectives, gather_a2a(): return lax.all_to_all(spread, axis, 0, 0, tiled=False)  13 us
    unnamed x16, local copies, waits for them, and re-layouts  11 us
    dot_general x1, matrix products, on_device(): term = jnp.dot(hidden, down_weight, preferred_element_type=jnp.float32)  10.7 us
    ppermute x2, waiting for transfers between devices, from_last(): farther = lax.ppermute(far, axis, [(1, 0)])  10.3 us
  transfers between devices with their start and end apart: 10, of which 5 were waited for; matrix products, arithmetic and copies ran while one was open for 14% of the time, Pallas kernels for 0%

profile of v7, /device:TPU:16, one launch (start us, length us, event | category | flops | bytes accessed | tf_op | source)
XLA Modules:
  0.0 210.2 jit_solution(4046633186509216902)
XLA Ops:
  1.0 2.5 %broadcast_in_dim.22 = bf16[32,32,2048]{2,1,0:T(8,128)(2,1)} broadcast(bf16[32,2048]{1,0:T(8,128)(2,1)S(1)} %pad_maximum_fusion), dimensions={1,2} | broadcast | bytes 4325376 | tf_op jit(solution)/shard_map/broadcast_in_dim | solution.py:38
  3.5 8.8 %all-to-all-start = ((bf16[32,32,2048]{2,1,0:T(8,128)(2,1)}), bf16[32,32,2048]{2,1,0:T(8,128)(2,1)}, u32[]{:S(2)}, u32[]{:S(2)}) async-start(bf16[32,32,2048]{2,1,0:T(8,128)(2,1)} %broadcast_in_dim.22), calls=%async_computation | async-start | bytes 8388608 | tf_op jit(solution)/shard_map/all_to_all | solution.py:39
  12.4 3.9 %copy.32 = bf16[1,1024,1024]{1,2,0:T(8,128)(2,1)} copy(bf16[1,1024,1024]{2,1,0:T(8,128)(2,1)} %param.10) | data formatting | bytes 4194304 | tf_op args[0]
  17.1 2.0 convert_reduce_fusion.1
  19.0 51.0 %all-to-all-done = bf16[32,32,2048]{2,1,0:T(8,128)(2,1)} async-done(((bf16[32,32,2048]{2,1,0:T(8,128)(2,1)}), bf16[32,32,2048]{2,1,0:T(8,128)(2,1)}, u32[]{:S(2)}, u32[]{:S(2)}) %all-to-all-start) | async-done | bytes 4194336 | tf_op jit(solution)/shard_map/all_to_all | solution.py:39
  70.0 2.0 collective-permute-start.1
  72.0 2.2 %fusion.8 = f32[1024]{0:T(1024)S(1)} fusion(f32[1024]{0:T(1024)S(1)} %broadcast_multiply_fusion.2, bf16[1,1024,1024]{1,2,0:T(8,128)(2,1)} %copy.32), kind=kLoop, calls=%fused_computation.19 | loop fusion | flops 4193280 | bytes 2105344 | tf_op jit(solution)/shard_map/reduce_sum | solution.py:12
  74.2 2.0 collective-permute-start
  76.2 7.3 %fusion.30 = f32[1024,2048]{1,0:T(8,128)S(1)} fusion(bf16[1024,2048]{1,0:T(8,128)(2,1)} %bitcast.4, f32[1024]{0:T(1024)S(1)} %bitcast.87, f32[1024]{0:T(1024)S(1)} %add_rsqrt_fusion.2, f32[1024]{0:T(1024)S(1)} %broadcast_multiply_fusion.2, bf16[1,1024,1024]{1,2,0:T(8,128)(2,1)} %copy.32), kind=kOutput, calls=%fused_computation.44 | convolution fusion | flops 4300210176 | bytes 14692352 | tf_op jit(solution)/shard_map/dot_general | solution.py:90
  83.5 3.2 %copy-done.1 = f32[1024,2048]{1,0:T(8,128)} copy-done((f32[1024,2048]{1,0:T(8,128)}, f32[1024,2048]{1,0:T(8,128)S(1)}, u32[]{:S(2)}) %copy-start.1) | copy-done | bytes 8388632
  86.7 3.6 %convert_reduce_fusion.2 = (f32[1024]{0:T(1024)S(1)}, bf16[1024,1024]{1,0:T(8,128)(2,1)}) fusion(f32[1024,2048]{1,0:T(8,128)S(1)} %fusion.30, pred[1024]{0:T(1024)(128)(4,1)S(1)} %iota_compare_fusion), kind=kLoop, calls=%fused_computation.39 | loop fusion | flops 8387584 | bytes 6296576 | tf_op jit(solution)/shard_map/reduce_sum | solution.py:101
  90.3 4.0 %copy.48 = bf16[1024,1024]{0,1:T(8,128)(2,1)} copy(bf16[1024,1024]{1,0:T(8,128)(2,1)} %get-tuple-element.14) | data formatting | bytes 4194304 | tf_op jit(solution)/shard_map/reshape | solution.py:97
  94.3 1.3 collective-permute-start.2
  95.6 3.6 %fusion.37 = f32[8,128,128]{2,1,0:T(8,128)S(1)} fusion(bf16[1024,8,128]{0,2,1:T(8,128)(2,1)} %bitcast.75, f32[1024,2048]{1,0:T(8,128)} %copy-done.1), kind=kOutput, calls=%fused_computation.49 | convolution fusion | flops 268435456 | bytes 4718592 | tf_op jit(solution)/shard_map/yzl,yzn->zln/dot_general | solution.py:95
  99.4 19.0 %all_to_all.20 = f32[32,33,128]{2,1,0:T(8,128)S(1)} all-to-all(f32[32,33,128]{2,1,0:T(8,128)S(1)} %reshape.87), channel_id=1, replica_groups=mesh['sec'=4,'pts'=32] {'pts'}, dimensions={0} | all-to-all | bytes 1081344 | tf_op jit(solution)/shard_map/all_to_all | solution.py:113
  118.5 13.0 %all_to_all.21 = bf16[4,33,128]{2,1,0:T(8,128)(2,1)S(1)} all-to-all(bf16[4,33,128]{2,1,0:T(8,128)(2,1)S(1)} %broadcast_in_dim.26), channel_id=1, replica_groups=mesh['sec'=4,'pts'=32] {'sec'}, dimensions={0} | all-to-all | bytes 67584 | tf_op jit(solution)/shard_map/all_to_all | solution.py:39
  132.7 5.4 %all-to-all-start.3 = ((bf16[32,4,33,128]{3,1,2,0:T(4,128)(2,1)}), bf16[32,4,33,128]{3,1,2,0:T(4,128)(2,1)S(1)}, u32[]{:S(2)}, u32[]{:S(2)}) async-start(bf16[32,4,33,128]{3,1,2,0:T(4,128)(2,1)} %broadcast_in_dim.27), calls=%async_computation.3 | async-start | bytes 2162688 | tf_op jit(solution)/shard_map/all_to_all | solution.py:39
  139.5 1.5 collective-permute-start.5
  141.0 10.3 %collective-permute-done.5 = f32[1024]{0:T(1024)S(1)} collective-permute-done((f32[1024]{0:T(1024)S(1)}, f32[1024]{0:T(1024)S(1)}, u32[]{:S(2)}, u32[]{:S(2)}) %collective-permute-start.5) | collective-permute-done | bytes 4128 | tf_op jit(solution)/shard_map/ppermute | solution.py:31
  151.3 2.8 %all-to-all-done.3 = bf16[32,4,33,128]{3,1,2,0:T(4,128)(2,1)S(1)} async-done(((bf16[32,4,33,128]{3,1,2,0:T(4,128)(2,1)}), bf16[32,4,33,128]{3,1,2,0:T(4,128)(2,1)S(1)}, u32[]{:S(2)}, u32[]{:S(2)}) %all-to-all-start.3) | async-done | bytes 1081376 | tf_op jit(solution)/shard_map/all_to_all | solution.py:39
  154.5 3.8 %convert_reduce_fusion = (f32[1024]{0:T(1024)S(1)}, bf16[1024,1024]{0,1:T(8,128)(2,1)S(1)}) fusion(bf16[1024,1024]{0,1:T(8,128)(2,1)} %bitcast.74, bf16[1024,1024]{0,1:T(8,128)(2,1)} %collective-permute-done, bf16[1024,1024]{0,1:T(8,128)(2,1)} %collective-permute-done.1, bf16[1024,1024]{0,1:T(8,128)(2,1)} %collective-permute-done.2, pred[]{:T(512)S(6)} %eq.16, ...), kind=kLoop, calls=%fused_computation.9 | loop fusion | flops 5241856 | bytes 10489859 | tf_op jit(solution)/shard_map/reduce_sum | solution.py:10
  158.9 4.1 %fusion.24 = bf16[1024,1024]{1,0:T(8,128)(2,1)S(1)} fusion(bf16[1024,1024]{1,0:T(8,128)(2,1)S(1)} %copy-done.5, bf16[1024,1024]{0,1:T(8,128)(2,1)S(1)} %get-tuple-element.12, f32[1024]{0:T(1024)S(1)} %select_select_fusion.1, f32[1024]{0:T(1024)S(1)} %add_rsqrt_fusion.1, f32[1024]{0:T(1024)S(1)} %broadcast_multiply_fusion.1), kind=kOutput, calls=%fused_computation.35 | convolution fusion | flops 2157969408 | bytes 6303744 | tf_op jit(solution)/shard_map/dot_general | solution.py:124
  164.3 3.5 %fusion = bf16[1024,8,128]{0,2,1:T(8,128)(2,1)S(1)} fusion(f32[4,1024,8]{1,0,2:T(4,128)S(1)} %fusion.56, bf16[1024,8,128,1]{2,1,0,3:T(8,128)(2,1)S(1)} %bitcast.81, bf16[4,8,128,128]{3,0,2,1:T(4,128)(2,1)S(1)} %bitcast.83), kind=kOutput, calls=%fused_computation.1 | convolution fusion | flops 1081081856 | bytes 5373952 | tf_op jit(solution)/shard_map/rhk,shkv->srhv/dot_general | solution.py:127
  167.8 2.6 %fusion.70 = (f32[1024]{0:T(1024)S(1)}, f32[1024,1024]{0,1:T(8,128)S(1)}) fusion(bf16[1024,1024]{0,1:T(8,128)(2,1)S(1)} %bitcast.91, bf16[1024,1024]{1,0:T(8,128)(2,1)S(1)} %copy-done, bf16[1024,1024]{0,1:T(8,128)(2,1)S(1)} %get-tuple-element.12), kind=kOutput, calls=%fused_computation.92 | convolution fusion | flops 2150628352 | bytes 10489856 | tf_op jit(solution)/shard_map/dot_general | solution.py:136
  170.5 1.9 copy-done.2
  172.9 10.7 %fusion.28 = f32[1024,1024]{0,1:T(8,128)} fusion(bf16[1024,1024]{1,0:T(8,128)(2,1)} %param.19, bf16[1024,1024]{1,0:T(8,128)(2,1)} %param.18, f32[1024,1024]{0,1:T(8,128)} %copy-done.2, f32[1024]{0:T(1024)S(1)} %copy-done.6, f32[1024]{0:T(1024)S(1)} %add_rsqrt_fusion, f32[1024]{0:T(1024)S(1)} %broadcast_multiply_fusion), kind=kOutput, calls=%fused_computation.43 | convolution fusion | flops 4308598784 | bytes 12595200 | tf_op jit(solution)/shard_map/dot_general | solution.py:143
  183.6 1.7 fusion.59
  185.5 2.7 %collective-permute-done.6 = bf16[1024,2,256]{0,2,1:T(8,128)(2,1)} collective-permute-done((bf16[1024,2,256]{0,2,1:T(8,128)(2,1)S(1)}, bf16[1024,2,256]{0,2,1:T(8,128)(2,1)}, u32[]{:S(2)}, u32[]{:S(2)}) %collective-permute-start.6) | collective-permute-done | bytes 1048608 | tf_op jit(solution)/shard_map/ppermute | solution.py:53
  188.2 2.2 %bitcast_add_fusion = f32[1024,2,256]{0,2,1:T(8,128)S(1)} fusion(bf16[1024,2,256]{0,2,1:T(8,128)(2,1)} %collective-permute-done.6, f32[1024,2,2,256]{0,3,2,1:T(8,128)} %bitcast.79, s32[]{:T(128)S(6)} %select_n.107), kind=kLoop, calls=%fused_computation.53 | loop fusion | flops 1048576 | bytes 5242884 | tf_op jit(solution)/shard_map/add | solution.py:54
  190.4 1.3 copy-done.3
  192.7 14.7 %collective-permute-done.7 = bf16[1024,256]{0,1:T(8,128)(2,1)S(1)} collective-permute-done((bf16[1024,256]{0,1:T(8,128)(2,1)S(1)}, bf16[1024,256]{0,1:T(8,128)(2,1)S(1)}, u32[]{:S(2)}, u32[]{:S(2)}) %collective-permute-start.7) | collective-permute-done | bytes 524320 | tf_op jit(solution)/shard_map/ppermute | solution.py:58
  207.4 1.8 fusion.61
  (44 shorter events, 8.8 us)
Async XLA Ops:
  0.0 167.8 %copy-start = (bf16[1024,1024]{1,0:T(8,128)(2,1)S(1)}, bf16[1024,1024]{1,0:T(8,128)(2,1)}, u32[]{:S(2)}) copy-start(bf16[1024,1024]{1,0:T(8,128)(2,1)} %param.16) | copy-start | bytes 6291460
  3.5 66.5 %all-to-all-start = ((bf16[32,32,2048]{2,1,0:T(8,128)(2,1)}), bf16[32,32,2048]{2,1,0:T(8,128)(2,1)}, u32[]{:S(2)}, u32[]{:S(2)}) async-start(bf16[32,32,2048]{2,1,0:T(8,128)(2,1)} %broadcast_in_dim.22), calls=%async_computation | async-start | bytes 8388608 | tf_op jit(solution)/shard_map/all_to_all | solution.py:39
  12.4 63.8 %copy-start.4 = (f32[1,1024]{1,0:T(1,128)S(1)}, f32[1,1024]{1,0:T(1,128)}, u32[]{:S(2)}) copy-start(f32[1,1024]{1,0:T(1,128)} %param.12) | copy-start | bytes 12292
  70.0 24.3 %collective-permute-start.1 = (bf16[1024,1024]{0,1:T(8,128)(2,1)}, bf16[1024,1024]{0,1:T(8,128)(2,1)}, u32[]{:S(2)}, u32[]{:S(2)}) collective-permute-start(bf16[1024,1024]{0,1:T(8,128)(2,1)} %bitcast.72), channel_id=1, source_target_pairs={{96,32},{97,33},{98,34},{99,35},{100,36},{101,37},{102,38},{103,39... | collective-permute-start | bytes 6291464 | tf_op jit(solution)/shard_map/ppermute | solution.py:29
  74.2 80.2 %collective-permute-start = (bf16[1024,1024]{0,1:T(8,128)(2,1)}, bf16[1024,1024]{0,1:T(8,128)(2,1)}, u32[]{:S(2)}, u32[]{:S(2)}) collective-permute-start(bf16[1024,1024]{0,1:T(8,128)(2,1)} %bitcast.73), channel_id=1, source_target_pairs={{96,64},{97,65},{98,66},{99,67},{100,68},{101,69},{102,70},{103,71... | collective-permute-start | bytes 6291464 | tf_op jit(solution)/shard_map/ppermute | solution.py:30
  83.5 3.2 %copy-start.1 = (f32[1024,2048]{1,0:T(8,128)}, f32[1024,2048]{1,0:T(8,128)S(1)}, u32[]{:S(2)}) copy-start(f32[1024,2048]{1,0:T(8,128)S(1)} %fusion.30) | copy-start | bytes 25165828
  94.3 60.2 %collective-permute-start.2 = (bf16[1024,1024]{0,1:T(8,128)(2,1)}, bf16[1024,1024]{0,1:T(8,128)(2,1)}, u32[]{:S(2)}, u32[]{:S(2)}) collective-permute-start(bf16[1024,1024]{0,1:T(8,128)(2,1)} %collective-permute-done.1), channel_id=1, source_target_pairs={{32,0},{33,1},{34,2},{35,3},{36,4},{37,5},{38,6},{39,7},{40,8},{41... | collective-permute-start | bytes 6291464 | tf_op jit(solution)/shard_map/ppermute | solution.py:31
  132.7 21.3 %all-to-all-start.3 = ((bf16[32,4,33,128]{3,1,2,0:T(4,128)(2,1)}), bf16[32,4,33,128]{3,1,2,0:T(4,128)(2,1)S(1)}, u32[]{:S(2)}, u32[]{:S(2)}) async-start(bf16[32,4,33,128]{3,1,2,0:T(4,128)(2,1)} %broadcast_in_dim.27), calls=%async_computation.3 | async-start | bytes 2162688 | tf_op jit(solution)/shard_map/all_to_all | solution.py:39
  138.1 1.3 collective-permute-start.4
  138.8 2.2 %collective-permute-start.3 = (f32[1024]{0:T(1024)S(1)}, f32[1024]{0:T(1024)S(1)}, u32[]{:S(2)}, u32[]{:S(2)}) collective-permute-start(f32[1024]{0:T(1024)S(1)} %bitcast.89), channel_id=1, source_target_pairs={{96,64},{97,65},{98,66},{99,67},{100,68},{101,69},{102,70},{103,71... | collective-permute-start | bytes 12296 | tf_op jit(solution)/shard_map/ppermute | solution.py:30
  139.5 11.8 %collective-permute-start.5 = (f32[1024]{0:T(1024)S(1)}, f32[1024]{0:T(1024)S(1)}, u32[]{:S(2)}, u32[]{:S(2)}) collective-permute-start(f32[1024]{0:T(1024)S(1)} %collective-permute-done.4), channel_id=1, source_target_pairs={{32,0},{33,1},{34,2},{35,3},{36,4},{37,5},{38,6},{39,7},{40,8},{41... | collective-permute-start | bytes 12296 | tf_op jit(solution)/shard_map/ppermute | solution.py:31
  154.4 4.4 %copy-start.5 = (bf16[1024,1024]{1,0:T(8,128)(2,1)S(1)}, bf16[1024,1024]{1,0:T(8,128)(2,1)}, u32[]{:S(2)}) copy-start(bf16[1024,1024]{1,0:T(8,128)(2,1)} %param.15) | copy-start | bytes 6291460
  170.4 1.9 copy-start.2
  170.5 2.4 %copy-start.6 = (f32[1024]{0:T(1024)S(1)}, f32[1024]{0:T(1024)}, u32[]{:S(2)}) copy-start(f32[1024]{0:T(1024)} %param.17) | copy-start | bytes 12292
  185.3 2.9 %collective-permute-start.6 = (bf16[1024,2,256]{0,2,1:T(8,128)(2,1)S(1)}, bf16[1024,2,256]{0,2,1:T(8,128)(2,1)}, u32[]{:S(2)}, u32[]{:S(2)}) collective-permute-start(bf16[1024,2,256]{0,2,1:T(8,128)(2,1)S(1)} %fusion.59), channel_id=1, source_target_pairs={{0,32},{32,0},{64,96},{96,64},{1,33},{33,1},{65,97},{97,65},{2,34}... | collective-permute-start | bytes 3145736 | tf_op jit(solution)/shard_map/ppermute | solution.py:53
  190.4 1.3 copy-start.3
  191.8 15.5 %collective-permute-start.7 = (bf16[1024,256]{0,1:T(8,128)(2,1)S(1)}, bf16[1024,256]{0,1:T(8,128)(2,1)S(1)}, u32[]{:S(2)}, u32[]{:S(2)}) collective-permute-start(bf16[1024,256]{0,1:T(8,128)(2,1)S(1)} %fusion.63), channel_id=1, source_target_pairs={{0,64},{64,0},{32,96},{96,32},{1,65},{65,1},{33,97},{97,33},{2,66}... | collective-permute-start | bytes 1572872 | tf_op jit(solution)/shard_map/ppermute | solution.py:58

commit v8 on v7

--- a/solution.py
+++ b/solution.py
@@ -37,6 +37,17 @@
 def gather_a2a(value, axis, count):
     spread = jnp.broadcast_to(value[None], (count,) + value.shape)
     return lax.all_to_all(spread, axis, 0, 0, tiled=False)
+
+
+def gather_sec(value, me, sections):
+    if sections != 4:
+        return gather_a2a(value, "sec", sections)
+    got = lax.ppermute(value, "sec", [(0, 1), (1, 0), (2, 3), (3, 2)])
+    first = me % 2 == 0
+    pair = jnp.where(first, jnp.stack([value, got]), jnp.stack([got, value]))
+    other = lax.ppermute(pair, "sec", [(0, 2), (2, 0), (1, 3), (3, 1)])
+    lower = me // 2 == 0
+    return jnp.where(lower, jnp.concatenate([pair, other]), jnp.concatenate([other, pair]))
 
 
 def scatter_sum(term, me, sections):
@@ -111,7 +122,7 @@
         axis=0,
     ).reshape(blocks, piece, HEAD_DIM)
     reduced = jnp.sum(lax.all_to_all(packed, "pts", 0, 0, tiled=False), axis=0)
-    by_section = gather_a2a(reduced.astype(jnp.bfloat16), "sec", sections)
+    by_section = gather_sec(reduced.astype(jnp.bfloat16), me, sections)
     whole = gather_a2a(by_section, "pts", blocks).astype(jnp.float32)
     whole = whole.transpose(1, 0, 2, 3).reshape(sections, blocks * piece, HEAD_DIM)
     state_heads = whole[:, :width].reshape(sections, heads, HEAD_DIM, HEAD_DIM)

time: 212 us -> 208 us (0.981)
  blocking collectives: 31.9 us -> 21.1 us
  starting transfers between devices: 23.2 us -> 31.3 us
    all_to_all x1 -> x0, blocking collectives: 13 us -> none  [gather_a2a(): return lax.all_to_all(spread, axis, 0, 0, tiled=False)]
    ppermute x2, waiting for transfers between devices: 10.3 us -> 4.76 us  [from_last(): farther = lax.ppermute(far, axis, [(1, 0)])]
    ppermute x0 -> x2, starting transfers between devices: none -> 4.87 us  [the longest x1 3.74 us: gather_sec(): other = lax.ppermute(pair, 'sec', [(0, 2), (2, 0), (1, 3), (3, 1)])]
    all_to_all x2, waiting for transfers between devices: 53.8 us -> 57.5 us  [gather_a2a(): return lax.all_to_all(spread, axis, 0, 0, tiled=False)]
    ppermute x1, starting transfers between devices: 0.81 us -> 3.94 us  [scatter_sum(): lax.ppermute(other.astype(jnp.bfloat16), 'sec', [(0, 2), (2, 0), (1, 3),...]
    ppermute x0 -> x2, waiting for transfers between devices: none -> 2.59 us  [the longest x1 1.76 us: gather_sec(): other = lax.ppermute(pair, 'sec', [(0, 2), (2, 0), (1, 3), (3, 1)])]
    ppermute x1, waiting for transfers between devices: 14.7 us -> 12.2 us  [scatter_sum(): lax.ppermute(other.astype(jnp.bfloat16), 'sec', [(0, 2), (2, 0), (1, 3),...]
  transfers between devices with their start and end apart: 10 -> 12, of which waited for: 5 -> 7; matrix products, arithmetic and copies ran while one was open for 14% -> 14% of each run, Pallas kernels for 0% -> 0%
where the time goes in v8:
time: 208 us; the launch traced here: 206 us
  waiting for transfers between devices  79.9 us (38%)
  matrix products  32.4 us (16%)
  starting transfers between devices  31.3 us (15%)
  local copies, waits for them, and re-layouts  22.1 us (11%)
  blocking collectives  21.1 us (10%)
  other arithmetic  18 us (9%)
    all_to_all x2, waiting for transfers between devices, gather_a2a(): return lax.all_to_all(spread, axis, 0, 0, tiled=False)  57.5 us
    all_to_all x1, blocking collectives, on_device(): reduced = jnp.sum(lax.all_to_all(packed, 'pts', 0, 0, tiled=False), axis=0)  21.1 us
    all_to_all x2, starting transfers between devices, gather_a2a(): return lax.all_to_all(spread, axis, 0, 0, tiled=False)  14.3 us
    ppermute x1, waiting for transfers between devices, scatter_sum(): lax.ppermute(other.astype(jnp.bfloat16), 'sec', [(0, 2), (2, 0), (1, 3),...  12.2 us
    unnamed x16, local copies, waits for them, and re-layouts  11 us
    dot_general x1, matrix products, on_device(): term = jnp.dot(hidden, down_weight, preferred_element_type=jnp.float32)  10.7 us
    dot_general x1, matrix products, on_device(): projected = jnp.dot(normed, weights, preferred_element_type=jnp.float32)  7.25 us
    reduce_sum x2, other arithmetic, layer_normalizer(): mean = jnp.mean(values, axis=-1, keepdims=True)  5.74 us
  transfers between devices with their start and end apart: 12, of which 7 were waited for; matrix products, arithmetic and copies ran while one was open for 14% of the time, Pallas kernels for 0%

profile of v8, /device:TPU:16, one launch (start us, length us, event | category | flops | bytes accessed | tf_op | source)
XLA Modules:
  0.0 205.8 jit_solution(7776082860700603575)
XLA Ops:
  1.0 2.5 %broadcast_in_dim.20 = bf16[32,32,2048]{2,1,0:T(8,128)(2,1)} broadcast(bf16[32,2048]{1,0:T(8,128)(2,1)S(1)} %pad_maximum_fusion), dimensions={1,2} | broadcast | bytes 4325376 | tf_op jit(solution)/shard_map/broadcast_in_dim | solution.py:38
  3.5 8.8 %all-to-all-start = ((bf16[32,32,2048]{2,1,0:T(8,128)(2,1)}), bf16[32,32,2048]{2,1,0:T(8,128)(2,1)}, u32[]{:S(2)}, u32[]{:S(2)}) async-start(bf16[32,32,2048]{2,1,0:T(8,128)(2,1)} %broadcast_in_dim.20), calls=%async_computation | async-start | bytes 8388608 | tf_op jit(solution)/shard_map/all_to_all | solution.py:39
  12.4 3.9 %copy.33 = bf16[1,1024,1024]{1,2,0:T(8,128)(2,1)} copy(bf16[1,1024,1024]{2,1,0:T(8,128)(2,1)} %param.10) | data formatting | bytes 4194304 | tf_op args[0]
  16.3 2.0 convert_reduce_fusion.1
  18.3 2.2 %fusion.8 = f32[1024]{0:T(1024)S(1)} fusion(f32[1024]{0:T(1024)S(1)} %broadcast_multiply_fusion.2, bf16[1,1024,1024]{1,2,0:T(8,128)(2,1)} %copy.33), kind=kLoop, calls=%fused_computation.19 | loop fusion | flops 4193280 | bytes 2105344 | tf_op jit(solution)/shard_map/reduce_sum | solution.py:12
  20.5 49.5 %all-to-all-done = bf16[32,32,2048]{2,1,0:T(8,128)(2,1)} async-done(((bf16[32,32,2048]{2,1,0:T(8,128)(2,1)}), bf16[32,32,2048]{2,1,0:T(8,128)(2,1)}, u32[]{:S(2)}, u32[]{:S(2)}) %all-to-all-start) | async-done | bytes 4194336 | tf_op jit(solution)/shard_map/all_to_all | solution.py:39
  70.0 2.0 collective-permute-start.1
  72.8 2.0 collective-permute-start
  74.8 7.3 %fusion.30 = f32[1024,2048]{1,0:T(8,128)S(1)} fusion(bf16[1024,2048]{1,0:T(8,128)(2,1)} %bitcast.4, f32[1024]{0:T(1024)S(1)} %bitcast.91, f32[1024]{0:T(1024)S(1)} %add_rsqrt_fusion.2, f32[1024]{0:T(1024)S(1)} %broadcast_multiply_fusion.2, bf16[1,1024,1024]{1,2,0:T(8,128)(2,1)} %copy.33), kind=kOutput, calls=%fused_computation.44 | convolution fusion | flops 4300210176 | bytes 14692352 | tf_op jit(solution)/shard_map/dot_general | solution.py:101
  82.0 3.2 %copy-done.1 = f32[1024,2048]{1,0:T(8,128)} copy-done((f32[1024,2048]{1,0:T(8,128)}, f32[1024,2048]{1,0:T(8,128)S(1)}, u32[]{:S(2)}) %copy-start.1) | copy-done | bytes 8388632
  85.2 3.6 %convert_reduce_fusion.2 = (f32[1024]{0:T(1024)S(1)}, bf16[1024,1024]{1,0:T(8,128)(2,1)}) fusion(f32[1024,2048]{1,0:T(8,128)S(1)} %fusion.30, pred[1024]{0:T(1024)(128)(4,1)S(1)} %iota_compare_fusion), kind=kLoop, calls=%fused_computation.39 | loop fusion | flops 8387584 | bytes 6296576 | tf_op jit(solution)/shard_map/reduce_sum | solution.py:112
  88.9 3.9 %copy.49 = bf16[1024,1024]{0,1:T(8,128)(2,1)} copy(bf16[1024,1024]{1,0:T(8,128)(2,1)} %get-tuple-element.14) | data formatting | bytes 4194304 | tf_op jit(solution)/shard_map/reshape | solution.py:108
  92.8 3.6 %fusion.37 = f32[8,128,128]{2,1,0:T(8,128)S(1)} fusion(bf16[1024,8,128]{0,2,1:T(8,128)(2,1)} %bitcast.77, f32[1024,2048]{1,0:T(8,128)} %copy-done.1), kind=kOutput, calls=%fused_computation.49 | convolution fusion | flops 268435456 | bytes 4718592 | tf_op jit(solution)/shard_map/yzl,yzn->zln/dot_general | solution.py:106
  98.0 21.1 %all_to_all.15 = f32[32,33,128]{2,1,0:T(8,128)S(1)} all-to-all(f32[32,33,128]{2,1,0:T(8,128)S(1)} %reshape.138), channel_id=1, replica_groups=mesh['sec'=4,'pts'=32] {'pts'}, dimensions={0} | all-to-all | bytes 1081344 | tf_op jit(solution)/shard_map/all_to_all | solution.py:124
  121.1 3.7 %collective-permute-start.4 = (bf16[2,33,128]{2,1,0:T(8,128)(2,1)S(1)}, bf16[2,33,128]{2,1,0:T(8,128)(2,1)S(1)}, u32[]{:S(2)}, u32[]{:S(2)}) collective-permute-start(bf16[2,33,128]{2,1,0:T(8,128)(2,1)S(1)} %maximum_select_fusion.1), channel_id=1, source_target_pairs={{0,64},{64,0},{32,96},{96,32},{1,65},{65,1},{33,97},{97,33},{2,66}... | collective-permute-start | bytes 50696 | tf_op jit(solution)/shard_map/ppermute | solution.py:48
  124.8 1.8 collective-permute-done.4
  127.9 5.5 %all-to-all-start.2 = ((bf16[32,4,33,128]{3,1,2,0:T(4,128)(2,1)}), bf16[32,4,33,128]{3,1,2,0:T(4,128)(2,1)S(1)}, u32[]{:S(2)}, u32[]{:S(2)}) async-start(bf16[32,4,33,128]{3,1,2,0:T(4,128)(2,1)} %broadcast_in_dim.24), calls=%async_computation.2 | async-start | bytes 2162688 | tf_op jit(solution)/shard_map/all_to_all | solution.py:39
  134.8 1.5 collective-permute-start.7
  136.3 4.8 %collective-permute-done.7 = f32[1024]{0:T(1024)S(1)} collective-permute-done((f32[1024]{0:T(1024)S(1)}, f32[1024]{0:T(1024)S(1)}, u32[]{:S(2)}, u32[]{:S(2)}) %collective-permute-start.7) | collective-permute-done | bytes 4128 | tf_op jit(solution)/shard_map/ppermute | solution.py:31
  141.0 8.0 %all-to-all-done.2 = bf16[32,4,33,128]{3,1,2,0:T(4,128)(2,1)S(1)} async-done(((bf16[32,4,33,128]{3,1,2,0:T(4,128)(2,1)}), bf16[32,4,33,128]{3,1,2,0:T(4,128)(2,1)S(1)}, u32[]{:S(2)}, u32[]{:S(2)}) %all-to-all-start.2) | async-done | bytes 1081376 | tf_op jit(solution)/shard_map/all_to_all | solution.py:39
  149.4 3.8 %convert_reduce_fusion = (f32[1024]{0:T(1024)S(1)}, bf16[1024,1024]{0,1:T(8,128)(2,1)S(1)}) fusion(bf16[1024,1024]{0,1:T(8,128)(2,1)} %bitcast.76, bf16[1024,1024]{0,1:T(8,128)(2,1)} %collective-permute-done, bf16[1024,1024]{0,1:T(8,128)(2,1)} %collective-permute-done.1, bf16[1024,1024]{0,1:T(8,128)(2,1)} %collective-permute-done.2, pred[]{:T(512)S(6)} %eq.23, ...), kind=kLoop, calls=%fused_computation.9 | loop fusion | flops 5241856 | bytes 10489859 | tf_op jit(solution)/shard_map/reduce_sum | solution.py:10
  153.8 4.1 %fusion.24 = bf16[1024,1024]{1,0:T(8,128)(2,1)S(1)} fusion(bf16[1024,1024]{1,0:T(8,128)(2,1)S(1)} %copy-done.5, bf16[1024,1024]{0,1:T(8,128)(2,1)S(1)} %get-tuple-element.12, f32[1024]{0:T(1024)S(1)} %select_select_fusion.1, f32[1024]{0:T(1024)S(1)} %add_rsqrt_fusion.1, f32[1024]{0:T(1024)S(1)} %broadcast_multiply_fusion.1), kind=kOutput, calls=%fused_computation.35 | convolution fusion | flops 2157969408 | bytes 6303744 | tf_op jit(solution)/shard_map/dot_general | solution.py:135
  159.2 3.5 %fusion = bf16[1024,8,128]{0,2,1:T(8,128)(2,1)S(1)} fusion(f32[4,1024,8]{1,0,2:T(4,128)S(1)} %fusion.56, bf16[1024,8,128,1]{2,1,0,3:T(8,128)(2,1)S(1)} %bitcast.83, bf16[4,8,128,128]{3,0,2,1:T(4,128)(2,1)S(1)} %bitcast.85), kind=kOutput, calls=%fused_computation.1 | convolution fusion | flops 1081081856 | bytes 5373952 | tf_op jit(solution)/shard_map/rhk,shkv->srhv/dot_general | solution.py:138
  162.8 2.6 %fusion.70 = (f32[1024]{0:T(1024)S(1)}, f32[1024,1024]{0,1:T(8,128)S(1)}) fusion(bf16[1024,1024]{0,1:T(8,128)(2,1)S(1)} %bitcast.95, bf16[1024,1024]{1,0:T(8,128)(2,1)S(1)} %copy-done, bf16[1024,1024]{0,1:T(8,128)(2,1)S(1)} %get-tuple-element.12), kind=kOutput, calls=%fused_computation.94 | convolution fusion | flops 2150628352 | bytes 10489856 | tf_op jit(solution)/shard_map/dot_general | solution.py:147
  165.4 1.9 copy-done.2
  167.8 10.7 %fusion.28 = f32[1024,1024]{0,1:T(8,128)} fusion(bf16[1024,1024]{1,0:T(8,128)(2,1)} %param.19, bf16[1024,1024]{1,0:T(8,128)(2,1)} %param.18, f32[1024,1024]{0,1:T(8,128)} %copy-done.2, f32[1024]{0:T(1024)S(1)} %copy-done.6, f32[1024]{0:T(1024)S(1)} %add_rsqrt_fusion, f32[1024]{0:T(1024)S(1)} %broadcast_multiply_fusion), kind=kOutput, calls=%fused_computation.43 | convolution fusion | flops 4308598784 | bytes 12595200 | tf_op jit(solution)/shard_map/dot_general | solution.py:154
  178.5 1.7 fusion.59
  180.4 2.8 %collective-permute-done.8 = bf16[1024,2,256]{0,2,1:T(8,128)(2,1)} collective-permute-done((bf16[1024,2,256]{0,2,1:T(8,128)(2,1)S(1)}, bf16[1024,2,256]{0,2,1:T(8,128)(2,1)}, u32[]{:S(2)}, u32[]{:S(2)}) %collective-permute-start.8) | collective-permute-done | bytes 1048608 | tf_op jit(solution)/shard_map/ppermute | solution.py:64
  183.2 2.2 %bitcast_add_fusion = f32[1024,2,256]{0,2,1:T(8,128)S(1)} fusion(bf16[1024,2,256]{0,2,1:T(8,128)(2,1)} %collective-permute-done.8, f32[1024,2,2,256]{0,3,2,1:T(8,128)} %bitcast.81, s32[]{:T(128)S(6)} %select_n.138), kind=kLoop, calls=%fused_computation.53 | loop fusion | flops 1048576 | bytes 5242884 | tf_op jit(solution)/shard_map/add | solution.py:65
  186.8 3.9 %collective-permute-start.9 = (bf16[1024,256]{0,1:T(8,128)(2,1)S(1)}, bf16[1024,256]{0,1:T(8,128)(2,1)S(1)}, u32[]{:S(2)}, u32[]{:S(2)}) collective-permute-start(bf16[1024,256]{0,1:T(8,128)(2,1)S(1)} %fusion.63), channel_id=1, source_target_pairs={{0,64},{64,0},{32,96},{96,32},{1,65},{65,1},{33,97},{97,33},{2,66}... | collective-permute-start | bytes 1572872 | tf_op jit(solution)/shard_map/ppermute | solution.py:69
  190.7 12.2 %collective-permute-done.9 = bf16[1024,256]{0,1:T(8,128)(2,1)S(1)} collective-permute-done((bf16[1024,256]{0,1:T(8,128)(2,1)S(1)}, bf16[1024,256]{0,1:T(8,128)(2,1)S(1)}, u32[]{:S(2)}, u32[]{:S(2)}) %collective-permute-start.9) | collective-permute-done | bytes 524320 | tf_op jit(solution)/shard_map/ppermute | solution.py:69
  203.0 1.8 fusion.61
  (48 shorter events, 12.6 us)
Async XLA Ops:
  0.0 162.7 %copy-start = (bf16[1024,1024]{1,0:T(8,128)(2,1)S(1)}, bf16[1024,1024]{1,0:T(8,128)(2,1)}, u32[]{:S(2)}) copy-start(bf16[1024,1024]{1,0:T(8,128)(2,1)} %param.16) | copy-start | bytes 6291460
  3.5 66.5 %all-to-all-start = ((bf16[32,32,2048]{2,1,0:T(8,128)(2,1)}), bf16[32,32,2048]{2,1,0:T(8,128)(2,1)}, u32[]{:S(2)}, u32[]{:S(2)}) async-start(bf16[32,32,2048]{2,1,0:T(8,128)(2,1)} %broadcast_in_dim.20), calls=%async_computation | async-start | bytes 8388608 | tf_op jit(solution)/shard_map/all_to_all | solution.py:39
  12.4 62.4 %copy-start.4 = (f32[1,1024]{1,0:T(1,128)S(1)}, f32[1,1024]{1,0:T(1,128)}, u32[]{:S(2)}) copy-start(f32[1,1024]{1,0:T(1,128)} %param.12) | copy-start | bytes 12292
  70.0 26.4 %collective-permute-start.1 = (bf16[1024,1024]{0,1:T(8,128)(2,1)}, bf16[1024,1024]{0,1:T(8,128)(2,1)}, u32[]{:S(2)}, u32[]{:S(2)}) collective-permute-start(bf16[1024,1024]{0,1:T(8,128)(2,1)} %bitcast.74), channel_id=1, source_target_pairs={{96,32},{97,33},{98,34},{99,35},{100,36},{101,37},{102,38},{103,39... | collective-permute-start | bytes 6291464 | tf_op jit(solution)/shard_map/ppermute | solution.py:29
  72.8 76.6 %collective-permute-start = (bf16[1024,1024]{0,1:T(8,128)(2,1)}, bf16[1024,1024]{0,1:T(8,128)(2,1)}, u32[]{:S(2)}, u32[]{:S(2)}) collective-permute-start(bf16[1024,1024]{0,1:T(8,128)(2,1)} %bitcast.75), channel_id=1, source_target_pairs={{96,64},{97,65},{98,66},{99,67},{100,68},{101,69},{102,70},{103,71... | collective-permute-start | bytes 6291464 | tf_op jit(solution)/shard_map/ppermute | solution.py:30
  82.0 3.2 %copy-start.1 = (f32[1024,2048]{1,0:T(8,128)}, f32[1024,2048]{1,0:T(8,128)S(1)}, u32[]{:S(2)}) copy-start(f32[1024,2048]{1,0:T(8,128)S(1)} %fusion.30) | copy-start | bytes 25165828
  96.4 53.0 %collective-permute-start.2 = (bf16[1024,1024]{0,1:T(8,128)(2,1)}, bf16[1024,1024]{0,1:T(8,128)(2,1)}, u32[]{:S(2)}, u32[]{:S(2)}) collective-permute-start(bf16[1024,1024]{0,1:T(8,128)(2,1)} %collective-permute-done.1), channel_id=1, source_target_pairs={{32,0},{33,1},{34,2},{35,3},{36,4},{37,5},{38,6},{39,7},{40,8},{41... | collective-permute-start | bytes 6291464 | tf_op jit(solution)/shard_map/ppermute | solution.py:31
  119.1 2.0 collective-permute-start.3
  121.1 5.5 %collective-permute-start.4 = (bf16[2,33,128]{2,1,0:T(8,128)(2,1)S(1)}, bf16[2,33,128]{2,1,0:T(8,128)(2,1)S(1)}, u32[]{:S(2)}, u32[]{:S(2)}) collective-permute-start(bf16[2,33,128]{2,1,0:T(8,128)(2,1)S(1)} %maximum_select_fusion.1), channel_id=1, source_target_pairs={{0,64},{64,0},{32,96},{96,32},{1,65},{65,1},{33,97},{97,33},{2,66}... | collective-permute-start | bytes 50696 | tf_op jit(solution)/shard_map/ppermute | solution.py:48
  127.9 21.1 %all-to-all-start.2 = ((bf16[32,4,33,128]{3,1,2,0:T(4,128)(2,1)}), bf16[32,4,33,128]{3,1,2,0:T(4,128)(2,1)S(1)}, u32[]{:S(2)}, u32[]{:S(2)}) async-start(bf16[32,4,33,128]{3,1,2,0:T(4,128)(2,1)} %broadcast_in_dim.24), calls=%async_computation.2 | async-start | bytes 2162688 | tf_op jit(solution)/shard_map/all_to_all | solution.py:39
  133.4 1.3 collective-permute-start.6
  134.1 2.2 %collective-permute-start.5 = (f32[1024]{0:T(1024)S(1)}, f32[1024]{0:T(1024)S(1)}, u32[]{:S(2)}, u32[]{:S(2)}) collective-permute-start(f32[1024]{0:T(1024)S(1)} %bitcast.93), channel_id=1, source_target_pairs={{96,64},{97,65},{98,66},{99,67},{100,68},{101,69},{102,70},{103,71... | collective-permute-start | bytes 12296 | tf_op jit(solution)/shard_map/ppermute | solution.py:30
  134.8 6.3 %collective-permute-start.7 = (f32[1024]{0:T(1024)S(1)}, f32[1024]{0:T(1024)S(1)}, u32[]{:S(2)}, u32[]{:S(2)}) collective-permute-start(f32[1024]{0:T(1024)S(1)} %collective-permute-done.6), channel_id=1, source_target_pairs={{32,0},{33,1},{34,2},{35,3},{36,4},{37,5},{38,6},{39,7},{40,8},{41... | collective-permute-start | bytes 12296 | tf_op jit(solution)/shard_map/ppermute | solution.py:31
  149.4 4.4 %copy-start.5 = (bf16[1024,1024]{1,0:T(8,128)(2,1)S(1)}, bf16[1024,1024]{1,0:T(8,128)(2,1)}, u32[]{:S(2)}) copy-start(bf16[1024,1024]{1,0:T(8,128)(2,1)} %param.15) | copy-start | bytes 6291460
  165.4 1.9 copy-start.2
  165.4 2.4 %copy-start.6 = (f32[1024]{0:T(1024)S(1)}, f32[1024]{0:T(1024)}, u32[]{:S(2)}) copy-start(f32[1024]{0:T(1024)} %param.17) | copy-start | bytes 12292
  180.3 2.9 %collective-permute-start.8 = (bf16[1024,2,256]{0,2,1:T(8,128)(2,1)S(1)}, bf16[1024,2,256]{0,2,1:T(8,128)(2,1)}, u32[]{:S(2)}, u32[]{:S(2)}) collective-permute-start(bf16[1024,2,256]{0,2,1:T(8,128)(2,1)S(1)} %fusion.59), channel_id=1, source_target_pairs={{0,32},{32,0},{64,96},{96,64},{1,33},{33,1},{65,97},{97,65},{2,34}... | collective-permute-start | bytes 3145736 | tf_op jit(solution)/shard_map/ppermute | solution.py:64
  185.4 1.3 copy-start.3
  186.8 16.2 %collective-permute-start.9 = (bf16[1024,256]{0,1:T(8,128)(2,1)S(1)}, bf16[1024,256]{0,1:T(8,128)(2,1)S(1)}, u32[]{:S(2)}, u32[]{:S(2)}) collective-permute-start(bf16[1024,256]{0,1:T(8,128)(2,1)S(1)} %fusion.63), channel_id=1, source_target_pairs={{0,64},{64,0},{32,96},{96,32},{1,65},{65,1},{33,97},{97,33},{2,66}... | collective-permute-start | bytes 1572872 | tf_op jit(solution)/shard_map/ppermute | solution.py:69

commit v9 on v8

--- a/solution.py
+++ b/solution.py
@@ -93,11 +93,12 @@
     stacked = jnp.concatenate([key_weight[0], value_weight[0]], axis=1)
     weights = gather_a2a(stacked, "pts", blocks).reshape(width, 2 * width)
 
-    late_block, late_gain, weights = lax.optimization_barrier((block, input_gain[0], weights))
-    query_block = from_last(late_block, "sec", sections)
-    query_gain = from_last(late_gain, "sec", sections)
-
     normed = layer_normalizer(block.astype(jnp.float32), input_gain[0]).astype(jnp.bfloat16)
+    own_feats = feature_map(
+        jnp.dot(normed, query_weight, preferred_element_type=jnp.float32)
+    ).astype(jnp.bfloat16)
+    late, weights = lax.optimization_barrier((jnp.stack([own_feats, block]), weights))
+    query_feats, query_block = from_last(late, "sec", sections)
     projected = jnp.dot(normed, weights, preferred_element_type=jnp.float32)
     valid = jnp.arange(rows) < counts[0, 0]
     key_feats = feature_map(projected[:, :width]).astype(jnp.bfloat16)
@@ -128,12 +129,6 @@
     state_heads = whole[:, :width].reshape(sections, heads, HEAD_DIM, HEAD_DIM)
     total_heads = whole[:, width:packed_rows].reshape(sections, heads, HEAD_DIM)
 
-    query_normed = layer_normalizer(query_block.astype(jnp.float32), query_gain).astype(
-        jnp.bfloat16
-    )
-    query_feats = feature_map(
-        jnp.dot(query_normed, query_weight, preferred_element_type=jnp.float32)
-    ).astype(jnp.bfloat16)
     per_head_queries = query_feats.astype(jnp.float32).reshape(rows, heads, HEAD_DIM)
     numerator = jnp.einsum(
         "rhk,shkv->srhv", per_head_queries, state_heads, precision=lax.Precision.HIGH

time: 208 us -> 251 us (1.21)
  starting transfers between devices: 31.3 us -> 71.1 us
  waiting for transfers between devices: 79.9 us -> 82.8 us
  local copies, waits for them, and re-layouts: 22.1 us -> 24.7 us
    ppermute x1, starting transfers between devices: 1.13 us -> 48.2 us  [gather_sec(): got = lax.ppermute(value, 'sec', [(0, 1), (1, 0), (2, 3), (3, 2)])]
    dynamic_slice x0 -> x3, local copies, waits for them, and re-layouts: none -> 7.9 us  [the longest x2 6.15 us: scatter_sum(): kept = lax.dynamic_index_in_dim(quarters, parity, axis=2, keepdims=False)]
    all_to_all x2, waiting for transfers between devices: 57.5 us -> 62.7 us  [gather_a2a(): return lax.all_to_all(spread, axis, 0, 0, tiled=False)]
    ppermute x2 -> x1, waiting for transfers between devices: 4.76 us -> 0.01 us  [from_last(): farther = lax.ppermute(far, axis, [(1, 0)])]
    ppermute x1, starting transfers between devices: 3.74 us -> 0.09 us  [gather_sec(): other = lax.ppermute(pair, 'sec', [(0, 2), (2, 0), (1, 3), (3, 1)])]
    reduce_sum x2 -> x1, other arithmetic: 5.74 us -> 2.08 us  [layer_normalizer(): mean = jnp.mean(values, axis=-1, keepdims=True)]
    ppermute x1, waiting for transfers between devices: 1.76 us -> 5.26 us  [gather_sec(): other = lax.ppermute(pair, 'sec', [(0, 2), (2, 0), (1, 3), (3, 1)])]
    ppermute x1, waiting for transfers between devices: 2.76 us -> 0.01 us  [scatter_sum(): lax.ppermute(sent.astype(jnp.bfloat16), 'sec', [(0, 1), (1, 0), (2, 3), (...]
  transfers between devices with their start and end apart: 12 -> 9, of which waited for: 7 -> 5; matrix products, arithmetic and copies ran while one was open for 14% -> 15% of each run, Pallas kernels for 0% -> 0%
where the time goes in v9:
time: 251 us; the launch traced here: 249 us
  waiting for transfers between devices  82.8 us (33%)
  starting transfers between devices  71.1 us (28%)
  matrix products  31 us (12%)
  local copies, waits for them, and re-layouts  24.7 us (10%)
  other arithmetic  19.2 us (8%)
  blocking collectives  18.8 us (7%)
    all_to_all x2, waiting for transfers between devices, gather_a2a(): return lax.all_to_all(spread, axis, 0, 0, tiled=False)  62.7 us
    ppermute x1, starting transfers between devices, gather_sec(): got = lax.ppermute(value, 'sec', [(0, 1), (1, 0), (2, 3), (3, 2)])  48.2 us
    all_to_all x1, blocking collectives, on_device(): reduced = jnp.sum(lax.all_to_all(packed, 'pts', 0, 0, tiled=False), axis=0)  18.8 us
    all_to_all x2, starting transfers between devices, gather_a2a(): return lax.all_to_all(spread, axis, 0, 0, tiled=False)  14.5 us
    ppermute x1, waiting for transfers between devices, scatter_sum(): lax.ppermute(other.astype(jnp.bfloat16), 'sec', [(0, 2), (2, 0), (1, 3),...  14 us
    dot_general x1, matrix products, on_device(): term = jnp.dot(hidden, down_weight, preferred_element_type=jnp.float32)  10.1 us
    unnamed x19, local copies, waits for them, and re-layouts  8.59 us
    dot_general x1, matrix products, on_device(): projected = jnp.dot(normed, weights, preferred_element_type=jnp.float32)  7.07 us
  transfers between devices with their start and end apart: 9, of which 5 were waited for; matrix products, arithmetic and copies ran while one was open for 15% of the time, Pallas kernels for 0%

profile of v9, /device:TPU:16, one launch (start us, length us, event | category | flops | bytes accessed | tf_op | source)
XLA Modules:
  0.0 248.5 jit_solution(3339333924869615228)
XLA Ops:
  1.0 2.5 %broadcast_in_dim.20 = bf16[32,32,2048]{2,1,0:T(8,128)(2,1)} broadcast(bf16[32,2048]{1,0:T(8,128)(2,1)S(1)} %pad_maximum_fusion.1), dimensions={1,2} | broadcast | bytes 4325376 | tf_op jit(solution)/shard_map/broadcast_in_dim | solution.py:38
  3.5 8.8 %all-to-all-start = ((bf16[32,32,2048]{2,1,0:T(8,128)(2,1)}), bf16[32,32,2048]{2,1,0:T(8,128)(2,1)}, u32[]{:S(2)}, u32[]{:S(2)}) async-start(bf16[32,32,2048]{2,1,0:T(8,128)(2,1)} %broadcast_in_dim.20), calls=%async_computation | async-start | bytes 8388608 | tf_op jit(solution)/shard_map/all_to_all | solution.py:39
  12.4 2.1 convert_reduce_fusion
  14.5 2.3 fusion.4
  16.8 3.5 %fusion.24 = bf16[1,1024,1024]{2,1,0:T(8,128)(2,1)S(1)} fusion(bf16[1024,1024]{1,0:T(8,128)(2,1)S(1)} %copy-done.5, bf16[1,1024,1024]{2,1,0:T(8,128)(2,1)S(1)} %copy-done.1, f32[1024]{0:T(1024)S(1)} %bitcast.98, f32[1024]{0:T(1024)S(1)} %add_rsqrt_fusion.1, f32[1024]{0:T(1024)S(1)} %broadcast_multiply_fusion.1), kind=kOutput, calls=%fused_computation.39 | convolution fusion | flops 2157969408 | bytes 6303744 | tf_op jit(solution)/shard_map/dot_general | solution.py:98
  20.4 2.3 pad_maximum_fusion
  22.7 47.3 %all-to-all-done = bf16[32,32,2048]{2,1,0:T(8,128)(2,1)} async-done(((bf16[32,32,2048]{2,1,0:T(8,128)(2,1)}), bf16[32,32,2048]{2,1,0:T(8,128)(2,1)}, u32[]{:S(2)}, u32[]{:S(2)}) %all-to-all-start) | async-done | bytes 4194336 | tf_op jit(solution)/shard_map/all_to_all | solution.py:39
  70.0 2.6 %collective-permute-start.1 = (bf16[2,1024,1024]{2,1,0:T(8,128)(2,1)}, bf16[2,1024,1024]{2,1,0:T(8,128)(2,1)}, u32[]{:S(2)}, u32[]{:S(2)}) collective-permute-start(bf16[2,1024,1024]{2,1,0:T(8,128)(2,1)} %pad_maximum_fusion), channel_id=1, source_target_pairs={{96,32},{97,33},{98,34},{99,35},{100,36},{101,37},{102,38},{103,39... | collective-permute-start | bytes 12582920 | tf_op jit(solution)/shard_map/ppermute | solution.py:29
  73.4 2.6 %collective-permute-start = (bf16[2,1024,1024]{2,1,0:T(8,128)(2,1)}, bf16[2,1024,1024]{2,1,0:T(8,128)(2,1)}, u32[]{:S(2)}, u32[]{:S(2)}) collective-permute-start(bf16[2,1024,1024]{2,1,0:T(8,128)(2,1)} %pad_maximum_fusion), channel_id=1, source_target_pairs={{96,64},{97,65},{98,66},{99,67},{100,68},{101,69},{102,70},{103,71... | collective-permute-start | bytes 12582920 | tf_op jit(solution)/shard_map/ppermute | solution.py:30
  77.3 7.1 %fusion.51 = f32[1024,2048]{1,0:T(8,128)S(1)} fusion(bf16[1024,2048]{1,0:T(8,128)(2,1)} %bitcast.5, bf16[1,1024,1024]{2,1,0:T(8,128)(2,1)} %param.10, f32[1024]{0:T(1024)S(1)} %bitcast.99, f32[1024]{0:T(1024)S(1)} %add_rsqrt_fusion.1, f32[1024]{0:T(1024)S(1)} %broadcast_multiply_fusion.1), kind=kOutput, calls=%fused_computation.80 | convolution fusion | flops 4300210176 | bytes 14692352 | tf_op jit(solution)/shard_map/dot_general | solution.py:102
  84.3 3.2 %copy-done.2 = f32[1024,2048]{1,0:T(8,128)} copy-done((f32[1024,2048]{1,0:T(8,128)}, f32[1024,2048]{1,0:T(8,128)S(1)}, u32[]{:S(2)}) %copy-start.2) | copy-done | bytes 8388632
  87.6 3.6 %convert_reduce_fusion.1 = (f32[1024]{0:T(1024)S(1)}, bf16[1024,1024]{1,0:T(8,128)(2,1)}) fusion(f32[1024,2048]{1,0:T(8,128)S(1)} %fusion.51, pred[1024]{0:T(1024)(128)(4,1)S(1)} %iota_compare_fusion), kind=kLoop, calls=%fused_computation.34 | loop fusion | flops 8387584 | bytes 6296576 | tf_op jit(solution)/shard_map/reduce_sum | solution.py:113
  91.1 3.9 %copy.39 = bf16[1024,1024]{0,1:T(8,128)(2,1)} copy(bf16[1024,1024]{1,0:T(8,128)(2,1)} %get-tuple-element.12) | data formatting | bytes 4194304 | tf_op jit(solution)/shard_map/reshape | solution.py:109
  95.1 3.6 %fusion.27 = f32[8,128,128]{2,1,0:T(8,128)S(1)} fusion(bf16[1024,8,128]{0,2,1:T(8,128)(2,1)} %bitcast.83, f32[1024,2048]{1,0:T(8,128)} %copy-done.2), kind=kOutput, calls=%fused_computation.41 | convolution fusion | flops 268435456 | bytes 4718592 | tf_op jit(solution)/shard_map/yzl,yzn->zln/dot_general | solution.py:107
  98.9 18.8 %all_to_all.15 = f32[32,33,128]{2,1,0:T(8,128)S(1)} all-to-all(f32[32,33,128]{2,1,0:T(8,128)S(1)} %reshape.129), channel_id=1, replica_groups=mesh['sec'=4,'pts'=32] {'pts'}, dimensions={0} | all-to-all | bytes 1081344 | tf_op jit(solution)/shard_map/all_to_all | solution.py:125
  117.8 48.2 %collective-permute-start.3 = (bf16[33,128]{1,0:T(8,128)(2,1)S(1)}, bf16[33,128]{1,0:T(8,128)(2,1)S(1)}, u32[]{:S(2)}, u32[]{:S(2)}) collective-permute-start(bf16[33,128]{1,0:T(8,128)(2,1)S(1)} %reduce_sum.66), channel_id=1, source_target_pairs={{0,32},{32,0},{64,96},{96,64},{1,33},{33,1},{65,97},{97,65},{2,34}... | collective-permute-start | bytes 25352 | tf_op jit(solution)/shard_map/ppermute | solution.py:45
  166.9 5.3 %collective-permute-done.4 = bf16[2,33,128]{2,1,0:T(8,128)(2,1)S(1)} collective-permute-done((bf16[2,33,128]{2,1,0:T(8,128)(2,1)S(1)}, bf16[2,33,128]{2,1,0:T(8,128)(2,1)S(1)}, u32[]{:S(2)}, u32[]{:S(2)}) %collective-permute-start.4) | collective-permute-done | bytes 16928 | tf_op jit(solution)/shard_map/ppermute | solution.py:48
  173.5 5.6 %all-to-all-start.2 = ((bf16[32,4,33,128]{3,1,2,0:T(4,128)(2,1)}), bf16[32,4,33,128]{3,1,2,0:T(4,128)(2,1)S(1)}, u32[]{:S(2)}, u32[]{:S(2)}) async-start(bf16[32,4,33,128]{3,1,2,0:T(4,128)(2,1)} %broadcast_in_dim.24), calls=%async_computation.2 | async-start | bytes 2162688 | tf_op jit(solution)/shard_map/all_to_all | solution.py:39
  179.1 15.4 %all-to-all-done.2 = bf16[32,4,33,128]{3,1,2,0:T(4,128)(2,1)S(1)} async-done(((bf16[32,4,33,128]{3,1,2,0:T(4,128)(2,1)}), bf16[32,4,33,128]{3,1,2,0:T(4,128)(2,1)S(1)}, u32[]{:S(2)}, u32[]{:S(2)}) %all-to-all-start.2) | async-done | bytes 1081376 | tf_op jit(solution)/shard_map/all_to_all | solution.py:39
  194.9 2.6 %select_select_fusion = bf16[2,1024,1024]{2,1,0:T(8,128)(2,1)S(1)} fusion(bf16[2,1024,1024]{2,1,0:T(8,128)(2,1)} %pad_maximum_fusion, bf16[2,1024,1024]{2,1,0:T(8,128)(2,1)} %collective-permute-done, bf16[2,1024,1024]{2,1,0:T(8,128)(2,1)} %collective-permute-done.1, bf16[2,1024,1024]{2,1,0:T(8,128)(2,1)} %collective-permute-done.2, pred[]{:T(512)S(6)} %eq.20, ...), kind=kLoop, calls=%fused_computation.35 | loop fusion | flops 6291456 | bytes 20971524 | tf_op jit(solution)/shard_map/jit(_where)/select_n | solution.py:32
  199.0 3.3 %fusion = bf16[1024,8,128]{0,2,1:T(8,128)(2,1)S(1)} fusion(f32[4,1024,8]{1,0,2:T(4,128)S(1)} %fusion.40, bf16[1024,8,128,1]{2,1,0,3:T(8,128)(2,1)S(1)} %bitcast.89, bf16[4,8,128,128]{3,0,2,1:T(4,128)(2,1)S(1)} %bitcast.92), kind=kOutput, calls=%fused_computation.1 | convolution fusion | flops 1081081856 | bytes 5373952 | tf_op jit(solution)/shard_map/rhk,shkv->srhv/dot_general | solution.py:133
  202.3 2.7 %fusion.57 = (f32[1024]{0:T(1024)S(1)}, f32[1024,1024]{1,0:T(8,128)S(1)}) fusion(bf16[2,1024,1024]{2,1,0:T(8,128)(2,1)S(1)} %select_select_fusion, bf16[1024,1024]{0,1:T(8,128)(2,1)S(1)} %bitcast.100, bf16[1024,1024]{1,0:T(8,128)(2,1)S(1)} %copy-done), kind=kOutput, calls=%fused_computation.82 | convolution fusion | flops 2150628352 | bytes 10489856 | tf_op jit(solution)/shard_map/dot_general | solution.py:142
  205.0 1.9 copy-done.3
  207.5 10.1 %fusion.25 = f32[1024,1024]{0,1:T(8,128)} fusion(bf16[1024,1024]{1,0:T(8,128)(2,1)} %param.19, bf16[1024,1024]{1,0:T(8,128)(2,1)} %param.18, f32[1024,1024]{1,0:T(8,128)} %copy-done.3, f32[1024]{0:T(1024)S(1)} %copy-done.7, f32[1024]{0:T(1024)S(1)} %add_rsqrt_fusion, f32[1024]{0:T(1024)S(1)} %broadcast_multiply_fusion), kind=kOutput, calls=%fused_computation.40 | convolution fusion | flops 4308598784 | bytes 12595200 | tf_op jit(solution)/shard_map/dot_general | solution.py:149
  217.7 1.7 constant_dynamic-slice_fusion
  219.4 1.3 copy.45
  220.8 3.2 %constant_dynamic-slice_fusion.1 = f32[1024,2,1,256]{0,3,2,1:T(8,128)} fusion(f32[1024,2,2,256]{0,3,2,1:T(8,128)} %bitcast.87, s32[]{:T(128)S(6)} %select_n.112), kind=kLoop, calls=%fused_computation.75 | loop fusion | bytes 4194308 | tf_op jit(solution)/shard_map/jit(dynamic_index_in_dim)/dynamic_slice | solution.py:62
  224.0 2.9 %copy.34 = f32[1024,2,1,256]{3,0,1,2:T(8,128)} copy(f32[1024,2,1,256]{0,3,2,1:T(8,128)} %constant_dynamic-slice_fusion.1) | data formatting | bytes 4194304 | tf_op jit(solution)/shard_map/jit(dynamic_index_in_dim)/dynamic_slice | solution.py:62
  226.9 1.8 bitcast_add_fusion
  230.1 1.9 collective-permute-start.6
  232.0 14.0 %collective-permute-done.6 = bf16[1024,256]{1,0:T(8,128)(2,1)S(1)} collective-permute-done((bf16[1024,256]{1,0:T(8,128)(2,1)S(1)}, bf16[1024,256]{1,0:T(8,128)(2,1)S(1)}, u32[]{:S(2)}, u32[]{:S(2)}) %collective-permute-start.6) | collective-permute-done | bytes 524320 | tf_op jit(solution)/shard_map/ppermute | solution.py:69
  246.0 2.5 %fusion.44 = bf16[1024,256]{1,0:T(8,128)(2,1)} fusion(bf16[1024,256]{1,0:T(8,128)(2,1)S(1)} %collective-permute-done.6, f32[1024,2,256]{2,0,1:T(8,128)} %copy-done.4, s32[]{:T(128)S(6)} %select_n.114, f32[1024,1024]{1,0:T(8,128)} %copy-done.3, s32[]{:T(128)S(6)} %select_n.111), kind=kLoop, calls=%fused_computation.60 | loop fusion | flops 1048576 | bytes 3145736 | tf_op jit(solution)/shard_map/convert_element_type | solution.py:152
  (43 shorter events, 8.7 us)
Async XLA Ops:
  0.0 202.3 %copy-start = (bf16[1024,1024]{1,0:T(8,128)(2,1)S(1)}, bf16[1024,1024]{1,0:T(8,128)(2,1)}, u32[]{:S(2)}) copy-start(bf16[1024,1024]{1,0:T(8,128)(2,1)} %param.16) | copy-start | bytes 6291460
  3.5 66.5 %all-to-all-start = ((bf16[32,32,2048]{2,1,0:T(8,128)(2,1)}), bf16[32,32,2048]{2,1,0:T(8,128)(2,1)}, u32[]{:S(2)}, u32[]{:S(2)}) async-start(bf16[32,32,2048]{2,1,0:T(8,128)(2,1)} %broadcast_in_dim.20), calls=%async_computation | async-start | bytes 8388608 | tf_op jit(solution)/shard_map/all_to_all | solution.py:39
  12.4 4.4 %copy-start.1 = (bf16[1,1024,1024]{2,1,0:T(8,128)(2,1)S(1)}, bf16[1,1024,1024]{2,1,0:T(8,128)(2,1)}, u32[]{:S(2)}) copy-start(bf16[1,1024,1024]{2,1,0:T(8,128)(2,1)} %param.10) | copy-start | bytes 6291460
  12.4 4.4 %copy-start.5 = (bf16[1024,1024]{1,0:T(8,128)(2,1)S(1)}, bf16[1024,1024]{1,0:T(8,128)(2,1)}, u32[]{:S(2)}) copy-start(bf16[1024,1024]{1,0:T(8,128)(2,1)} %param.15) | copy-start | bytes 6291460
  12.4 4.4 %copy-start.6 = (f32[1,1024]{1,0:T(1,128)S(1)}, f32[1,1024]{1,0:T(1,128)}, u32[]{:S(2)}) copy-start(f32[1,1024]{1,0:T(1,128)} %param.12) | copy-start | bytes 12292
  70.0 6.0 %collective-permute-start.1 = (bf16[2,1024,1024]{2,1,0:T(8,128)(2,1)}, bf16[2,1024,1024]{2,1,0:T(8,128)(2,1)}, u32[]{:S(2)}, u32[]{:S(2)}) collective-permute-start(bf16[2,1024,1024]{2,1,0:T(8,128)(2,1)} %pad_maximum_fusion), channel_id=1, source_target_pairs={{96,32},{97,33},{98,34},{99,35},{100,36},{101,37},{102,38},{103,39... | collective-permute-start | bytes 12582920 | tf_op jit(solution)/shard_map/ppermute | solution.py:29
  73.4 121.5 %collective-permute-start = (bf16[2,1024,1024]{2,1,0:T(8,128)(2,1)}, bf16[2,1024,1024]{2,1,0:T(8,128)(2,1)}, u32[]{:S(2)}, u32[]{:S(2)}) collective-permute-start(bf16[2,1024,1024]{2,1,0:T(8,128)(2,1)} %pad_maximum_fusion), channel_id=1, source_target_pairs={{96,64},{97,65},{98,66},{99,67},{100,68},{101,69},{102,70},{103,71... | collective-permute-start | bytes 12582920 | tf_op jit(solution)/shard_map/ppermute | solution.py:30
  76.0 118.9 %collective-permute-start.2 = (bf16[2,1024,1024]{2,1,0:T(8,128)(2,1)}, bf16[2,1024,1024]{2,1,0:T(8,128)(2,1)}, u32[]{:S(2)}, u32[]{:S(2)}) collective-permute-start(bf16[2,1024,1024]{2,1,0:T(8,128)(2,1)} %collective-permute-done.1), channel_id=1, source_target_pairs={{32,0},{33,1},{34,2},{35,3},{36,4},{37,5},{38,6},{39,7},{40,8},{41... | collective-permute-start | bytes 12582920 | tf_op jit(solution)/shard_map/ppermute | solution.py:31
  84.3 3.2 %copy-start.2 = (f32[1024,2048]{1,0:T(8,128)}, f32[1024,2048]{1,0:T(8,128)S(1)}, u32[]{:S(2)}) copy-start(f32[1024,2048]{1,0:T(8,128)S(1)} %fusion.51) | copy-start | bytes 25165828
  117.8 49.0 %collective-permute-start.3 = (bf16[33,128]{1,0:T(8,128)(2,1)S(1)}, bf16[33,128]{1,0:T(8,128)(2,1)S(1)}, u32[]{:S(2)}, u32[]{:S(2)}) collective-permute-start(bf16[33,128]{1,0:T(8,128)(2,1)S(1)} %reduce_sum.66), channel_id=1, source_target_pairs={{0,32},{32,0},{64,96},{96,64},{1,33},{33,1},{65,97},{97,65},{2,34}... | collective-permute-start | bytes 25352 | tf_op jit(solution)/shard_map/ppermute | solution.py:45
  166.8 5.4 %collective-permute-start.4 = (bf16[2,33,128]{2,1,0:T(8,128)(2,1)S(1)}, bf16[2,33,128]{2,1,0:T(8,128)(2,1)S(1)}, u32[]{:S(2)}, u32[]{:S(2)}) collective-permute-start(bf16[2,33,128]{2,1,0:T(8,128)(2,1)S(1)} %maximum_select_fusion.1), channel_id=1, source_target_pairs={{0,64},{64,0},{32,96},{96,32},{1,65},{65,1},{33,97},{97,33},{2,66}... | collective-permute-start | bytes 50696 | tf_op jit(solution)/shard_map/ppermute | solution.py:48
  173.5 21.0 %all-to-all-start.2 = ((bf16[32,4,33,128]{3,1,2,0:T(4,128)(2,1)}), bf16[32,4,33,128]{3,1,2,0:T(4,128)(2,1)S(1)}, u32[]{:S(2)}, u32[]{:S(2)}) async-start(bf16[32,4,33,128]{3,1,2,0:T(4,128)(2,1)} %broadcast_in_dim.24), calls=%async_computation.2 | async-start | bytes 2162688 | tf_op jit(solution)/shard_map/all_to_all | solution.py:39
  205.0 1.9 copy-start.3
  205.0 2.5 %copy-start.7 = (f32[1024]{0:T(1024)S(1)}, f32[1024]{0:T(1024)}, u32[]{:S(2)}) copy-start(f32[1024]{0:T(1024)} %param.17) | copy-start | bytes 12292
  220.8 6.2 %collective-permute-start.5 = (bf16[1024,2,256]{2,0,1:T(8,128)(2,1)}, bf16[1024,2,256]{2,0,1:T(8,128)(2,1)S(1)}, u32[]{:S(2)}, u32[]{:S(2)}) collective-permute-start(bf16[1024,2,256]{2,0,1:T(8,128)(2,1)} %bitcast.91), channel_id=1, source_target_pairs={{0,32},{32,0},{64,96},{96,64},{1,33},{33,1},{65,97},{97,65},{2,34}... | collective-permute-start | bytes 3145736 | tf_op jit(solution)/shard_map/ppermute | solution.py:64
  228.7 1.3 copy-start.4
  230.1 15.9 %collective-permute-start.6 = (bf16[1024,256]{1,0:T(8,128)(2,1)S(1)}, bf16[1024,256]{1,0:T(8,128)(2,1)S(1)}, u32[]{:S(2)}, u32[]{:S(2)}) collective-permute-start(bf16[1024,256]{1,0:T(8,128)(2,1)S(1)} %fusion.46), channel_id=1, source_target_pairs={{0,64},{64,0},{32,96},{96,32},{1,65},{65,1},{33,97},{97,33},{2,66}... | collective-permute-start | bytes 1572872 | tf_op jit(solution)/shard_map/ppermute | solution.py:69

commit v10 on v8

--- a/solution.py
+++ b/solution.py
@@ -93,9 +93,9 @@
     stacked = jnp.concatenate([key_weight[0], value_weight[0]], axis=1)
     weights = gather_a2a(stacked, "pts", blocks).reshape(width, 2 * width)
 
-    late_block, late_gain, weights = lax.optimization_barrier((block, input_gain[0], weights))
+    query_gain = from_last(input_gain[0], "sec", sections)
+    late_block, weights = lax.optimization_barrier((block, weights))
     query_block = from_last(late_block, "sec", sections)
-    query_gain = from_last(late_gain, "sec", sections)
 
     normed = layer_normalizer(block.astype(jnp.float32), input_gain[0]).astype(jnp.bfloat16)
     projected = jnp.dot(normed, weights, preferred_element_type=jnp.float32)
@@ -121,6 +121,7 @@
         ],
         axis=0,
     ).reshape(blocks, piece, HEAD_DIM)
+    packed, query_block, query_gain = lax.optimization_barrier((packed, query_block, query_gain))
     reduced = jnp.sum(lax.all_to_all(packed, "pts", 0, 0, tiled=False), axis=0)
     by_section = gather_sec(reduced.astype(jnp.bfloat16), me, sections)
     whole = gather_a2a(by_section, "pts", blocks).astype(jnp.float32)
@@ -170,6 +171,7 @@
         P(None, "sec"),
         P("sec", None),
     )
+
     return jax.shard_map(
         on_device, mesh=mesh, in_specs=placed, out_specs=P("pts", "sec"), check_vma=False
     )

time: 208 us -> 231 us (1.11)
  waiting for transfers between devices: 79.9 us -> 111 us
  blocking collectives: 21.1 us -> 0 us
  matrix products: 32.4 us -> 36.3 us
  local copies, waits for them, and re-layouts: 22.1 us -> 25.6 us
  starting transfers between devices: 31.3 us -> 34.5 us
  other arithmetic: 18 us -> 21.1 us
    all_to_all x1 -> x0, blocking collectives: 21.1 us -> none  [on_device(): reduced = jnp.sum(lax.all_to_all(packed, 'pts', 0, 0, tiled=False), axis=0)]
    ppermute x2, waiting for transfers between devices: 4.76 us -> 19.7 us  [from_last(): farther = lax.ppermute(far, axis, [(1, 0)])]
    all_to_all x0 -> x1, waiting for transfers between devices: none -> 11.4 us  [on_device(): reduced = jnp.sum(lax.all_to_all(packed, 'pts', 0, 0, tiled=False), axis=0)]
    all_to_all x0 -> x1, starting transfers between devices: none -> 10 us  [on_device(): reduced = jnp.sum(lax.all_to_all(packed, 'pts', 0, 0, tiled=False), axis=0)]
    ppermute x1, starting transfers between devices: 3.74 us -> 0.09 us  [gather_sec(): other = lax.ppermute(pair, 'sec', [(0, 2), (2, 0), (1, 3), (3, 1)])]
    ppermute x1, waiting for transfers between devices: 1.76 us -> 5.26 us  [gather_sec(): other = lax.ppermute(pair, 'sec', [(0, 2), (2, 0), (1, 3), (3, 1)])]
    select_n x1 -> x2, other arithmetic: 0.01 us -> 3.32 us  [from_last(): jnp.where(me == 3, value, jnp.where(me == 2, near, jnp.where(me == 1, far...]
    ppermute x1, starting transfers between devices: 3.94 us -> 0.83 us  [scatter_sum(): lax.ppermute(other.astype(jnp.bfloat16), 'sec', [(0, 2), (2, 0), (1, 3),...]
  transfers between devices with their start and end apart: 12 -> 13, of which waited for: 7 -> 7; matrix products, arithmetic and copies ran while one was open for 14% -> 17% of each run, Pallas kernels for 0% -> 0%
where the time goes in v10:
time: 231 us; the launch traced here: 229 us
  waiting for transfers between devices  111 us (48%)
  matrix products  36.3 us (16%)
  starting transfers between devices  34.5 us (15%)
  local copies, waits for them, and re-layouts  25.6 us (11%)
  other arithmetic  21.1 us (9%)
    all_to_all x2, waiting for transfers between devices, gather_a2a(): return lax.all_to_all(spread, axis, 0, 0, tiled=False)  56.9 us
    ppermute x2, waiting for transfers between devices, from_last(): farther = lax.ppermute(far, axis, [(1, 0)])  19.7 us
    ppermute x1, waiting for transfers between devices, scatter_sum(): lax.ppermute(other.astype(jnp.bfloat16), 'sec', [(0, 2), (2, 0), (1, 3),...  14.7 us
    all_to_all x2, starting transfers between devices, gather_a2a(): return lax.all_to_all(spread, axis, 0, 0, tiled=False)  14.5 us
    unnamed x20, local copies, waits for them, and re-layouts  13.6 us
    all_to_all x1, waiting for transfers between devices, on_device(): reduced = jnp.sum(lax.all_to_all(packed, 'pts', 0, 0, tiled=False), axis=0)  11.4 us
    dot_general x1, matrix products, on_device(): term = jnp.dot(hidden, down_weight, preferred_element_type=jnp.float32)  10.7 us
    all_to_all x1, starting transfers between devices, on_device(): reduced = jnp.sum(lax.all_to_all(packed, 'pts', 0, 0, tiled=False), axis=0)  10 us
  transfers between devices with their start and end apart: 13, of which 7 were waited for; matrix products, arithmetic and copies ran while one was open for 17% of the time, Pallas kernels for 0%

profile of v10, /device:TPU:16, one launch (start us, length us, event | category | flops | bytes accessed | tf_op | source)
XLA Modules:
  0.0 229.3 jit_solution(8529290251303421661)
XLA Ops:
  1.0 2.5 %broadcast_in_dim.21 = bf16[32,32,2048]{2,1,0:T(8,128)(2,1)} broadcast(bf16[32,2048]{1,0:T(8,128)(2,1)S(1)} %pad_maximum_fusion), dimensions={1,2} | broadcast | bytes 4325376 | tf_op jit(solution)/shard_map/broadcast_in_dim | solution.py:38
  3.5 8.8 %all-to-all-start = ((bf16[32,32,2048]{2,1,0:T(8,128)(2,1)}), bf16[32,32,2048]{2,1,0:T(8,128)(2,1)}, u32[]{:S(2)}, u32[]{:S(2)}) async-start(bf16[32,32,2048]{2,1,0:T(8,128)(2,1)} %broadcast_in_dim.21), calls=%async_computation | async-start | bytes 8388608 | tf_op jit(solution)/shard_map/all_to_all | solution.py:39
  12.4 3.9 %copy.33 = bf16[1,1024,1024]{1,2,0:T(8,128)(2,1)} copy(bf16[1,1024,1024]{2,1,0:T(8,128)(2,1)} %param.10) | data formatting | bytes 4194304 | tf_op args[0]
  16.3 53.7 %all-to-all-done = bf16[32,32,2048]{2,1,0:T(8,128)(2,1)} async-done(((bf16[32,32,2048]{2,1,0:T(8,128)(2,1)}), bf16[32,32,2048]{2,1,0:T(8,128)(2,1)}, u32[]{:S(2)}, u32[]{:S(2)}) %all-to-all-start) | async-done | bytes 4194336 | tf_op jit(solution)/shard_map/all_to_all | solution.py:39
  70.0 2.0 collective-permute-start.1
  73.3 2.0 convert_reduce_fusion.1
  75.3 2.2 fusion.8
  79.6 19.7 %collective-permute-done.5 = f32[1024]{0:T(1024)S(1)} collective-permute-done((f32[1024]{0:T(1024)S(1)}, f32[1024]{0:T(1024)S(1)}, u32[]{:S(2)}, u32[]{:S(2)}) %collective-permute-start.5) | collective-permute-done | bytes 4128 | tf_op jit(solution)/shard_map/ppermute | solution.py:31
  99.3 2.0 collective-permute-start
  102.6 7.3 %fusion.30 = f32[1024,2048]{1,0:T(8,128)S(1)} fusion(bf16[1024,2048]{1,0:T(8,128)(2,1)} %bitcast.5, f32[1024]{0:T(1024)S(1)} %bitcast.94, f32[1024]{0:T(1024)S(1)} %add_rsqrt_fusion.2, f32[1024]{0:T(1024)S(1)} %broadcast_multiply_fusion.2, bf16[1,1024,1024]{1,2,0:T(8,128)(2,1)} %copy.33), kind=kOutput, calls=%fused_computation.44 | convolution fusion | flops 4300210176 | bytes 14692352 | tf_op jit(solution)/shard_map/dot_general | solution.py:101
  109.9 3.2 %copy-done.2 = f32[1024,2048]{1,0:T(8,128)} copy-done((f32[1024,2048]{1,0:T(8,128)}, f32[1024,2048]{1,0:T(8,128)S(1)}, u32[]{:S(2)}) %copy-start.2) | copy-done | bytes 8388632
  113.1 3.6 %convert_reduce_fusion.2 = (f32[1024]{0:T(1024)S(1)}, bf16[1024,1024]{1,0:T(8,128)(2,1)}) fusion(f32[1024,2048]{1,0:T(8,128)S(1)} %fusion.30, pred[1024]{0:T(1024)(128)(4,1)S(1)} %iota_compare_fusion), kind=kLoop, calls=%fused_computation.39 | loop fusion | flops 8387584 | bytes 6296576 | tf_op jit(solution)/shard_map/reduce_sum | solution.py:112
  116.7 4.0 %copy.49 = bf16[1024,1024]{0,1:T(8,128)(2,1)} copy(bf16[1024,1024]{1,0:T(8,128)(2,1)} %get-tuple-element.16) | data formatting | bytes 4194304 | tf_op jit(solution)/shard_map/reshape | solution.py:108
  120.6 3.6 %fusion.37 = f32[8,128,128]{2,1,0:T(8,128)S(1)} fusion(bf16[1024,8,128]{0,2,1:T(8,128)(2,1)} %bitcast.77, f32[1024,2048]{1,0:T(8,128)} %copy-done.2), kind=kOutput, calls=%fused_computation.49 | convolution fusion | flops 268435456 | bytes 4718592 | tf_op jit(solution)/shard_map/yzl,yzn->zln/dot_general | solution.py:106
  125.3 3.3 %select_select_fusion = bf16[1024,1024]{0,1:T(8,128)(2,1)} fusion(bf16[1024,1024]{0,1:T(8,128)(2,1)} %bitcast.76, bf16[1024,1024]{0,1:T(8,128)(2,1)} %collective-permute-done, bf16[1024,1024]{0,1:T(8,128)(2,1)} %collective-permute-done.1, bf16[1024,1024]{0,1:T(8,128)(2,1)} %collective-permute-done.2, pred[]{:T(512)S(6)} %eq.23, pred[]{:T(512)S(6)} %eq.22, ...), kind=kLoop, calls=%fused_computation.64 | loop fusion | flops 3145728 | bytes 10485763 | tf_op jit(solution)/shard_map/jit(_where)/select_n | solution.py:32
  128.7 10.0 %all-to-all-start.1 = ((f32[32,33,128]{2,1,0:T(8,128)}), f32[32,33,128]{2,1,0:T(8,128)S(1)}, u32[]{:S(2)}, u32[]{:S(2)}) async-start(f32[32,33,128]{2,1,0:T(8,128)} %reshape.138), calls=%async_computation.1 | async-start | bytes 1310720 | tf_op jit(solution)/shard_map/all_to_all | solution.py:125
  138.7 11.4 %all-to-all-done.1 = f32[32,33,128]{2,1,0:T(8,128)S(1)} async-done(((f32[32,33,128]{2,1,0:T(8,128)}), f32[32,33,128]{2,1,0:T(8,128)S(1)}, u32[]{:S(2)}, u32[]{:S(2)}) %all-to-all-start.1) | async-done | bytes 540704 | tf_op jit(solution)/shard_map/all_to_all | solution.py:125
  151.3 2.0 convert_reduce_fusion
  153.4 5.3 %collective-permute-done.7 = bf16[2,33,128]{2,1,0:T(8,128)(2,1)S(1)} collective-permute-done((bf16[2,33,128]{2,1,0:T(8,128)(2,1)S(1)}, bf16[2,33,128]{2,1,0:T(8,128)(2,1)S(1)}, u32[]{:S(2)}, u32[]{:S(2)}) %collective-permute-start.7) | collective-permute-done | bytes 16928 | tf_op jit(solution)/shard_map/ppermute | solution.py:48
  160.0 5.6 %all-to-all-start.2 = ((bf16[32,4,33,128]{3,1,2,0:T(4,128)(2,1)}), bf16[32,4,33,128]{3,1,2,0:T(4,128)(2,1)S(1)}, u32[]{:S(2)}, u32[]{:S(2)}) async-start(bf16[32,4,33,128]{3,1,2,0:T(4,128)(2,1)} %broadcast_in_dim.24), calls=%async_computation.2 | async-start | bytes 2162688 | tf_op jit(solution)/shard_map/all_to_all | solution.py:39
  165.7 2.2 fusion.5
  167.9 6.2 %fusion.24 = bf16[1024,1024]{1,0:T(8,128)(2,1)S(1)} fusion(bf16[1024,1024]{1,0:T(8,128)(2,1)} %param.15, bf16[1024,1024]{0,1:T(8,128)(2,1)} %select_select_fusion, f32[1024]{0:T(1024)S(1)} %select_select_fusion.1, f32[1024]{0:T(1024)S(1)} %add_rsqrt_fusion.1, f32[1024]{0:T(1024)S(1)} %broadcast_multiply_fusion.1), kind=kOutput, calls=%fused_computation.35 | convolution fusion | flops 2157969408 | bytes 6303744 | tf_op jit(solution)/shard_map/dot_general | solution.py:136
  175.4 2.0 copy.58
  177.3 3.2 %all-to-all-done.2 = bf16[32,4,33,128]{3,1,2,0:T(4,128)(2,1)S(1)} async-done(((bf16[32,4,33,128]{3,1,2,0:T(4,128)(2,1)}), bf16[32,4,33,128]{3,1,2,0:T(4,128)(2,1)S(1)}, u32[]{:S(2)}, u32[]{:S(2)}) %all-to-all-start.2) | async-done | bytes 1081376 | tf_op jit(solution)/shard_map/all_to_all | solution.py:39
  180.5 2.4 %fusion.56 = f32[4,1024,8]{1,0,2:T(4,128)S(1)} fusion(bf16[4,1056,128]{2,0,1:T(4,128)(2,1)S(1)} %bitcast.78, bf16[1024,1024]{1,0:T(8,128)(2,1)} %copy-done.5), kind=kOutput, calls=%fused_computation.69 | convolution fusion | flops 8388608 | bytes 3309568 | tf_op jit(solution)/shard_map/rhk,shk->srh/dot_general | solution.py:142
  183.3 3.5 %fusion = bf16[1024,8,128]{0,2,1:T(8,128)(2,1)S(1)} fusion(f32[4,1024,8]{1,0,2:T(4,128)S(1)} %fusion.56, bf16[1024,8,128,1]{2,1,0,3:T(8,128)(2,1)S(1)} %bitcast.83, bf16[4,8,128,128]{3,0,2,1:T(4,128)(2,1)S(1)} %bitcast.85), kind=kOutput, calls=%fused_computation.1 | convolution fusion | flops 1081081856 | bytes 5373952 | tf_op jit(solution)/shard_map/rhk,shkv->srhv/dot_general | solution.py:139
  186.9 2.6 %fusion.70 = (f32[1024]{0:T(1024)S(1)}, f32[1024,1024]{0,1:T(8,128)S(1)}) fusion(bf16[1024,1024]{0,1:T(8,128)(2,1)S(1)} %bitcast.95, bf16[1024,1024]{1,0:T(8,128)(2,1)S(1)} %copy-done, bf16[1024,1024]{0,1:T(8,128)(2,1)S(1)} %copy-done.1), kind=kOutput, calls=%fused_computation.94 | convolution fusion | flops 2150628352 | bytes 10489856 | tf_op jit(solution)/shard_map/dot_general | solution.py:148
  189.5 1.9 copy-done.3
  191.9 10.7 %fusion.28 = f32[1024,1024]{0,1:T(8,128)} fusion(bf16[1024,1024]{1,0:T(8,128)(2,1)} %param.19, bf16[1024,1024]{1,0:T(8,128)(2,1)} %param.18, f32[1024,1024]{0,1:T(8,128)} %copy-done.3, f32[1024]{0:T(1024)S(1)} %copy-done.8, f32[1024]{0:T(1024)S(1)} %add_rsqrt_fusion, f32[1024]{0:T(1024)S(1)} %broadcast_multiply_fusion), kind=kOutput, calls=%fused_computation.43 | convolution fusion | flops 4308598784 | bytes 12595200 | tf_op jit(solution)/shard_map/dot_general | solution.py:155
  204.5 2.8 %collective-permute-done.8 = bf16[1024,2,256]{0,2,1:T(8,128)(2,1)} collective-permute-done((bf16[1024,2,256]{0,2,1:T(8,128)(2,1)S(1)}, bf16[1024,2,256]{0,2,1:T(8,128)(2,1)}, u32[]{:S(2)}, u32[]{:S(2)}) %collective-permute-start.8) | collective-permute-done | bytes 1048608 | tf_op jit(solution)/shard_map/ppermute | solution.py:64
  207.3 2.2 bitcast_add_fusion
  211.7 14.7 %collective-permute-done.9 = bf16[1024,256]{0,1:T(8,128)(2,1)S(1)} collective-permute-done((bf16[1024,256]{0,1:T(8,128)(2,1)S(1)}, bf16[1024,256]{0,1:T(8,128)(2,1)S(1)}, u32[]{:S(2)}, u32[]{:S(2)}) %collective-permute-start.9) | collective-permute-done | bytes 524320 | tf_op jit(solution)/shard_map/ppermute | solution.py:69
  (54 shorter events, 17.8 us)
Async XLA Ops:
  0.0 186.8 %copy-start = (bf16[1024,1024]{1,0:T(8,128)(2,1)S(1)}, bf16[1024,1024]{1,0:T(8,128)(2,1)}, u32[]{:S(2)}) copy-start(bf16[1024,1024]{1,0:T(8,128)(2,1)} %param.16) | copy-start | bytes 6291460
  3.5 66.5 %all-to-all-start = ((bf16[32,32,2048]{2,1,0:T(8,128)(2,1)}), bf16[32,32,2048]{2,1,0:T(8,128)(2,1)}, u32[]{:S(2)}, u32[]{:S(2)}) async-start(bf16[32,32,2048]{2,1,0:T(8,128)(2,1)} %broadcast_in_dim.21), calls=%async_computation | async-start | bytes 8388608 | tf_op jit(solution)/shard_map/all_to_all | solution.py:39
  12.4 59.7 %copy-start.7 = (f32[1,1024]{1,0:T(1,128)S(1)}, f32[1,1024]{1,0:T(1,128)}, u32[]{:S(2)}) copy-start(f32[1,1024]{1,0:T(1,128)} %param.12) | copy-start | bytes 12292
  70.0 31.3 %collective-permute-start.1 = (bf16[1024,1024]{0,1:T(8,128)(2,1)}, bf16[1024,1024]{0,1:T(8,128)(2,1)}, u32[]{:S(2)}, u32[]{:S(2)}) collective-permute-start(bf16[1024,1024]{0,1:T(8,128)(2,1)} %bitcast.74), channel_id=1, source_target_pairs={{96,32},{97,33},{98,34},{99,35},{100,36},{101,37},{102,38},{103,39... | collective-permute-start | bytes 6291464 | tf_op jit(solution)/shard_map/ppermute | solution.py:29
  72.0 6.2 %collective-permute-start.4 = (f32[1024]{0:T(1024)S(1)}, f32[1024]{0:T(1024)S(1)}, u32[]{:S(2)}, u32[]{:S(2)}) collective-permute-start(f32[1024]{0:T(1024)S(1)} %bitcast.91), channel_id=1, source_target_pairs={{96,32},{97,33},{98,34},{99,35},{100,36},{101,37},{102,38},{103,39... | collective-permute-start | bytes 12296 | tf_op jit(solution)/shard_map/ppermute | solution.py:29
  72.7 6.9 %collective-permute-start.3 = (f32[1024]{0:T(1024)S(1)}, f32[1024]{0:T(1024)S(1)}, u32[]{:S(2)}, u32[]{:S(2)}) collective-permute-start(f32[1024]{0:T(1024)S(1)} %bitcast.92), channel_id=1, source_target_pairs={{96,64},{97,65},{98,66},{99,67},{100,68},{101,69},{102,70},{103,71... | collective-permute-start | bytes 12296 | tf_op jit(solution)/shard_map/ppermute | solution.py:30
  78.2 21.1 %collective-permute-start.5 = (f32[1024]{0:T(1024)S(1)}, f32[1024]{0:T(1024)S(1)}, u32[]{:S(2)}, u32[]{:S(2)}) collective-permute-start(f32[1024]{0:T(1024)S(1)} %collective-permute-done.4), channel_id=1, source_target_pairs={{32,0},{33,1},{34,2},{35,3},{36,4},{37,5},{38,6},{39,7},{40,8},{41... | collective-permute-start | bytes 12296 | tf_op jit(solution)/shard_map/ppermute | solution.py:31
  99.3 26.0 %collective-permute-start = (bf16[1024,1024]{0,1:T(8,128)(2,1)}, bf16[1024,1024]{0,1:T(8,128)(2,1)}, u32[]{:S(2)}, u32[]{:S(2)}) collective-permute-start(bf16[1024,1024]{0,1:T(8,128)(2,1)} %bitcast.75), channel_id=1, source_target_pairs={{96,64},{97,65},{98,66},{99,67},{100,68},{101,69},{102,70},{103,71... | collective-permute-start | bytes 6291464 | tf_op jit(solution)/shard_map/ppermute | solution.py:30
  101.3 24.1 %collective-permute-start.2 = (bf16[1024,1024]{0,1:T(8,128)(2,1)}, bf16[1024,1024]{0,1:T(8,128)(2,1)}, u32[]{:S(2)}, u32[]{:S(2)}) collective-permute-start(bf16[1024,1024]{0,1:T(8,128)(2,1)} %collective-permute-done.1), channel_id=1, source_target_pairs={{32,0},{33,1},{34,2},{35,3},{36,4},{37,5},{38,6},{39,7},{40,8},{41... | collective-permute-start | bytes 6291464 | tf_op jit(solution)/shard_map/ppermute | solution.py:31
  109.8 3.2 %copy-start.2 = (f32[1024,2048]{1,0:T(8,128)}, f32[1024,2048]{1,0:T(8,128)S(1)}, u32[]{:S(2)}) copy-start(f32[1024,2048]{1,0:T(8,128)S(1)} %fusion.30) | copy-start | bytes 25165828
  128.7 21.5 %all-to-all-start.1 = ((f32[32,33,128]{2,1,0:T(8,128)}), f32[32,33,128]{2,1,0:T(8,128)S(1)}, u32[]{:S(2)}, u32[]{:S(2)}) async-start(f32[32,33,128]{2,1,0:T(8,128)} %reshape.138), calls=%async_computation.1 | async-start | bytes 1310720 | tf_op jit(solution)/shard_map/all_to_all | solution.py:125
  150.2 3.1 %collective-permute-start.6 = (bf16[33,128]{1,0:T(8,128)(2,1)S(1)}, bf16[33,128]{1,0:T(8,128)(2,1)S(1)}, u32[]{:S(2)}, u32[]{:S(2)}) collective-permute-start(bf16[33,128]{1,0:T(8,128)(2,1)S(1)} %reduce_sum.84), channel_id=1, source_target_pairs={{0,32},{32,0},{64,96},{96,64},{1,33},{33,1},{65,97},{97,65},{2,34}... | collective-permute-start | bytes 25352 | tf_op jit(solution)/shard_map/ppermute | solution.py:45
  153.3 5.4 %collective-permute-start.7 = (bf16[2,33,128]{2,1,0:T(8,128)(2,1)S(1)}, bf16[2,33,128]{2,1,0:T(8,128)(2,1)S(1)}, u32[]{:S(2)}, u32[]{:S(2)}) collective-permute-start(bf16[2,33,128]{2,1,0:T(8,128)(2,1)S(1)} %maximum_select_fusion.1), channel_id=1, source_target_pairs={{0,64},{64,0},{32,96},{96,32},{1,65},{65,1},{33,97},{97,33},{2,66}... | collective-permute-start | bytes 50696 | tf_op jit(solution)/shard_map/ppermute | solution.py:48
  160.0 20.5 %all-to-all-start.2 = ((bf16[32,4,33,128]{3,1,2,0:T(4,128)(2,1)}), bf16[32,4,33,128]{3,1,2,0:T(4,128)(2,1)S(1)}, u32[]{:S(2)}, u32[]{:S(2)}) async-start(bf16[32,4,33,128]{3,1,2,0:T(4,128)(2,1)} %broadcast_in_dim.24), calls=%async_computation.2 | async-start | bytes 2162688 | tf_op jit(solution)/shard_map/all_to_all | solution.py:39
  174.1 1.3 copy-start.5
  180.5 2.8 %copy-start.6 = (bf16[128,8,8,128]{3,2,1,0:T(8,128)(2,1)S(1)}, bf16[128,8,8,128]{3,2,1,0:T(8,128)(2,1)}, u32[]{:S(2)}) copy-start(bf16[128,8,8,128]{3,2,1,0:T(8,128)(2,1)} %copy.58) | copy-start | bytes 6291460
  183.3 3.5 %copy-start.1 = (bf16[1024,1024]{0,1:T(8,128)(2,1)S(1)}, bf16[1024,1024]{0,1:T(8,128)(2,1)}, u32[]{:S(2)}) copy-start(bf16[1024,1024]{0,1:T(8,128)(2,1)} %select_select_fusion) | copy-start | bytes 6291460
  189.5 1.9 copy-start.3
  189.5 2.4 %copy-start.8 = (f32[1024]{0:T(1024)S(1)}, f32[1024]{0:T(1024)}, u32[]{:S(2)}) copy-start(f32[1024]{0:T(1024)} %param.17) | copy-start | bytes 12292
  204.4 2.9 %collective-permute-start.8 = (bf16[1024,2,256]{0,2,1:T(8,128)(2,1)S(1)}, bf16[1024,2,256]{0,2,1:T(8,128)(2,1)}, u32[]{:S(2)}, u32[]{:S(2)}) collective-permute-start(bf16[1024,2,256]{0,2,1:T(8,128)(2,1)S(1)} %fusion.59), channel_id=1, source_target_pairs={{0,32},{32,0},{64,96},{96,64},{1,33},{33,1},{65,97},{97,65},{2,34}... | collective-permute-start | bytes 3145736 | tf_op jit(solution)/shard_map/ppermute | solution.py:64
  209.5 1.3 copy-start.4
  210.9 15.5 %collective-permute-start.9 = (bf16[1024,256]{0,1:T(8,128)(2,1)S(1)}, bf16[1024,256]{0,1:T(8,128)(2,1)S(1)}, u32[]{:S(2)}, u32[]{:S(2)}) collective-permute-start(bf16[1024,256]{0,1:T(8,128)(2,1)S(1)} %fusion.63), channel_id=1, source_target_pairs={{0,64},{64,0},{32,96},{96,32},{1,65},{65,1},{33,97},{97,33},{2,66}... | collective-permute-start | bytes 1572872 | tf_op jit(solution)/shard_map/ppermute | solution.py:69

commit v11 on v8

--- a/solution.py
+++ b/solution.py
@@ -103,12 +103,16 @@
     key_feats = feature_map(projected[:, :width]).astype(jnp.bfloat16)
     key_feats = jnp.where(valid[:, None], key_feats, jnp.zeros_like(key_feats))
     value_rows = projected[:, width:].astype(jnp.bfloat16)
-    local_state = jnp.einsum(
-        "yzl,yzn->zln",
-        key_feats.reshape(rows, heads, HEAD_DIM),
-        value_rows.reshape(rows, heads, HEAD_DIM),
-        preferred_element_type=jnp.float32,
-    ).reshape(width, HEAD_DIM)
+    crossed = lax.dot_general(
+        key_feats, value_rows, (((0,), (0,)), ((), ())), preferred_element_type=jnp.float32
+    )
+    local_state = jnp.concatenate(
+        [
+            crossed[h * HEAD_DIM : (h + 1) * HEAD_DIM, h * HEAD_DIM : (h + 1) * HEAD_DIM]
+            for h in range(heads)
+        ],
+        axis=0,
+    )
     local_total = jnp.sum(key_feats.astype(jnp.float32), axis=0).reshape(heads, HEAD_DIM)
 
     packed_rows = width + heads

time: 208 us -> 212 us (1.019)
  starting transfers between devices: 31.3 us -> 43.1 us
  local copies, waits for them, and re-layouts: 22.1 us -> 14.9 us
  waiting for transfers between devices: 79.9 us -> 84.2 us
  blocking collectives: 21.1 us -> 18.8 us
    ppermute x1, starting transfers between devices: 1.13 us -> 19 us  [gather_sec(): got = lax.ppermute(value, 'sec', [(0, 1), (1, 0), (2, 3), (3, 2)])]
    all_to_all x2, waiting for transfers between devices: 57.5 us -> 51.9 us  [gather_a2a(): return lax.all_to_all(spread, axis, 0, 0, tiled=False)]
    ppermute x2, waiting for transfers between devices: 4.76 us -> 9.35 us  [from_last(): farther = lax.ppermute(far, axis, [(1, 0)])]
    reshape x1 -> x0, local copies, waits for them, and re-layouts: 3.94 us -> none  [on_device(): key_feats.reshape(rows, heads, HEAD_DIM)]
    ppermute x1, starting transfers between devices: 3.74 us -> 0.09 us  [gather_sec(): other = lax.ppermute(pair, 'sec', [(0, 2), (2, 0), (1, 3), (3, 1)])]
    ppermute x1, waiting for transfers between devices: 1.76 us -> 5.26 us  [gather_sec(): other = lax.ppermute(pair, 'sec', [(0, 2), (2, 0), (1, 3), (3, 1)])]
    unnamed x16 -> x23, local copies, waits for them, and re-layouts: 11 us -> 7.92 us
    ppermute x1, starting transfers between devices: 3.94 us -> 1.46 us  [scatter_sum(): lax.ppermute(other.astype(jnp.bfloat16), 'sec', [(0, 2), (2, 0), (1, 3),...]
  transfers between devices with their start and end apart: 12 -> 12, of which waited for: 7 -> 7; matrix products, arithmetic and copies ran while one was open for 14% -> 11% of each run, Pallas kernels for 0% -> 0%
where the time goes in v11:
time: 212 us; the launch traced here: 210 us
  waiting for transfers between devices  84.2 us (40%)
  starting transfers between devices  43.1 us (20%)
  matrix products  31.3 us (15%)
  blocking collectives  18.8 us (9%)
  other arithmetic  16.8 us (8%)
  local copies, waits for them, and re-layouts  14.9 us (7%)
    all_to_all x2, waiting for transfers between devices, gather_a2a(): return lax.all_to_all(spread, axis, 0, 0, tiled=False)  51.9 us
    ppermute x1, starting transfers between devices, gather_sec(): got = lax.ppermute(value, 'sec', [(0, 1), (1, 0), (2, 3), (3, 2)])  19 us
    all_to_all x1, blocking collectives, on_device(): reduced = jnp.sum(lax.all_to_all(packed, 'pts', 0, 0, tiled=False), axis=0)  18.8 us
    all_to_all x2, starting transfers between devices, gather_a2a(): return lax.all_to_all(spread, axis, 0, 0, tiled=False)  14.5 us
    ppermute x1, waiting for transfers between devices, scatter_sum(): lax.ppermute(other.astype(jnp.bfloat16), 'sec', [(0, 2), (2, 0), (1, 3),...  14.1 us
    dot_general x1, matrix products, on_device(): term = jnp.dot(hidden, down_weight, preferred_element_type=jnp.float32)  10.7 us
    ppermute x2, waiting for transfers between devices, from_last(): farther = lax.ppermute(far, axis, [(1, 0)])  9.35 us
    unnamed x23, local copies, waits for them, and re-layouts  7.92 us
  transfers between devices with their start and end apart: 12, of which 7 were waited for; matrix products, arithmetic and copies ran while one was open for 11% of the time, Pallas kernels for 0%

profile of v11, /device:TPU:16, one launch (start us, length us, event | category | flops | bytes accessed | tf_op | source)
XLA Modules:
  0.0 210.3 jit_solution(5014349947765242094)
XLA Ops:
  1.0 2.5 %broadcast_in_dim.20 = bf16[32,32,2048]{2,1,0:T(8,128)(2,1)} broadcast(bf16[32,2048]{1,0:T(8,128)(2,1)S(1)} %pad_maximum_fusion), dimensions={1,2} | broadcast | bytes 4325376 | tf_op jit(solution)/shard_map/broadcast_in_dim | solution.py:38
  3.5 8.8 %all-to-all-start = ((bf16[32,32,2048]{2,1,0:T(8,128)(2,1)}), bf16[32,32,2048]{2,1,0:T(8,128)(2,1)}, u32[]{:S(2)}, u32[]{:S(2)}) async-start(bf16[32,32,2048]{2,1,0:T(8,128)(2,1)} %broadcast_in_dim.20), calls=%async_computation | async-start | bytes 8388608 | tf_op jit(solution)/shard_map/all_to_all | solution.py:39
  12.4 3.9 %copy.29 = bf16[1,1024,1024]{1,2,0:T(8,128)(2,1)} copy(bf16[1,1024,1024]{2,1,0:T(8,128)(2,1)} %param.10) | data formatting | bytes 4194304 | tf_op args[0]
  17.0 2.0 convert_reduce_fusion.1
  19.0 2.2 %fusion.8 = f32[1024]{0:T(1024)S(1)} fusion(f32[1024]{0:T(1024)S(1)} %broadcast_multiply_fusion.2, bf16[1,1024,1024]{1,2,0:T(8,128)(2,1)} %copy.29), kind=kLoop, calls=%fused_computation.19 | loop fusion | flops 4193280 | bytes 2105344 | tf_op jit(solution)/shard_map/reduce_sum | solution.py:12
  21.2 48.9 %all-to-all-done = bf16[32,32,2048]{2,1,0:T(8,128)(2,1)} async-done(((bf16[32,32,2048]{2,1,0:T(8,128)(2,1)}), bf16[32,32,2048]{2,1,0:T(8,128)(2,1)}, u32[]{:S(2)}, u32[]{:S(2)}) %all-to-all-start) | async-done | bytes 4194336 | tf_op jit(solution)/shard_map/all_to_all | solution.py:39
  70.0 2.0 collective-permute-start
  72.0 2.0 collective-permute-start.1
  74.0 7.3 %fusion.30 = f32[1024,2048]{1,0:T(8,128)S(1)} fusion(bf16[1024,2048]{1,0:T(8,128)(2,1)} %bitcast.4, f32[1024]{0:T(1024)S(1)} %bitcast.80, f32[1024]{0:T(1024)S(1)} %add_rsqrt_fusion.2, f32[1024]{0:T(1024)S(1)} %broadcast_multiply_fusion.2, bf16[1,1024,1024]{1,2,0:T(8,128)(2,1)} %copy.29), kind=kOutput, calls=%fused_computation.44 | convolution fusion | flops 4300210176 | bytes 14692352 | tf_op jit(solution)/shard_map/dot_general | solution.py:101
  81.3 2.7 %convert_reduce_fusion.2 = (f32[1024]{0:T(1024)S(1)}, bf16[1024,1024]{1,0:T(8,128)(2,1)S(1)}) fusion(f32[1024,2048]{1,0:T(8,128)S(1)} %fusion.30, pred[1024]{0:T(1024)(128)(4,1)S(1)} %iota_compare_fusion), kind=kLoop, calls=%fused_computation.39 | loop fusion | flops 8387584 | bytes 6296576 | tf_op jit(solution)/shard_map/reduce_sum | solution.py:116
  83.9 2.4 %fusion.26 = f32[1024,1024]{1,0:T(8,128)S(1)} fusion(bf16[1024,1024]{1,0:T(8,128)(2,1)S(1)} %get-tuple-element.14, f32[1024,2048]{1,0:T(8,128)S(1)} %fusion.30), kind=kOutput, calls=%fused_computation.41 | convolution fusion | flops 2147483648 | bytes 8388608 | tf_op jit(solution)/shard_map/dot_general | solution.py:106
  86.6 1.3 collective-permute-start.2
  87.9 18.8 %all_to_all.15 = f32[32,33,128]{2,1,0:T(8,128)S(1)} all-to-all(f32[32,33,128]{2,1,0:T(8,128)S(1)} %reshape.126), channel_id=1, replica_groups=mesh['sec'=4,'pts'=32] {'pts'}, dimensions={0} | all-to-all | bytes 1081344 | tf_op jit(solution)/shard_map/all_to_all | solution.py:128
  106.8 19.0 %collective-permute-start.3 = (bf16[33,128]{1,0:T(8,128)(2,1)S(1)}, bf16[33,128]{1,0:T(8,128)(2,1)S(1)}, u32[]{:S(2)}, u32[]{:S(2)}) collective-permute-start(bf16[33,128]{1,0:T(8,128)(2,1)S(1)} %reduce_sum.84), channel_id=1, source_target_pairs={{0,32},{32,0},{64,96},{96,64},{1,33},{33,1},{65,97},{97,65},{2,34}... | collective-permute-start | bytes 25352 | tf_op jit(solution)/shard_map/ppermute | solution.py:45
  126.7 5.3 %collective-permute-done.4 = bf16[2,33,128]{2,1,0:T(8,128)(2,1)S(1)} collective-permute-done((bf16[2,33,128]{2,1,0:T(8,128)(2,1)S(1)}, bf16[2,33,128]{2,1,0:T(8,128)(2,1)S(1)}, u32[]{:S(2)}, u32[]{:S(2)}) %collective-permute-start.4) | collective-permute-done | bytes 16928 | tf_op jit(solution)/shard_map/ppermute | solution.py:48
  133.3 5.6 %all-to-all-start.2 = ((bf16[32,4,33,128]{3,1,2,0:T(4,128)(2,1)}), bf16[32,4,33,128]{3,1,2,0:T(4,128)(2,1)S(1)}, u32[]{:S(2)}, u32[]{:S(2)}) async-start(bf16[32,4,33,128]{3,1,2,0:T(4,128)(2,1)} %broadcast_in_dim.24), calls=%async_computation.2 | async-start | bytes 2162688 | tf_op jit(solution)/shard_map/all_to_all | solution.py:39
  140.3 1.5 collective-permute-start.7
  141.8 9.4 %collective-permute-done.7 = f32[1024]{0:T(1024)S(1)} collective-permute-done((f32[1024]{0:T(1024)S(1)}, f32[1024]{0:T(1024)S(1)}, u32[]{:S(2)}, u32[]{:S(2)}) %collective-permute-start.7) | collective-permute-done | bytes 4128 | tf_op jit(solution)/shard_map/ppermute | solution.py:31
  151.1 3.0 %all-to-all-done.2 = bf16[32,4,33,128]{3,1,2,0:T(4,128)(2,1)S(1)} async-done(((bf16[32,4,33,128]{3,1,2,0:T(4,128)(2,1)}), bf16[32,4,33,128]{3,1,2,0:T(4,128)(2,1)S(1)}, u32[]{:S(2)}, u32[]{:S(2)}) %all-to-all-start.2) | async-done | bytes 1081376 | tf_op jit(solution)/shard_map/all_to_all | solution.py:39
  154.5 3.8 %convert_reduce_fusion = (f32[1024]{0:T(1024)S(1)}, bf16[1024,1024]{0,1:T(8,128)(2,1)S(1)}) fusion(bf16[1024,1024]{0,1:T(8,128)(2,1)} %bitcast.68, bf16[1024,1024]{0,1:T(8,128)(2,1)} %collective-permute-done, bf16[1024,1024]{0,1:T(8,128)(2,1)} %collective-permute-done.1, bf16[1024,1024]{0,1:T(8,128)(2,1)} %collective-permute-done.2, pred[]{:T(512)S(6)} %eq.23, ...), kind=kLoop, calls=%fused_computation.9 | loop fusion | flops 5241856 | bytes 10489859 | tf_op jit(solution)/shard_map/reduce_sum | solution.py:10
  159.0 4.1 %fusion.24 = bf16[1024,1024]{1,0:T(8,128)(2,1)S(1)} fusion(bf16[1024,1024]{1,0:T(8,128)(2,1)S(1)} %copy-done.4, bf16[1024,1024]{0,1:T(8,128)(2,1)S(1)} %get-tuple-element.12, f32[1024]{0:T(1024)S(1)} %select_select_fusion.1, f32[1024]{0:T(1024)S(1)} %add_rsqrt_fusion.1, f32[1024]{0:T(1024)S(1)} %broadcast_multiply_fusion.1), kind=kOutput, calls=%fused_computation.35 | convolution fusion | flops 2157969408 | bytes 6303744 | tf_op jit(solution)/shard_map/dot_general | solution.py:139
  164.3 3.5 %fusion = bf16[1024,8,128]{0,2,1:T(8,128)(2,1)S(1)} fusion(f32[4,1024,8]{1,0,2:T(4,128)S(1)} %fusion.53, bf16[1024,8,128,1]{2,1,0,3:T(8,128)(2,1)S(1)} %bitcast.74, bf16[4,8,128,128]{3,0,2,1:T(4,128)(2,1)S(1)} %bitcast.75), kind=kOutput, calls=%fused_computation.1 | convolution fusion | flops 1081081856 | bytes 5373952 | tf_op jit(solution)/shard_map/rhk,shkv->srhv/dot_general | solution.py:142
  167.9 2.6 %fusion.67 = (f32[1024]{0:T(1024)S(1)}, f32[1024,1024]{0,1:T(8,128)S(1)}) fusion(bf16[1024,1024]{0,1:T(8,128)(2,1)S(1)} %bitcast.84, bf16[1024,1024]{1,0:T(8,128)(2,1)S(1)} %copy-done, bf16[1024,1024]{0,1:T(8,128)(2,1)S(1)} %get-tuple-element.12), kind=kOutput, calls=%fused_computation.100 | convolution fusion | flops 2150628352 | bytes 10489856 | tf_op jit(solution)/shard_map/dot_general | solution.py:151
  170.5 1.9 copy-done.1
  172.9 10.7 %fusion.28 = f32[1024,1024]{0,1:T(8,128)} fusion(bf16[1024,1024]{1,0:T(8,128)(2,1)} %param.19, bf16[1024,1024]{1,0:T(8,128)(2,1)} %param.18, f32[1024,1024]{0,1:T(8,128)} %copy-done.1, f32[1024]{0:T(1024)S(1)} %copy-done.5, f32[1024]{0:T(1024)S(1)} %add_rsqrt_fusion, f32[1024]{0:T(1024)S(1)} %broadcast_multiply_fusion), kind=kOutput, calls=%fused_computation.43 | convolution fusion | flops 4308598784 | bytes 12595200 | tf_op jit(solution)/shard_map/dot_general | solution.py:158
  183.6 1.7 fusion.56
  185.5 2.8 %collective-permute-done.8 = bf16[1024,2,256]{0,2,1:T(8,128)(2,1)} collective-permute-done((bf16[1024,2,256]{0,2,1:T(8,128)(2,1)S(1)}, bf16[1024,2,256]{0,2,1:T(8,128)(2,1)}, u32[]{:S(2)}, u32[]{:S(2)}) %collective-permute-start.8) | collective-permute-done | bytes 1048608 | tf_op jit(solution)/shard_map/ppermute | solution.py:64
  188.3 2.2 %bitcast_add_fusion = f32[1024,2,256]{0,2,1:T(8,128)S(1)} fusion(bf16[1024,2,256]{0,2,1:T(8,128)(2,1)} %collective-permute-done.8, f32[1024,2,2,256]{0,3,2,1:T(8,128)} %bitcast.72, s32[]{:T(128)S(6)} %select_n.138), kind=kLoop, calls=%fused_computation.50 | loop fusion | flops 1048576 | bytes 5242884 | tf_op jit(solution)/shard_map/add | solution.py:65
  190.5 1.3 copy-done.2
  191.9 1.5 collective-permute-start.9
  193.4 14.1 %collective-permute-done.9 = bf16[1024,256]{0,1:T(8,128)(2,1)S(1)} collective-permute-done((bf16[1024,256]{0,1:T(8,128)(2,1)S(1)}, bf16[1024,256]{0,1:T(8,128)(2,1)S(1)}, u32[]{:S(2)}, u32[]{:S(2)}) %collective-permute-start.9) | collective-permute-done | bytes 524320 | tf_op jit(solution)/shard_map/ppermute | solution.py:69
  207.5 1.8 fusion.58
  (52 shorter events, 8.8 us)
Async XLA Ops:
  0.0 167.8 %copy-start = (bf16[1024,1024]{1,0:T(8,128)(2,1)S(1)}, bf16[1024,1024]{1,0:T(8,128)(2,1)}, u32[]{:S(2)}) copy-start(bf16[1024,1024]{1,0:T(8,128)(2,1)} %param.16) | copy-start | bytes 6291460
  3.5 66.5 %all-to-all-start = ((bf16[32,32,2048]{2,1,0:T(8,128)(2,1)}), bf16[32,32,2048]{2,1,0:T(8,128)(2,1)}, u32[]{:S(2)}, u32[]{:S(2)}) async-start(bf16[32,32,2048]{2,1,0:T(8,128)(2,1)} %broadcast_in_dim.20), calls=%async_computation | async-start | bytes 8388608 | tf_op jit(solution)/shard_map/all_to_all | solution.py:39
  12.4 61.6 %copy-start.3 = (f32[1,1024]{1,0:T(1,128)S(1)}, f32[1,1024]{1,0:T(1,128)}, u32[]{:S(2)}) copy-start(f32[1,1024]{1,0:T(1,128)} %param.12) | copy-start | bytes 12292
  70.0 84.5 %collective-permute-start = (bf16[1024,1024]{0,1:T(8,128)(2,1)}, bf16[1024,1024]{0,1:T(8,128)(2,1)}, u32[]{:S(2)}, u32[]{:S(2)}) collective-permute-start(bf16[1024,1024]{0,1:T(8,128)(2,1)} %bitcast.66), channel_id=1, source_target_pairs={{96,64},{97,65},{98,66},{99,67},{100,68},{101,69},{102,70},{103,71... | collective-permute-start | bytes 6291464 | tf_op jit(solution)/shard_map/ppermute | solution.py:30
  72.0 14.5 %collective-permute-start.1 = (bf16[1024,1024]{0,1:T(8,128)(2,1)}, bf16[1024,1024]{0,1:T(8,128)(2,1)}, u32[]{:S(2)}, u32[]{:S(2)}) collective-permute-start(bf16[1024,1024]{0,1:T(8,128)(2,1)} %bitcast.67), channel_id=1, source_target_pairs={{96,32},{97,33},{98,34},{99,35},{100,36},{101,37},{102,38},{103,39... | collective-permute-start | bytes 6291464 | tf_op jit(solution)/shard_map/ppermute | solution.py:29
  86.6 68.0 %collective-permute-start.2 = (bf16[1024,1024]{0,1:T(8,128)(2,1)}, bf16[1024,1024]{0,1:T(8,128)(2,1)}, u32[]{:S(2)}, u32[]{:S(2)}) collective-permute-start(bf16[1024,1024]{0,1:T(8,128)(2,1)} %collective-permute-done.1), channel_id=1, source_target_pairs={{32,0},{33,1},{34,2},{35,3},{36,4},{37,5},{38,6},{39,7},{40,8},{41... | collective-permute-start | bytes 6291464 | tf_op jit(solution)/shard_map/ppermute | solution.py:31
  106.8 19.8 %collective-permute-start.3 = (bf16[33,128]{1,0:T(8,128)(2,1)S(1)}, bf16[33,128]{1,0:T(8,128)(2,1)S(1)}, u32[]{:S(2)}, u32[]{:S(2)}) collective-permute-start(bf16[33,128]{1,0:T(8,128)(2,1)S(1)} %reduce_sum.84), channel_id=1, source_target_pairs={{0,32},{32,0},{64,96},{96,64},{1,33},{33,1},{65,97},{97,65},{2,34}... | collective-permute-start | bytes 25352 | tf_op jit(solution)/shard_map/ppermute | solution.py:45
  126.6 5.4 %collective-permute-start.4 = (bf16[2,33,128]{2,1,0:T(8,128)(2,1)S(1)}, bf16[2,33,128]{2,1,0:T(8,128)(2,1)S(1)}, u32[]{:S(2)}, u32[]{:S(2)}) collective-permute-start(bf16[2,33,128]{2,1,0:T(8,128)(2,1)S(1)} %maximum_select_fusion.1), channel_id=1, source_target_pairs={{0,64},{64,0},{32,96},{96,32},{1,65},{65,1},{33,97},{97,33},{2,66}... | collective-permute-start | bytes 50696 | tf_op jit(solution)/shard_map/ppermute | solution.py:48
  133.3 20.8 %all-to-all-start.2 = ((bf16[32,4,33,128]{3,1,2,0:T(4,128)(2,1)}), bf16[32,4,33,128]{3,1,2,0:T(4,128)(2,1)S(1)}, u32[]{:S(2)}, u32[]{:S(2)}) async-start(bf16[32,4,33,128]{3,1,2,0:T(4,128)(2,1)} %broadcast_in_dim.24), calls=%async_computation.2 | async-start | bytes 2162688 | tf_op jit(solution)/shard_map/all_to_all | solution.py:39
  138.9 1.3 collective-permute-start.6
  139.6 2.2 %collective-permute-start.5 = (f32[1024]{0:T(1024)S(1)}, f32[1024]{0:T(1024)S(1)}, u32[]{:S(2)}, u32[]{:S(2)}) collective-permute-start(f32[1024]{0:T(1024)S(1)} %bitcast.82), channel_id=1, source_target_pairs={{96,64},{97,65},{98,66},{99,67},{100,68},{101,69},{102,70},{103,71... | collective-permute-start | bytes 12296 | tf_op jit(solution)/shard_map/ppermute | solution.py:30
  140.3 10.9 %collective-permute-start.7 = (f32[1024]{0:T(1024)S(1)}, f32[1024]{0:T(1024)S(1)}, u32[]{:S(2)}, u32[]{:S(2)}) collective-permute-start(f32[1024]{0:T(1024)S(1)} %collective-permute-done.6), channel_id=1, source_target_pairs={{32,0},{33,1},{34,2},{35,3},{36,4},{37,5},{38,6},{39,7},{40,8},{41... | collective-permute-start | bytes 12296 | tf_op jit(solution)/shard_map/ppermute | solution.py:31
  154.5 4.4 %copy-start.4 = (bf16[1024,1024]{1,0:T(8,128)(2,1)S(1)}, bf16[1024,1024]{1,0:T(8,128)(2,1)}, u32[]{:S(2)}) copy-start(bf16[1024,1024]{1,0:T(8,128)(2,1)} %param.15) | copy-start | bytes 6291460
  170.5 1.9 copy-start.1
  170.5 2.4 %copy-start.5 = (f32[1024]{0:T(1024)S(1)}, f32[1024]{0:T(1024)}, u32[]{:S(2)}) copy-start(f32[1024]{0:T(1024)} %param.17) | copy-start | bytes 12292
  185.4 2.9 %collective-permute-start.8 = (bf16[1024,2,256]{0,2,1:T(8,128)(2,1)S(1)}, bf16[1024,2,256]{0,2,1:T(8,128)(2,1)}, u32[]{:S(2)}, u32[]{:S(2)}) collective-permute-start(bf16[1024,2,256]{0,2,1:T(8,128)(2,1)S(1)} %fusion.56), channel_id=1, source_target_pairs={{0,32},{32,0},{64,96},{96,64},{1,33},{33,1},{65,97},{97,65},{2,34}... | collective-permute-start | bytes 3145736 | tf_op jit(solution)/shard_map/ppermute | solution.py:64
  190.5 1.3 copy-start.2
  191.9 15.5 %collective-permute-start.9 = (bf16[1024,256]{0,1:T(8,128)(2,1)S(1)}, bf16[1024,256]{0,1:T(8,128)(2,1)S(1)}, u32[]{:S(2)}, u32[]{:S(2)}) collective-permute-start(bf16[1024,256]{0,1:T(8,128)(2,1)S(1)} %fusion.60), channel_id=1, source_target_pairs={{0,64},{64,0},{32,96},{96,32},{1,65},{65,1},{33,97},{97,33},{2,66}... | collective-permute-start | bytes 1572872 | tf_op jit(solution)/shard_map/ppermute | solution.py:69

commit v12 on v11

--- a/solution.py
+++ b/solution.py
@@ -126,7 +126,7 @@
         axis=0,
     ).reshape(blocks, piece, HEAD_DIM)
     reduced = jnp.sum(lax.all_to_all(packed, "pts", 0, 0, tiled=False), axis=0)
-    by_section = gather_sec(reduced.astype(jnp.bfloat16), me, sections)
+    by_section = gather_a2a(reduced.astype(jnp.bfloat16), "sec", sections)
     whole = gather_a2a(by_section, "pts", blocks).astype(jnp.float32)
     whole = whole.transpose(1, 0, 2, 3).reshape(sections, blocks * piece, HEAD_DIM)
     state_heads = whole[:, :width].reshape(sections, heads, HEAD_DIM, HEAD_DIM)

time: 212 us -> 213 us (level)
  blocking collectives: 18.8 us -> 44.3 us
  starting transfers between devices: 43.1 us -> 24.7 us
  waiting for transfers between devices: 84.2 us -> 78 us
    all_to_all x0 -> x1, blocking collectives: none -> 25.5 us  [gather_a2a(): return lax.all_to_all(spread, axis, 0, 0, tiled=False)]
    ppermute x2 -> x0, starting transfers between devices: 19.1 us -> none  [the longest x1 19 us: gather_sec(): got = lax.ppermute(value, 'sec', [(0, 1), (1, 0), (2, 3), (3, 2)])]
    ppermute x2 -> x0, waiting for transfers between devices: 6.09 us -> none  [the longest x1 5.26 us: gather_sec(): other = lax.ppermute(pair, 'sec', [(0, 2), (2, 0), (1, 3), (3, 1)])]
  transfers between devices with their start and end apart: 12 -> 10, of which waited for: 7 -> 5; matrix products, arithmetic and copies ran while one was open for 11% -> 11% of each run, Pallas kernels for 0% -> 0%
where the time goes in v12:
time: 213 us; the launch traced here: 211 us
  waiting for transfers between devices  78 us (37%)
  blocking collectives  44.3 us (21%)
  matrix products  31.3 us (15%)
  starting transfers between devices  24.7 us (12%)
  other arithmetic  16.8 us (8%)
  local copies, waits for them, and re-layouts  14.9 us (7%)
    all_to_all x2, waiting for transfers between devices, gather_a2a(): return lax.all_to_all(spread, axis, 0, 0, tiled=False)  50.5 us
    all_to_all x1, blocking collectives, gather_a2a(): return lax.all_to_all(spread, axis, 0, 0, tiled=False)  25.5 us
    all_to_all x1, blocking collectives, on_device(): reduced = jnp.sum(lax.all_to_all(packed, 'pts', 0, 0, tiled=False), axis=0)  18.8 us
    all_to_all x2, starting transfers between devices, gather_a2a(): return lax.all_to_all(spread, axis, 0, 0, tiled=False)  14.5 us
    ppermute x1, waiting for transfers between devices, scatter_sum(): lax.ppermute(other.astype(jnp.bfloat16), 'sec', [(0, 2), (2, 0), (1, 3),...  13.5 us
    ppermute x2, waiting for transfers between devices, from_last(): farther = lax.ppermute(far, axis, [(1, 0)])  11.2 us
    dot_general x1, matrix products, on_device(): term = jnp.dot(hidden, down_weight, preferred_element_type=jnp.float32)  10.7 us
    unnamed x23, local copies, waits for them, and re-layouts  7.92 us
  transfers between devices with their start and end apart: 10, of which 5 were waited for; matrix products, arithmetic and copies ran while one was open for 11% of the time, Pallas kernels for 0%

profile of v12, /device:TPU:16, one launch (start us, length us, event | category | flops | bytes accessed | tf_op | source)
XLA Modules:
  0.0 211.1 jit_solution(7309813213929212552)
XLA Ops:
  1.0 2.5 %broadcast_in_dim.22 = bf16[32,32,2048]{2,1,0:T(8,128)(2,1)} broadcast(bf16[32,2048]{1,0:T(8,128)(2,1)S(1)} %pad_maximum_fusion), dimensions={1,2} | broadcast | bytes 4325376 | tf_op jit(solution)/shard_map/broadcast_in_dim | solution.py:38
  3.5 8.8 %all-to-all-start = ((bf16[32,32,2048]{2,1,0:T(8,128)(2,1)}), bf16[32,32,2048]{2,1,0:T(8,128)(2,1)}, u32[]{:S(2)}, u32[]{:S(2)}) async-start(bf16[32,32,2048]{2,1,0:T(8,128)(2,1)} %broadcast_in_dim.22), calls=%async_computation | async-start | bytes 8388608 | tf_op jit(solution)/shard_map/all_to_all | solution.py:39
  12.4 3.9 %copy.28 = bf16[1,1024,1024]{1,2,0:T(8,128)(2,1)} copy(bf16[1,1024,1024]{2,1,0:T(8,128)(2,1)} %param.10) | data formatting | bytes 4194304 | tf_op args[0]
  17.0 2.0 convert_reduce_fusion.1
  19.0 2.2 %fusion.8 = f32[1024]{0:T(1024)S(1)} fusion(f32[1024]{0:T(1024)S(1)} %broadcast_multiply_fusion.2, bf16[1,1024,1024]{1,2,0:T(8,128)(2,1)} %copy.28), kind=kLoop, calls=%fused_computation.19 | loop fusion | flops 4193280 | bytes 2105344 | tf_op jit(solution)/shard_map/reduce_sum | solution.py:12
  21.2 48.9 %all-to-all-done = bf16[32,32,2048]{2,1,0:T(8,128)(2,1)} async-done(((bf16[32,32,2048]{2,1,0:T(8,128)(2,1)}), bf16[32,32,2048]{2,1,0:T(8,128)(2,1)}, u32[]{:S(2)}, u32[]{:S(2)}) %all-to-all-start) | async-done | bytes 4194336 | tf_op jit(solution)/shard_map/all_to_all | solution.py:39
  70.0 2.0 collective-permute-start
  72.0 2.0 collective-permute-start.1
  74.0 7.3 %fusion.30 = f32[1024,2048]{1,0:T(8,128)S(1)} fusion(bf16[1024,2048]{1,0:T(8,128)(2,1)} %bitcast.4, f32[1024]{0:T(1024)S(1)} %bitcast.76, f32[1024]{0:T(1024)S(1)} %add_rsqrt_fusion.2, f32[1024]{0:T(1024)S(1)} %broadcast_multiply_fusion.2, bf16[1,1024,1024]{1,2,0:T(8,128)(2,1)} %copy.28), kind=kOutput, calls=%fused_computation.44 | convolution fusion | flops 4300210176 | bytes 14692352 | tf_op jit(solution)/shard_map/dot_general | solution.py:101
  81.3 2.7 %convert_reduce_fusion.2 = (f32[1024]{0:T(1024)S(1)}, bf16[1024,1024]{1,0:T(8,128)(2,1)S(1)}) fusion(f32[1024,2048]{1,0:T(8,128)S(1)} %fusion.30, pred[1024]{0:T(1024)(128)(4,1)S(1)} %iota_compare_fusion), kind=kLoop, calls=%fused_computation.39 | loop fusion | flops 8387584 | bytes 6296576 | tf_op jit(solution)/shard_map/reduce_sum | solution.py:116
  83.9 2.4 %fusion.26 = f32[1024,1024]{1,0:T(8,128)S(1)} fusion(bf16[1024,1024]{1,0:T(8,128)(2,1)S(1)} %get-tuple-element.14, f32[1024,2048]{1,0:T(8,128)S(1)} %fusion.30), kind=kOutput, calls=%fused_computation.41 | convolution fusion | flops 2147483648 | bytes 8388608 | tf_op jit(solution)/shard_map/dot_general | solution.py:106
  86.5 1.3 collective-permute-start.2
  87.9 18.8 %all_to_all.20 = f32[32,33,128]{2,1,0:T(8,128)S(1)} all-to-all(f32[32,33,128]{2,1,0:T(8,128)S(1)} %reshape.75), channel_id=1, replica_groups=mesh['sec'=4,'pts'=32] {'pts'}, dimensions={0} | all-to-all | bytes 1081344 | tf_op jit(solution)/shard_map/all_to_all | solution.py:128
  106.8 25.5 %all_to_all.21 = bf16[4,33,128]{2,1,0:T(8,128)(2,1)S(1)} all-to-all(bf16[4,33,128]{2,1,0:T(8,128)(2,1)S(1)} %broadcast_in_dim.26), channel_id=1, replica_groups=mesh['sec'=4,'pts'=32] {'sec'}, dimensions={0} | all-to-all | bytes 67584 | tf_op jit(solution)/shard_map/all_to_all | solution.py:39
  132.3 1.3 broadcast_in_dim.27
  133.6 5.6 %all-to-all-start.3 = ((bf16[32,4,33,128]{3,1,2,0:T(4,128)(2,1)}), bf16[32,4,33,128]{3,1,2,0:T(4,128)(2,1)S(1)}, u32[]{:S(2)}, u32[]{:S(2)}) async-start(bf16[32,4,33,128]{3,1,2,0:T(4,128)(2,1)} %broadcast_in_dim.27), calls=%async_computation.3 | async-start | bytes 2162688 | tf_op jit(solution)/shard_map/all_to_all | solution.py:39
  140.6 1.5 collective-permute-start.5
  142.1 11.2 %collective-permute-done.5 = f32[1024]{0:T(1024)S(1)} collective-permute-done((f32[1024]{0:T(1024)S(1)}, f32[1024]{0:T(1024)S(1)}, u32[]{:S(2)}, u32[]{:S(2)}) %collective-permute-start.5) | collective-permute-done | bytes 4128 | tf_op jit(solution)/shard_map/ppermute | solution.py:31
  153.3 1.6 all-to-all-done.3
  155.4 3.8 %convert_reduce_fusion = (f32[1024]{0:T(1024)S(1)}, bf16[1024,1024]{0,1:T(8,128)(2,1)S(1)}) fusion(bf16[1024,1024]{0,1:T(8,128)(2,1)} %bitcast.66, bf16[1024,1024]{0,1:T(8,128)(2,1)} %collective-permute-done, bf16[1024,1024]{0,1:T(8,128)(2,1)} %collective-permute-done.1, bf16[1024,1024]{0,1:T(8,128)(2,1)} %collective-permute-done.2, pred[]{:T(512)S(6)} %eq.16, ...), kind=kLoop, calls=%fused_computation.9 | loop fusion | flops 5241856 | bytes 10489859 | tf_op jit(solution)/shard_map/reduce_sum | solution.py:10
  159.8 4.1 %fusion.24 = bf16[1024,1024]{1,0:T(8,128)(2,1)S(1)} fusion(bf16[1024,1024]{1,0:T(8,128)(2,1)S(1)} %copy-done.4, bf16[1024,1024]{0,1:T(8,128)(2,1)S(1)} %get-tuple-element.12, f32[1024]{0:T(1024)S(1)} %select_select_fusion.1, f32[1024]{0:T(1024)S(1)} %add_rsqrt_fusion.1, f32[1024]{0:T(1024)S(1)} %broadcast_multiply_fusion.1), kind=kOutput, calls=%fused_computation.35 | convolution fusion | flops 2157969408 | bytes 6303744 | tf_op jit(solution)/shard_map/dot_general | solution.py:139
  165.1 3.5 %fusion = bf16[1024,8,128]{0,2,1:T(8,128)(2,1)S(1)} fusion(f32[4,1024,8]{1,0,2:T(4,128)S(1)} %fusion.53, bf16[1024,8,128,1]{2,1,0,3:T(8,128)(2,1)S(1)} %bitcast.72, bf16[4,8,128,128]{3,0,2,1:T(4,128)(2,1)S(1)} %bitcast.73), kind=kOutput, calls=%fused_computation.1 | convolution fusion | flops 1081081856 | bytes 5373952 | tf_op jit(solution)/shard_map/rhk,shkv->srhv/dot_general | solution.py:142
  168.7 2.6 %fusion.67 = (f32[1024]{0:T(1024)S(1)}, f32[1024,1024]{0,1:T(8,128)S(1)}) fusion(bf16[1024,1024]{0,1:T(8,128)(2,1)S(1)} %bitcast.80, bf16[1024,1024]{1,0:T(8,128)(2,1)S(1)} %copy-done, bf16[1024,1024]{0,1:T(8,128)(2,1)S(1)} %get-tuple-element.12), kind=kOutput, calls=%fused_computation.98 | convolution fusion | flops 2150628352 | bytes 10489856 | tf_op jit(solution)/shard_map/dot_general | solution.py:151
  171.4 1.9 copy-done.1
  173.7 10.7 %fusion.28 = f32[1024,1024]{0,1:T(8,128)} fusion(bf16[1024,1024]{1,0:T(8,128)(2,1)} %param.19, bf16[1024,1024]{1,0:T(8,128)(2,1)} %param.18, f32[1024,1024]{0,1:T(8,128)} %copy-done.1, f32[1024]{0:T(1024)S(1)} %copy-done.5, f32[1024]{0:T(1024)S(1)} %add_rsqrt_fusion, f32[1024]{0:T(1024)S(1)} %broadcast_multiply_fusion), kind=kOutput, calls=%fused_computation.43 | convolution fusion | flops 4308598784 | bytes 12595200 | tf_op jit(solution)/shard_map/dot_general | solution.py:158
  184.5 1.7 fusion.56
  186.3 2.7 %collective-permute-done.6 = bf16[1024,2,256]{0,2,1:T(8,128)(2,1)} collective-permute-done((bf16[1024,2,256]{0,2,1:T(8,128)(2,1)S(1)}, bf16[1024,2,256]{0,2,1:T(8,128)(2,1)}, u32[]{:S(2)}, u32[]{:S(2)}) %collective-permute-start.6) | collective-permute-done | bytes 1048608 | tf_op jit(solution)/shard_map/ppermute | solution.py:64
  189.1 2.2 %bitcast_add_fusion = f32[1024,2,256]{0,2,1:T(8,128)S(1)} fusion(bf16[1024,2,256]{0,2,1:T(8,128)(2,1)} %collective-permute-done.6, f32[1024,2,2,256]{0,3,2,1:T(8,128)} %bitcast.70, s32[]{:T(128)S(6)} %select_n.107), kind=kLoop, calls=%fused_computation.50 | loop fusion | flops 1048576 | bytes 5242884 | tf_op jit(solution)/shard_map/add | solution.py:65
  191.3 1.3 copy-done.2
  192.7 2.1 collective-permute-start.7
  194.8 13.5 %collective-permute-done.7 = bf16[1024,256]{0,1:T(8,128)(2,1)S(1)} collective-permute-done((bf16[1024,256]{0,1:T(8,128)(2,1)S(1)}, bf16[1024,256]{0,1:T(8,128)(2,1)S(1)}, u32[]{:S(2)}, u32[]{:S(2)}) %collective-permute-start.7) | collective-permute-done | bytes 524320 | tf_op jit(solution)/shard_map/ppermute | solution.py:69
  208.3 1.8 fusion.58
  (48 shorter events, 6.5 us)
Async XLA Ops:
  0.0 168.7 %copy-start = (bf16[1024,1024]{1,0:T(8,128)(2,1)S(1)}, bf16[1024,1024]{1,0:T(8,128)(2,1)}, u32[]{:S(2)}) copy-start(bf16[1024,1024]{1,0:T(8,128)(2,1)} %param.16) | copy-start | bytes 6291460
  3.5 66.5 %all-to-all-start = ((bf16[32,32,2048]{2,1,0:T(8,128)(2,1)}), bf16[32,32,2048]{2,1,0:T(8,128)(2,1)}, u32[]{:S(2)}, u32[]{:S(2)}) async-start(bf16[32,32,2048]{2,1,0:T(8,128)(2,1)} %broadcast_in_dim.22), calls=%async_computation | async-start | bytes 8388608 | tf_op jit(solution)/shard_map/all_to_all | solution.py:39
  12.4 61.6 %copy-start.3 = (f32[1,1024]{1,0:T(1,128)S(1)}, f32[1,1024]{1,0:T(1,128)}, u32[]{:S(2)}) copy-start(f32[1,1024]{1,0:T(1,128)} %param.12) | copy-start | bytes 12292
  70.0 85.3 %collective-permute-start = (bf16[1024,1024]{0,1:T(8,128)(2,1)}, bf16[1024,1024]{0,1:T(8,128)(2,1)}, u32[]{:S(2)}, u32[]{:S(2)}) collective-permute-start(bf16[1024,1024]{0,1:T(8,128)(2,1)} %bitcast.64), channel_id=1, source_target_pairs={{96,64},{97,65},{98,66},{99,67},{100,68},{101,69},{102,70},{103,71... | collective-permute-start | bytes 6291464 | tf_op jit(solution)/shard_map/ppermute | solution.py:30
  72.0 14.5 %collective-permute-start.1 = (bf16[1024,1024]{0,1:T(8,128)(2,1)}, bf16[1024,1024]{0,1:T(8,128)(2,1)}, u32[]{:S(2)}, u32[]{:S(2)}) collective-permute-start(bf16[1024,1024]{0,1:T(8,128)(2,1)} %bitcast.65), channel_id=1, source_target_pairs={{96,32},{97,33},{98,34},{99,35},{100,36},{101,37},{102,38},{103,39... | collective-permute-start | bytes 6291464 | tf_op jit(solution)/shard_map/ppermute | solution.py:29
  86.5 68.8 %collective-permute-start.2 = (bf16[1024,1024]{0,1:T(8,128)(2,1)}, bf16[1024,1024]{0,1:T(8,128)(2,1)}, u32[]{:S(2)}, u32[]{:S(2)}) collective-permute-start(bf16[1024,1024]{0,1:T(8,128)(2,1)} %collective-permute-done.1), channel_id=1, source_target_pairs={{32,0},{33,1},{34,2},{35,3},{36,4},{37,5},{38,6},{39,7},{40,8},{41... | collective-permute-start | bytes 6291464 | tf_op jit(solution)/shard_map/ppermute | solution.py:31
  133.6 21.4 %all-to-all-start.3 = ((bf16[32,4,33,128]{3,1,2,0:T(4,128)(2,1)}), bf16[32,4,33,128]{3,1,2,0:T(4,128)(2,1)S(1)}, u32[]{:S(2)}, u32[]{:S(2)}) async-start(bf16[32,4,33,128]{3,1,2,0:T(4,128)(2,1)} %broadcast_in_dim.27), calls=%async_computation.3 | async-start | bytes 2162688 | tf_op jit(solution)/shard_map/all_to_all | solution.py:39
  139.2 1.3 collective-permute-start.4
  139.9 2.2 %collective-permute-start.3 = (f32[1024]{0:T(1024)S(1)}, f32[1024]{0:T(1024)S(1)}, u32[]{:S(2)}, u32[]{:S(2)}) collective-permute-start(f32[1024]{0:T(1024)S(1)} %bitcast.78), channel_id=1, source_target_pairs={{96,64},{97,65},{98,66},{99,67},{100,68},{101,69},{102,70},{103,71... | collective-permute-start | bytes 12296 | tf_op jit(solution)/shard_map/ppermute | solution.py:30
  140.6 12.8 %collective-permute-start.5 = (f32[1024]{0:T(1024)S(1)}, f32[1024]{0:T(1024)S(1)}, u32[]{:S(2)}, u32[]{:S(2)}) collective-permute-start(f32[1024]{0:T(1024)S(1)} %collective-permute-done.4), channel_id=1, source_target_pairs={{32,0},{33,1},{34,2},{35,3},{36,4},{37,5},{38,6},{39,7},{40,8},{41... | collective-permute-start | bytes 12296 | tf_op jit(solution)/shard_map/ppermute | solution.py:31
  155.3 4.4 %copy-start.4 = (bf16[1024,1024]{1,0:T(8,128)(2,1)S(1)}, bf16[1024,1024]{1,0:T(8,128)(2,1)}, u32[]{:S(2)}) copy-start(bf16[1024,1024]{1,0:T(8,128)(2,1)} %param.15) | copy-start | bytes 6291460
  171.3 1.9 copy-start.1
  171.3 2.4 %copy-start.5 = (f32[1024]{0:T(1024)S(1)}, f32[1024]{0:T(1024)}, u32[]{:S(2)}) copy-start(f32[1024]{0:T(1024)} %param.17) | copy-start | bytes 12292
  186.2 2.9 %collective-permute-start.6 = (bf16[1024,2,256]{0,2,1:T(8,128)(2,1)S(1)}, bf16[1024,2,256]{0,2,1:T(8,128)(2,1)}, u32[]{:S(2)}, u32[]{:S(2)}) collective-permute-start(bf16[1024,2,256]{0,2,1:T(8,128)(2,1)S(1)} %fusion.56), channel_id=1, source_target_pairs={{0,32},{32,0},{64,96},{96,64},{1,33},{33,1},{65,97},{97,65},{2,34}... | collective-permute-start | bytes 3145736 | tf_op jit(solution)/shard_map/ppermute | solution.py:64
  191.3 1.3 copy-start.2
  192.7 15.5 %collective-permute-start.7 = (bf16[1024,256]{0,1:T(8,128)(2,1)S(1)}, bf16[1024,256]{0,1:T(8,128)(2,1)S(1)}, u32[]{:S(2)}, u32[]{:S(2)}) collective-permute-start(bf16[1024,256]{0,1:T(8,128)(2,1)S(1)} %fusion.60), channel_id=1, source_target_pairs={{0,64},{64,0},{32,96},{96,32},{1,65},{65,1},{33,97},{97,33},{2,66}... | collective-permute-start | bytes 1572872 | tf_op jit(solution)/shard_map/ppermute | solution.py:69

commit v13 on v11

--- a/solution.py
+++ b/solution.py
@@ -93,9 +93,8 @@
     stacked = jnp.concatenate([key_weight[0], value_weight[0]], axis=1)
     weights = gather_a2a(stacked, "pts", blocks).reshape(width, 2 * width)
 
-    late_block, late_gain, weights = lax.optimization_barrier((block, input_gain[0], weights))
-    query_block = from_last(late_block, "sec", sections)
-    query_gain = from_last(late_gain, "sec", sections)
+    query_block = from_last(block, "sec", sections)
+    query_gain = from_last(input_gain[0], "sec", sections)
 
     normed = layer_normalizer(block.astype(jnp.float32), input_gain[0]).astype(jnp.bfloat16)
     projected = jnp.dot(normed, weights, preferred_element_type=jnp.float32)

time: 212 us -> 200 us (0.943)
  blocking collectives: 18.8 us -> 0 us
  starting transfers between devices: 43.1 us -> 32.9 us
  waiting for transfers between devices: 84.2 us -> 93.1 us
  local copies, waits for them, and re-layouts: 14.9 us -> 18.6 us
  matrix products: 31.3 us -> 34.9 us
    all_to_all x2, waiting for transfers between devices: 51.9 us -> 3.32 us  [gather_a2a(): return lax.all_to_all(spread, axis, 0, 0, tiled=False)]
    ppermute x2, waiting for transfers between devices: 9.35 us -> 57.9 us  [from_last(): farther = lax.ppermute(far, axis, [(1, 0)])]
    ppermute x1, starting transfers between devices: 19 us -> 0.09 us  [gather_sec(): got = lax.ppermute(value, 'sec', [(0, 1), (1, 0), (2, 3), (3, 2)])]
    all_to_all x1 -> x0, blocking collectives: 18.8 us -> none  [on_device(): reduced = jnp.sum(lax.all_to_all(packed, 'pts', 0, 0, tiled=False), axis=0)]
    all_to_all x0 -> x1, waiting for transfers between devices: none -> 8.91 us  [on_device(): reduced = jnp.sum(lax.all_to_all(packed, 'pts', 0, 0, tiled=False), axis=0)]
    all_to_all x0 -> x1, starting transfers between devices: none -> 8.5 us  [on_device(): reduced = jnp.sum(lax.all_to_all(packed, 'pts', 0, 0, tiled=False), axis=0)]
    unnamed x23 -> x31, local copies, waits for them, and re-layouts: 7.92 us -> 10.7 us
    dot_general x1, matrix products: 4.07 us -> 6.21 us  [on_device(): jnp.dot(query_normed, query_weight, preferred_element_type=jnp.float32)]
  transfers between devices with their start and end apart: 12 -> 13, of which waited for: 7 -> 7; matrix products, arithmetic and copies ran while one was open for 11% -> 10% of each run, Pallas kernels for 0% -> 0%
where the time goes in v13:
time: 200 us; the launch traced here: 198 us
  waiting for transfers between devices  93.1 us (47%)
  matrix products  34.9 us (17%)
  starting transfers between devices  32.9 us (16%)
  local copies, waits for them, and re-layouts  18.6 us (9%)
  other arithmetic  17 us (8%)
    ppermute x2, waiting for transfers between devices, from_last(): farther = lax.ppermute(far, axis, [(1, 0)])  57.9 us
    ppermute x1, waiting for transfers between devices, scatter_sum(): lax.ppermute(other.astype(jnp.bfloat16), 'sec', [(0, 2), (2, 0), (1, 3),...  14.7 us
    all_to_all x2, starting transfers between devices, gather_a2a(): return lax.all_to_all(spread, axis, 0, 0, tiled=False)  14.5 us
    dot_general x1, matrix products, on_device(): term = jnp.dot(hidden, down_weight, preferred_element_type=jnp.float32)  10.7 us
    unnamed x31, local copies, waits for them, and re-layouts  10.7 us
    all_to_all x1, waiting for transfers between devices, on_device(): reduced = jnp.sum(lax.all_to_all(packed, 'pts', 0, 0, tiled=False), axis=0)  8.91 us
    all_to_all x1, starting transfers between devices, on_device(): reduced = jnp.sum(lax.all_to_all(packed, 'pts', 0, 0, tiled=False), axis=0)  8.5 us
    reduce_sum x2, other arithmetic, layer_normalizer(): mean = jnp.mean(values, axis=-1, keepdims=True)  7.57 us
  transfers between devices with their start and end apart: 13, of which 7 were waited for; matrix products, arithmetic and copies ran while one was open for 10% of the time, Pallas kernels for 0%

profile of v13, /device:TPU:16, one launch (start us, length us, event | category | flops | bytes accessed | tf_op | source)
XLA Modules:
  0.0 197.7 jit_solution(9978603962513748499)
XLA Ops:
  0.0 4.1 %copy.29 = bf16[1,1024,1024]{1,2,0:T(8,128)(2,1)} copy(bf16[1,1024,1024]{2,1,0:T(8,128)(2,1)} %param.10) | data formatting | bytes 4194304 | tf_op args[0]
  4.1 2.0 %collective-permute-start.1 = (bf16[1024,1024]{0,1:T(8,128)(2,1)}, bf16[1024,1024]{0,1:T(8,128)(2,1)}, u32[]{:S(2)}, u32[]{:S(2)}) collective-permute-start(bf16[1024,1024]{0,1:T(8,128)(2,1)} %bitcast.67), channel_id=1, source_target_pairs={{96,32},{97,33},{98,34},{99,35},{100,36},{101,37},{102,38},{103,39... | collective-permute-start | bytes 6291464 | tf_op jit(solution)/shard_map/ppermute | solution.py:29
  6.2 2.5 %broadcast_in_dim.21 = bf16[32,32,2048]{2,1,0:T(8,128)(2,1)} broadcast(bf16[32,2048]{1,0:T(8,128)(2,1)S(1)} %pad_maximum_fusion), dimensions={1,2} | broadcast | bytes 4325376 | tf_op jit(solution)/shard_map/broadcast_in_dim | solution.py:38
  8.7 8.8 %all-to-all-start = ((bf16[32,32,2048]{2,1,0:T(8,128)(2,1)}), bf16[32,32,2048]{2,1,0:T(8,128)(2,1)}, u32[]{:S(2)}, u32[]{:S(2)}) async-start(bf16[32,32,2048]{2,1,0:T(8,128)(2,1)} %broadcast_in_dim.21), calls=%async_computation | async-start | bytes 8388608 | tf_op jit(solution)/shard_map/all_to_all | solution.py:39
  17.5 2.0 %collective-permute-start = (bf16[1024,1024]{0,1:T(8,128)(2,1)}, bf16[1024,1024]{0,1:T(8,128)(2,1)}, u32[]{:S(2)}, u32[]{:S(2)}) collective-permute-start(bf16[1024,1024]{0,1:T(8,128)(2,1)} %bitcast.68), channel_id=1, source_target_pairs={{96,64},{97,65},{98,66},{99,67},{100,68},{101,69},{102,70},{103,71... | collective-permute-start | bytes 6291464 | tf_op jit(solution)/shard_map/ppermute | solution.py:30
  21.5 2.0 convert_reduce_fusion.1
  23.4 57.9 %collective-permute-done.2 = bf16[1024,1024]{0,1:T(8,128)(2,1)} collective-permute-done((bf16[1024,1024]{0,1:T(8,128)(2,1)}, bf16[1024,1024]{0,1:T(8,128)(2,1)}, u32[]{:S(2)}, u32[]{:S(2)}) %collective-permute-start.2) | collective-permute-done | bytes 2097184 | tf_op jit(solution)/shard_map/ppermute | solution.py:31
  81.3 5.6 %convert_reduce_fusion = (f32[1024]{0:T(1024)S(1)}, bf16[1024,1024]{0,1:T(8,128)(2,1)}, f32[1024]{0:T(1024)S(1)}) fusion(bf16[1024,1024]{0,1:T(8,128)(2,1)} %collective-permute-done, bf16[1024,1024]{0,1:T(8,128)(2,1)} %collective-permute-done.1, bf16[1024,1024]{0,1:T(8,128)(2,1)} %collective-permute-done.2, pred[]{:T(512)S(6)} %eq.23, pred[]{:T(512)S(6)} %eq.22, ...), kind=kLoop, calls=%fused_computation.9 | loop fusion | flops 9435136 | bytes 10498051 | tf_op jit(solution)/shard_map/reduce_sum | solution.py:10
  87.0 7.0 %fusion.23 = f32[1024,2048]{1,0:T(8,128)S(1)} fusion(bf16[1024,2048]{1,0:T(8,128)(2,1)} %bitcast.6, bf16[1,1024,1024]{2,1,0:T(8,128)(2,1)} %param.10, f32[1024]{0:T(1024)S(1)} %bitcast.80, f32[1024]{0:T(1024)S(1)} %add_rsqrt_fusion.2, f32[1024]{0:T(1024)S(1)} %broadcast_multiply_fusion.2), kind=kOutput, calls=%fused_computation.39 | convolution fusion | flops 4300210176 | bytes 14692352 | tf_op jit(solution)/shard_map/dot_general | solution.py:100
  94.0 2.7 %convert_reduce_fusion.2 = (f32[1024]{0:T(1024)S(1)}, bf16[1024,1024]{1,0:T(8,128)(2,1)S(1)}) fusion(f32[1024,2048]{1,0:T(8,128)S(1)} %fusion.23, pred[1024]{0:T(1024)(128)(4,1)S(1)} %iota_compare_fusion), kind=kLoop, calls=%fused_computation.36 | loop fusion | flops 8387584 | bytes 6296576 | tf_op jit(solution)/shard_map/reduce_sum | solution.py:115
  96.7 2.4 %fusion.26 = f32[1024,1024]{1,0:T(8,128)S(1)} fusion(bf16[1024,1024]{1,0:T(8,128)(2,1)S(1)} %get-tuple-element.8, f32[1024,2048]{1,0:T(8,128)S(1)} %fusion.23), kind=kOutput, calls=%fused_computation.41 | convolution fusion | flops 2147483648 | bytes 8388608 | tf_op jit(solution)/shard_map/dot_general | solution.py:105
  100.2 8.5 %all-to-all-start.1 = ((f32[32,33,128]{2,1,0:T(8,128)}), f32[32,33,128]{2,1,0:T(8,128)S(1)}, u32[]{:S(2)}, u32[]{:S(2)}) async-start(f32[32,33,128]{2,1,0:T(8,128)} %reshape.147), calls=%async_computation.1 | async-start | bytes 1310720 | tf_op jit(solution)/shard_map/all_to_all | solution.py:127
  110.1 1.3 collective-permute-start.7
  111.4 8.9 %all-to-all-done.1 = f32[32,33,128]{2,1,0:T(8,128)S(1)} async-done(((f32[32,33,128]{2,1,0:T(8,128)}), f32[32,33,128]{2,1,0:T(8,128)S(1)}, u32[]{:S(2)}, u32[]{:S(2)}) %all-to-all-start.1) | async-done | bytes 540704 | tf_op jit(solution)/shard_map/all_to_all | solution.py:127
  122.6 4.4 %collective-permute-done.4 = bf16[2,33,128]{2,1,0:T(8,128)(2,1)S(1)} collective-permute-done((bf16[2,33,128]{2,1,0:T(8,128)(2,1)S(1)}, bf16[2,33,128]{2,1,0:T(8,128)(2,1)S(1)}, u32[]{:S(2)}, u32[]{:S(2)}) %collective-permute-start.4) | collective-permute-done | bytes 16928 | tf_op jit(solution)/shard_map/ppermute | solution.py:48
  128.3 5.6 %all-to-all-start.2 = ((bf16[32,4,33,128]{3,1,2,0:T(4,128)(2,1)}), bf16[32,4,33,128]{3,1,2,0:T(4,128)(2,1)S(1)}, u32[]{:S(2)}, u32[]{:S(2)}) async-start(bf16[32,4,33,128]{3,1,2,0:T(4,128)(2,1)} %broadcast_in_dim.24), calls=%async_computation.2 | async-start | bytes 2162688 | tf_op jit(solution)/shard_map/all_to_all | solution.py:39
  133.9 2.2 %fusion.3 = f32[1024]{0:T(1024)S(1)} fusion(bf16[1024,1024]{0,1:T(8,128)(2,1)} %get-tuple-element.6, f32[1024]{0:T(1024)S(1)} %broadcast_multiply_fusion.1), kind=kLoop, calls=%fused_computation.14 | loop fusion | flops 4193280 | bytes 2105344 | tf_op jit(solution)/shard_map/reduce_sum | solution.py:12
  136.2 6.2 %fusion.21 = bf16[1024,1024]{1,0:T(8,128)(2,1)S(1)} fusion(bf16[1024,1024]{1,0:T(8,128)(2,1)} %param.15, bf16[1024,1024]{0,1:T(8,128)(2,1)} %get-tuple-element.6, f32[1024]{0:T(1024)S(1)} %select_select_fusion.1, f32[1024]{0:T(1024)S(1)} %add_rsqrt_fusion.1, f32[1024]{0:T(1024)S(1)} %broadcast_multiply_fusion.1), kind=kOutput, calls=%fused_computation.32 | convolution fusion | flops 2157969408 | bytes 6303744 | tf_op jit(solution)/shard_map/dot_general | solution.py:138
  142.4 1.3 copy-done.4
  143.7 1.9 copy.50
  145.6 3.3 %all-to-all-done.2 = bf16[32,4,33,128]{3,1,2,0:T(4,128)(2,1)S(1)} async-done(((bf16[32,4,33,128]{3,1,2,0:T(4,128)(2,1)}), bf16[32,4,33,128]{3,1,2,0:T(4,128)(2,1)S(1)}, u32[]{:S(2)}, u32[]{:S(2)}) %all-to-all-start.2) | async-done | bytes 1081376 | tf_op jit(solution)/shard_map/all_to_all | solution.py:39
  149.0 2.4 %fusion.51 = f32[4,1024,8]{1,0,2:T(4,128)S(1)} fusion(bf16[4,1056,128]{2,0,1:T(4,128)(2,1)S(1)} %bitcast.69, bf16[1024,1024]{1,0:T(8,128)(2,1)} %copy-done.4), kind=kOutput, calls=%fused_computation.65 | convolution fusion | flops 8388608 | bytes 3309568 | tf_op jit(solution)/shard_map/rhk,shk->srh/dot_general | solution.py:144
  151.7 3.5 %fusion = bf16[1024,8,128]{0,2,1:T(8,128)(2,1)S(1)} fusion(f32[4,1024,8]{1,0,2:T(4,128)S(1)} %fusion.51, bf16[1024,8,128,1]{2,1,0,3:T(8,128)(2,1)S(1)} %bitcast.74, bf16[4,8,128,128]{3,0,2,1:T(4,128)(2,1)S(1)} %bitcast.75), kind=kOutput, calls=%fused_computation.1 | convolution fusion | flops 1081081856 | bytes 5373952 | tf_op jit(solution)/shard_map/rhk,shkv->srhv/dot_general | solution.py:141
  155.3 2.6 %fusion.64 = (f32[1024]{0:T(1024)S(1)}, f32[1024,1024]{0,1:T(8,128)S(1)}) fusion(bf16[1024,1024]{0,1:T(8,128)(2,1)S(1)} %bitcast.84, bf16[1024,1024]{1,0:T(8,128)(2,1)S(1)} %copy-done, bf16[1024,1024]{0,1:T(8,128)(2,1)S(1)} %copy-done.1), kind=kOutput, calls=%fused_computation.98 | convolution fusion | flops 2150628352 | bytes 10489856 | tf_op jit(solution)/shard_map/dot_general | solution.py:150
  158.0 1.9 copy-done.2
  160.4 10.7 %fusion.28 = f32[1024,1024]{0,1:T(8,128)} fusion(bf16[1024,1024]{1,0:T(8,128)(2,1)} %param.19, bf16[1024,1024]{1,0:T(8,128)(2,1)} %param.18, f32[1024,1024]{0,1:T(8,128)} %copy-done.2, f32[1024]{0:T(1024)S(1)} %copy-done.9, f32[1024]{0:T(1024)S(1)} %add_rsqrt_fusion, f32[1024]{0:T(1024)S(1)} %broadcast_multiply_fusion), kind=kOutput, calls=%fused_computation.43 | convolution fusion | flops 4308598784 | bytes 12595200 | tf_op jit(solution)/shard_map/dot_general | solution.py:157
  171.1 1.7 fusion.54
  172.9 2.8 %collective-permute-done.8 = bf16[1024,2,256]{0,2,1:T(8,128)(2,1)} collective-permute-done((bf16[1024,2,256]{0,2,1:T(8,128)(2,1)S(1)}, bf16[1024,2,256]{0,2,1:T(8,128)(2,1)}, u32[]{:S(2)}, u32[]{:S(2)}) %collective-permute-start.8) | collective-permute-done | bytes 1048608 | tf_op jit(solution)/shard_map/ppermute | solution.py:64
  175.7 2.2 %bitcast_add_fusion = f32[1024,2,256]{0,2,1:T(8,128)S(1)} fusion(bf16[1024,2,256]{0,2,1:T(8,128)(2,1)} %collective-permute-done.8, f32[1024,2,2,256]{0,3,2,1:T(8,128)} %bitcast.72, s32[]{:T(128)S(6)} %select_n.138), kind=kLoop, calls=%fused_computation.49 | loop fusion | flops 1048576 | bytes 5242884 | tf_op jit(solution)/shard_map/add | solution.py:65
  177.9 1.3 copy-done.3
  180.2 14.7 %collective-permute-done.9 = bf16[1024,256]{0,1:T(8,128)(2,1)S(1)} collective-permute-done((bf16[1024,256]{0,1:T(8,128)(2,1)S(1)}, bf16[1024,256]{0,1:T(8,128)(2,1)S(1)}, u32[]{:S(2)}, u32[]{:S(2)}) %collective-permute-start.9) | collective-permute-done | bytes 524320 | tf_op jit(solution)/shard_map/ppermute | solution.py:69
  194.9 1.8 fusion.56
  (60 shorter events, 10.1 us)
Async XLA Ops:
  0.0 155.3 %copy-start = (bf16[1024,1024]{1,0:T(8,128)(2,1)S(1)}, bf16[1024,1024]{1,0:T(8,128)(2,1)}, u32[]{:S(2)}) copy-start(bf16[1024,1024]{1,0:T(8,128)(2,1)} %param.16) | copy-start | bytes 6291460
  0.0 6.1 %copy-start.6 = (bf16[1,32,1024]{2,1,0:T(8,128)(2,1)S(1)}, bf16[1,32,1024]{2,1,0:T(8,128)(2,1)}, u32[]{:S(2)}) copy-start(bf16[1,32,1024]{2,1,0:T(8,128)(2,1)} %param.14) | copy-start | bytes 196612
  0.0 6.1 %copy-start.7 = (bf16[1,32,1024]{2,1,0:T(8,128)(2,1)S(1)}, bf16[1,32,1024]{2,1,0:T(8,128)(2,1)}, u32[]{:S(2)}) copy-start(bf16[1,32,1024]{2,1,0:T(8,128)(2,1)} %param.13) | copy-start | bytes 196612
  4.1 15.4 %collective-permute-start.1 = (bf16[1024,1024]{0,1:T(8,128)(2,1)}, bf16[1024,1024]{0,1:T(8,128)(2,1)}, u32[]{:S(2)}, u32[]{:S(2)}) collective-permute-start(bf16[1024,1024]{0,1:T(8,128)(2,1)} %bitcast.67), channel_id=1, source_target_pairs={{96,32},{97,33},{98,34},{99,35},{100,36},{101,37},{102,38},{103,39... | collective-permute-start | bytes 6291464 | tf_op jit(solution)/shard_map/ppermute | solution.py:29
  8.7 78.3 %all-to-all-start = ((bf16[32,32,2048]{2,1,0:T(8,128)(2,1)}), bf16[32,32,2048]{2,1,0:T(8,128)(2,1)}, u32[]{:S(2)}, u32[]{:S(2)}) async-start(bf16[32,32,2048]{2,1,0:T(8,128)(2,1)} %broadcast_in_dim.21), calls=%async_computation | async-start | bytes 8388608 | tf_op jit(solution)/shard_map/all_to_all | solution.py:39
  17.5 5.9 %collective-permute-start = (bf16[1024,1024]{0,1:T(8,128)(2,1)}, bf16[1024,1024]{0,1:T(8,128)(2,1)}, u32[]{:S(2)}, u32[]{:S(2)}) collective-permute-start(bf16[1024,1024]{0,1:T(8,128)(2,1)} %bitcast.68), channel_id=1, source_target_pairs={{96,64},{97,65},{98,66},{99,67},{100,68},{101,69},{102,70},{103,71... | collective-permute-start | bytes 6291464 | tf_op jit(solution)/shard_map/ppermute | solution.py:30
  19.5 61.8 %collective-permute-start.2 = (bf16[1024,1024]{0,1:T(8,128)(2,1)}, bf16[1024,1024]{0,1:T(8,128)(2,1)}, u32[]{:S(2)}, u32[]{:S(2)}) collective-permute-start(bf16[1024,1024]{0,1:T(8,128)(2,1)} %collective-permute-done.1), channel_id=1, source_target_pairs={{32,0},{33,1},{34,2},{35,3},{36,4},{37,5},{38,6},{39,7},{40,8},{41... | collective-permute-start | bytes 6291464 | tf_op jit(solution)/shard_map/ppermute | solution.py:31
  23.4 63.5 %copy-start.8 = (f32[1,1024]{1,0:T(1,128)S(1)}, f32[1,1024]{1,0:T(1,128)}, u32[]{:S(2)}) copy-start(f32[1,1024]{1,0:T(1,128)} %param.12) | copy-start | bytes 12292
  100.2 20.1 %all-to-all-start.1 = ((f32[32,33,128]{2,1,0:T(8,128)}), f32[32,33,128]{2,1,0:T(8,128)S(1)}, u32[]{:S(2)}, u32[]{:S(2)}) async-start(f32[32,33,128]{2,1,0:T(8,128)} %reshape.147), calls=%async_computation.1 | async-start | bytes 1310720 | tf_op jit(solution)/shard_map/all_to_all | solution.py:127
  108.7 1.3 collective-permute-start.6
  109.4 11.1 %collective-permute-start.5 = (f32[1024]{0:T(1024)S(1)}, f32[1024]{0:T(1024)S(1)}, u32[]{:S(2)}, u32[]{:S(2)}) collective-permute-start(f32[1024]{0:T(1024)S(1)} %bitcast.82), channel_id=1, source_target_pairs={{96,64},{97,65},{98,66},{99,67},{100,68},{101,69},{102,70},{103,71... | collective-permute-start | bytes 12296 | tf_op jit(solution)/shard_map/ppermute | solution.py:30
  110.1 10.4 %collective-permute-start.7 = (f32[1024]{0:T(1024)S(1)}, f32[1024]{0:T(1024)S(1)}, u32[]{:S(2)}, u32[]{:S(2)}) collective-permute-start(f32[1024]{0:T(1024)S(1)} %collective-permute-done.6), channel_id=1, source_target_pairs={{32,0},{33,1},{34,2},{35,3},{36,4},{37,5},{38,6},{39,7},{40,8},{41... | collective-permute-start | bytes 12296 | tf_op jit(solution)/shard_map/ppermute | solution.py:31
  120.4 1.3 collective-permute-start.3
  121.6 5.4 %collective-permute-start.4 = (bf16[2,33,128]{2,1,0:T(8,128)(2,1)S(1)}, bf16[2,33,128]{2,1,0:T(8,128)(2,1)S(1)}, u32[]{:S(2)}, u32[]{:S(2)}) collective-permute-start(bf16[2,33,128]{2,1,0:T(8,128)(2,1)S(1)} %maximum_select_fusion.1), channel_id=1, source_target_pairs={{0,64},{64,0},{32,96},{96,32},{1,65},{65,1},{33,97},{97,33},{2,66}... | collective-permute-start | bytes 50696 | tf_op jit(solution)/shard_map/ppermute | solution.py:48
  128.3 20.6 %all-to-all-start.2 = ((bf16[32,4,33,128]{3,1,2,0:T(4,128)(2,1)}), bf16[32,4,33,128]{3,1,2,0:T(4,128)(2,1)S(1)}, u32[]{:S(2)}, u32[]{:S(2)}) async-start(bf16[32,4,33,128]{3,1,2,0:T(4,128)(2,1)} %broadcast_in_dim.24), calls=%async_computation.2 | async-start | bytes 2162688 | tf_op jit(solution)/shard_map/all_to_all | solution.py:39
  142.4 1.3 copy-start.4
  149.0 2.8 %copy-start.5 = (bf16[128,8,8,128]{3,2,1,0:T(8,128)(2,1)S(1)}, bf16[128,8,8,128]{3,2,1,0:T(8,128)(2,1)}, u32[]{:S(2)}) copy-start(bf16[128,8,8,128]{3,2,1,0:T(8,128)(2,1)} %copy.50) | copy-start | bytes 6291460
  151.7 3.5 %copy-start.1 = (bf16[1024,1024]{0,1:T(8,128)(2,1)S(1)}, bf16[1024,1024]{0,1:T(8,128)(2,1)}, u32[]{:S(2)}) copy-start(bf16[1024,1024]{0,1:T(8,128)(2,1)} %get-tuple-element.6) | copy-start | bytes 6291460
  157.9 1.9 copy-start.2
  157.9 2.4 %copy-start.9 = (f32[1024]{0:T(1024)S(1)}, f32[1024]{0:T(1024)}, u32[]{:S(2)}) copy-start(f32[1024]{0:T(1024)} %param.17) | copy-start | bytes 12292
  172.8 2.9 %collective-permute-start.8 = (bf16[1024,2,256]{0,2,1:T(8,128)(2,1)S(1)}, bf16[1024,2,256]{0,2,1:T(8,128)(2,1)}, u32[]{:S(2)}, u32[]{:S(2)}) collective-permute-start(bf16[1024,2,256]{0,2,1:T(8,128)(2,1)S(1)} %fusion.54), channel_id=1, source_target_pairs={{0,32},{32,0},{64,96},{96,64},{1,33},{33,1},{65,97},{97,65},{2,34}... | collective-permute-start | bytes 3145736 | tf_op jit(solution)/shard_map/ppermute | solution.py:64
  177.9 1.3 copy-start.3
  179.3 15.5 %collective-permute-start.9 = (bf16[1024,256]{0,1:T(8,128)(2,1)S(1)}, bf16[1024,256]{0,1:T(8,128)(2,1)S(1)}, u32[]{:S(2)}, u32[]{:S(2)}) collective-permute-start(bf16[1024,256]{0,1:T(8,128)(2,1)S(1)} %fusion.58), channel_id=1, source_target_pairs={{0,64},{64,0},{32,96},{96,32},{1,65},{65,1},{33,97},{97,33},{2,66}... | collective-permute-start | bytes 1572872 | tf_op jit(solution)/shard_map/ppermute | solution.py:69

commit v14 on v13

--- a/solution.py
+++ b/solution.py
@@ -154,10 +154,27 @@
     hidden = jax.nn.gelu(
         jnp.dot(centred, up_weight, preferred_element_type=jnp.float32), approximate=True
     ).astype(jnp.bfloat16)
-    term = jnp.dot(hidden, down_weight, preferred_element_type=jnp.float32)
     share = width // sections
     own_mixed = lax.dynamic_slice_in_dim(mixed, me * share, share, axis=1)
-    return (own_mixed + scatter_sum(term, me, sections)).astype(jnp.bfloat16)
+    if sections != 4:
+        term = jnp.dot(hidden, down_weight, preferred_element_type=jnp.float32)
+        return (own_mixed + scatter_sum(term, me, sections)).astype(jnp.bfloat16)
+    side = me // 2
+    parity = me % 2
+    quarters = down_weight.reshape(down_weight.shape[0], 2, 2, share)
+    on_chip = [(0, 1), (1, 0), (2, 3), (3, 2)]
+
+    def half_of(which):
+        weights_half = lax.dynamic_index_in_dim(quarters, which, axis=1, keepdims=False)
+        made = jnp.einsum("rf,fps->rps", hidden, weights_half, preferred_element_type=jnp.float32)
+        kept = lax.dynamic_index_in_dim(made, parity, axis=1, keepdims=False)
+        sent = lax.dynamic_index_in_dim(made, 1 - parity, axis=1, keepdims=False)
+        return kept + lax.ppermute(sent.astype(jnp.bfloat16), "sec", on_chip).astype(jnp.float32)
+
+    crossing = half_of(1 - side)
+    arrived = lax.ppermute(crossing.astype(jnp.bfloat16), "sec", [(0, 2), (2, 0), (1, 3), (3, 1)])
+    staying = half_of(side)
+    return (own_mixed + staying + arrived.astype(jnp.float32)).astype(jnp.bfloat16)
 
 
 def solution(mesh):

time: 200 us -> 203 us (1.015)
  waiting for transfers between devices: 93.1 us -> 75.1 us
  local copies, waits for them, and re-layouts: 18.6 us -> 35.6 us
  starting transfers between devices: 32.9 us -> 41.7 us
  matrix products: 34.9 us -> 30.4 us
    dynamic_slice x0 -> x6, local copies, waits for them, and re-layouts: none -> 10.4 us  [the longest x4 5.21 us: half_of(): kept = lax.dynamic_index_in_dim(made, parity, axis=1, keepdims=False)]
    all_to_all x1, waiting for transfers between devices: 8.91 us -> 0.01 us  [on_device(): reduced = jnp.sum(lax.all_to_all(packed, 'pts', 0, 0, tiled=False), axis=0)]
    ppermute x2 -> x3, waiting for transfers between devices: 17.5 us -> 10.3 us  [the longest x1 10.3 us: on_device(): lax.ppermute(crossing.astype(jnp.bfloat16), 'sec', [(0, 2), (2, 0), (1, 3...]
    dot_general x1 -> x3, matrix products: 10.7 us -> 6.17 us  [the longest x1 3.66 us: on_device(): jnp.dot(centred, up_weight, preferred_element_type=jnp.float32)]
    reshape x0 -> x1, local copies, waits for them, and re-layouts: none -> 4.47 us  [on_device(): quarters = down_weight.reshape(down_weight.shape[0], 2, 2, share)]
    unnamed x31 -> x41, local copies, waits for them, and re-layouts: 10.7 us -> 14.6 us
    all_to_all x2, starting transfers between devices: 14.5 us -> 17.7 us  [gather_a2a(): return lax.all_to_all(spread, axis, 0, 0, tiled=False)]
    convert_element_type x1 -> x2, other arithmetic: 1.79 us -> 4.47 us  [the longest x1 2.3 us: on_device(): crossing.astype(jnp.bfloat16)]
  transfers between devices with their start and end apart: 13 -> 14, of which waited for: 7 -> 5; matrix products, arithmetic and copies ran while one was open for 10% -> 19% of each run, Pallas kernels for 0% -> 0%
where the time goes in v14:
time: 203 us; the launch traced here: 201 us
  waiting for transfers between devices  75.1 us (37%)
  starting transfers between devices  41.7 us (21%)
  local copies, waits for them, and re-layouts  35.6 us (18%)
  matrix products  30.4 us (15%)
  other arithmetic  17.5 us (9%)
    ppermute x2, waiting for transfers between devices, from_last(): farther = lax.ppermute(far, axis, [(1, 0)])  57.9 us
    all_to_all x2, starting transfers between devices, gather_a2a(): return lax.all_to_all(spread, axis, 0, 0, tiled=False)  17.7 us
    unnamed x41, local copies, waits for them, and re-layouts  14.6 us
    ppermute x1, waiting for transfers between devices, on_device(): lax.ppermute(crossing.astype(jnp.bfloat16), 'sec', [(0, 2), (2, 0), (1, 3...  10.3 us
    all_to_all x1, starting transfers between devices, on_device(): reduced = jnp.sum(lax.all_to_all(packed, 'pts', 0, 0, tiled=False), axis=0)  8.49 us
    reduce_sum x2, other arithmetic, layer_normalizer(): mean = jnp.mean(values, axis=-1, keepdims=True)  7.61 us
    dot_general x1, matrix products, on_device(): projected = jnp.dot(normed, weights, preferred_element_type=jnp.float32)  7.05 us
    dot_general x1, matrix products, on_device(): jnp.dot(query_normed, query_weight, preferred_element_type=jnp.float32)  6.21 us
  transfers between devices with their start and end apart: 14, of which 5 were waited for; matrix products, arithmetic and copies ran while one was open for 19% of the time, Pallas kernels for 0%

profile of v14, /device:TPU:16, one launch (start us, length us, event | category | flops | bytes accessed | tf_op | source)
XLA Modules:
  0.0 201.4 jit_solution(2575614722818690080)
XLA Ops:
  0.0 4.1 %copy.40 = bf16[1,1024,1024]{1,2,0:T(8,128)(2,1)} copy(bf16[1,1024,1024]{2,1,0:T(8,128)(2,1)} %param.10) | data formatting | bytes 4194304 | tf_op args[0]
  4.1 2.0 %collective-permute-start.1 = (bf16[1024,1024]{0,1:T(8,128)(2,1)}, bf16[1024,1024]{0,1:T(8,128)(2,1)}, u32[]{:S(2)}, u32[]{:S(2)}) collective-permute-start(bf16[1024,1024]{0,1:T(8,128)(2,1)} %bitcast.78), channel_id=1, source_target_pairs={{96,32},{97,33},{98,34},{99,35},{100,36},{101,37},{102,38},{103,39... | collective-permute-start | bytes 6291464 | tf_op jit(solution)/shard_map/ppermute | solution.py:29
  6.1 2.5 %broadcast_in_dim.21 = bf16[32,32,2048]{2,1,0:T(8,128)(2,1)} broadcast(bf16[32,2048]{1,0:T(8,128)(2,1)S(1)} %pad_maximum_fusion), dimensions={1,2} | broadcast | bytes 4325376 | tf_op jit(solution)/shard_map/broadcast_in_dim | solution.py:38
  8.6 8.8 %all-to-all-start = ((bf16[32,32,2048]{2,1,0:T(8,128)(2,1)}), bf16[32,32,2048]{2,1,0:T(8,128)(2,1)}, u32[]{:S(2)}, u32[]{:S(2)}) async-start(bf16[32,32,2048]{2,1,0:T(8,128)(2,1)} %broadcast_in_dim.21), calls=%async_computation | async-start | bytes 8388608 | tf_op jit(solution)/shard_map/all_to_all | solution.py:39
  17.5 2.0 collective-permute-start
  21.4 2.0 convert_reduce_fusion.1
  23.4 57.9 %collective-permute-done.2 = bf16[1024,1024]{0,1:T(8,128)(2,1)} collective-permute-done((bf16[1024,1024]{0,1:T(8,128)(2,1)}, bf16[1024,1024]{0,1:T(8,128)(2,1)}, u32[]{:S(2)}, u32[]{:S(2)}) %collective-permute-start.2) | collective-permute-done | bytes 2097184 | tf_op jit(solution)/shard_map/ppermute | solution.py:31
  81.3 5.6 %convert_reduce_fusion = (f32[1024]{0:T(1024)S(1)}, bf16[1024,1024]{0,1:T(8,128)(2,1)}, f32[1024]{0:T(1024)S(1)}) fusion(bf16[1024,1024]{0,1:T(8,128)(2,1)} %collective-permute-done, bf16[1024,1024]{0,1:T(8,128)(2,1)} %collective-permute-done.1, bf16[1024,1024]{0,1:T(8,128)(2,1)} %collective-permute-done.2, pred[]{:T(512)S(6)} %eq.23, pred[]{:T(512)S(6)} %eq.22, ...), kind=kLoop, calls=%fused_computation.9 | loop fusion | flops 9435136 | bytes 10498051 | tf_op jit(solution)/shard_map/reduce_sum | solution.py:10
  87.0 7.1 %fusion.23 = f32[1024,2048]{1,0:T(8,128)S(1)} fusion(bf16[1024,2048]{1,0:T(8,128)(2,1)} %bitcast.6, bf16[1,1024,1024]{2,1,0:T(8,128)(2,1)} %param.10, f32[1024]{0:T(1024)S(1)} %bitcast.89, f32[1024]{0:T(1024)S(1)} %add_rsqrt_fusion.2, f32[1024]{0:T(1024)S(1)} %broadcast_multiply_fusion.2), kind=kOutput, calls=%fused_computation.39 | convolution fusion | flops 4300210176 | bytes 14692352 | tf_op jit(solution)/shard_map/dot_general | solution.py:100
  94.1 2.7 %convert_reduce_fusion.2 = (f32[1024]{0:T(1024)S(1)}, bf16[1024,1024]{1,0:T(8,128)(2,1)S(1)}) fusion(f32[1024,2048]{1,0:T(8,128)S(1)} %fusion.23, pred[1024]{0:T(1024)(128)(4,1)S(1)} %iota_compare_fusion), kind=kLoop, calls=%fused_computation.36 | loop fusion | flops 8387584 | bytes 6296576 | tf_op jit(solution)/shard_map/reduce_sum | solution.py:115
  96.7 2.4 %fusion.26 = f32[1024,1024]{1,0:T(8,128)S(1)} fusion(bf16[1024,1024]{1,0:T(8,128)(2,1)S(1)} %get-tuple-element.8, f32[1024,2048]{1,0:T(8,128)S(1)} %fusion.23), kind=kOutput, calls=%fused_computation.41 | convolution fusion | flops 2147483648 | bytes 8388608 | tf_op jit(solution)/shard_map/dot_general | solution.py:105
  100.3 8.5 %all-to-all-start.1 = ((f32[32,33,128]{2,1,0:T(8,128)}), f32[32,33,128]{2,1,0:T(8,128)S(1)}, u32[]{:S(2)}, u32[]{:S(2)}) async-start(f32[32,33,128]{2,1,0:T(8,128)} %reshape.147), calls=%async_computation.1 | async-start | bytes 1310720 | tf_op jit(solution)/shard_map/all_to_all | solution.py:127
  110.1 4.5 %reshape.151 = bf16[1024,2,2,256]{3,2,1,0:T(2,128)(2,1)} reshape(bf16[1024,1024]{1,0:T(8,128)(2,1)} %param.19) | data formatting | bytes 4194304 | tf_op jit(solution)/shard_map/reshape | solution.py:164
  116.1 4.3 %constant_dynamic-slice_fusion.2 = (bf16[1024,1,2,256]{3,2,1,0:T(2,128)(2,1)}, bf16[1024,1,2,256]{3,2,1,0:T(2,128)(2,1)}) fusion(bf16[1024,2,2,256]{3,2,1,0:T(2,128)(2,1)} %reshape.151, s32[]{:T(128)S(6)} %select_n.143, s32[]{:T(128)S(6)} %select_n.140), kind=kLoop, calls=%fused_computation.97 | loop fusion | bytes 4194312 | tf_op jit(solution)/shard_map/jit(dynamic_index_in_dim)/dynamic_slice | solution.py:168
  120.5 1.5 collective-permute-start.3
  122.8 2.7 %collective-permute-start.4 = (bf16[2,33,128]{2,1,0:T(8,128)(2,1)S(1)}, bf16[2,33,128]{2,1,0:T(8,128)(2,1)S(1)}, u32[]{:S(2)}, u32[]{:S(2)}) collective-permute-start(bf16[2,33,128]{2,1,0:T(8,128)(2,1)S(1)} %maximum_select_fusion.1), channel_id=1, source_target_pairs={{0,64},{64,0},{32,96},{96,32},{1,65},{65,1},{33,97},{97,33},{2,66}... | collective-permute-start | bytes 50696 | tf_op jit(solution)/shard_map/ppermute | solution.py:48
  125.6 2.6 %collective-permute-done.4 = bf16[2,33,128]{2,1,0:T(8,128)(2,1)S(1)} collective-permute-done((bf16[2,33,128]{2,1,0:T(8,128)(2,1)S(1)}, bf16[2,33,128]{2,1,0:T(8,128)(2,1)S(1)}, u32[]{:S(2)}, u32[]{:S(2)}) %collective-permute-start.4) | collective-permute-done | bytes 16928 | tf_op jit(solution)/shard_map/ppermute | solution.py:48
  129.5 8.8 %all-to-all-start.2 = ((bf16[32,4,33,128]{3,1,2,0:T(4,128)(2,1)}), bf16[32,4,33,128]{3,1,2,0:T(4,128)(2,1)S(1)}, u32[]{:S(2)}, u32[]{:S(2)}) async-start(bf16[32,4,33,128]{3,1,2,0:T(4,128)(2,1)} %broadcast_in_dim.24), calls=%async_computation.2 | async-start | bytes 2162688 | tf_op jit(solution)/shard_map/all_to_all | solution.py:39
  138.3 2.2 %fusion.3 = f32[1024]{0:T(1024)S(1)} fusion(bf16[1024,1024]{0,1:T(8,128)(2,1)} %get-tuple-element.6, f32[1024]{0:T(1024)S(1)} %broadcast_multiply_fusion.1), kind=kLoop, calls=%fused_computation.14 | loop fusion | flops 4193280 | bytes 2105344 | tf_op jit(solution)/shard_map/reduce_sum | solution.py:12
  140.5 6.2 %fusion.21 = bf16[1024,1024]{1,0:T(8,128)(2,1)S(1)} fusion(bf16[1024,1024]{1,0:T(8,128)(2,1)} %param.15, bf16[1024,1024]{0,1:T(8,128)(2,1)} %get-tuple-element.6, f32[1024]{0:T(1024)S(1)} %select_select_fusion.1, f32[1024]{0:T(1024)S(1)} %add_rsqrt_fusion.1, f32[1024]{0:T(1024)S(1)} %broadcast_multiply_fusion.1), kind=kOutput, calls=%fused_computation.32 | convolution fusion | flops 2157969408 | bytes 6303744 | tf_op jit(solution)/shard_map/dot_general | solution.py:138
  148.1 1.9 copy.69
  150.0 3.4 %all-to-all-done.2 = bf16[32,4,33,128]{3,1,2,0:T(4,128)(2,1)S(1)} async-done(((bf16[32,4,33,128]{3,1,2,0:T(4,128)(2,1)}), bf16[32,4,33,128]{3,1,2,0:T(4,128)(2,1)S(1)}, u32[]{:S(2)}, u32[]{:S(2)}) %all-to-all-start.2) | async-done | bytes 1081376 | tf_op jit(solution)/shard_map/all_to_all | solution.py:39
  153.4 2.4 %fusion.49 = f32[4,1024,8]{1,0,2:T(4,128)S(1)} fusion(bf16[4,1056,128]{2,0,1:T(4,128)(2,1)S(1)} %bitcast.80, bf16[1024,1024]{1,0:T(8,128)(2,1)} %copy-done.3), kind=kOutput, calls=%fused_computation.62 | convolution fusion | flops 8388608 | bytes 3309568 | tf_op jit(solution)/shard_map/rhk,shk->srh/dot_general | solution.py:144
  156.2 3.5 %fusion = bf16[1024,8,128]{0,2,1:T(8,128)(2,1)S(1)} fusion(f32[4,1024,8]{1,0,2:T(4,128)S(1)} %fusion.49, bf16[1024,8,128,1]{2,1,0,3:T(8,128)(2,1)S(1)} %bitcast.83, bf16[4,8,128,128]{3,0,2,1:T(4,128)(2,1)S(1)} %bitcast.84), kind=kOutput, calls=%fused_computation.1 | convolution fusion | flops 1081081856 | bytes 5373952 | tf_op jit(solution)/shard_map/rhk,shkv->srhv/dot_general | solution.py:141
  159.7 2.6 %fusion.58 = (f32[1024]{0:T(1024)S(1)}, f32[1024,1024]{0,1:T(8,128)S(1)}) fusion(bf16[1024,1024]{0,1:T(8,128)(2,1)S(1)} %bitcast.93, bf16[1024,1024]{1,0:T(8,128)(2,1)S(1)} %copy-done, bf16[1024,1024]{0,1:T(8,128)(2,1)S(1)} %copy-done.1), kind=kOutput, calls=%fused_computation.101 | convolution fusion | flops 2150628352 | bytes 10489856 | tf_op jit(solution)/shard_map/dot_general | solution.py:150
  162.9 2.6 %copy-done.12 = bf16[1024,1024]{1,0:T(8,128)(2,1)S(1)} copy-done((bf16[1024,1024]{1,0:T(8,128)(2,1)S(1)}, bf16[1024,1024]{1,0:T(8,128)(2,1)}, u32[]{:S(2)}) %copy-start.12) | copy-done | bytes 2097176
  165.5 3.7 %fusion.15 = bf16[1024,1024]{1,0:T(8,128)(2,1)S(1)} fusion(bf16[1024,1024]{1,0:T(8,128)(2,1)S(1)} %copy-done.12, f32[1024,1024]{0,1:T(8,128)S(1)} %get-tuple-element.13, f32[1024]{0:T(1024)S(1)} %copy-done.13, f32[1024]{0:T(1024)S(1)} %add_rsqrt_fusion, f32[1024]{0:T(1024)S(1)} %broadcast_multiply_fusion), kind=kOutput, calls=%fused_computation.26 | convolution fusion | flops 2161115136 | bytes 8400896 | tf_op jit(solution)/shard_map/dot_general | solution.py:155
  177.7 2.1 %copy.65 = bf16[1024,1,256]{0,2,1:T(8,128)(2,1)} copy(bf16[1024,1,256]{2,0,1:T(8,128)(2,1)} %get-tuple-element.15) | data formatting | bytes 1048576
  180.3 2.3 %fusion.52 = bf16[1024,256]{0,1:T(8,128)(2,1)} fusion(f32[1024,1,256]{0,2,1:T(8,128)} %copy.53, bf16[1024,256]{0,1:T(8,128)(2,1)} %collective-permute-done.9), kind=kLoop, calls=%fused_computation.66 | loop fusion | flops 786432 | bytes 2097152 | tf_op jit(solution)/shard_map/convert_element_type | solution.py:175
  182.6 2.7 %collective-permute-start.10 = (bf16[1024,256]{0,1:T(8,128)(2,1)}, bf16[1024,256]{0,1:T(8,128)(2,1)}, u32[]{:S(2)}, u32[]{:S(2)}) collective-permute-start(bf16[1024,256]{0,1:T(8,128)(2,1)} %fusion.52), channel_id=1, source_target_pairs={{0,64},{64,0},{32,96},{96,32},{1,65},{65,1},{33,97},{97,33},{2,66}... | collective-permute-start | bytes 1572872 | tf_op jit(solution)/shard_map/ppermute | solution.py:175
  187.9 10.3 %collective-permute-done.10 = bf16[1024,256]{0,1:T(8,128)(2,1)} collective-permute-done((bf16[1024,256]{0,1:T(8,128)(2,1)}, bf16[1024,256]{0,1:T(8,128)(2,1)}, u32[]{:S(2)}, u32[]{:S(2)}) %collective-permute-start.10) | collective-permute-done | bytes 524320 | tf_op jit(solution)/shard_map/ppermute | solution.py:175
  198.2 2.2 %fusion.55 = bf16[1024,256]{0,1:T(8,128)(2,1)S(1)} fusion(f32[1024,1,256]{0,2,1:T(8,128)} %copy.50, bf16[1024,256]{0,1:T(8,128)(2,1)} %collective-permute-done.10, bf16[1024,256]{0,1:T(8,128)(2,1)} %collective-permute-done.8, f32[1024,1024]{0,1:T(8,128)} %copy-done.2, s32[]{:T(128)S(6)} %select_n.139), kind=kLoop, calls=%fused_computation.70 | loop fusion | flops 1572864 | bytes 3670020 | tf_op jit(solution)/shard_map/convert_element_type | solution.py:177
  (79 shorter events, 22.1 us)
Async XLA Ops:
  0.0 159.7 %copy-start = (bf16[1024,1024]{1,0:T(8,128)(2,1)S(1)}, bf16[1024,1024]{1,0:T(8,128)(2,1)}, u32[]{:S(2)}) copy-start(bf16[1024,1024]{1,0:T(8,128)(2,1)} %param.16) | copy-start | bytes 6291460
  0.0 6.1 %copy-start.9 = (bf16[1,32,1024]{2,1,0:T(8,128)(2,1)S(1)}, bf16[1,32,1024]{2,1,0:T(8,128)(2,1)}, u32[]{:S(2)}) copy-start(bf16[1,32,1024]{2,1,0:T(8,128)(2,1)} %param.14) | copy-start | bytes 196612
  0.0 6.1 %copy-start.10 = (bf16[1,32,1024]{2,1,0:T(8,128)(2,1)S(1)}, bf16[1,32,1024]{2,1,0:T(8,128)(2,1)}, u32[]{:S(2)}) copy-start(bf16[1,32,1024]{2,1,0:T(8,128)(2,1)} %param.13) | copy-start | bytes 196612
  4.1 15.4 %collective-permute-start.1 = (bf16[1024,1024]{0,1:T(8,128)(2,1)}, bf16[1024,1024]{0,1:T(8,128)(2,1)}, u32[]{:S(2)}, u32[]{:S(2)}) collective-permute-start(bf16[1024,1024]{0,1:T(8,128)(2,1)} %bitcast.78), channel_id=1, source_target_pairs={{96,32},{97,33},{98,34},{99,35},{100,36},{101,37},{102,38},{103,39... | collective-permute-start | bytes 6291464 | tf_op jit(solution)/shard_map/ppermute | solution.py:29
  8.6 78.3 %all-to-all-start = ((bf16[32,32,2048]{2,1,0:T(8,128)(2,1)}), bf16[32,32,2048]{2,1,0:T(8,128)(2,1)}, u32[]{:S(2)}, u32[]{:S(2)}) async-start(bf16[32,32,2048]{2,1,0:T(8,128)(2,1)} %broadcast_in_dim.21), calls=%async_computation | async-start | bytes 8388608 | tf_op jit(solution)/shard_map/all_to_all | solution.py:39
  17.5 5.9 %collective-permute-start = (bf16[1024,1024]{0,1:T(8,128)(2,1)}, bf16[1024,1024]{0,1:T(8,128)(2,1)}, u32[]{:S(2)}, u32[]{:S(2)}) collective-permute-start(bf16[1024,1024]{0,1:T(8,128)(2,1)} %bitcast.79), channel_id=1, source_target_pairs={{96,64},{97,65},{98,66},{99,67},{100,68},{101,69},{102,70},{103,71... | collective-permute-start | bytes 6291464 | tf_op jit(solution)/shard_map/ppermute | solution.py:30
  19.5 61.9 %collective-permute-start.2 = (bf16[1024,1024]{0,1:T(8,128)(2,1)}, bf16[1024,1024]{0,1:T(8,128)(2,1)}, u32[]{:S(2)}, u32[]{:S(2)}) collective-permute-start(bf16[1024,1024]{0,1:T(8,128)(2,1)} %collective-permute-done.1), channel_id=1, source_target_pairs={{32,0},{33,1},{34,2},{35,3},{36,4},{37,5},{38,6},{39,7},{40,8},{41... | collective-permute-start | bytes 6291464 | tf_op jit(solution)/shard_map/ppermute | solution.py:31
  23.4 63.6 %copy-start.11 = (f32[1,1024]{1,0:T(1,128)S(1)}, f32[1,1024]{1,0:T(1,128)}, u32[]{:S(2)}) copy-start(f32[1,1024]{1,0:T(1,128)} %param.12) | copy-start | bytes 12292
  100.3 20.1 %all-to-all-start.1 = ((f32[32,33,128]{2,1,0:T(8,128)}), f32[32,33,128]{2,1,0:T(8,128)S(1)}, u32[]{:S(2)}, u32[]{:S(2)}) async-start(f32[32,33,128]{2,1,0:T(8,128)} %reshape.147), calls=%async_computation.1 | async-start | bytes 1310720 | tf_op jit(solution)/shard_map/all_to_all | solution.py:127
  108.8 5.8 %collective-permute-start.6 = (f32[1024]{0:T(1024)S(1)}, f32[1024]{0:T(1024)S(1)}, u32[]{:S(2)}, u32[]{:S(2)}) collective-permute-start(f32[1024]{0:T(1024)S(1)} %bitcast.90), channel_id=1, source_target_pairs={{96,32},{97,33},{98,34},{99,35},{100,36},{101,37},{102,38},{103,39... | collective-permute-start | bytes 12296 | tf_op jit(solution)/shard_map/ppermute | solution.py:29
  109.5 12.5 %collective-permute-start.5 = (f32[1024]{0:T(1024)S(1)}, f32[1024]{0:T(1024)S(1)}, u32[]{:S(2)}, u32[]{:S(2)}) collective-permute-start(f32[1024]{0:T(1024)S(1)} %bitcast.91), channel_id=1, source_target_pairs={{96,64},{97,65},{98,66},{99,67},{100,68},{101,69},{102,70},{103,71... | collective-permute-start | bytes 12296 | tf_op jit(solution)/shard_map/ppermute | solution.py:30
  114.6 7.4 %collective-permute-start.7 = (f32[1024]{0:T(1024)S(1)}, f32[1024]{0:T(1024)S(1)}, u32[]{:S(2)}, u32[]{:S(2)}) collective-permute-start(f32[1024]{0:T(1024)S(1)} %collective-permute-done.6), channel_id=1, source_target_pairs={{32,0},{33,1},{34,2},{35,3},{36,4},{37,5},{38,6},{39,7},{40,8},{41... | collective-permute-start | bytes 12296 | tf_op jit(solution)/shard_map/ppermute | solution.py:31
  120.5 2.3 %collective-permute-start.3 = (bf16[33,128]{1,0:T(8,128)(2,1)S(1)}, bf16[33,128]{1,0:T(8,128)(2,1)S(1)}, u32[]{:S(2)}, u32[]{:S(2)}) collective-permute-start(bf16[33,128]{1,0:T(8,128)(2,1)S(1)} %reduce_sum.84), channel_id=1, source_target_pairs={{0,32},{32,0},{64,96},{96,64},{1,33},{33,1},{65,97},{97,65},{2,34}... | collective-permute-start | bytes 25352 | tf_op jit(solution)/shard_map/ppermute | solution.py:45
  122.8 5.4 %collective-permute-start.4 = (bf16[2,33,128]{2,1,0:T(8,128)(2,1)S(1)}, bf16[2,33,128]{2,1,0:T(8,128)(2,1)S(1)}, u32[]{:S(2)}, u32[]{:S(2)}) collective-permute-start(bf16[2,33,128]{2,1,0:T(8,128)(2,1)S(1)} %maximum_select_fusion.1), channel_id=1, source_target_pairs={{0,64},{64,0},{32,96},{96,32},{1,65},{65,1},{33,97},{97,33},{2,66}... | collective-permute-start | bytes 50696 | tf_op jit(solution)/shard_map/ppermute | solution.py:48
  129.5 23.9 %all-to-all-start.2 = ((bf16[32,4,33,128]{3,1,2,0:T(4,128)(2,1)}), bf16[32,4,33,128]{3,1,2,0:T(4,128)(2,1)S(1)}, u32[]{:S(2)}, u32[]{:S(2)}) async-start(bf16[32,4,33,128]{3,1,2,0:T(4,128)(2,1)} %broadcast_in_dim.24), calls=%async_computation.2 | async-start | bytes 2162688 | tf_op jit(solution)/shard_map/all_to_all | solution.py:39
  146.8 1.3 copy-start.3
  153.4 2.8 %copy-start.4 = (bf16[128,8,8,128]{3,2,1,0:T(8,128)(2,1)S(1)}, bf16[128,8,8,128]{3,2,1,0:T(8,128)(2,1)}, u32[]{:S(2)}) copy-start(bf16[128,8,8,128]{3,2,1,0:T(8,128)(2,1)} %copy.69) | copy-start | bytes 6291460
  156.2 3.5 %copy-start.1 = (bf16[1024,1024]{0,1:T(8,128)(2,1)S(1)}, bf16[1024,1024]{0,1:T(8,128)(2,1)}, u32[]{:S(2)}) copy-start(bf16[1024,1024]{0,1:T(8,128)(2,1)} %get-tuple-element.6) | copy-start | bytes 6291460
  162.4 6.8 %copy-start.2 = (f32[1024,1024]{0,1:T(8,128)}, f32[1024,1024]{0,1:T(8,128)S(1)}, u32[]{:S(2)}) copy-start(f32[1024,1024]{0,1:T(8,128)S(1)} %get-tuple-element.13) | copy-start | bytes 12582916
  162.4 3.1 %copy-start.12 = (bf16[1024,1024]{1,0:T(8,128)(2,1)S(1)}, bf16[1024,1024]{1,0:T(8,128)(2,1)}, u32[]{:S(2)}) copy-start(bf16[1024,1024]{1,0:T(8,128)(2,1)} %param.18) | copy-start | bytes 6291460
  162.4 3.1 %copy-start.13 = (f32[1024]{0:T(1024)S(1)}, f32[1024]{0:T(1024)}, u32[]{:S(2)}) copy-start(f32[1024]{0:T(1024)} %param.17) | copy-start | bytes 12292
  165.5 3.7 %copy-start.8 = (bf16[1024,1,2,256]{3,2,1,0:T(2,128)(2,1)S(1)}, bf16[1024,1,2,256]{3,2,1,0:T(2,128)(2,1)}, u32[]{:S(2)}) copy-start(bf16[1024,1,2,256]{3,2,1,0:T(2,128)(2,1)} %get-tuple-element.10) | copy-start | bytes 3145732
  169.2 1.3 copy-start.7
  170.5 3.5 %copy-start.5 = (f32[1024,2,256]{2,0,1:T(8,128)}, f32[1024,2,256]{2,0,1:T(8,128)S(1)}, u32[]{:S(2)}) copy-start(f32[1024,2,256]{2,0,1:T(8,128)S(1)} %fusion.35) | copy-start | bytes 6291460
  171.7 1.4 copy-start.6
  175.0 5.2 %collective-permute-start.9 = (bf16[1024,256]{0,1:T(8,128)(2,1)}, bf16[1024,256]{0,1:T(8,128)(2,1)}, u32[]{:S(2)}, u32[]{:S(2)}) collective-permute-start(bf16[1024,256]{0,1:T(8,128)(2,1)} %bitcast.64), channel_id=1, source_target_pairs={{0,32},{32,0},{64,96},{96,64},{1,33},{33,1},{65,97},{97,65},{2,34}... | collective-permute-start | bytes 1572872 | tf_op jit(solution)/shard_map/ppermute | solution.py:172
  179.8 8.1 %collective-permute-start.8 = (bf16[1024,256]{0,1:T(8,128)(2,1)}, bf16[1024,256]{0,1:T(8,128)(2,1)}, u32[]{:S(2)}, u32[]{:S(2)}) collective-permute-start(bf16[1024,256]{0,1:T(8,128)(2,1)} %bitcast.65), channel_id=1, source_target_pairs={{0,32},{32,0},{64,96},{96,64},{1,33},{33,1},{65,97},{97,65},{2,34}... | collective-permute-start | bytes 1572872 | tf_op jit(solution)/shard_map/ppermute | solution.py:172
  182.6 15.7 %collective-permute-start.10 = (bf16[1024,256]{0,1:T(8,128)(2,1)}, bf16[1024,256]{0,1:T(8,128)(2,1)}, u32[]{:S(2)}, u32[]{:S(2)}) collective-permute-start(bf16[1024,256]{0,1:T(8,128)(2,1)} %fusion.52), channel_id=1, source_target_pairs={{0,64},{64,0},{32,96},{96,32},{1,65},{65,1},{33,97},{97,33},{2,66}... | collective-permute-start | bytes 1572872 | tf_op jit(solution)/shard_map/ppermute | solution.py:175

commit v15 on v13

--- a/solution.py
+++ b/solution.py
@@ -91,9 +91,11 @@
     me = lax.axis_index("sec")
 
     stacked = jnp.concatenate([key_weight[0], value_weight[0]], axis=1)
-    weights = gather_a2a(stacked, "pts", blocks).reshape(width, 2 * width)
+    spread = jnp.broadcast_to(stacked[None], (blocks,) + stacked.shape)
+    spread, first_block = lax.optimization_barrier((spread, block))
+    weights = lax.all_to_all(spread, "pts", 0, 0, tiled=False).reshape(width, 2 * width)
 
-    query_block = from_last(block, "sec", sections)
+    query_block = from_last(first_block, "sec", sections)
     query_gain = from_last(input_gain[0], "sec", sections)
 
     normed = layer_normalizer(block.astype(jnp.float32), input_gain[0]).astype(jnp.bfloat16)

time: 200 us -> 204 us (1.020)
  starting transfers between devices: 32.9 us -> 36.8 us
    all_to_all x0 -> x1, waiting for transfers between devices: none -> 47.5 us  [on_device(): lax.all_to_all(spread, 'pts', 0, 0, tiled=False).reshape(width, 2 * width)]
    ppermute x2, waiting for transfers between devices: 57.9 us -> 18.5 us  [from_last(): farther = lax.ppermute(far, axis, [(1, 0)])]
    all_to_all x1, waiting for transfers between devices: 8.91 us -> 0.01 us  [on_device(): reduced = jnp.sum(lax.all_to_all(packed, 'pts', 0, 0, tiled=False), axis=0)]
    all_to_all x0 -> x1, starting transfers between devices: none -> 8.83 us  [on_device(): lax.all_to_all(spread, 'pts', 0, 0, tiled=False).reshape(width, 2 * width)]
    all_to_all x2 -> x1, starting transfers between devices: 14.5 us -> 8.1 us  [gather_a2a(): return lax.all_to_all(spread, axis, 0, 0, tiled=False)]
    broadcast_in_dim x0 -> x1, local copies, waits for them, and re-layouts: none -> 2.5 us  [on_device(): spread = jnp.broadcast_to(stacked[None], (blocks,) + stacked.shape)]
    broadcast_in_dim x2 -> x1, local copies, waits for them, and re-layouts: 3.77 us -> 1.29 us  [gather_a2a(): spread = jnp.broadcast_to(value[None], (count,) + value.shape)]
    reduce_sum x2 -> x3, other arithmetic: 2.68 us -> 4.87 us  [layer_normalizer(): spread = jnp.mean(centred * centred, axis=-1, keepdims=True)]
  transfers between devices with their start and end apart: 13 -> 13, of which waited for: 7 -> 6; matrix products, arithmetic and copies ran while one was open for 10% -> 16% of each run, Pallas kernels for 0% -> 0%
where the time goes in v15:
time: 204 us; the launch traced here: 202 us
  waiting for transfers between devices  91.6 us (45%)
  starting transfers between devices  36.8 us (18%)
  matrix products  34.9 us (17%)
  other arithmetic  18.6 us (9%)
  local copies, waits for them, and re-layouts  18.5 us (9%)
    all_to_all x1, waiting for transfers between devices, on_device(): lax.all_to_all(spread, 'pts', 0, 0, tiled=False).reshape(width, 2 * width)  47.5 us
    ppermute x2, waiting for transfers between devices, from_last(): farther = lax.ppermute(far, axis, [(1, 0)])  18.5 us
    ppermute x1, waiting for transfers between devices, scatter_sum(): lax.ppermute(other.astype(jnp.bfloat16), 'sec', [(0, 2), (2, 0), (1, 3),...  14.6 us
    dot_general x1, matrix products, on_device(): term = jnp.dot(hidden, down_weight, preferred_element_type=jnp.float32)  10.7 us
    unnamed x31, local copies, waits for them, and re-layouts  10.7 us
    all_to_all x1, starting transfers between devices, on_device(): reduced = jnp.sum(lax.all_to_all(packed, 'pts', 0, 0, tiled=False), axis=0)  9.78 us
    all_to_all x1, starting transfers between devices, on_device(): lax.all_to_all(spread, 'pts', 0, 0, tiled=False).reshape(width, 2 * width)  8.83 us
    all_to_all x1, starting transfers between devices, gather_a2a(): return lax.all_to_all(spread, axis, 0, 0, tiled=False)  8.1 us
  transfers between devices with their start and end apart: 13, of which 6 were waited for; matrix products, arithmetic and copies ran while one was open for 16% of the time, Pallas kernels for 0%

profile of v15, /device:TPU:16, one launch (start us, length us, event | category | flops | bytes accessed | tf_op | source)
XLA Modules:
  0.0 201.5 jit_solution(6490818374325483883)
XLA Ops:
  0.0 4.1 %copy.29 = bf16[1,1024,1024]{1,2,0:T(8,128)(2,1)} copy(bf16[1,1024,1024]{2,1,0:T(8,128)(2,1)} %param.10) | data formatting | bytes 4194304 | tf_op args[0]
  4.1 2.5 %broadcast_in_dim.20 = bf16[32,32,2048]{2,1,0:T(8,128)(2,1)} broadcast(bf16[32,2048]{1,0:T(8,128)(2,1)S(1)} %pad_maximum_fusion), dimensions={1,2} | broadcast | bytes 4325376 | tf_op jit(solution)/shard_map/broadcast_in_dim | solution.py:94
  6.6 8.8 %all-to-all-start = ((bf16[32,32,2048]{2,1,0:T(8,128)(2,1)}), bf16[32,32,2048]{2,1,0:T(8,128)(2,1)}, u32[]{:S(2)}, u32[]{:S(2)}) async-start(bf16[32,32,2048]{2,1,0:T(8,128)(2,1)} %broadcast_in_dim.20), calls=%async_computation | async-start | bytes 8388608 | tf_op jit(solution)/shard_map/all_to_all | solution.py:96
  15.5 2.0 collective-permute-start.1
  17.5 2.0 collective-permute-start
  20.1 2.0 convert_reduce_fusion.1
  22.0 2.2 %fusion.7 = f32[1024]{0:T(1024)S(1)} fusion(f32[1024]{0:T(1024)S(1)} %broadcast_multiply_fusion.2, bf16[1,1024,1024]{1,2,0:T(8,128)(2,1)} %copy.29), kind=kLoop, calls=%fused_computation.18 | loop fusion | flops 4193280 | bytes 2105344 | tf_op jit(solution)/shard_map/reduce_sum | solution.py:12
  25.6 47.5 %all-to-all-done = bf16[32,32,2048]{2,1,0:T(8,128)(2,1)} async-done(((bf16[32,32,2048]{2,1,0:T(8,128)(2,1)}), bf16[32,32,2048]{2,1,0:T(8,128)(2,1)}, u32[]{:S(2)}, u32[]{:S(2)}) %all-to-all-start) | async-done | bytes 4194336 | tf_op jit(solution)/shard_map/all_to_all | solution.py:96
  73.1 7.0 %fusion.23 = f32[1024,2048]{1,0:T(8,128)S(1)} fusion(bf16[1024,2048]{1,0:T(8,128)(2,1)} %bitcast.6, bf16[1,1024,1024]{2,1,0:T(8,128)(2,1)} %param.10, f32[1024]{0:T(1024)S(1)} %bitcast.79, f32[1024]{0:T(1024)S(1)} %add_rsqrt_fusion.2, f32[1024]{0:T(1024)S(1)} %broadcast_multiply_fusion.2), kind=kOutput, calls=%fused_computation.39 | convolution fusion | flops 4300210176 | bytes 14692352 | tf_op jit(solution)/shard_map/dot_general | solution.py:102
  80.1 2.7 %convert_reduce_fusion.2 = (f32[1024]{0:T(1024)S(1)}, bf16[1024,1024]{1,0:T(8,128)(2,1)S(1)}) fusion(f32[1024,2048]{1,0:T(8,128)S(1)} %fusion.23, pred[1024]{0:T(1024)(128)(4,1)S(1)} %iota_compare_fusion), kind=kLoop, calls=%fused_computation.36 | loop fusion | flops 8387584 | bytes 6296576 | tf_op jit(solution)/shard_map/reduce_sum | solution.py:117
  82.8 2.4 %fusion.26 = f32[1024,1024]{1,0:T(8,128)S(1)} fusion(bf16[1024,1024]{1,0:T(8,128)(2,1)S(1)} %get-tuple-element.12, f32[1024,2048]{1,0:T(8,128)S(1)} %fusion.23), kind=kOutput, calls=%fused_computation.41 | convolution fusion | flops 2147483648 | bytes 8388608 | tf_op jit(solution)/shard_map/dot_general | solution.py:107
  86.3 9.8 %all-to-all-start.1 = ((f32[32,33,128]{2,1,0:T(8,128)}), f32[32,33,128]{2,1,0:T(8,128)S(1)}, u32[]{:S(2)}, u32[]{:S(2)}) async-start(f32[32,33,128]{2,1,0:T(8,128)} %reshape.147), calls=%async_computation.1 | async-start | bytes 1310720 | tf_op jit(solution)/shard_map/all_to_all | solution.py:129
  98.8 18.5 %collective-permute-done.7 = f32[1024]{0:T(1024)S(1)} collective-permute-done((f32[1024]{0:T(1024)S(1)}, f32[1024]{0:T(1024)S(1)}, u32[]{:S(2)}, u32[]{:S(2)}) %collective-permute-start.7) | collective-permute-done | bytes 4128 | tf_op jit(solution)/shard_map/ppermute | solution.py:31
  118.0 5.0 %convert_reduce_fusion = (f32[1024]{0:T(1024)S(1)}, bf16[1024,1024]{0,1:T(8,128)(2,1)}) fusion(bf16[1024,1024]{0,1:T(8,128)(2,1)} %bitcast.67, bf16[1024,1024]{0,1:T(8,128)(2,1)} %collective-permute-done, bf16[1024,1024]{0,1:T(8,128)(2,1)} %collective-permute-done.1, bf16[1024,1024]{0,1:T(8,128)(2,1)} %collective-permute-done.2, pred[]{:T(512)S(6)} %eq.23, ...), kind=kLoop, calls=%fused_computation.9 | loop fusion | flops 5241856 | bytes 10489859 | tf_op jit(solution)/shard_map/reduce_sum | solution.py:10
  123.5 4.8 %collective-permute-done.4 = bf16[2,33,128]{2,1,0:T(8,128)(2,1)S(1)} collective-permute-done((bf16[2,33,128]{2,1,0:T(8,128)(2,1)S(1)}, bf16[2,33,128]{2,1,0:T(8,128)(2,1)S(1)}, u32[]{:S(2)}, u32[]{:S(2)}) %collective-permute-start.4) | collective-permute-done | bytes 16928 | tf_op jit(solution)/shard_map/ppermute | solution.py:48
  129.6 8.1 %all-to-all-start.2 = ((bf16[32,4,33,128]{3,1,2,0:T(4,128)(2,1)}), bf16[32,4,33,128]{3,1,2,0:T(4,128)(2,1)S(1)}, u32[]{:S(2)}, u32[]{:S(2)}) async-start(bf16[32,4,33,128]{3,1,2,0:T(4,128)(2,1)} %broadcast_in_dim.24), calls=%async_computation.2 | async-start | bytes 2162688 | tf_op jit(solution)/shard_map/all_to_all | solution.py:39
  137.7 2.2 %fusion.3 = f32[1024]{0:T(1024)S(1)} fusion(bf16[1024,1024]{0,1:T(8,128)(2,1)} %get-tuple-element.10, f32[1024]{0:T(1024)S(1)} %broadcast_multiply_fusion.1), kind=kLoop, calls=%fused_computation.14 | loop fusion | flops 4193280 | bytes 2105344 | tf_op jit(solution)/shard_map/reduce_sum | solution.py:12
  139.9 6.2 %fusion.21 = bf16[1024,1024]{1,0:T(8,128)(2,1)S(1)} fusion(bf16[1024,1024]{1,0:T(8,128)(2,1)} %param.15, bf16[1024,1024]{0,1:T(8,128)(2,1)} %get-tuple-element.10, f32[1024]{0:T(1024)S(1)} %select_select_fusion.1, f32[1024]{0:T(1024)S(1)} %add_rsqrt_fusion.1, f32[1024]{0:T(1024)S(1)} %broadcast_multiply_fusion.1), kind=kOutput, calls=%fused_computation.32 | convolution fusion | flops 2157969408 | bytes 6303744 | tf_op jit(solution)/shard_map/dot_general | solution.py:140
  146.2 1.3 copy-done.4
  147.5 1.9 copy.50
  149.4 3.4 %all-to-all-done.2 = bf16[32,4,33,128]{3,1,2,0:T(4,128)(2,1)S(1)} async-done(((bf16[32,4,33,128]{3,1,2,0:T(4,128)(2,1)}), bf16[32,4,33,128]{3,1,2,0:T(4,128)(2,1)S(1)}, u32[]{:S(2)}, u32[]{:S(2)}) %all-to-all-start.2) | async-done | bytes 1081376 | tf_op jit(solution)/shard_map/all_to_all | solution.py:39
  152.8 2.4 %fusion.51 = f32[4,1024,8]{1,0,2:T(4,128)S(1)} fusion(bf16[4,1056,128]{2,0,1:T(4,128)(2,1)S(1)} %bitcast.68, bf16[1024,1024]{1,0:T(8,128)(2,1)} %copy-done.4), kind=kOutput, calls=%fused_computation.65 | convolution fusion | flops 8388608 | bytes 3309568 | tf_op jit(solution)/shard_map/rhk,shk->srh/dot_general | solution.py:146
  155.6 3.5 %fusion = bf16[1024,8,128]{0,2,1:T(8,128)(2,1)S(1)} fusion(f32[4,1024,8]{1,0,2:T(4,128)S(1)} %fusion.51, bf16[1024,8,128,1]{2,1,0,3:T(8,128)(2,1)S(1)} %bitcast.73, bf16[4,8,128,128]{3,0,2,1:T(4,128)(2,1)S(1)} %bitcast.74), kind=kOutput, calls=%fused_computation.1 | convolution fusion | flops 1081081856 | bytes 5373952 | tf_op jit(solution)/shard_map/rhk,shkv->srhv/dot_general | solution.py:143
  159.1 2.6 %fusion.64 = (f32[1024]{0:T(1024)S(1)}, f32[1024,1024]{0,1:T(8,128)S(1)}) fusion(bf16[1024,1024]{0,1:T(8,128)(2,1)S(1)} %bitcast.83, bf16[1024,1024]{1,0:T(8,128)(2,1)S(1)} %copy-done, bf16[1024,1024]{0,1:T(8,128)(2,1)S(1)} %copy-done.1), kind=kOutput, calls=%fused_computation.98 | convolution fusion | flops 2150628352 | bytes 10489856 | tf_op jit(solution)/shard_map/dot_general | solution.py:152
  161.8 1.9 copy-done.2
  164.2 10.7 %fusion.28 = f32[1024,1024]{0,1:T(8,128)} fusion(bf16[1024,1024]{1,0:T(8,128)(2,1)} %param.19, bf16[1024,1024]{1,0:T(8,128)(2,1)} %param.18, f32[1024,1024]{0,1:T(8,128)} %copy-done.2, f32[1024]{0:T(1024)S(1)} %copy-done.9, f32[1024]{0:T(1024)S(1)} %add_rsqrt_fusion, f32[1024]{0:T(1024)S(1)} %broadcast_multiply_fusion), kind=kOutput, calls=%fused_computation.43 | convolution fusion | flops 4308598784 | bytes 12595200 | tf_op jit(solution)/shard_map/dot_general | solution.py:159
  174.9 1.7 fusion.54
  176.8 2.8 %collective-permute-done.8 = bf16[1024,2,256]{0,2,1:T(8,128)(2,1)} collective-permute-done((bf16[1024,2,256]{0,2,1:T(8,128)(2,1)S(1)}, bf16[1024,2,256]{0,2,1:T(8,128)(2,1)}, u32[]{:S(2)}, u32[]{:S(2)}) %collective-permute-start.8) | collective-permute-done | bytes 1048608 | tf_op jit(solution)/shard_map/ppermute | solution.py:64
  179.6 2.2 %bitcast_add_fusion = f32[1024,2,256]{0,2,1:T(8,128)S(1)} fusion(bf16[1024,2,256]{0,2,1:T(8,128)(2,1)} %collective-permute-done.8, f32[1024,2,2,256]{0,3,2,1:T(8,128)} %bitcast.71, s32[]{:T(128)S(6)} %select_n.138), kind=kLoop, calls=%fused_computation.49 | loop fusion | flops 1048576 | bytes 5242884 | tf_op jit(solution)/shard_map/add | solution.py:65
  181.8 1.3 copy-done.3
  184.2 14.6 %collective-permute-done.9 = bf16[1024,256]{0,1:T(8,128)(2,1)S(1)} collective-permute-done((bf16[1024,256]{0,1:T(8,128)(2,1)S(1)}, bf16[1024,256]{0,1:T(8,128)(2,1)S(1)}, u32[]{:S(2)}, u32[]{:S(2)}) %collective-permute-start.9) | collective-permute-done | bytes 524320 | tf_op jit(solution)/shard_map/ppermute | solution.py:69
  198.7 1.8 fusion.56
  (61 shorter events, 10.5 us)
Async XLA Ops:
  0.0 159.1 %copy-start = (bf16[1024,1024]{1,0:T(8,128)(2,1)S(1)}, bf16[1024,1024]{1,0:T(8,128)(2,1)}, u32[]{:S(2)}) copy-start(bf16[1024,1024]{1,0:T(8,128)(2,1)} %param.16) | copy-start | bytes 6291460
  0.0 4.1 %copy-start.6 = (bf16[1,32,1024]{2,1,0:T(8,128)(2,1)S(1)}, bf16[1,32,1024]{2,1,0:T(8,128)(2,1)}, u32[]{:S(2)}) copy-start(bf16[1,32,1024]{2,1,0:T(8,128)(2,1)} %param.14) | copy-start | bytes 196612
  0.0 4.1 %copy-start.7 = (bf16[1,32,1024]{2,1,0:T(8,128)(2,1)S(1)}, bf16[1,32,1024]{2,1,0:T(8,128)(2,1)}, u32[]{:S(2)}) copy-start(bf16[1,32,1024]{2,1,0:T(8,128)(2,1)} %param.13) | copy-start | bytes 196612
  6.6 66.5 %all-to-all-start = ((bf16[32,32,2048]{2,1,0:T(8,128)(2,1)}), bf16[32,32,2048]{2,1,0:T(8,128)(2,1)}, u32[]{:S(2)}, u32[]{:S(2)}) async-start(bf16[32,32,2048]{2,1,0:T(8,128)(2,1)} %broadcast_in_dim.20), calls=%async_computation | async-start | bytes 8388608 | tf_op jit(solution)/shard_map/all_to_all | solution.py:96
  15.4 57.7 %copy-start.8 = (f32[1,1024]{1,0:T(1,128)S(1)}, f32[1,1024]{1,0:T(1,128)}, u32[]{:S(2)}) copy-start(f32[1,1024]{1,0:T(1,128)} %param.12) | copy-start | bytes 12292
  15.5 8.8 %collective-permute-start.1 = (bf16[1024,1024]{0,1:T(8,128)(2,1)}, bf16[1024,1024]{0,1:T(8,128)(2,1)}, u32[]{:S(2)}, u32[]{:S(2)}) collective-permute-start(bf16[1024,1024]{0,1:T(8,128)(2,1)} %bitcast.65), channel_id=1, source_target_pairs={{96,32},{97,33},{98,34},{99,35},{100,36},{101,37},{102,38},{103,39... | collective-permute-start | bytes 6291464 | tf_op jit(solution)/shard_map/ppermute | solution.py:29
  17.5 100.5 %collective-permute-start = (bf16[1024,1024]{0,1:T(8,128)(2,1)}, bf16[1024,1024]{0,1:T(8,128)(2,1)}, u32[]{:S(2)}, u32[]{:S(2)}) collective-permute-start(bf16[1024,1024]{0,1:T(8,128)(2,1)} %bitcast.66), channel_id=1, source_target_pairs={{96,64},{97,65},{98,66},{99,67},{100,68},{101,69},{102,70},{103,71... | collective-permute-start | bytes 6291464 | tf_op jit(solution)/shard_map/ppermute | solution.py:30
  24.3 93.7 %collective-permute-start.2 = (bf16[1024,1024]{0,1:T(8,128)(2,1)}, bf16[1024,1024]{0,1:T(8,128)(2,1)}, u32[]{:S(2)}, u32[]{:S(2)}) collective-permute-start(bf16[1024,1024]{0,1:T(8,128)(2,1)} %collective-permute-done.1), channel_id=1, source_target_pairs={{32,0},{33,1},{34,2},{35,3},{36,4},{37,5},{38,6},{39,7},{40,8},{41... | collective-permute-start | bytes 6291464 | tf_op jit(solution)/shard_map/ppermute | solution.py:31
  86.3 31.0 %all-to-all-start.1 = ((f32[32,33,128]{2,1,0:T(8,128)}), f32[32,33,128]{2,1,0:T(8,128)S(1)}, u32[]{:S(2)}, u32[]{:S(2)}) async-start(f32[32,33,128]{2,1,0:T(8,128)} %reshape.147), calls=%async_computation.1 | async-start | bytes 1310720 | tf_op jit(solution)/shard_map/all_to_all | solution.py:129
  96.1 1.3 collective-permute-start.6
  96.8 2.0 %collective-permute-start.5 = (f32[1024]{0:T(1024)S(1)}, f32[1024]{0:T(1024)S(1)}, u32[]{:S(2)}, u32[]{:S(2)}) collective-permute-start(f32[1024]{0:T(1024)S(1)} %bitcast.81), channel_id=1, source_target_pairs={{96,64},{97,65},{98,66},{99,67},{100,68},{101,69},{102,70},{103,71... | collective-permute-start | bytes 12296 | tf_op jit(solution)/shard_map/ppermute | solution.py:30
  97.5 19.8 %collective-permute-start.7 = (f32[1024]{0:T(1024)S(1)}, f32[1024]{0:T(1024)S(1)}, u32[]{:S(2)}, u32[]{:S(2)}) collective-permute-start(f32[1024]{0:T(1024)S(1)} %collective-permute-done.6), channel_id=1, source_target_pairs={{32,0},{33,1},{34,2},{35,3},{36,4},{37,5},{38,6},{39,7},{40,8},{41... | collective-permute-start | bytes 12296 | tf_op jit(solution)/shard_map/ppermute | solution.py:31
  117.3 5.6 %collective-permute-start.3 = (bf16[33,128]{1,0:T(8,128)(2,1)S(1)}, bf16[33,128]{1,0:T(8,128)(2,1)S(1)}, u32[]{:S(2)}, u32[]{:S(2)}) collective-permute-start(bf16[33,128]{1,0:T(8,128)(2,1)S(1)} %reduce_sum.84), channel_id=1, source_target_pairs={{0,32},{32,0},{64,96},{96,64},{1,33},{33,1},{65,97},{97,65},{2,34}... | collective-permute-start | bytes 25352 | tf_op jit(solution)/shard_map/ppermute | solution.py:45
  122.9 5.4 %collective-permute-start.4 = (bf16[2,33,128]{2,1,0:T(8,128)(2,1)S(1)}, bf16[2,33,128]{2,1,0:T(8,128)(2,1)S(1)}, u32[]{:S(2)}, u32[]{:S(2)}) collective-permute-start(bf16[2,33,128]{2,1,0:T(8,128)(2,1)S(1)} %maximum_select_fusion.1), channel_id=1, source_target_pairs={{0,64},{64,0},{32,96},{96,32},{1,65},{65,1},{33,97},{97,33},{2,66}... | collective-permute-start | bytes 50696 | tf_op jit(solution)/shard_map/ppermute | solution.py:48
  129.6 23.2 %all-to-all-start.2 = ((bf16[32,4,33,128]{3,1,2,0:T(4,128)(2,1)}), bf16[32,4,33,128]{3,1,2,0:T(4,128)(2,1)S(1)}, u32[]{:S(2)}, u32[]{:S(2)}) async-start(bf16[32,4,33,128]{3,1,2,0:T(4,128)(2,1)} %broadcast_in_dim.24), calls=%async_computation.2 | async-start | bytes 2162688 | tf_op jit(solution)/shard_map/all_to_all | solution.py:39
  146.2 1.3 copy-start.4
  152.8 2.8 %copy-start.5 = (bf16[128,8,8,128]{3,2,1,0:T(8,128)(2,1)S(1)}, bf16[128,8,8,128]{3,2,1,0:T(8,128)(2,1)}, u32[]{:S(2)}) copy-start(bf16[128,8,8,128]{3,2,1,0:T(8,128)(2,1)} %copy.50) | copy-start | bytes 6291460
  155.6 3.5 %copy-start.1 = (bf16[1024,1024]{0,1:T(8,128)(2,1)S(1)}, bf16[1024,1024]{0,1:T(8,128)(2,1)}, u32[]{:S(2)}) copy-start(bf16[1024,1024]{0,1:T(8,128)(2,1)} %get-tuple-element.10) | copy-start | bytes 6291460
  161.8 1.9 copy-start.2
  161.8 2.4 %copy-start.9 = (f32[1024]{0:T(1024)S(1)}, f32[1024]{0:T(1024)}, u32[]{:S(2)}) copy-start(f32[1024]{0:T(1024)} %param.17) | copy-start | bytes 12292
  176.7 2.9 %collective-permute-start.8 = (bf16[1024,2,256]{0,2,1:T(8,128)(2,1)S(1)}, bf16[1024,2,256]{0,2,1:T(8,128)(2,1)}, u32[]{:S(2)}, u32[]{:S(2)}) collective-permute-start(bf16[1024,2,256]{0,2,1:T(8,128)(2,1)S(1)} %fusion.54), channel_id=1, source_target_pairs={{0,32},{32,0},{64,96},{96,64},{1,33},{33,1},{65,97},{97,65},{2,34}... | collective-permute-start | bytes 3145736 | tf_op jit(solution)/shard_map/ppermute | solution.py:64
  181.8 1.3 copy-start.3
  183.2 15.5 %collective-permute-start.9 = (bf16[1024,256]{0,1:T(8,128)(2,1)S(1)}, bf16[1024,256]{0,1:T(8,128)(2,1)S(1)}, u32[]{:S(2)}, u32[]{:S(2)}) collective-permute-start(bf16[1024,256]{0,1:T(8,128)(2,1)S(1)} %fusion.58), channel_id=1, source_target_pairs={{0,64},{64,0},{32,96},{96,32},{1,65},{65,1},{33,97},{97,33},{2,66}... | collective-permute-start | bytes 1572872 | tf_op jit(solution)/shard_map/ppermute | solution.py:69

commit v16 on v13

--- a/solution.py
+++ b/solution.py
@@ -97,11 +97,14 @@
     query_gain = from_last(input_gain[0], "sec", sections)
 
     normed = layer_normalizer(block.astype(jnp.float32), input_gain[0]).astype(jnp.bfloat16)
-    projected = jnp.dot(normed, weights, preferred_element_type=jnp.float32)
     valid = jnp.arange(rows) < counts[0, 0]
-    key_feats = feature_map(projected[:, :width]).astype(jnp.bfloat16)
+    key_feats = feature_map(
+        jnp.dot(normed, weights[:, :width], preferred_element_type=jnp.float32)
+    ).astype(jnp.bfloat16)
     key_feats = jnp.where(valid[:, None], key_feats, jnp.zeros_like(key_feats))
-    value_rows = projected[:, width:].astype(jnp.bfloat16)
+    value_rows = jnp.dot(normed, weights[:, width:], preferred_element_type=jnp.float32).astype(
+        jnp.bfloat16
+    )
     crossed = lax.dot_general(
         key_feats, value_rows, (((0,), (0,)), ((), ())), preferred_element_type=jnp.float32
     )

time: 200 us -> 212 us (1.060)
  matrix products: 34.9 us -> 43 us
  local copies, waits for them, and re-layouts: 18.6 us -> 25.2 us
  other arithmetic: 17 us -> 14.5 us
    dot_general x1, matrix products: 2.45 us -> 9.63 us  [on_device(): lax.dot_general(key_feats, value_rows, (((0,), (0,)), ((), ())), preferre...]
    unnamed x31, local copies, waits for them, and re-layouts: 10.7 us -> 17.4 us
    reduce_sum x1 -> x0, other arithmetic: 2.66 us -> none  [on_device(): jnp.sum(key_feats.astype(jnp.float32), axis=0).reshape(heads, HEAD_DIM)]
where the time goes in v16:
time: 212 us; the launch traced here: 210 us
  waiting for transfers between devices  93.1 us (44%)
  matrix products  43 us (20%)
  starting transfers between devices  32.9 us (16%)
  local copies, waits for them, and re-layouts  25.2 us (12%)
  other arithmetic  14.5 us (7%)
    ppermute x2, waiting for transfers between devices, from_last(): farther = lax.ppermute(far, axis, [(1, 0)])  57.9 us
    unnamed x31, local copies, waits for them, and re-layouts  17.4 us
    ppermute x1, waiting for transfers between devices, scatter_sum(): lax.ppermute(other.astype(jnp.bfloat16), 'sec', [(0, 2), (2, 0), (1, 3),...  14.7 us
    all_to_all x2, starting transfers between devices, gather_a2a(): return lax.all_to_all(spread, axis, 0, 0, tiled=False)  14.5 us
    dot_general x1, matrix products, on_device(): term = jnp.dot(hidden, down_weight, preferred_element_type=jnp.float32)  10.7 us
    dot_general x1, matrix products, on_device(): lax.dot_general(key_feats, value_rows, (((0,), (0,)), ((), ())), preferre...  9.63 us
    all_to_all x1, waiting for transfers between devices, on_device(): reduced = jnp.sum(lax.all_to_all(packed, 'pts', 0, 0, tiled=False), axis=0)  8.74 us
    all_to_all x1, starting transfers between devices, on_device(): reduced = jnp.sum(lax.all_to_all(packed, 'pts', 0, 0, tiled=False), axis=0)  8.52 us
  transfers between devices with their start and end apart: 13, of which 7 were waited for; matrix products, arithmetic and copies ran while one was open for 10% of the time, Pallas kernels for 0%

profile of v16, /device:TPU:16, one launch (start us, length us, event | category | flops | bytes accessed | tf_op | source)
XLA Modules:
  0.0 209.7 jit_solution(186925652363274197)
XLA Ops:
  0.0 4.1 %copy.29 = bf16[1,1024,1024]{1,2,0:T(8,128)(2,1)} copy(bf16[1,1024,1024]{2,1,0:T(8,128)(2,1)} %param.10) | data formatting | bytes 4194304 | tf_op args[0]
  4.1 2.0 collective-permute-start.1
  6.1 2.5 %broadcast_in_dim.21 = bf16[32,32,2048]{2,1,0:T(8,128)(2,1)} broadcast(bf16[32,2048]{1,0:T(8,128)(2,1)S(1)} %pad_maximum_fusion), dimensions={1,2} | broadcast | bytes 4325376 | tf_op jit(solution)/shard_map/broadcast_in_dim | solution.py:38
  8.6 8.8 %all-to-all-start = ((bf16[32,32,2048]{2,1,0:T(8,128)(2,1)}), bf16[32,32,2048]{2,1,0:T(8,128)(2,1)}, u32[]{:S(2)}, u32[]{:S(2)}) async-start(bf16[32,32,2048]{2,1,0:T(8,128)(2,1)} %broadcast_in_dim.21), calls=%async_computation | async-start | bytes 8388608 | tf_op jit(solution)/shard_map/all_to_all | solution.py:39
  17.5 2.0 collective-permute-start
  19.4 1.3 collective-permute-start.2
  21.4 2.0 convert_reduce_fusion.1
  23.4 57.9 %collective-permute-done.2 = bf16[1024,1024]{0,1:T(8,128)(2,1)} collective-permute-done((bf16[1024,1024]{0,1:T(8,128)(2,1)}, bf16[1024,1024]{0,1:T(8,128)(2,1)}, u32[]{:S(2)}, u32[]{:S(2)}) %collective-permute-start.2) | collective-permute-done | bytes 2097184 | tf_op jit(solution)/shard_map/ppermute | solution.py:31
  81.3 5.7 %convert_reduce_fusion = (f32[1024]{0:T(1024)S(1)}, bf16[1024,1024]{0,1:T(8,128)(2,1)}, f32[1024]{0:T(1024)S(1)}) fusion(bf16[1024,1024]{0,1:T(8,128)(2,1)} %collective-permute-done, bf16[1024,1024]{0,1:T(8,128)(2,1)} %collective-permute-done.1, bf16[1024,1024]{0,1:T(8,128)(2,1)} %collective-permute-done.2, pred[]{:T(512)S(6)} %eq.23, pred[]{:T(512)S(6)} %eq.22, ...), kind=kLoop, calls=%fused_computation.9 | loop fusion | flops 9435136 | bytes 10498051 | tf_op jit(solution)/shard_map/reduce_sum | solution.py:10
  87.0 7.9 %convert_reduce_fusion.2 = (f32[1024]{0:T(1024)S(1)}, bf16[1024,1024]{1,0:T(8,128)(2,1)}) fusion(bf16[1024,2048]{1,0:T(8,128)(2,1)} %bitcast.5, f32[1024]{0:T(1024)S(1)} %bitcast.87, f32[1024]{0:T(1024)S(1)} %add_rsqrt_fusion.2, f32[1024]{0:T(1024)S(1)} %broadcast_multiply_fusion.2, bf16[1,1024,1024]{1,2,0:T(8,128)(2,1)} %copy.29, ...), kind=kOutput, calls=%fused_computation.38 | convolution fusion | flops 2161114112 | bytes 6308864 | tf_op jit(solution)/shard_map/dot_general | solution.py:102
  94.9 9.6 %fusion.48 = f32[1024,1024]{1,0:T(8,128)} fusion(bf16[1024,1024]{1,0:T(8,128)(2,1)} %get-tuple-element.9, bf16[1024,2048]{1,0:T(8,128)(2,1)} %bitcast.5, f32[1024]{0:T(1024)S(1)} %bitcast.88, f32[1024]{0:T(1024)S(1)} %add_rsqrt_fusion.2, f32[1024]{0:T(1024)S(1)} %broadcast_multiply_fusion.2, bf16[1,1024,1024]{1,2,0:T(8,128)(2,1)} %copy.29), kind=kOutput, calls=%fused_computation.62 | convolution fusion | flops 4301258752 | bytes 10498048 | tf_op jit(solution)/shard_map/dot_general | solution.py:108
  112.2 8.5 %all-to-all-start.1 = ((f32[32,33,128]{2,1,0:T(8,128)}), f32[32,33,128]{2,1,0:T(8,128)S(1)}, u32[]{:S(2)}, u32[]{:S(2)}) async-start(f32[32,33,128]{2,1,0:T(8,128)} %reshape.126), calls=%async_computation.1 | async-start | bytes 1310720 | tf_op jit(solution)/shard_map/all_to_all | solution.py:130
  122.3 1.3 collective-permute-start.7
  123.6 8.7 %all-to-all-done.1 = f32[32,33,128]{2,1,0:T(8,128)S(1)} async-done(((f32[32,33,128]{2,1,0:T(8,128)}), f32[32,33,128]{2,1,0:T(8,128)S(1)}, u32[]{:S(2)}, u32[]{:S(2)}) %all-to-all-start.1) | async-done | bytes 540704 | tf_op jit(solution)/shard_map/all_to_all | solution.py:130
  134.5 4.5 %collective-permute-done.4 = bf16[2,33,128]{2,1,0:T(8,128)(2,1)S(1)} collective-permute-done((bf16[2,33,128]{2,1,0:T(8,128)(2,1)S(1)}, bf16[2,33,128]{2,1,0:T(8,128)(2,1)S(1)}, u32[]{:S(2)}, u32[]{:S(2)}) %collective-permute-start.4) | collective-permute-done | bytes 16928 | tf_op jit(solution)/shard_map/ppermute | solution.py:48
  140.3 5.6 %all-to-all-start.2 = ((bf16[32,4,33,128]{3,1,2,0:T(4,128)(2,1)}), bf16[32,4,33,128]{3,1,2,0:T(4,128)(2,1)S(1)}, u32[]{:S(2)}, u32[]{:S(2)}) async-start(bf16[32,4,33,128]{3,1,2,0:T(4,128)(2,1)} %broadcast_in_dim.24), calls=%async_computation.2 | async-start | bytes 2162688 | tf_op jit(solution)/shard_map/all_to_all | solution.py:39
  146.0 2.2 %fusion.5 = f32[1024]{0:T(1024)S(1)} fusion(bf16[1024,1024]{0,1:T(8,128)(2,1)} %get-tuple-element.6, f32[1024]{0:T(1024)S(1)} %broadcast_multiply_fusion.1), kind=kLoop, calls=%fused_computation.16 | loop fusion | flops 4193280 | bytes 2105344 | tf_op jit(solution)/shard_map/reduce_sum | solution.py:12
  148.2 6.2 %fusion.24 = bf16[1024,1024]{1,0:T(8,128)(2,1)S(1)} fusion(bf16[1024,1024]{1,0:T(8,128)(2,1)} %param.15, bf16[1024,1024]{0,1:T(8,128)(2,1)} %get-tuple-element.6, f32[1024]{0:T(1024)S(1)} %select_select_fusion.1, f32[1024]{0:T(1024)S(1)} %add_rsqrt_fusion.1, f32[1024]{0:T(1024)S(1)} %broadcast_multiply_fusion.1), kind=kOutput, calls=%fused_computation.35 | convolution fusion | flops 2157969408 | bytes 6303744 | tf_op jit(solution)/shard_map/dot_general | solution.py:141
  154.4 1.3 copy-done.4
  155.7 1.9 copy.50
  157.6 3.3 %all-to-all-done.2 = bf16[32,4,33,128]{3,1,2,0:T(4,128)(2,1)S(1)} async-done(((bf16[32,4,33,128]{3,1,2,0:T(4,128)(2,1)}), bf16[32,4,33,128]{3,1,2,0:T(4,128)(2,1)S(1)}, u32[]{:S(2)}, u32[]{:S(2)}) %all-to-all-start.2) | async-done | bytes 1081376 | tf_op jit(solution)/shard_map/all_to_all | solution.py:39
  161.0 2.4 %fusion.55 = f32[4,1024,8]{1,0,2:T(4,128)S(1)} fusion(bf16[4,1056,128]{2,0,1:T(4,128)(2,1)S(1)} %bitcast.76, bf16[1024,1024]{1,0:T(8,128)(2,1)} %copy-done.4), kind=kOutput, calls=%fused_computation.66 | convolution fusion | flops 8388608 | bytes 3309568 | tf_op jit(solution)/shard_map/rhk,shk->srh/dot_general | solution.py:147
  163.8 3.5 %fusion = bf16[1024,8,128]{0,2,1:T(8,128)(2,1)S(1)} fusion(f32[4,1024,8]{1,0,2:T(4,128)S(1)} %fusion.55, bf16[1024,8,128,1]{2,1,0,3:T(8,128)(2,1)S(1)} %bitcast.81, bf16[4,8,128,128]{3,0,2,1:T(4,128)(2,1)S(1)} %bitcast.82), kind=kOutput, calls=%fused_computation.1 | convolution fusion | flops 1081081856 | bytes 5373952 | tf_op jit(solution)/shard_map/rhk,shkv->srhv/dot_general | solution.py:144
  167.3 2.6 %fusion.77 = (f32[1024]{0:T(1024)S(1)}, f32[1024,1024]{0,1:T(8,128)S(1)}) fusion(bf16[1024,1024]{0,1:T(8,128)(2,1)S(1)} %bitcast.92, bf16[1024,1024]{1,0:T(8,128)(2,1)S(1)} %copy-done, bf16[1024,1024]{0,1:T(8,128)(2,1)S(1)} %copy-done.1), kind=kOutput, calls=%fused_computation.101 | convolution fusion | flops 2150628352 | bytes 10489856 | tf_op jit(solution)/shard_map/dot_general | solution.py:153
  170.0 1.9 copy-done.2
  172.4 10.7 %fusion.27 = f32[1024,1024]{0,1:T(8,128)} fusion(bf16[1024,1024]{1,0:T(8,128)(2,1)} %param.19, bf16[1024,1024]{1,0:T(8,128)(2,1)} %param.18, f32[1024,1024]{0,1:T(8,128)} %copy-done.2, f32[1024]{0:T(1024)S(1)} %copy-done.9, f32[1024]{0:T(1024)S(1)} %add_rsqrt_fusion, f32[1024]{0:T(1024)S(1)} %broadcast_multiply_fusion), kind=kOutput, calls=%fused_computation.41 | convolution fusion | flops 4308598784 | bytes 12595200 | tf_op jit(solution)/shard_map/dot_general | solution.py:160
  183.1 1.7 fusion.62
  185.0 2.8 %collective-permute-done.8 = bf16[1024,2,256]{0,2,1:T(8,128)(2,1)} collective-permute-done((bf16[1024,2,256]{0,2,1:T(8,128)(2,1)S(1)}, bf16[1024,2,256]{0,2,1:T(8,128)(2,1)}, u32[]{:S(2)}, u32[]{:S(2)}) %collective-permute-start.8) | collective-permute-done | bytes 1048608 | tf_op jit(solution)/shard_map/ppermute | solution.py:64
  187.7 2.2 %bitcast_add_fusion = f32[1024,2,256]{0,2,1:T(8,128)S(1)} fusion(bf16[1024,2,256]{0,2,1:T(8,128)(2,1)} %collective-permute-done.8, f32[1024,2,2,256]{0,3,2,1:T(8,128)} %bitcast.79, s32[]{:T(128)S(6)} %select_n.138), kind=kLoop, calls=%fused_computation.51 | loop fusion | flops 1048576 | bytes 5242884 | tf_op jit(solution)/shard_map/add | solution.py:65
  190.0 1.3 copy-done.3
  192.2 14.7 %collective-permute-done.9 = bf16[1024,256]{0,1:T(8,128)(2,1)S(1)} collective-permute-done((bf16[1024,256]{0,1:T(8,128)(2,1)S(1)}, bf16[1024,256]{0,1:T(8,128)(2,1)S(1)}, u32[]{:S(2)}, u32[]{:S(2)}) %collective-permute-start.9) | collective-permute-done | bytes 524320 | tf_op jit(solution)/shard_map/ppermute | solution.py:69
  206.9 1.8 fusion.64
  (59 shorter events, 15.6 us)
Async XLA Ops:
  0.0 167.3 %copy-start = (bf16[1024,1024]{1,0:T(8,128)(2,1)S(1)}, bf16[1024,1024]{1,0:T(8,128)(2,1)}, u32[]{:S(2)}) copy-start(bf16[1024,1024]{1,0:T(8,128)(2,1)} %param.16) | copy-start | bytes 6291460
  0.0 6.1 %copy-start.6 = (bf16[1,32,1024]{2,1,0:T(8,128)(2,1)S(1)}, bf16[1,32,1024]{2,1,0:T(8,128)(2,1)}, u32[]{:S(2)}) copy-start(bf16[1,32,1024]{2,1,0:T(8,128)(2,1)} %param.14) | copy-start | bytes 196612
  0.0 6.1 %copy-start.7 = (bf16[1,32,1024]{2,1,0:T(8,128)(2,1)S(1)}, bf16[1,32,1024]{2,1,0:T(8,128)(2,1)}, u32[]{:S(2)}) copy-start(bf16[1,32,1024]{2,1,0:T(8,128)(2,1)} %param.13) | copy-start | bytes 196612
  4.1 15.3 %collective-permute-start.1 = (bf16[1024,1024]{0,1:T(8,128)(2,1)}, bf16[1024,1024]{0,1:T(8,128)(2,1)}, u32[]{:S(2)}, u32[]{:S(2)}) collective-permute-start(bf16[1024,1024]{0,1:T(8,128)(2,1)} %bitcast.74), channel_id=1, source_target_pairs={{96,32},{97,33},{98,34},{99,35},{100,36},{101,37},{102,38},{103,39... | collective-permute-start | bytes 6291464 | tf_op jit(solution)/shard_map/ppermute | solution.py:29
  8.6 78.4 %all-to-all-start = ((bf16[32,32,2048]{2,1,0:T(8,128)(2,1)}), bf16[32,32,2048]{2,1,0:T(8,128)(2,1)}, u32[]{:S(2)}, u32[]{:S(2)}) async-start(bf16[32,32,2048]{2,1,0:T(8,128)(2,1)} %broadcast_in_dim.21), calls=%async_computation | async-start | bytes 8388608 | tf_op jit(solution)/shard_map/all_to_all | solution.py:39
  17.5 5.9 %collective-permute-start = (bf16[1024,1024]{0,1:T(8,128)(2,1)}, bf16[1024,1024]{0,1:T(8,128)(2,1)}, u32[]{:S(2)}, u32[]{:S(2)}) collective-permute-start(bf16[1024,1024]{0,1:T(8,128)(2,1)} %bitcast.75), channel_id=1, source_target_pairs={{96,64},{97,65},{98,66},{99,67},{100,68},{101,69},{102,70},{103,71... | collective-permute-start | bytes 6291464 | tf_op jit(solution)/shard_map/ppermute | solution.py:30
  19.4 61.9 %collective-permute-start.2 = (bf16[1024,1024]{0,1:T(8,128)(2,1)}, bf16[1024,1024]{0,1:T(8,128)(2,1)}, u32[]{:S(2)}, u32[]{:S(2)}) collective-permute-start(bf16[1024,1024]{0,1:T(8,128)(2,1)} %collective-permute-done.1), channel_id=1, source_target_pairs={{32,0},{33,1},{34,2},{35,3},{36,4},{37,5},{38,6},{39,7},{40,8},{41... | collective-permute-start | bytes 6291464 | tf_op jit(solution)/shard_map/ppermute | solution.py:31
  23.4 63.7 %copy-start.8 = (f32[1,1024]{1,0:T(1,128)S(1)}, f32[1,1024]{1,0:T(1,128)}, u32[]{:S(2)}) copy-start(f32[1,1024]{1,0:T(1,128)} %param.12) | copy-start | bytes 12292
  112.2 20.1 %all-to-all-start.1 = ((f32[32,33,128]{2,1,0:T(8,128)}), f32[32,33,128]{2,1,0:T(8,128)S(1)}, u32[]{:S(2)}, u32[]{:S(2)}) async-start(f32[32,33,128]{2,1,0:T(8,128)} %reshape.126), calls=%async_computation.1 | async-start | bytes 1310720 | tf_op jit(solution)/shard_map/all_to_all | solution.py:130
  120.7 1.5 collective-permute-start.6
  121.6 10.9 %collective-permute-start.5 = (f32[1024]{0:T(1024)S(1)}, f32[1024]{0:T(1024)S(1)}, u32[]{:S(2)}, u32[]{:S(2)}) collective-permute-start(f32[1024]{0:T(1024)S(1)} %bitcast.90), channel_id=1, source_target_pairs={{96,64},{97,65},{98,66},{99,67},{100,68},{101,69},{102,70},{103,71... | collective-permute-start | bytes 12296 | tf_op jit(solution)/shard_map/ppermute | solution.py:30
  122.3 10.2 %collective-permute-start.7 = (f32[1024]{0:T(1024)S(1)}, f32[1024]{0:T(1024)S(1)}, u32[]{:S(2)}, u32[]{:S(2)}) collective-permute-start(f32[1024]{0:T(1024)S(1)} %collective-permute-done.6), channel_id=1, source_target_pairs={{32,0},{33,1},{34,2},{35,3},{36,4},{37,5},{38,6},{39,7},{40,8},{41... | collective-permute-start | bytes 12296 | tf_op jit(solution)/shard_map/ppermute | solution.py:31
  132.4 1.3 collective-permute-start.3
  133.7 5.4 %collective-permute-start.4 = (bf16[2,33,128]{2,1,0:T(8,128)(2,1)S(1)}, bf16[2,33,128]{2,1,0:T(8,128)(2,1)S(1)}, u32[]{:S(2)}, u32[]{:S(2)}) collective-permute-start(bf16[2,33,128]{2,1,0:T(8,128)(2,1)S(1)} %maximum_select_fusion.1), channel_id=1, source_target_pairs={{0,64},{64,0},{32,96},{96,32},{1,65},{65,1},{33,97},{97,33},{2,66}... | collective-permute-start | bytes 50696 | tf_op jit(solution)/shard_map/ppermute | solution.py:48
  140.3 20.6 %all-to-all-start.2 = ((bf16[32,4,33,128]{3,1,2,0:T(4,128)(2,1)}), bf16[32,4,33,128]{3,1,2,0:T(4,128)(2,1)S(1)}, u32[]{:S(2)}, u32[]{:S(2)}) async-start(bf16[32,4,33,128]{3,1,2,0:T(4,128)(2,1)} %broadcast_in_dim.24), calls=%async_computation.2 | async-start | bytes 2162688 | tf_op jit(solution)/shard_map/all_to_all | solution.py:39
  154.4 1.3 copy-start.4
  161.0 2.8 %copy-start.5 = (bf16[128,8,8,128]{3,2,1,0:T(8,128)(2,1)S(1)}, bf16[128,8,8,128]{3,2,1,0:T(8,128)(2,1)}, u32[]{:S(2)}) copy-start(bf16[128,8,8,128]{3,2,1,0:T(8,128)(2,1)} %copy.50) | copy-start | bytes 6291460
  163.7 3.5 %copy-start.1 = (bf16[1024,1024]{0,1:T(8,128)(2,1)S(1)}, bf16[1024,1024]{0,1:T(8,128)(2,1)}, u32[]{:S(2)}) copy-start(bf16[1024,1024]{0,1:T(8,128)(2,1)} %get-tuple-element.6) | copy-start | bytes 6291460
  169.9 1.9 copy-start.2
  170.0 2.4 %copy-start.9 = (f32[1024]{0:T(1024)S(1)}, f32[1024]{0:T(1024)}, u32[]{:S(2)}) copy-start(f32[1024]{0:T(1024)} %param.17) | copy-start | bytes 12292
  184.8 2.9 %collective-permute-start.8 = (bf16[1024,2,256]{0,2,1:T(8,128)(2,1)S(1)}, bf16[1024,2,256]{0,2,1:T(8,128)(2,1)}, u32[]{:S(2)}, u32[]{:S(2)}) collective-permute-start(bf16[1024,2,256]{0,2,1:T(8,128)(2,1)S(1)} %fusion.62), channel_id=1, source_target_pairs={{0,32},{32,0},{64,96},{96,64},{1,33},{33,1},{65,97},{97,65},{2,34}... | collective-permute-start | bytes 3145736 | tf_op jit(solution)/shard_map/ppermute | solution.py:64
  189.9 1.3 copy-start.3
  191.3 15.5 %collective-permute-start.9 = (bf16[1024,256]{0,1:T(8,128)(2,1)S(1)}, bf16[1024,256]{0,1:T(8,128)(2,1)S(1)}, u32[]{:S(2)}, u32[]{:S(2)}) collective-permute-start(bf16[1024,256]{0,1:T(8,128)(2,1)S(1)} %fusion.66), channel_id=1, source_target_pairs={{0,64},{64,0},{32,96},{96,32},{1,65},{65,1},{33,97},{97,33},{2,66}... | collective-permute-start | bytes 1572872 | tf_op jit(solution)/shard_map/ppermute | solution.py:69

commit v17 on v13

--- a/solution.py
+++ b/solution.py
@@ -93,7 +93,7 @@
     stacked = jnp.concatenate([key_weight[0], value_weight[0]], axis=1)
     weights = gather_a2a(stacked, "pts", blocks).reshape(width, 2 * width)
 
-    query_block = from_last(block, "sec", sections)
+    query_block = from_last(points, "sec", sections)[0]
     query_gain = from_last(input_gain[0], "sec", sections)
 
     normed = layer_normalizer(block.astype(jnp.float32), input_gain[0]).astype(jnp.bfloat16)

time: 200 us -> 201 us (level)
  waiting for transfers between devices: 93.1 us -> 87.5 us
  starting transfers between devices: 32.9 us -> 36.8 us
  other arithmetic: 17 us -> 19.7 us
    all_to_all x2, waiting for transfers between devices: 3.32 us -> 46.8 us  [gather_a2a(): return lax.all_to_all(spread, axis, 0, 0, tiled=False)]
    ppermute x2, waiting for transfers between devices: 57.9 us -> 18.5 us  [from_last(): farther = lax.ppermute(far, axis, [(1, 0)])]
    all_to_all x1, waiting for transfers between devices: 8.91 us -> 0.01 us  [on_device(): reduced = jnp.sum(lax.all_to_all(packed, 'pts', 0, 0, tiled=False), axis=0)]
    all_to_all x2, starting transfers between devices: 14.5 us -> 16.9 us  [gather_a2a(): return lax.all_to_all(spread, axis, 0, 0, tiled=False)]
    reduce_sum x2 -> x3, other arithmetic: 2.68 us -> 4.95 us  [layer_normalizer(): spread = jnp.mean(centred * centred, axis=-1, keepdims=True)]
    unnamed x31 -> x27, local copies, waits for them, and re-layouts: 10.7 us -> 10.6 us
  transfers between devices with their start and end apart: 13 -> 13, of which waited for: 7 -> 6; matrix products, arithmetic and copies ran while one was open for 10% -> 18% of each run, Pallas kernels for 0% -> 0%
where the time goes in v17:
time: 201 us; the launch traced here: 198 us
  waiting for transfers between devices  87.5 us (44%)
  starting transfers between devices  36.8 us (18%)
  matrix products  34.9 us (17%)
  other arithmetic  19.7 us (10%)
  local copies, waits for them, and re-layouts  18.4 us (9%)
    all_to_all x2, waiting for transfers between devices, gather_a2a(): return lax.all_to_all(spread, axis, 0, 0, tiled=False)  46.8 us
    ppermute x2, waiting for transfers between devices, from_last(): farther = lax.ppermute(far, axis, [(1, 0)])  18.5 us
    all_to_all x2, starting transfers between devices, gather_a2a(): return lax.all_to_all(spread, axis, 0, 0, tiled=False)  16.9 us
    ppermute x1, waiting for transfers between devices, scatter_sum(): lax.ppermute(other.astype(jnp.bfloat16), 'sec', [(0, 2), (2, 0), (1, 3),...  14.6 us
    dot_general x1, matrix products, on_device(): term = jnp.dot(hidden, down_weight, preferred_element_type=jnp.float32)  10.7 us
    unnamed x27, local copies, waits for them, and re-layouts  10.6 us
    all_to_all x1, starting transfers between devices, on_device(): reduced = jnp.sum(lax.all_to_all(packed, 'pts', 0, 0, tiled=False), axis=0)  9.79 us
    dot_general x1, matrix products, on_device(): projected = jnp.dot(normed, weights, preferred_element_type=jnp.float32)  7.03 us
  transfers between devices with their start and end apart: 13, of which 6 were waited for; matrix products, arithmetic and copies ran while one was open for 18% of the time, Pallas kernels for 0%

profile of v17, /device:TPU:16, one launch (start us, length us, event | category | flops | bytes accessed | tf_op | source)
XLA Modules:
  0.0 198.5 jit_solution(6711489557928542359)
XLA Ops:
  1.0 2.5 %broadcast_in_dim.21 = bf16[32,32,2048]{2,1,0:T(8,128)(2,1)} broadcast(bf16[32,2048]{1,0:T(8,128)(2,1)S(1)} %pad_maximum_fusion), dimensions={1,2} | broadcast | bytes 4325376 | tf_op jit(solution)/shard_map/broadcast_in_dim | solution.py:38
  3.5 8.8 %all-to-all-start = ((bf16[32,32,2048]{2,1,0:T(8,128)(2,1)}), bf16[32,32,2048]{2,1,0:T(8,128)(2,1)}, u32[]{:S(2)}, u32[]{:S(2)}) async-start(bf16[32,32,2048]{2,1,0:T(8,128)(2,1)} %broadcast_in_dim.21), calls=%async_computation | async-start | bytes 8388608 | tf_op jit(solution)/shard_map/all_to_all | solution.py:39
  12.4 4.0 %copy.35 = bf16[1,1024,1024]{1,2,0:T(8,128)(2,1)} copy(bf16[1,1024,1024]{2,1,0:T(8,128)(2,1)} %param.10) | data formatting | bytes 4194304 | tf_op args[0]
  16.3 2.0 collective-permute-start.1
  18.3 2.0 %collective-permute-start = (bf16[1,1024,1024]{1,2,0:T(8,128)(2,1)}, bf16[1,1024,1024]{1,2,0:T(8,128)(2,1)}, u32[]{:S(2)}, u32[]{:S(2)}) collective-permute-start(bf16[1,1024,1024]{1,2,0:T(8,128)(2,1)} %copy.35), channel_id=1, source_target_pairs={{96,64},{97,65},{98,66},{99,67},{100,68},{101,69},{102,70},{103,71... | collective-permute-start | bytes 6291464 | tf_op jit(solution)/shard_map/ppermute | solution.py:30
  21.0 1.9 convert_reduce_fusion
  23.0 2.3 %fusion.13 = f32[1024]{0:T(1024)S(1)} fusion(bf16[1,1024,1024]{2,1,0:T(8,128)(2,1)} %param.10, f32[1024]{0:T(1024)S(1)} %broadcast_multiply_fusion.2), kind=kLoop, calls=%fused_computation.24 | loop fusion | flops 4193280 | bytes 2105344 | tf_op jit(solution)/shard_map/reduce_sum | solution.py:12
  26.6 43.5 %all-to-all-done = bf16[32,32,2048]{2,1,0:T(8,128)(2,1)} async-done(((bf16[32,32,2048]{2,1,0:T(8,128)(2,1)}), bf16[32,32,2048]{2,1,0:T(8,128)(2,1)}, u32[]{:S(2)}, u32[]{:S(2)}) %all-to-all-start) | async-done | bytes 4194336 | tf_op jit(solution)/shard_map/all_to_all | solution.py:39
  70.0 7.0 %fusion.34 = f32[1024,2048]{1,0:T(8,128)S(1)} fusion(bf16[1024,2048]{1,0:T(8,128)(2,1)} %bitcast.7, bf16[1,1024,1024]{2,1,0:T(8,128)(2,1)} %param.10, f32[1024]{0:T(1024)S(1)} %bitcast.100, f32[1024]{0:T(1024)S(1)} %add_rsqrt_fusion.2, f32[1024]{0:T(1024)S(1)} %broadcast_multiply_fusion.2), kind=kOutput, calls=%fused_computation.48 | convolution fusion | flops 4300210176 | bytes 14692352 | tf_op jit(solution)/shard_map/dot_general | solution.py:100
  77.1 2.7 %convert_reduce_fusion.2 = (f32[1024]{0:T(1024)S(1)}, bf16[1024,1024]{1,0:T(8,128)(2,1)S(1)}) fusion(f32[1024,2048]{1,0:T(8,128)S(1)} %fusion.34, pred[1024]{0:T(1024)(128)(4,1)S(1)} %iota_compare_fusion), kind=kLoop, calls=%fused_computation.42 | loop fusion | flops 8387584 | bytes 6296576 | tf_op jit(solution)/shard_map/reduce_sum | solution.py:115
  79.7 2.4 %fusion.29 = f32[1024,1024]{1,0:T(8,128)S(1)} fusion(bf16[1024,1024]{1,0:T(8,128)(2,1)S(1)} %get-tuple-element.8, f32[1024,2048]{1,0:T(8,128)S(1)} %fusion.34), kind=kOutput, calls=%fused_computation.44 | convolution fusion | flops 2147483648 | bytes 8388608 | tf_op jit(solution)/shard_map/dot_general | solution.py:105
  83.2 9.8 %all-to-all-start.1 = ((f32[32,33,128]{2,1,0:T(8,128)}), f32[32,33,128]{2,1,0:T(8,128)S(1)}, u32[]{:S(2)}, u32[]{:S(2)}) async-start(f32[32,33,128]{2,1,0:T(8,128)} %reshape.149), calls=%async_computation.1 | async-start | bytes 1310720 | tf_op jit(solution)/shard_map/all_to_all | solution.py:127
  95.7 18.5 %collective-permute-done.7 = f32[1024]{0:T(1024)S(1)} collective-permute-done((f32[1024]{0:T(1024)S(1)}, f32[1024]{0:T(1024)S(1)}, u32[]{:S(2)}, u32[]{:S(2)}) %collective-permute-start.7) | collective-permute-done | bytes 4128 | tf_op jit(solution)/shard_map/ppermute | solution.py:31
  114.9 5.0 %convert_reduce_fusion.1 = (f32[1024]{0:T(1024)S(1)}, bf16[1,1024,1024]{1,2,0:T(8,128)(2,1)}) fusion(bf16[1,1024,1024]{1,2,0:T(8,128)(2,1)} %copy.35, bf16[1,1024,1024]{1,2,0:T(8,128)(2,1)} %collective-permute-done, bf16[1,1024,1024]{1,2,0:T(8,128)(2,1)} %collective-permute-done.1, bf16[1,1024,1024]{1,2,0:T(8,128)(2,1)} %collective-permute-done.2, ...), kind=kLoop, calls=%fused_computation.10 | loop fusion | flops 5241856 | bytes 10489859 | tf_op jit(solution)/shard_map/reduce_sum | solution.py:10
  120.4 4.8 %collective-permute-done.4 = bf16[2,33,128]{2,1,0:T(8,128)(2,1)S(1)} collective-permute-done((bf16[2,33,128]{2,1,0:T(8,128)(2,1)S(1)}, bf16[2,33,128]{2,1,0:T(8,128)(2,1)S(1)}, u32[]{:S(2)}, u32[]{:S(2)}) %collective-permute-start.4) | collective-permute-done | bytes 16928 | tf_op jit(solution)/shard_map/ppermute | solution.py:48
  126.6 8.1 %all-to-all-start.2 = ((bf16[32,4,33,128]{3,1,2,0:T(4,128)(2,1)}), bf16[32,4,33,128]{3,1,2,0:T(4,128)(2,1)S(1)}, u32[]{:S(2)}, u32[]{:S(2)}) async-start(bf16[32,4,33,128]{3,1,2,0:T(4,128)(2,1)} %broadcast_in_dim.24), calls=%async_computation.2 | async-start | bytes 2162688 | tf_op jit(solution)/shard_map/all_to_all | solution.py:39
  134.7 2.2 %fusion.5 = f32[1024]{0:T(1024)S(1)} fusion(bf16[1,1024,1024]{1,2,0:T(8,128)(2,1)} %get-tuple-element.6, f32[1024]{0:T(1024)S(1)} %broadcast_multiply_fusion.1), kind=kLoop, calls=%fused_computation.16 | loop fusion | flops 4193280 | bytes 2105344 | tf_op jit(solution)/shard_map/reduce_sum | solution.py:12
  136.9 6.2 %fusion.27 = bf16[1024,1024]{1,0:T(8,128)(2,1)S(1)} fusion(bf16[1024,1024]{1,0:T(8,128)(2,1)} %param.15, bf16[1,1024,1024]{1,2,0:T(8,128)(2,1)} %get-tuple-element.6, f32[1024]{0:T(1024)S(1)} %select_select_fusion.1, f32[1024]{0:T(1024)S(1)} %add_rsqrt_fusion.1, f32[1024]{0:T(1024)S(1)} %broadcast_multiply_fusion.1), kind=kOutput, calls=%fused_computation.38 | convolution fusion | flops 2157969408 | bytes 6303744 | tf_op jit(solution)/shard_map/dot_general | solution.py:138
  143.1 1.3 copy-done.4
  144.4 1.9 copy.56
  146.4 3.4 %all-to-all-done.2 = bf16[32,4,33,128]{3,1,2,0:T(4,128)(2,1)S(1)} async-done(((bf16[32,4,33,128]{3,1,2,0:T(4,128)(2,1)}), bf16[32,4,33,128]{3,1,2,0:T(4,128)(2,1)S(1)}, u32[]{:S(2)}, u32[]{:S(2)}) %all-to-all-start.2) | async-done | bytes 1081376 | tf_op jit(solution)/shard_map/all_to_all | solution.py:39
  149.8 2.4 %fusion.57 = f32[4,1024,8]{1,0,2:T(4,128)S(1)} fusion(bf16[4,1056,128]{2,0,1:T(4,128)(2,1)S(1)} %bitcast.89, bf16[1024,1024]{1,0:T(8,128)(2,1)} %copy-done.4), kind=kOutput, calls=%fused_computation.70 | convolution fusion | flops 8388608 | bytes 3309568 | tf_op jit(solution)/shard_map/rhk,shk->srh/dot_general | solution.py:144
  152.5 3.5 %fusion = bf16[1024,8,128]{0,2,1:T(8,128)(2,1)S(1)} fusion(f32[4,1024,8]{1,0,2:T(4,128)S(1)} %fusion.57, bf16[1024,8,128,1]{2,1,0,3:T(8,128)(2,1)S(1)} %bitcast.94, bf16[4,8,128,128]{3,0,2,1:T(4,128)(2,1)S(1)} %bitcast.95), kind=kOutput, calls=%fused_computation.1 | convolution fusion | flops 1081081856 | bytes 5373952 | tf_op jit(solution)/shard_map/rhk,shkv->srhv/dot_general | solution.py:141
  156.1 2.6 %fusion.70 = (f32[1024]{0:T(1024)S(1)}, f32[1024,1024]{0,1:T(8,128)S(1)}) fusion(bf16[1024,1024]{0,1:T(8,128)(2,1)S(1)} %bitcast.104, bf16[1024,1024]{1,0:T(8,128)(2,1)S(1)} %copy-done, bf16[1,1024,1024]{1,2,0:T(8,128)(2,1)S(1)} %copy-done.1), kind=kOutput, calls=%fused_computation.103 | convolution fusion | flops 2150628352 | bytes 10489856 | tf_op jit(solution)/shard_map/dot_general | solution.py:150
  158.8 1.9 copy-done.2
  161.2 10.7 %fusion.31 = f32[1024,1024]{0,1:T(8,128)} fusion(bf16[1024,1024]{1,0:T(8,128)(2,1)} %param.19, bf16[1024,1024]{1,0:T(8,128)(2,1)} %param.18, f32[1024,1024]{0,1:T(8,128)} %copy-done.2, f32[1024]{0:T(1024)S(1)} %copy-done.7, f32[1024]{0:T(1024)S(1)} %add_rsqrt_fusion, f32[1024]{0:T(1024)S(1)} %broadcast_multiply_fusion), kind=kOutput, calls=%fused_computation.46 | convolution fusion | flops 4308598784 | bytes 12595200 | tf_op jit(solution)/shard_map/dot_general | solution.py:157
  171.9 1.7 fusion.60
  173.7 2.8 %collective-permute-done.8 = bf16[1024,2,256]{0,2,1:T(8,128)(2,1)} collective-permute-done((bf16[1024,2,256]{0,2,1:T(8,128)(2,1)S(1)}, bf16[1024,2,256]{0,2,1:T(8,128)(2,1)}, u32[]{:S(2)}, u32[]{:S(2)}) %collective-permute-start.8) | collective-permute-done | bytes 1048608 | tf_op jit(solution)/shard_map/ppermute | solution.py:64
  176.5 2.2 %bitcast_add_fusion = f32[1024,2,256]{0,2,1:T(8,128)S(1)} fusion(bf16[1024,2,256]{0,2,1:T(8,128)(2,1)} %collective-permute-done.8, f32[1024,2,2,256]{0,3,2,1:T(8,128)} %bitcast.92, s32[]{:T(128)S(6)} %select_n.138), kind=kLoop, calls=%fused_computation.54 | loop fusion | flops 1048576 | bytes 5242884 | tf_op jit(solution)/shard_map/add | solution.py:65
  178.7 1.3 copy-done.3
  181.1 14.6 %collective-permute-done.9 = bf16[1024,256]{0,1:T(8,128)(2,1)S(1)} collective-permute-done((bf16[1024,256]{0,1:T(8,128)(2,1)S(1)}, bf16[1024,256]{0,1:T(8,128)(2,1)S(1)}, u32[]{:S(2)}, u32[]{:S(2)}) %collective-permute-start.9) | collective-permute-done | bytes 524320 | tf_op jit(solution)/shard_map/ppermute | solution.py:69
  195.7 1.8 fusion.62
  (57 shorter events, 11.5 us)
Async XLA Ops:
  0.0 156.1 %copy-start = (bf16[1024,1024]{1,0:T(8,128)(2,1)S(1)}, bf16[1024,1024]{1,0:T(8,128)(2,1)}, u32[]{:S(2)}) copy-start(bf16[1024,1024]{1,0:T(8,128)(2,1)} %param.16) | copy-start | bytes 6291460
  3.5 66.5 %all-to-all-start = ((bf16[32,32,2048]{2,1,0:T(8,128)(2,1)}), bf16[32,32,2048]{2,1,0:T(8,128)(2,1)}, u32[]{:S(2)}, u32[]{:S(2)}) async-start(bf16[32,32,2048]{2,1,0:T(8,128)(2,1)} %broadcast_in_dim.21), calls=%async_computation | async-start | bytes 8388608 | tf_op jit(solution)/shard_map/all_to_all | solution.py:39
  12.4 57.7 %copy-start.6 = (f32[1,1024]{1,0:T(1,128)S(1)}, f32[1,1024]{1,0:T(1,128)}, u32[]{:S(2)}) copy-start(f32[1,1024]{1,0:T(1,128)} %param.12) | copy-start | bytes 12292
  16.3 8.9 %collective-permute-start.1 = (bf16[1,1024,1024]{1,2,0:T(8,128)(2,1)}, bf16[1,1024,1024]{1,2,0:T(8,128)(2,1)}, u32[]{:S(2)}, u32[]{:S(2)}) collective-permute-start(bf16[1,1024,1024]{1,2,0:T(8,128)(2,1)} %copy.35), channel_id=1, source_target_pairs={{96,32},{97,33},{98,34},{99,35},{100,36},{101,37},{102,38},{103,39... | collective-permute-start | bytes 6291464 | tf_op jit(solution)/shard_map/ppermute | solution.py:29
  18.3 96.6 %collective-permute-start = (bf16[1,1024,1024]{1,2,0:T(8,128)(2,1)}, bf16[1,1024,1024]{1,2,0:T(8,128)(2,1)}, u32[]{:S(2)}, u32[]{:S(2)}) collective-permute-start(bf16[1,1024,1024]{1,2,0:T(8,128)(2,1)} %copy.35), channel_id=1, source_target_pairs={{96,64},{97,65},{98,66},{99,67},{100,68},{101,69},{102,70},{103,71... | collective-permute-start | bytes 6291464 | tf_op jit(solution)/shard_map/ppermute | solution.py:30
  25.3 89.7 %collective-permute-start.2 = (bf16[1,1024,1024]{1,2,0:T(8,128)(2,1)}, bf16[1,1024,1024]{1,2,0:T(8,128)(2,1)}, u32[]{:S(2)}, u32[]{:S(2)}) collective-permute-start(bf16[1,1024,1024]{1,2,0:T(8,128)(2,1)} %collective-permute-done.1), channel_id=1, source_target_pairs={{32,0},{33,1},{34,2},{35,3},{36,4},{37,5},{38,6},{39,7},{40,8},{41... | collective-permute-start | bytes 6291464 | tf_op jit(solution)/shard_map/ppermute | solution.py:31
  83.2 31.0 %all-to-all-start.1 = ((f32[32,33,128]{2,1,0:T(8,128)}), f32[32,33,128]{2,1,0:T(8,128)S(1)}, u32[]{:S(2)}, u32[]{:S(2)}) async-start(f32[32,33,128]{2,1,0:T(8,128)} %reshape.149), calls=%async_computation.1 | async-start | bytes 1310720 | tf_op jit(solution)/shard_map/all_to_all | solution.py:127
  93.0 1.3 collective-permute-start.6
  93.7 2.0 %collective-permute-start.5 = (f32[1024]{0:T(1024)S(1)}, f32[1024]{0:T(1024)S(1)}, u32[]{:S(2)}, u32[]{:S(2)}) collective-permute-start(f32[1024]{0:T(1024)S(1)} %bitcast.102), channel_id=1, source_target_pairs={{96,64},{97,65},{98,66},{99,67},{100,68},{101,69},{102,70},{103,71... | collective-permute-start | bytes 12296 | tf_op jit(solution)/shard_map/ppermute | solution.py:30
  94.4 19.8 %collective-permute-start.7 = (f32[1024]{0:T(1024)S(1)}, f32[1024]{0:T(1024)S(1)}, u32[]{:S(2)}, u32[]{:S(2)}) collective-permute-start(f32[1024]{0:T(1024)S(1)} %collective-permute-done.6), channel_id=1, source_target_pairs={{32,0},{33,1},{34,2},{35,3},{36,4},{37,5},{38,6},{39,7},{40,8},{41... | collective-permute-start | bytes 12296 | tf_op jit(solution)/shard_map/ppermute | solution.py:31
  114.3 5.6 %collective-permute-start.3 = (bf16[33,128]{1,0:T(8,128)(2,1)S(1)}, bf16[33,128]{1,0:T(8,128)(2,1)S(1)}, u32[]{:S(2)}, u32[]{:S(2)}) collective-permute-start(bf16[33,128]{1,0:T(8,128)(2,1)S(1)} %reduce_sum.84), channel_id=1, source_target_pairs={{0,32},{32,0},{64,96},{96,64},{1,33},{33,1},{65,97},{97,65},{2,34}... | collective-permute-start | bytes 25352 | tf_op jit(solution)/shard_map/ppermute | solution.py:45
  119.9 5.4 %collective-permute-start.4 = (bf16[2,33,128]{2,1,0:T(8,128)(2,1)S(1)}, bf16[2,33,128]{2,1,0:T(8,128)(2,1)S(1)}, u32[]{:S(2)}, u32[]{:S(2)}) collective-permute-start(bf16[2,33,128]{2,1,0:T(8,128)(2,1)S(1)} %maximum_select_fusion.1), channel_id=1, source_target_pairs={{0,64},{64,0},{32,96},{96,32},{1,65},{65,1},{33,97},{97,33},{2,66}... | collective-permute-start | bytes 50696 | tf_op jit(solution)/shard_map/ppermute | solution.py:48
  126.6 23.2 %all-to-all-start.2 = ((bf16[32,4,33,128]{3,1,2,0:T(4,128)(2,1)}), bf16[32,4,33,128]{3,1,2,0:T(4,128)(2,1)S(1)}, u32[]{:S(2)}, u32[]{:S(2)}) async-start(bf16[32,4,33,128]{3,1,2,0:T(4,128)(2,1)} %broadcast_in_dim.24), calls=%async_computation.2 | async-start | bytes 2162688 | tf_op jit(solution)/shard_map/all_to_all | solution.py:39
  143.1 1.3 copy-start.4
  149.8 2.8 %copy-start.5 = (bf16[128,8,8,128]{3,2,1,0:T(8,128)(2,1)S(1)}, bf16[128,8,8,128]{3,2,1,0:T(8,128)(2,1)}, u32[]{:S(2)}) copy-start(bf16[128,8,8,128]{3,2,1,0:T(8,128)(2,1)} %copy.56) | copy-start | bytes 6291460
  152.5 3.5 %copy-start.1 = (bf16[1,1024,1024]{1,2,0:T(8,128)(2,1)S(1)}, bf16[1,1024,1024]{1,2,0:T(8,128)(2,1)}, u32[]{:S(2)}) copy-start(bf16[1,1024,1024]{1,2,0:T(8,128)(2,1)} %get-tuple-element.6) | copy-start | bytes 6291460
  158.7 1.9 copy-start.2
  158.7 2.4 %copy-start.7 = (f32[1024]{0:T(1024)S(1)}, f32[1024]{0:T(1024)}, u32[]{:S(2)}) copy-start(f32[1024]{0:T(1024)} %param.17) | copy-start | bytes 12292
  173.6 2.9 %collective-permute-start.8 = (bf16[1024,2,256]{0,2,1:T(8,128)(2,1)S(1)}, bf16[1024,2,256]{0,2,1:T(8,128)(2,1)}, u32[]{:S(2)}, u32[]{:S(2)}) collective-permute-start(bf16[1024,2,256]{0,2,1:T(8,128)(2,1)S(1)} %fusion.60), channel_id=1, source_target_pairs={{0,32},{32,0},{64,96},{96,64},{1,33},{33,1},{65,97},{97,65},{2,34}... | collective-permute-start | bytes 3145736 | tf_op jit(solution)/shard_map/ppermute | solution.py:64
  178.7 1.3 copy-start.3
  180.1 15.5 %collective-permute-start.9 = (bf16[1024,256]{0,1:T(8,128)(2,1)S(1)}, bf16[1024,256]{0,1:T(8,128)(2,1)S(1)}, u32[]{:S(2)}, u32[]{:S(2)}) collective-permute-start(bf16[1024,256]{0,1:T(8,128)(2,1)S(1)} %fusion.64), channel_id=1, source_target_pairs={{0,64},{64,0},{32,96},{96,32},{1,65},{65,1},{33,97},{97,33},{2,66}... | collective-permute-start | bytes 1572872 | tf_op jit(solution)/shard_map/ppermute | solution.py:69
